TPU v7x, 32 devices: a whole 2x2x4 slice. The times are simulated.
32 devices in a mesh: req: 8 (over z, x), grp: 4 (over y, core).
Axes of the slice: x: 2, y: 2, z: 4, core: 2. Of those that a mesh axis runs over, the one named last changes fastest.
Arguments:
- residual: bfloat16 [8192, 2048], P('req', 'grp'), may hold values from -6 to 6
- queries: bfloat16 [8192, 2048], P('req', 'grp'), may hold values from -26 to 26
- new_keys: bfloat16 [8192, 512], P('req', 'grp'), may hold values from -26 to 26
- new_values: bfloat16 [8192, 512], P('req', 'grp'), may hold values from -6 to 6
- pool_keys: bfloat16 [36864, 512], P('req', 'grp'), may hold values from -6 to 6
- pool_values: bfloat16 [36864, 512], P('req', 'grp'), may hold values from -6 to 6
- cache_len: int32 [64], P('req'), may hold values from 1 to 512, as said below
- prefix_group: int32 [64], P('req'), may hold values from 0 to 7, as said below
- prefix_len: int32 [64], P('req'), may hold values from 0 to 512, as said below
- span_rows: int32 [8], replicated, may hold values from 0 to 1008, as said below
- span_offset: int32 [8], P('req'), may hold values from 0 to 512
- out_weight: bfloat16 [2048, 2048], P('grp'), may hold values from -0.125 to 0.125
- norm_gain: float32 [2048], replicated, may hold values from 0.1 to 1.9
- gate_weight: bfloat16 [2048, 4096], P(None, 'grp'), may hold values from -0.125 to 0.125
- up_weight: bfloat16 [2048, 4096], P(None, 'grp'), may hold values from -0.125 to 0.125
- down_weight: bfloat16 [4096, 2048], P('grp'), may hold values from -0.09375 to 0.09375
Outputs:
- layer_out: bfloat16 [8192, 2048], P('req', 'grp')
Inputs may be any that keep to these rules, and one draw needn't show every extreme that they name: `cache_len`: the first decode request of every req index has a cache of 512 positions. `prefix_group`: the slot, within its req index, of the first request of the group; at or before the request's own slot; a group's requests stand in consecutive slots. `prefix_len`: equal within a group and at most the cache length of each of its requests; some request shares 512 positions. `span_rows`: exactly 4 req indices hold a span of 1008 rows, the others none.
All inputs are finite; a program needn't handle non-finite values.
Results may differ from a plain program's by a relative error of at most 0.014.
Values may be sent and summed in bfloat16 or wider, within the bound.
No kernel may reach another device: no remote copies, remote signals or barrier semaphores. Data moves between devices by JAX's collectives and lax.ppermute only.
A program may use at most 128 MiB of HBM per device.

v0:
```python
import jax
import jax.numpy as jnp
from jax import lax
from jax.sharding import PartitionSpec as P

HEADS = 32
KV_HEADS = 8
HEAD_DIM = 64
DEC = 8
BAL = 512
REG = 512


MASKED_SCORE = -1e30


def attend(query_rows, key_rows, value_rows, allowed):
    scores = jnp.dot(query_rows, key_rows.T, preferred_element_type=jnp.float32) * query_rows.shape[
        1
    ] ** (-0.5)
    scores = jnp.where(allowed, scores, MASKED_SCORE)
    highest = jnp.max(scores, axis=1, keepdims=True)
    expval = jnp.exp(scores - highest)
    totals = jnp.sum(expval, axis=1, keepdims=True)
    probs = (expval / totals).astype(jnp.bfloat16)
    return jnp.dot(probs, value_rows, preferred_element_type=jnp.float32).astype(jnp.bfloat16)


def build_masks(cache_len, prefix_group, prefix_len, span_count, span_start, total_rows):
    position = jnp.arange(DEC * REG, dtype=jnp.int32)
    region = position // REG
    offset = position % REG
    request = jnp.arange(DEC, dtype=jnp.int32)
    shared = (region[None, :] == prefix_group[:, None]) & (offset[None, :] < prefix_len[:, None])
    owned = (
        (region[None, :] == request[:, None])
        & (offset[None, :] >= prefix_len[:, None])
        & (offset[None, :] < cache_len[:, None])
    )
    decode_mask = jnp.concatenate([shared | owned, jnp.eye(DEC, dtype=jnp.bool_)], axis=1)
    span_total = total_rows - DEC
    within = jnp.arange(span_total, dtype=jnp.int32)
    in_span = within < span_count
    earlier = jnp.arange(REG, dtype=jnp.int32)
    prior = (earlier[None, :] < span_start) & in_span[:, None]
    lowest = jnp.where(in_span, 0, within)
    causal = (within[None, :] >= lowest[:, None]) & (within[None, :] <= within[:, None])
    span_mask = jnp.concatenate([prior, causal], axis=1)
    return (decode_mask, span_mask)


def attention(queries, new_keys, new_values, pool_keys, pool_values, decode_mask, span_mask):
    head_count = queries.shape[1] // HEAD_DIM
    per_kv = HEADS // KV_HEADS
    split_at = DEC * REG

    def one_head(head):
        query_rows = lax.dynamic_slice_in_dim(queries, head * HEAD_DIM, HEAD_DIM, 1)
        column = head // per_kv * HEAD_DIM
        fresh_keys = lax.dynamic_slice_in_dim(new_keys, column, HEAD_DIM, 1)
        fresh_values = lax.dynamic_slice_in_dim(new_values, column, HEAD_DIM, 1)
        cached_keys = lax.dynamic_slice_in_dim(pool_keys, column, HEAD_DIM, 1)
        cached_values = lax.dynamic_slice_in_dim(pool_values, column, HEAD_DIM, 1)
        decode_out = attend(
            query_rows[:DEC],
            jnp.concatenate([cached_keys[:split_at], fresh_keys[:DEC]], axis=0),
            jnp.concatenate([cached_values[:split_at], fresh_values[:DEC]], axis=0),
            decode_mask,
        )
        span_out = attend(
            query_rows[DEC:],
            jnp.concatenate([cached_keys[split_at:], fresh_keys[DEC:]], axis=0),
            jnp.concatenate([cached_values[split_at:], fresh_values[DEC:]], axis=0),
            span_mask,
        )
        return jnp.concatenate([decode_out, span_out], axis=0)

    outputs = lax.map(one_head, jnp.arange(head_count, dtype=jnp.int32))
    return jnp.transpose(outputs, (1, 0, 2)).reshape(queries.shape[0], head_count * HEAD_DIM)


def finish(attn_rows, resid_rows, out_weight, norm_gain, gate_weight, up_weight, down_weight):
    partial_value = jnp.dot(attn_rows, out_weight, preferred_element_type=jnp.float32)
    proj_cols = lax.psum_scatter(
        partial_value.astype(jnp.bfloat16), "grp", scatter_dimension=1, tiled=True
    ).astype(jnp.float32)
    state_cols = (resid_rows.astype(jnp.float32) + proj_cols).astype(jnp.bfloat16)
    state_full = lax.all_gather(state_cols, "grp", axis=1, tiled=True)
    state32 = state_full.astype(jnp.float32)
    normed = (
        state32 * lax.rsqrt(jnp.mean(state32 * state32, axis=1, keepdims=True) + 1e-05) * norm_gain
    ).astype(jnp.bfloat16)
    gate = jnp.dot(normed, gate_weight, preferred_element_type=jnp.float32)
    upval = jnp.dot(normed, up_weight, preferred_element_type=jnp.float32)
    inner = (jax.nn.silu(gate) * upval).astype(jnp.bfloat16)
    down_cols = lax.psum_scatter(
        jnp.dot(inner, down_weight, preferred_element_type=jnp.float32).astype(jnp.bfloat16),
        "grp",
        scatter_dimension=1,
        tiled=True,
    ).astype(jnp.float32)
    return (state_cols.astype(jnp.float32) + down_cols).astype(jnp.bfloat16)


def shards(
    residual,
    queries,
    new_keys,
    new_values,
    pool_keys,
    pool_values,
    cache_len,
    prefix_group,
    prefix_len,
    span_rows,
    span_offset,
    out_weight,
    norm_gain,
    gate_weight,
    up_weight,
    down_weight,
):
    total_rows = residual.shape[0]
    width = residual.shape[1]
    device = lax.axis_index("req")
    devices = lax.axis_size("req")
    own_span = span_rows[device]
    decode_mask, span_mask = build_masks(
        cache_len, prefix_group, prefix_len, own_span, span_offset[0], total_rows
    )
    attn = attention(queries, new_keys, new_values, pool_keys, pool_values, decode_mask, span_mask)
    row_index = jnp.arange(total_rows, dtype=jnp.int32)
    is_live = row_index < DEC + own_span
    zero_value = jnp.zeros((), jnp.bfloat16)
    counts = DEC + span_rows
    first = jnp.sum(jnp.where(jnp.arange(devices, dtype=jnp.int32) < device, counts, 0))
    target = jnp.where(is_live, first + row_index, -1)
    bucket = (total_rows - DEC + devices - 1) // devices
    owner_dev = jnp.where(is_live, target % devices, devices)
    bucket_pos = jnp.where(is_live, row_index // devices, 0)
    send_attn = (
        jnp.zeros((devices, bucket, width), jnp.bfloat16)
        .at[owner_dev, bucket_pos]
        .set(attn, mode="drop")
    )
    send_resid = (
        jnp.zeros((devices, bucket, width), jnp.bfloat16)
        .at[owner_dev, bucket_pos]
        .set(residual, mode="drop")
    )
    send_target = (
        jnp.full((devices, bucket), -1, jnp.int32)
        .at[owner_dev, bucket_pos]
        .set(target, mode="drop")
    )
    got_attn, got_resid, got_target = (
        lax.all_to_all(send_attn, "req", split_axis=0, concat_axis=0, tiled=True),
        lax.all_to_all(send_resid, "req", split_axis=0, concat_axis=0, tiled=True),
        lax.all_to_all(send_target, "req", split_axis=0, concat_axis=0, tiled=True),
    )
    flat_target = got_target.reshape(-1)
    has_row = flat_target >= 0
    bal_slot = jnp.where(has_row, flat_target // devices, BAL)
    dense_attn = (
        jnp.zeros((BAL, width), jnp.bfloat16)
        .at[bal_slot]
        .set(got_attn.reshape(-1, width), mode="drop")
    )
    dense_resid = (
        jnp.zeros((BAL, width), jnp.bfloat16)
        .at[bal_slot]
        .set(got_resid.reshape(-1, width), mode="drop")
    )
    mixed = finish(
        dense_attn, dense_resid, out_weight, norm_gain, gate_weight, up_weight, down_weight
    )
    picked = jnp.where(has_row[:, None], mixed[jnp.minimum(bal_slot, BAL - 1)], zero_value)
    returned = lax.all_to_all(
        picked.reshape(devices, bucket, width), "req", split_axis=0, concat_axis=0, tiled=True
    )
    layer_out = jnp.where(
        is_live[:, None], returned[jnp.minimum(owner_dev, devices - 1), bucket_pos], zero_value
    )
    return layer_out


def solution(mesh):
    placed = (
        P("req", "grp"),
        P("req", "grp"),
        P("req", "grp"),
        P("req", "grp"),
        P("req", "grp"),
        P("req", "grp"),
        P("req"),
        P("req"),
        P("req"),
        P(),
        P("req"),
        P("grp", None),
        P(),
        P(None, "grp"),
        P(None, "grp"),
        P("grp", None),
    )
    return jax.shard_map(
        shards, mesh=mesh, in_specs=placed, out_specs=P("req", "grp"), check_vma=False
    )
```

profile of v0, /device:TPU:0, one launch (start us, length us, event | category | flops | bytes accessed | tf_op | source)
XLA Modules:
  0.0 414.9 jit_solution(9925079914877743265)
XLA Ops:
  13.4 4.3 %scatter_custom_fusion.2 = s32[1016]{0:T(1024)S(1)} fusion(s32[1024]{0:T(1024)S(1)} %get-tuple-element.165, s32[1024]{0:T(1024)S(1)} %add_select_fusion.1, s32[]{:T(128)} %constant.165.clone.1), kind=kCustom, calls=%fused_computation.122 | custom fusion | bytes 4068
  18.4 7.3 %all-to-all-start = ((s32[8,1,127]{2,1,0:T(1,128)}), s32[8,1,127]{2,1,0:T(1,128)}, u32[]{:S(2)}, u32[]{:S(2)}) async-start(s32[8,1,127]{2,1,0:T(1,128)} %bitcast.3), calls=%async_computation | async-start | bytes 8192 | tf_op jit(solution)/shard_map/all_to_all | solution.py:159
  32.1 151.4 %while.12 = (s32[]{:T(128)}, bf16[8,1024,64]{1,2,0:T(8,128)(2,1)}, s32[8]{0:T(128)}, bf16[1024,512]{1,0:T(8,128)(2,1)}, bf16[4608,128]{1,0:T(8,128)(2,1)S(1)}, /...) while((s32[]{:T(128)}, bf16[8,1024,64]{1,2,0:T(8,128)(2,1)}, ...), condition=%wide.region_9.10_spmd, body=%wide.region_4.9_spmd.sunk | while | flops 421723168 | bytes 31715728 | solution.py:78
  38.5 3.2 fusion.80
  43.2 2.2 fusion.82
  57.4 3.2 fusion.80
  76.4 3.2 fusion.80
  95.3 3.2 fusion.80
  114.2 3.2 fusion.80
  133.2 3.2 fusion.80
  137.9 2.2 fusion.82
  152.1 3.2 fusion.80
  171.0 3.2 fusion.80
  183.5 2.3 copy.35
  185.8 5.8 %scatter_custom_fusion.4 = bf16[1016,512]{1,0:T(8,128)(2,1)S(1)} fusion(s32[1024]{0:T(1024)} %get-tuple-element.164, bf16[1024,512]{1,0:T(8,128)(2,1)} %copy.35, bf16[]{:T(256)} %constant.170.clone.1), kind=kCustom, calls=%fused_computation.64 | custom fusion | bytes 1040896
  192.9 6.0 %all-to-all-start.2 = ((bf16[8,127,512]{2,1,0:T(8,128)(2,1)}), bf16[8,127,512]{2,1,0:T(8,128)(2,1)S(1)}, u32[]{:S(2)}, u32[]{:S(2)}) async-start(bf16[8,127,512]{2,1,0:T(8,128)(2,1)} %copy.36), calls=%async_computation.2 | async-start | bytes 2097152 | tf_op jit(solution)/shard_map/all_to_all | solution.py:157
  201.1 23.3 %all-to-all-done.2 = bf16[8,127,512]{2,1,0:T(8,128)(2,1)S(1)} async-done(((bf16[8,127,512]{2,1,0:T(8,128)(2,1)}), bf16[8,127,512]{2,1,0:T(8,128)(2,1)S(1)}, u32[]{:S(2)}, u32[]{:S(2)}) %all-to-all-start.2) | async-done | bytes 1040416 | tf_op jit(solution)/shard_map/all_to_all | solution.py:157
  225.6 6.3 %scatter_custom_fusion.1 = bf16[512,512]{1,0:T(8,128)(2,1)S(1)} fusion(s32[1016]{0:T(1024)S(1)} %bitcast.38, bf16[1016,512]{1,0:T(8,128)(2,1)} %reshape.365, bf16[]{:T(256)} %constant.170.clone.1), kind=kCustom, calls=%fused_computation.68 | custom fusion | bytes 524800 | tf_op jit(solution)/shard_map/scatter | solution.py:167
  232.0 2.6 convolution_convert_fusion.2
  234.7 5.8 %scatter_custom_fusion.3 = bf16[1016,512]{1,0:T(8,128)(2,1)S(1)} fusion(s32[1024]{0:T(1024)} %get-tuple-element.164, bf16[1024,512]{1,0:T(8,128)(2,1)} %param.18, bf16[]{:T(256)} %constant.170.clone.1), kind=kCustom, calls=%fused_computation.66 | custom fusion | bytes 1040896
  240.9 29.1 %all_to_all.24 = bf16[8,127,512]{2,1,0:T(8,128)(2,1)S(1)} all-to-all(bf16[8,127,512]{2,1,0:T(8,128)(2,1)S(1)} %copy.34), channel_id=1, replica_groups=mesh['req'=8,'grp'=4] {'req'}, dimensions={0} | all-to-all | bytes 2080768 | tf_op jit(solution)/shard_map/all_to_all | solution.py:158
  271.2 6.3 %scatter_custom_fusion = bf16[512,512]{1,0:T(8,128)(2,1)S(1)} fusion(s32[1016]{0:T(1024)S(1)} %bitcast.39, bf16[1016,512]{1,0:T(8,128)(2,1)} %reshape.357, bf16[]{:T(256)} %constant.170.clone.1), kind=kCustom, calls=%fused_computation.70 | custom fusion | bytes 524800 | tf_op jit(solution)/shard_map/scatter | solution.py:172
  279.9 21.6 %all-gather.2.cloned.1.call-done = bf16[512,2048]{1,0:T(8,128)(2,1)} async-done(((bf16[512,512]{1,0:T(8,128)(2,1)}), bf16[512,2048]{1,0:T(8,128)(2,1)}) %all-gather.2.cloned.1.call-update) | async-done | bytes 2097168 | tf_op jit(solution)/shard_map/all_gather | solution.py:88
  301.4 2.2 fusion.27
  303.7 5.9 %fusion.33 = f32[512,1024]{1,0:T(8,128)} fusion(bf16[2048,1024]{1,0:T(8,128)(2,1)} %param.31, bf16[512,2048]{1,0:T(8,128)(2,1)S(1)} %copy-done.6, f32[2048]{0:T(1024)S(1)} %copy-done.8, f32[512]{0:T(512)S(1)} %add_rsqrt_fusion), kind=kOutput, calls=%fused_computation.63 | convolution fusion | flops 2151677952 | bytes 8398848 | tf_op jit(solution)/shard_map/dot_general | solution.py:93
  309.6 10.6 %convolution_convert_fusion.1 = bf16[512,2048]{1,0:T(8,128)(2,1)} fusion(bf16[1024,2048]{1,0:T(8,128)(2,1)} %param.33, f32[512,1024]{1,0:T(8,128)} %fusion.33, bf16[2048,1024]{1,0:T(8,128)(2,1)} %param.32, bf16[512,2048]{1,0:T(8,128)(2,1)} %all-gather.2.cloned.1.call-done, f32[2048]{0:T(1024)S(1)} %copy-done.8, f32[512]{0:T(512)S(1)} %add_rsqrt_fusion), kind=kOutput, calls=%fused_computation.55 | convolution fusion | flops 4303355904 | bytes 14690304 | tf_op jit(solution)/shard_map/dot_general | solution.py:97
  321.0 30.8 %reduce-scatter.5.cloned.1.call-done = bf16[512,512]{1,0:T(8,128)(2,1)} async-done(((bf16[512,2048]{1,0:T(8,128)(2,1)}), bf16[512,512]{1,0:T(8,128)(2,1)}) %reduce-scatter.5.cloned.1.call-update) | async-done | bytes 524304 | tf_op jit(solution)/shard_map/reduce_scatter | solution.py:96
  353.0 5.1 %gather_fusion = bf16[1016,512]{1,0:T(8,128)(2,1)} fusion(bf16[512,512]{1,0:T(8,128)(2,1)S(1)} %add_convert_fusion, s32[1024]{0:T(1024)S(1)} %pad_clamp_fusion), kind=kCustom, calls=%fused_computation | custom fusion | bytes 2084832 | tf_op jit(solution)/shard_map/gather | solution.py:177
  360.8 5.5 %all-to-all-start.3 = ((bf16[8,127,512]{2,1,0:T(8,128)(2,1)}), bf16[8,127,512]{2,1,0:T(8,128)(2,1)}, u32[]{:S(2)}, u32[]{:S(2)}) async-start(bf16[8,127,512]{2,1,0:T(8,128)(2,1)} %broadcast_select_fusion.1), calls=%async_computation.5 | async-start | bytes 2097152 | tf_op jit(solution)/shard_map/all_to_all | solution.py:178
  367.0 25.2 %all-to-all-done.3 = bf16[8,127,512]{2,1,0:T(8,128)(2,1)} async-done(((bf16[8,127,512]{2,1,0:T(8,128)(2,1)}), bf16[8,127,512]{2,1,0:T(8,128)(2,1)}, u32[]{:S(2)}, u32[]{:S(2)}) %all-to-all-start.3) | async-done | bytes 1040416 | tf_op jit(solution)/shard_map/all_to_all | solution.py:178
  394.0 12.0 %gather_fusion.1 = bf16[1024,512]{1,0:T(8,128)(2,1)} fusion(bf16[8,127,512]{2,0,1:T(8,128)(2,1)S(1)} %copy.37, s32[1024]{0:T(1024)S(1)} %bitcast.33), kind=kCustom, calls=%fused_computation.1 | custom fusion | bytes 2105344 | tf_op jit(solution)/shard_map/gather | solution.py:182
  406.0 2.4 broadcast_select_fusion
  (217 shorter events, 121.3 us)
Async XLA Ops:
  6.5 225.5 %copy-start = (bf16[512,2048]{1,0:T(8,128)(2,1)S(1)}, bf16[512,2048]{1,0:T(8,128)(2,1)}, u32[]{:S(2)}) copy-start(bf16[512,2048]{1,0:T(8,128)(2,1)} %param.29) | copy-start | bytes 6291460
  18.4 174.6 %all-to-all-start = ((s32[8,1,127]{2,1,0:T(1,128)}), s32[8,1,127]{2,1,0:T(1,128)}, u32[]{:S(2)}, u32[]{:S(2)}) async-start(s32[8,1,127]{2,1,0:T(1,128)} %bitcast.3), calls=%async_computation | async-start | bytes 8192 | tf_op jit(solution)/shard_map/all_to_all | solution.py:159
  27.6 4.5 %copy-start.1 = (bf16[4608,128]{1,0:T(8,128)(2,1)S(1)}, bf16[4608,128]{1,0:T(8,128)(2,1)}, u32[]{:S(2)}) copy-start(bf16[4608,128]{1,0:T(8,128)(2,1)} %param.22) | copy-start | bytes 3538948
  27.6 4.5 %copy-start.3 = (bf16[1024,128]{1,0:T(8,128)(2,1)S(1)}, bf16[1024,128]{1,0:T(8,128)(2,1)}, u32[]{:S(2)}) copy-start(bf16[1024,128]{1,0:T(8,128)(2,1)} %param.20) | copy-start | bytes 786436
  41.8 1.0 copy-start.4
  41.8 1.4 copy-start.2
  45.5 0.8 copy-start.7
  60.7 1.0 copy-start.4
  60.7 1.4 copy-start.2
  64.4 0.8 copy-start.7
  79.6 1.0 copy-start.4
  79.6 1.4 copy-start.2
  98.5 1.0 copy-start.4
  98.5 1.4 copy-start.2
  117.5 1.0 copy-start.4
  117.5 1.4 copy-start.2
  121.2 0.8 copy-start.7
  136.4 1.0 copy-start.4
  136.4 1.4 copy-start.2
  155.3 1.0 copy-start.4
  155.3 1.4 copy-start.2
  174.2 1.0 copy-start.4
  174.3 1.4 copy-start.2
  178.0 0.8 copy-start.7
  192.9 31.4 %all-to-all-start.2 = ((bf16[8,127,512]{2,1,0:T(8,128)(2,1)}), bf16[8,127,512]{2,1,0:T(8,128)(2,1)S(1)}, u32[]{:S(2)}, u32[]{:S(2)}) async-start(bf16[8,127,512]{2,1,0:T(8,128)(2,1)} %copy.36), calls=%async_computation.2 | async-start | bytes 2097152 | tf_op jit(solution)/shard_map/all_to_all | solution.py:157
  198.9 78.7 %reduce-scatter.3.cloned.1.call-start = ((), (), s32[]{:S(2)}) async-start(), calls=%async_computation.6 | async-start | bytes 2621440 | tf_op jit(solution)/shard_map/reduce_scatter | solution.py:84
  234.7 66.8 %all-gather.2.cloned.1.call-start = ((), (), s32[]{:S(2)}) async-start(), calls=%async_computation.7 | async-start | bytes 2621440 | tf_op jit(solution)/shard_map/all_gather | solution.py:88
  277.6 26.1 %copy-start.8 = (f32[2048]{0:T(1024)S(1)}, f32[2048]{0:T(1024)}, u32[]{:S(2)}) copy-start(f32[2048]{0:T(1024)} %param.30) | copy-start | bytes 24580
  279.6 72.3 %reduce-scatter.5.cloned.1.call-start = ((), (), s32[]{:S(2)}) async-start(), calls=%async_computation.8 | async-start | bytes 2621440 | tf_op jit(solution)/shard_map/reduce_scatter | solution.py:96
  301.4 2.2 copy-start.6
  320.2 31.6 %copy-start.5 = (bf16[512,512]{1,0:T(8,128)(2,1)S(1)}, bf16[512,512]{1,0:T(8,128)(2,1)}, u32[]{:S(2)}) copy-start(bf16[512,512]{1,0:T(8,128)(2,1)} %add_convert_fusion.1) | copy-start | bytes 1572868
  360.8 31.4 %all-to-all-start.3 = ((bf16[8,127,512]{2,1,0:T(8,128)(2,1)}), bf16[8,127,512]{2,1,0:T(8,128)(2,1)}, u32[]{:S(2)}, u32[]{:S(2)}) async-start(bf16[8,127,512]{2,1,0:T(8,128)(2,1)} %broadcast_select_fusion.1), calls=%async_computation.5 | async-start | bytes 2097152 | tf_op jit(solution)/shard_map/all_to_all | solution.py:178
  (4 other events, 3.0 us)
Sparse Core Ops, SparseCore 0:
  234.8 30.2 reduce-scatter.2
  279.7 21.6 all-gather.1
  320.4 31.4 reduce-scatter.4
where the time goes:
time: 418 us; the launch traced here: 415 us
  waiting for transfers between devices  101 us (24%)
  local copies, waits for them, and re-layouts  98.6 us (24%)
  matrix products  79.5 us (19%)
  other arithmetic  44.7 us (11%)
  blocking collectives  29.1 us (7%)
  loops' own time  28.2 us (7%)
  starting transfers between devices  19.1 us (5%)
  between operations  14.8 us (4%)
    dot_general x16, matrix products, attend(): jnp.dot(query_rows, key_rows.T, preferred_element_type=jnp.float32)  35.5 us
    reduce_scatter x1, waiting for transfers between devices, finish(): lax.psum_scatter(jnp.dot(inner, down_weight, preferred_element_type=jnp.f...  30.8 us
    all_to_all x1, blocking collectives, shards(): lax.all_to_all(send_resid, 'req', split_axis=0, concat_axis=0, tiled=True)  29.1 us
    another operation x1, loops' own time, attention(): outputs = lax.map(one_head, jnp.arange(head_count, dtype=jnp.int32))  28.2 us
    all_to_all x1, waiting for transfers between devices, shards(): lax.all_to_all(picked.reshape(devices, bucket, width), 'req', split_axis=...  25.2 us
    dot_general x16, matrix products, attend(): jnp.dot(probs, value_rows, preferred_element_type=jnp.float32)  24.8 us
    all_to_all x1, waiting for transfers between devices, shards(): lax.all_to_all(send_attn, 'req', split_axis=0, concat_axis=0, tiled=True)  23.3 us
    all_gather x1, waiting for transfers between devices, finish(): state_full = lax.all_gather(state_cols, 'grp', axis=1, tiled=True)  21.6 us
  transfers between devices with their start and end apart: 6, of which 4 were waited for; matrix products, arithmetic and copies ran while one was open for 37% of the time, Pallas kernels for 0%

commit v1 on v0

--- a/solution.py
+++ b/solution.py
@@ -1,6 +1,8 @@
 import jax
 import jax.numpy as jnp
 from jax import lax
+from jax.experimental import pallas as pl
+from jax.experimental.pallas import tpu as pltpu
 from jax.sharding import PartitionSpec as P
 
 HEADS = 32
@@ -14,19 +16,103 @@
 MASKED_SCORE = -1e30
 
 
-def attend(query_rows, key_rows, value_rows, allowed):
-    scores = jnp.dot(query_rows, key_rows.T, preferred_element_type=jnp.float32) * query_rows.shape[
-        1
-    ] ** (-0.5)
-    scores = jnp.where(allowed, scores, MASKED_SCORE)
-    highest = jnp.max(scores, axis=1, keepdims=True)
-    expval = jnp.exp(scores - highest)
-    totals = jnp.sum(expval, axis=1, keepdims=True)
-    probs = (expval / totals).astype(jnp.bfloat16)
-    return jnp.dot(probs, value_rows, preferred_element_type=jnp.float32).astype(jnp.bfloat16)
-
-
-def build_masks(cache_len, prefix_group, prefix_len, span_count, span_start, total_rows):
+SCALE = HEAD_DIM ** (-0.5)
+QBLK = 256
+
+
+def span_kernel(start_ref, q_ref, kp_ref, vp_ref, kf_ref, vf_ref, o_ref):
+    span_start = start_ref[0]
+    q_all = q_ref[0]
+    kp = kp_ref[0]
+    vp = vp_ref[0]
+    rows = q_all.shape[0]
+    prior = kp.shape[0]
+    for blk in range(rows // QBLK):
+        lo = blk * QBLK
+        hi = lo + QBLK
+        q = q_all[lo:hi]
+        kf = kf_ref[0, 0:hi]
+        vf = vf_ref[0, 0:hi]
+        s_p = lax.dot_general(
+            q, kp, (((1,), (1,)), ((), ())), preferred_element_type=jnp.float32
+        ) * SCALE
+        s_f = lax.dot_general(
+            q, kf, (((1,), (1,)), ((), ())), preferred_element_type=jnp.float32
+        ) * SCALE
+        t_p = lax.broadcasted_iota(jnp.int32, (QBLK, prior), 1)
+        s_p = jnp.where(t_p < span_start, s_p, MASKED_SCORE)
+        q_pos = lax.broadcasted_iota(jnp.int32, (QBLK, hi), 0) + lo
+        k_pos = lax.broadcasted_iota(jnp.int32, (QBLK, hi), 1)
+        seen = (k_pos >= DEC) & (k_pos <= q_pos)
+        s_f = jnp.where(seen, s_f, MASKED_SCORE)
+        highest = jnp.maximum(
+            jnp.max(s_p, axis=1, keepdims=True), jnp.max(s_f, axis=1, keepdims=True)
+        )
+        e_p = jnp.exp(s_p - highest)
+        e_f = jnp.exp(s_f - highest)
+        totals = jnp.sum(e_p, axis=1, keepdims=True) + jnp.sum(e_f, axis=1, keepdims=True)
+        p_p = (e_p / totals).astype(jnp.bfloat16)
+        p_f = (e_f / totals).astype(jnp.bfloat16)
+        out = jnp.dot(p_p, vp, preferred_element_type=jnp.float32) + jnp.dot(
+            p_f, vf, preferred_element_type=jnp.float32
+        )
+        o_ref[0, lo:hi, :] = out.astype(o_ref.dtype)
+
+
+def span_attention(q_heads, kp_heads, vp_heads, kf_heads, vf_heads, span_start):
+    heads, rows, dim = q_heads.shape
+    prior = kp_heads.shape[1]
+    per_kv = heads // kp_heads.shape[0]
+    q_spec = pl.BlockSpec((1, rows, dim), lambda h, s: (h, 0, 0))
+    p_spec = pl.BlockSpec((1, prior, dim), lambda h, s: (h // per_kv, 0, 0))
+    f_spec = pl.BlockSpec((1, rows, dim), lambda h, s: (h // per_kv, 0, 0))
+    flops = 4 * heads * rows * (prior + rows // 2) * dim
+    cost = pl.CostEstimate(
+        flops=flops,
+        transcendentals=heads * rows * (prior + rows // 2),
+        bytes_accessed=2 * (2 * heads * rows * dim + 4 * (prior + rows) * dim),
+    )
+    return pl.pallas_call(
+        span_kernel,
+        out_shape=jax.ShapeDtypeStruct((heads, rows, dim), jnp.bfloat16),
+        grid_spec=pltpu.PrefetchScalarGridSpec(
+            num_scalar_prefetch=1,
+            grid=(heads,),
+            in_specs=[q_spec, p_spec, p_spec, f_spec, f_spec],
+            out_specs=q_spec,
+        ),
+        cost_estimate=cost,
+    )(span_start.reshape(1).astype(jnp.int32), q_heads, kp_heads, vp_heads, kf_heads, vf_heads)
+
+
+def decode_attention(queries, new_keys, new_values, pool_keys, pool_values, decode_mask):
+    kv = new_keys.shape[1] // HEAD_DIM
+    per_kv = queries.shape[1] // HEAD_DIM // kv
+    cached = DEC * REG
+    q = queries[:DEC].reshape(DEC, kv, per_kv, HEAD_DIM)
+    kc = pool_keys[:cached].reshape(cached, kv, HEAD_DIM)
+    vc = pool_values[:cached].reshape(cached, kv, HEAD_DIM)
+    kn = new_keys[:DEC].reshape(DEC, kv, HEAD_DIM)
+    vn = new_values[:DEC].reshape(DEC, kv, HEAD_DIM)
+    s_c = jnp.einsum("rjhd,tjd->rjht", q, kc, preferred_element_type=jnp.float32) * SCALE
+    s_n = jnp.einsum("rjhd,tjd->rjht", q, kn, preferred_element_type=jnp.float32) * SCALE
+    s_c = jnp.where(decode_mask[:, None, None, :cached], s_c, MASKED_SCORE)
+    s_n = jnp.where(decode_mask[:, None, None, cached:], s_n, MASKED_SCORE)
+    highest = jnp.maximum(
+        jnp.max(s_c, axis=3, keepdims=True), jnp.max(s_n, axis=3, keepdims=True)
+    )
+    e_c = jnp.exp(s_c - highest)
+    e_n = jnp.exp(s_n - highest)
+    totals = jnp.sum(e_c, axis=3, keepdims=True) + jnp.sum(e_n, axis=3, keepdims=True)
+    p_c = (e_c / totals).astype(jnp.bfloat16)
+    p_n = (e_n / totals).astype(jnp.bfloat16)
+    out = jnp.einsum("rjht,tjd->rjhd", p_c, vc, preferred_element_type=jnp.float32) + jnp.einsum(
+        "rjht,tjd->rjhd", p_n, vn, preferred_element_type=jnp.float32
+    )
+    return out.astype(jnp.bfloat16).reshape(DEC, kv * per_kv * HEAD_DIM)
+
+
+def build_decode_mask(cache_len, prefix_group, prefix_len):
     position = jnp.arange(DEC * REG, dtype=jnp.int32)
     region = position // REG
     offset = position % REG
@@ -37,46 +123,31 @@
         & (offset[None, :] >= prefix_len[:, None])
         & (offset[None, :] < cache_len[:, None])
     )
-    decode_mask = jnp.concatenate([shared | owned, jnp.eye(DEC, dtype=jnp.bool_)], axis=1)
-    span_total = total_rows - DEC
-    within = jnp.arange(span_total, dtype=jnp.int32)
-    in_span = within < span_count
-    earlier = jnp.arange(REG, dtype=jnp.int32)
-    prior = (earlier[None, :] < span_start) & in_span[:, None]
-    lowest = jnp.where(in_span, 0, within)
-    causal = (within[None, :] >= lowest[:, None]) & (within[None, :] <= within[:, None])
-    span_mask = jnp.concatenate([prior, causal], axis=1)
-    return (decode_mask, span_mask)
-
-
-def attention(queries, new_keys, new_values, pool_keys, pool_values, decode_mask, span_mask):
-    head_count = queries.shape[1] // HEAD_DIM
-    per_kv = HEADS // KV_HEADS
-    split_at = DEC * REG
-
-    def one_head(head):
-        query_rows = lax.dynamic_slice_in_dim(queries, head * HEAD_DIM, HEAD_DIM, 1)
-        column = head // per_kv * HEAD_DIM
-        fresh_keys = lax.dynamic_slice_in_dim(new_keys, column, HEAD_DIM, 1)
-        fresh_values = lax.dynamic_slice_in_dim(new_values, column, HEAD_DIM, 1)
-        cached_keys = lax.dynamic_slice_in_dim(pool_keys, column, HEAD_DIM, 1)
-        cached_values = lax.dynamic_slice_in_dim(pool_values, column, HEAD_DIM, 1)
-        decode_out = attend(
-            query_rows[:DEC],
-            jnp.concatenate([cached_keys[:split_at], fresh_keys[:DEC]], axis=0),
-            jnp.concatenate([cached_values[:split_at], fresh_values[:DEC]], axis=0),
-            decode_mask,
-        )
-        span_out = attend(
-            query_rows[DEC:],
-            jnp.concatenate([cached_keys[split_at:], fresh_keys[DEC:]], axis=0),
-            jnp.concatenate([cached_values[split_at:], fresh_values[DEC:]], axis=0),
-            span_mask,
-        )
-        return jnp.concatenate([decode_out, span_out], axis=0)
-
-    outputs = lax.map(one_head, jnp.arange(head_count, dtype=jnp.int32))
-    return jnp.transpose(outputs, (1, 0, 2)).reshape(queries.shape[0], head_count * HEAD_DIM)
+    return jnp.concatenate([shared | owned, jnp.eye(DEC, dtype=jnp.bool_)], axis=1)
+
+
+def attention(queries, new_keys, new_values, pool_keys, pool_values, decode_mask, span_start):
+    rows = queries.shape[0]
+    heads = queries.shape[1] // HEAD_DIM
+    kv = new_keys.shape[1] // HEAD_DIM
+    cached = DEC * REG
+
+    def head_major(x, n):
+        return jnp.transpose(x.reshape(x.shape[0], n, HEAD_DIM), (1, 0, 2))
+
+    span_heads = span_attention(
+        head_major(queries, heads),
+        head_major(pool_keys[cached:], kv),
+        head_major(pool_values[cached:], kv),
+        head_major(new_keys, kv),
+        head_major(new_values, kv),
+        span_start,
+    )
+    span_rows = jnp.transpose(span_heads, (1, 0, 2)).reshape(rows, heads * HEAD_DIM)
+    decode_rows = decode_attention(
+        queries, new_keys, new_values, pool_keys, pool_values, decode_mask
+    )
+    return jnp.concatenate([decode_rows, span_rows[DEC:]], axis=0)
 
 
 def finish(attn_rows, resid_rows, out_weight, norm_gain, gate_weight, up_weight, down_weight):
@@ -125,10 +196,10 @@
     device = lax.axis_index("req")
     devices = lax.axis_size("req")
     own_span = span_rows[device]
-    decode_mask, span_mask = build_masks(
-        cache_len, prefix_group, prefix_len, own_span, span_offset[0], total_rows
-    )
-    attn = attention(queries, new_keys, new_values, pool_keys, pool_values, decode_mask, span_mask)
+    decode_mask = build_decode_mask(cache_len, prefix_group, prefix_len)
+    attn = attention(
+        queries, new_keys, new_values, pool_keys, pool_values, decode_mask, span_offset[0]
+    )
     row_index = jnp.arange(total_rows, dtype=jnp.int32)
     is_live = row_index < DEC + own_span
     zero_value = jnp.zeros((), jnp.bfloat16)

time: 418 us -> 315 us (0.75)
  matrix products: 79.5 us -> 22.8 us
  loops' own time: 28.2 us -> 0 us
  Pallas kernels: 0 us -> 26 us
  other arithmetic: 44.7 us -> 21.6 us
  local copies, waits for them, and re-layouts: 98.6 us -> 77.8 us
    dot_general x32 -> x4, matrix products: 60.3 us -> 3.67 us  [the longest x1 1.68 us: decode_attention(): jnp.einsum('rjht,tjd->rjhd', p_c, vc, preferred_element_type=jnp.float32)]
    another operation x1 -> x0, loops' own time: 28.2 us -> none  [attention(): outputs = lax.map(one_head, jnp.arange(head_count, dtype=jnp.int32))]
    pallas_call x0 -> x1, Pallas kernels: none -> 26 us  [span_attention(): pl.pallas_call(span_kernel, out_shape=jax.ShapeDtypeStruct((heads, rows,...]
    dynamic_update_slice x8 -> x0, other arithmetic: 13.3 us -> none  [attention(): outputs = lax.map(one_head, jnp.arange(head_count, dtype=jnp.int32))]
    dynamic_slice x8 -> x0, local copies, waits for them, and re-layouts: 10.6 us -> none  [attention(): outputs = lax.map(one_head, jnp.arange(head_count, dtype=jnp.int32))]
    reduce_sum x16 -> x2, other arithmetic: 9.65 us -> 0.34 us  [the longest x1 0.31 us: decode_attention(): jnp.sum(e_c, axis=3, keepdims=True) + jnp.sum(e_n, axis=3, keepdims=True)]
    slice x48 -> x17, local copies, waits for them, and re-layouts: 20.7 us -> 14.3 us  [the longest x3 6.27 us: attention(): return jnp.concatenate([decode_rows, span_rows[DEC:]], axis=0)]
    reshape x1 -> x9, local copies, waits for them, and re-layouts: 2.29 us -> 8.43 us  [the longest x5 7.5 us: head_major(): return jnp.transpose(x.reshape(x.shape[0], n, HEAD_DIM), (1, 0, 2))]
  transfers between devices with their start and end apart: 6 -> 6, of which waited for: 4 -> 4; matrix products, arithmetic and copies ran while one was open for 37% -> 17% of each run, Pallas kernels for 0% -> 8%
where the time goes in v1:
time: 315 us; the launch traced here: 314 us
  waiting for transfers between devices  102 us (32%)
  local copies, waits for them, and re-layouts  77.8 us (25%)
  blocking collectives  29.1 us (9%)
  Pallas kernels  26 us (8%)
  matrix products  22.8 us (7%)
  other arithmetic  21.6 us (7%)
  starting transfers between devices  19.3 us (6%)
  between operations  14.8 us (5%)
    reduce_scatter x1, waiting for transfers between devices, finish(): lax.psum_scatter(jnp.dot(inner, down_weight, preferred_element_type=jnp.f...  31.6 us
    all_to_all x1, blocking collectives, shards(): lax.all_to_all(send_resid, 'req', split_axis=0, concat_axis=0, tiled=True)  29.1 us
    pallas_call x1, Pallas kernels, span_attention(): pl.pallas_call(span_kernel, out_shape=jax.ShapeDtypeStruct((heads, rows,...  26 us
    all_to_all x1, waiting for transfers between devices, shards(): lax.all_to_all(picked.reshape(devices, bucket, width), 'req', split_axis=...  25.2 us
    all_to_all x1, waiting for transfers between devices, shards(): lax.all_to_all(send_attn, 'req', split_axis=0, concat_axis=0, tiled=True)  23.9 us
    all_gather x1, waiting for transfers between devices, finish(): state_full = lax.all_gather(state_cols, 'grp', axis=1, tiled=True)  21.6 us
    unnamed x35, local copies, waits for them, and re-layouts  15.3 us
    gather x1, local copies, waits for them, and re-layouts, shards(): returned[jnp.minimum(owner_dev, devices - 1), bucket_pos]  12 us
  transfers between devices with their start and end apart: 6, of which 4 were waited for; matrix products, arithmetic and copies ran while one was open for 17% of the time, Pallas kernels for 8%

profile of v1, /device:TPU:0, one launch (start us, length us, event | category | flops | bytes accessed | tf_op | source)
XLA Modules:
  0.0 313.6 jit_solution(12382049341726479632)
XLA Ops:
  13.4 4.3 %scatter_custom_fusion.2 = s32[1016]{0:T(1024)S(1)} fusion(s32[1024]{0:T(1024)S(1)} %get-tuple-element.10, s32[1024]{0:T(1024)S(1)} %add_select_fusion.1, s32[]{:T(128)} %constant.92.clone.1), kind=kCustom, calls=%fused_computation.100 | custom fusion | bytes 4068
  18.4 7.3 %all-to-all-start = ((s32[8,1,127]{2,1,0:T(1,128)}), s32[8,1,127]{2,1,0:T(1,128)S(1)}, u32[]{:S(2)}, u32[]{:S(2)}) async-start(s32[8,1,127]{2,1,0:T(1,128)} %bitcast.1), calls=%async_computation | async-start | bytes 8192 | tf_op jit(solution)/shard_map/all_to_all | solution.py:230
  28.0 1.8 copy.88
  29.8 2.4 slice.27
  33.3 2.3 copy.72
  38.8 2.3 copy.76
  41.8 1.8 copy.81
  43.6 2.0 copy.87
  45.7 1.9 copy.89
  52.1 26.0 %shard_map.154 = bf16[8,1024,64]{2,1,0:T(8,128)(2,1)} custom-call(s32[1]{0:T(128)S(6)} %copy.119.start_ref, bf16[8,1024,64]{2,1,0:T(8,128)(2,1)} %bitcast.61, bf16[2,512,64]{2,1,0:T(8,128)(2,1)} %bitcast.70, bf16[2,512,64]{2,1,0:T(8,128)(2,1)} %bitcast.71, bf16[2,1024,64]{2,1,0:T(8,128)(2,1)} %bitcast.68, bf16[2,1024,64]{2,1,0:T(8,128)(2,1)} %bitcast.69), custom_call_target="tpu_custom_call" | custom-call | flops 2147483648 | bytes 2883584 | tf_op jit(solution)/shard_map/pallas_call | solution.py:75
  78.2 3.1 slice.40
  81.3 1.9 copy.90
  84.5 5.8 %scatter_custom_fusion.4 = bf16[1016,512]{1,0:T(8,128)(2,1)S(1)} fusion(s32[1024]{0:T(1024)} %get-tuple-element.9, bf16[1016,512]{1,0:T(8,128)(2,1)} %copy.91, bf16[]{:T(256)} %constant.146, bf16[8,512]{1,0:T(8,128)(2,1)S(1)} %reshape.472, bf16[]{:T(256)} %constant.97.clone.1), kind=kCustom, calls=%fused_computation.24 | custom fusion | flops 2097152 | bytes 2089984
  91.6 6.0 %all-to-all-start.2 = ((bf16[8,127,512]{2,1,0:T(8,128)(2,1)}), bf16[8,127,512]{2,1,0:T(8,128)(2,1)S(1)}, u32[]{:S(2)}, u32[]{:S(2)}) async-start(bf16[8,127,512]{2,1,0:T(8,128)(2,1)} %copy.92), calls=%async_computation.2 | async-start | bytes 2097152 | tf_op jit(solution)/shard_map/all_to_all | solution.py:228
  99.1 23.9 %all-to-all-done.2 = bf16[8,127,512]{2,1,0:T(8,128)(2,1)S(1)} async-done(((bf16[8,127,512]{2,1,0:T(8,128)(2,1)}), bf16[8,127,512]{2,1,0:T(8,128)(2,1)S(1)}, u32[]{:S(2)}, u32[]{:S(2)}) %all-to-all-start.2) | async-done | bytes 1040416 | tf_op jit(solution)/shard_map/all_to_all | solution.py:228
  124.3 6.3 %scatter_custom_fusion.1 = bf16[512,512]{1,0:T(8,128)(2,1)S(1)} fusion(s32[1016]{0:T(1024)S(1)} %bitcast.76, bf16[1016,512]{1,0:T(8,128)(2,1)} %reshape.518, bf16[]{:T(256)} %constant.97.clone.1), kind=kCustom, calls=%fused_computation.40 | custom fusion | bytes 524800 | tf_op jit(solution)/shard_map/scatter | solution.py:238
  130.7 2.6 convolution_convert_fusion.1
  133.4 5.8 %scatter_custom_fusion.3 = bf16[1016,512]{1,0:T(8,128)(2,1)S(1)} fusion(s32[1024]{0:T(1024)} %get-tuple-element.9, bf16[1024,512]{1,0:T(8,128)(2,1)} %param.16, bf16[]{:T(256)} %constant.97.clone.1), kind=kCustom, calls=%fused_computation.38 | custom fusion | bytes 1040896
  139.5 29.1 %all_to_all.24 = bf16[8,127,512]{2,1,0:T(8,128)(2,1)S(1)} all-to-all(bf16[8,127,512]{2,1,0:T(8,128)(2,1)S(1)} %copy.71), channel_id=1, replica_groups=mesh['req'=8,'grp'=4] {'req'}, dimensions={0} | all-to-all | bytes 2080768 | tf_op jit(solution)/shard_map/all_to_all | solution.py:229
  169.9 6.3 %scatter_custom_fusion = bf16[512,512]{1,0:T(8,128)(2,1)S(1)} fusion(s32[1016]{0:T(1024)S(1)} %bitcast.77, bf16[1016,512]{1,0:T(8,128)(2,1)} %reshape.510, bf16[]{:T(256)} %constant.97.clone.1), kind=kCustom, calls=%fused_computation.42 | custom fusion | bytes 524800 | tf_op jit(solution)/shard_map/scatter | solution.py:243
  176.3 2.0 add_convert_fusion.1
  178.5 21.6 %all-gather.2.cloned.1.call-done = bf16[512,2048]{1,0:T(8,128)(2,1)} async-done(((bf16[512,512]{1,0:T(8,128)(2,1)}), bf16[512,2048]{1,0:T(8,128)(2,1)}) %all-gather.2.cloned.1.call-update) | async-done | bytes 2097168 | tf_op jit(solution)/shard_map/all_gather | solution.py:159
  200.1 2.2 fusion.2
  202.3 5.9 %fusion.16 = f32[512,1024]{1,0:T(8,128)} fusion(bf16[2048,1024]{1,0:T(8,128)(2,1)} %param.29, bf16[512,2048]{1,0:T(8,128)(2,1)S(1)} %copy-done.4, f32[2048]{0:T(1024)S(1)} %copy-done.13, f32[512]{0:T(512)S(1)} %add_rsqrt_fusion), kind=kOutput, calls=%fused_computation.35 | convolution fusion | flops 2151677952 | bytes 8398848 | tf_op jit(solution)/shard_map/dot_general | solution.py:164
  208.3 10.6 %convolution_convert_fusion = bf16[512,2048]{1,0:T(8,128)(2,1)} fusion(bf16[1024,2048]{1,0:T(8,128)(2,1)} %param.31, f32[512,1024]{1,0:T(8,128)} %fusion.16, bf16[2048,1024]{1,0:T(8,128)(2,1)} %param.30, bf16[512,2048]{1,0:T(8,128)(2,1)} %all-gather.2.cloned.1.call-done, f32[2048]{0:T(1024)S(1)} %copy-done.13, f32[512]{0:T(512)S(1)} %add_rsqrt_fusion), kind=kOutput, calls=%fused_computation.15 | convolution fusion | flops 4303355904 | bytes 14690304 | tf_op jit(solution)/shard_map/dot_general | solution.py:168
  218.9 31.6 %reduce-scatter.5.cloned.1.call-done = bf16[512,512]{1,0:T(8,128)(2,1)} async-done(((bf16[512,2048]{1,0:T(8,128)(2,1)}), bf16[512,512]{1,0:T(8,128)(2,1)}) %reduce-scatter.5.cloned.1.call-update) | async-done | bytes 524304 | tf_op jit(solution)/shard_map/reduce_scatter | solution.py:167
  251.7 5.1 %gather_fusion = bf16[1016,512]{1,0:T(8,128)(2,1)} fusion(bf16[512,512]{1,0:T(8,128)(2,1)S(1)} %add_convert_fusion, s32[1024]{0:T(1024)S(1)} %pad_clamp_fusion), kind=kCustom, calls=%fused_computation | custom fusion | bytes 2084832 | tf_op jit(solution)/shard_map/gather | solution.py:248
  259.5 5.5 %all-to-all-start.3 = ((bf16[8,127,512]{2,1,0:T(8,128)(2,1)}), bf16[8,127,512]{2,1,0:T(8,128)(2,1)}, u32[]{:S(2)}, u32[]{:S(2)}) async-start(bf16[8,127,512]{2,1,0:T(8,128)(2,1)} %broadcast_select_fusion.1), calls=%async_computation.5 | async-start | bytes 2097152 | tf_op jit(solution)/shard_map/all_to_all | solution.py:249
  265.7 25.2 %all-to-all-done.3 = bf16[8,127,512]{2,1,0:T(8,128)(2,1)} async-done(((bf16[8,127,512]{2,1,0:T(8,128)(2,1)}), bf16[8,127,512]{2,1,0:T(8,128)(2,1)}, u32[]{:S(2)}, u32[]{:S(2)}) %all-to-all-start.3) | async-done | bytes 1040416 | tf_op jit(solution)/shard_map/all_to_all | solution.py:249
  290.8 1.8 copy.93
  292.7 12.0 %gather_fusion.1 = bf16[1024,512]{1,0:T(8,128)(2,1)} fusion(bf16[8,127,512]{2,0,1:T(8,128)(2,1)S(1)} %copy.93, s32[1024]{0:T(1024)S(1)} %bitcast.55), kind=kCustom, calls=%fused_computation.1 | custom fusion | bytes 2105344 | tf_op jit(solution)/shard_map/gather | solution.py:253
  304.6 2.4 broadcast_select_fusion
  (95 shorter events, 30.0 us)
Async XLA Ops:
  6.5 124.1 %copy-start = (bf16[512,2048]{1,0:T(8,128)(2,1)S(1)}, bf16[512,2048]{1,0:T(8,128)(2,1)}, u32[]{:S(2)}) copy-start(bf16[512,2048]{1,0:T(8,128)(2,1)} %param.27) | copy-start | bytes 6291460
  6.5 20.6 %copy-start.6 = (bf16[1024,128]{1,0:T(8,128)(2,1)S(1)}, bf16[1024,128]{1,0:T(8,128)(2,1)}, u32[]{:S(2)}) copy-start(bf16[1024,128]{1,0:T(8,128)(2,1)} %param.18) | copy-start | bytes 786436
  18.4 73.3 %all-to-all-start = ((s32[8,1,127]{2,1,0:T(1,128)}), s32[8,1,127]{2,1,0:T(1,128)S(1)}, u32[]{:S(2)}, u32[]{:S(2)}) async-start(s32[8,1,127]{2,1,0:T(1,128)} %bitcast.1), calls=%async_computation | async-start | bytes 8192 | tf_op jit(solution)/shard_map/all_to_all | solution.py:230
  29.8 2.4 copy-start.5
  29.8 3.4 %slice-start.2 = ((bf16[1024,512]{1,0:T(8,128)(2,1)}), bf16[8,512]{1,0:T(8,128)(2,1)S(1)}, s32[]{:S(2)}) async-start(bf16[1024,512]{1,0:T(8,128)(2,1)} %param.17), calls=%async_computation.11 | async-start | bytes 16384 | tf_op jit(solution)/shard_map/slice | solution.py:92
  32.1 3.5 %slice-start.3 = ((bf16[1024,128]{1,0:T(8,128)(2,1)}), bf16[8,128]{1,0:T(8,128)(2,1)S(1)}, s32[]{:S(2)}) async-start(bf16[1024,128]{1,0:T(8,128)(2,1)} %param.18), calls=%async_computation.12 | async-start | bytes 4096 | tf_op jit(solution)/shard_map/slice | solution.py:95
  32.1 3.5 %copy-start.10 = (s32[8]{0:T(128)S(1)}, s32[8]{0:T(128)}, u32[]{:S(2)}) copy-start(s32[8]{0:T(128)} %param.22) | copy-start | bytes 100
  32.2 3.5 %copy-start.11 = (s32[8]{0:T(128)S(1)}, s32[8]{0:T(128)}, u32[]{:S(2)}) copy-start(s32[8]{0:T(128)} %param.23) | copy-start | bytes 100
  32.2 3.5 %copy-start.12 = (s32[8]{0:T(128)S(1)}, s32[8]{0:T(128)}, u32[]{:S(2)}) copy-start(s32[8]{0:T(128)} %param.24) | copy-start | bytes 100
  37.4 1.0 copy-start.2
  37.4 3.7 %slice-start.4 = ((bf16[1024,128]{1,0:T(8,128)(2,1)}), bf16[8,128]{1,0:T(8,128)(2,1)S(1)}, s32[]{:S(2)}) async-start(bf16[1024,128]{1,0:T(8,128)(2,1)} %param.19), calls=%async_computation.13 | async-start | bytes 4096 | tf_op jit(solution)/shard_map/slice | solution.py:96
  37.7 1.1 copy-start.7
  41.8 5.8 %slice-start = ((bf16[4608,128]{1,0:T(8,128)(2,1)}), bf16[512,128]{1,0:T(8,128)(2,1)S(1)}, s32[]{:S(2)}) async-start(bf16[4608,128]{1,0:T(8,128)(2,1)} %param.20), calls=%async_computation.9 | async-start | bytes 262144 | tf_op jit(solution)/shard_map/slice | solution.py:140
  41.8 6.8 %slice-start.1 = ((bf16[4608,128]{1,0:T(8,128)(2,1)}), bf16[512,128]{1,0:T(8,128)(2,1)S(1)}, s32[]{:S(2)}) async-start(bf16[4608,128]{1,0:T(8,128)(2,1)} %param.21), calls=%async_computation.10 | async-start | bytes 262144 | tf_op jit(solution)/shard_map/slice | solution.py:141
  43.6 6.6 %copy-start.3 = (f32[8,2,4,4096]{3,0,2,1:T(8,128)S(1)}, f32[8,2,4,4096]{3,0,2,1:T(8,128)}, u32[]{:S(2)}) copy-start(f32[8,2,4,4096]{3,0,2,1:T(8,128)} %copy-done.2) | copy-start | bytes 3145732
  50.2 1.7 copy-start.8
  50.2 1.7 copy-start.9
  91.6 31.4 %all-to-all-start.2 = ((bf16[8,127,512]{2,1,0:T(8,128)(2,1)}), bf16[8,127,512]{2,1,0:T(8,128)(2,1)S(1)}, u32[]{:S(2)}, u32[]{:S(2)}) async-start(bf16[8,127,512]{2,1,0:T(8,128)(2,1)} %copy.92), calls=%async_computation.2 | async-start | bytes 2097152 | tf_op jit(solution)/shard_map/all_to_all | solution.py:228
  97.6 78.6 %reduce-scatter.3.cloned.1.call-start = ((), (), s32[]{:S(2)}) async-start(), calls=%async_computation.6 | async-start | bytes 2621440 | tf_op jit(solution)/shard_map/reduce_scatter | solution.py:155
  133.3 66.8 %all-gather.2.cloned.1.call-start = ((), (), s32[]{:S(2)}) async-start(), calls=%async_computation.7 | async-start | bytes 2621440 | tf_op jit(solution)/shard_map/all_gather | solution.py:159
  176.2 26.1 %copy-start.13 = (f32[2048]{0:T(1024)S(1)}, f32[2048]{0:T(1024)}, u32[]{:S(2)}) copy-start(f32[2048]{0:T(1024)} %param.28) | copy-start | bytes 24580
  178.3 72.2 %reduce-scatter.5.cloned.1.call-start = ((), (), s32[]{:S(2)}) async-start(), calls=%async_computation.8 | async-start | bytes 2621440 | tf_op jit(solution)/shard_map/reduce_scatter | solution.py:167
  200.1 2.2 copy-start.4
  218.9 31.6 %copy-start.1 = (bf16[512,512]{1,0:T(8,128)(2,1)S(1)}, bf16[512,512]{1,0:T(8,128)(2,1)}, u32[]{:S(2)}) copy-start(bf16[512,512]{1,0:T(8,128)(2,1)} %add_convert_fusion.1) | copy-start | bytes 1572868
  259.5 31.4 %all-to-all-start.3 = ((bf16[8,127,512]{2,1,0:T(8,128)(2,1)}), bf16[8,127,512]{2,1,0:T(8,128)(2,1)}, u32[]{:S(2)}, u32[]{:S(2)}) async-start(bf16[8,127,512]{2,1,0:T(8,128)(2,1)} %broadcast_select_fusion.1), calls=%async_computation.5 | async-start | bytes 2097152 | tf_op jit(solution)/shard_map/all_to_all | solution.py:249
Sparse Core Ops, SparseCore 0:
  133.4 30.2 reduce-scatter.2
  178.4 21.6 all-gather.1
  219.0 31.4 reduce-scatter.4

commit v2 on v1

v2 whole, which is shorter than its diff:
```python
import jax
import jax.numpy as jnp
from jax import lax
from jax.experimental import pallas as pl
from jax.experimental.pallas import tpu as pltpu
from jax.sharding import PartitionSpec as P

HEADS = 32
KV_HEADS = 8
HEAD_DIM = 64
DEC = 8
REG = 512


MASKED_SCORE = -1e30


SCALE = HEAD_DIM ** (-0.5)
QBLK = 256


def span_kernel(start_ref, q_ref, kp_ref, vp_ref, kf_ref, vf_ref, o_ref):
    span_start = start_ref[0]
    first_kv = (pl.program_id(0) * 2 // (HEADS // KV_HEADS)) % 2 == 0
    half = HEAD_DIM

    def pick(ref, lo, hi):
        return jnp.where(first_kv, ref[lo:hi, 0:half], ref[lo:hi, half : 2 * half])

    rows = q_ref.shape[0]
    prior = kp_ref.shape[0]
    kp = pick(kp_ref, 0, prior)
    vp = pick(vp_ref, 0, prior)
    for blk in range(rows // QBLK):
        lo = blk * QBLK
        hi = lo + QBLK
        kf = pick(kf_ref, 0, hi)
        vf = pick(vf_ref, 0, hi)
        t_p = lax.broadcasted_iota(jnp.int32, (QBLK, prior), 1)
        prior_seen = t_p < span_start
        q_pos = lax.broadcasted_iota(jnp.int32, (QBLK, hi), 0) + lo
        k_pos = lax.broadcasted_iota(jnp.int32, (QBLK, hi), 1)
        seen = (k_pos >= DEC) & (k_pos <= q_pos)
        for hh in range(2):
            q = q_ref[lo:hi, hh * half : (hh + 1) * half]
            s_p = lax.dot_general(
                q, kp, (((1,), (1,)), ((), ())), preferred_element_type=jnp.float32
            ) * SCALE
            s_f = lax.dot_general(
                q, kf, (((1,), (1,)), ((), ())), preferred_element_type=jnp.float32
            ) * SCALE
            s_p = jnp.where(prior_seen, s_p, MASKED_SCORE)
            s_f = jnp.where(seen, s_f, MASKED_SCORE)
            highest = jnp.maximum(
                jnp.max(s_p, axis=1, keepdims=True), jnp.max(s_f, axis=1, keepdims=True)
            )
            e_p = jnp.exp(s_p - highest)
            e_f = jnp.exp(s_f - highest)
            totals = jnp.sum(e_p, axis=1, keepdims=True) + jnp.sum(e_f, axis=1, keepdims=True)
            p_p = (e_p / totals).astype(jnp.bfloat16)
            p_f = (e_f / totals).astype(jnp.bfloat16)
            out = jnp.dot(p_p, vp, preferred_element_type=jnp.float32) + jnp.dot(
                p_f, vf, preferred_element_type=jnp.float32
            )
            o_ref[lo:hi, hh * half : (hh + 1) * half] = out.astype(o_ref.dtype)


def span_attention(queries, pool_keys, pool_values, new_keys, new_values, span_start, cached):
    rows, width = queries.shape
    kv_width = new_keys.shape[1]
    prior = REG
    lanes = 2 * HEAD_DIM
    heads = width // HEAD_DIM
    q_spec = pl.BlockSpec((rows, lanes), lambda c, s: (0, c))
    p_spec = pl.BlockSpec((prior, kv_width), lambda c, s: (cached // prior, 0))
    f_spec = pl.BlockSpec((rows, kv_width), lambda c, s: (0, 0))
    flops = 4 * heads * rows * (prior + rows // 2) * HEAD_DIM
    cost = pl.CostEstimate(
        flops=flops,
        transcendentals=heads * rows * (prior + rows // 2),
        bytes_accessed=2 * (2 * rows * width + 2 * (prior + rows) * kv_width),
    )
    return pl.pallas_call(
        span_kernel,
        out_shape=jax.ShapeDtypeStruct((rows, width), jnp.bfloat16),
        grid_spec=pltpu.PrefetchScalarGridSpec(
            num_scalar_prefetch=1,
            grid=(width // lanes,),
            in_specs=[q_spec, p_spec, p_spec, f_spec, f_spec],
            out_specs=q_spec,
        ),
        cost_estimate=cost,
    )(span_start.reshape(1).astype(jnp.int32), queries, pool_keys, pool_values, new_keys, new_values)


def decode_attention(queries, new_keys, new_values, pool_keys, pool_values, decode_mask):
    kv = new_keys.shape[1] // HEAD_DIM
    per_kv = queries.shape[1] // HEAD_DIM // kv
    cached = DEC * REG
    q = queries[:DEC].reshape(DEC, kv, per_kv, HEAD_DIM)
    kc = pool_keys[:cached].reshape(cached, kv, HEAD_DIM)
    vc = pool_values[:cached].reshape(cached, kv, HEAD_DIM)
    kn = new_keys[:DEC].reshape(DEC, kv, HEAD_DIM)
    vn = new_values[:DEC].reshape(DEC, kv, HEAD_DIM)
    s_c = jnp.einsum("rjhd,tjd->rjht", q, kc, preferred_element_type=jnp.float32) * SCALE
    s_n = jnp.einsum("rjhd,tjd->rjht", q, kn, preferred_element_type=jnp.float32) * SCALE
    s_c = jnp.where(decode_mask[:, None, None, :cached], s_c, MASKED_SCORE)
    s_n = jnp.where(decode_mask[:, None, None, cached:], s_n, MASKED_SCORE)
    highest = jnp.maximum(
        jnp.max(s_c, axis=3, keepdims=True), jnp.max(s_n, axis=3, keepdims=True)
    )
    e_c = jnp.exp(s_c - highest)
    e_n = jnp.exp(s_n - highest)
    totals = jnp.sum(e_c, axis=3, keepdims=True) + jnp.sum(e_n, axis=3, keepdims=True)
    p_c = (e_c / totals).astype(jnp.bfloat16)
    p_n = (e_n / totals).astype(jnp.bfloat16)
    out = jnp.einsum("rjht,tjd->rjhd", p_c, vc, preferred_element_type=jnp.float32) + jnp.einsum(
        "rjht,tjd->rjhd", p_n, vn, preferred_element_type=jnp.float32
    )
    return out.astype(jnp.bfloat16).reshape(DEC, kv * per_kv * HEAD_DIM)


def build_decode_mask(cache_len, prefix_group, prefix_len):
    position = jnp.arange(DEC * REG, dtype=jnp.int32)
    region = position // REG
    offset = position % REG
    request = jnp.arange(DEC, dtype=jnp.int32)
    shared = (region[None, :] == prefix_group[:, None]) & (offset[None, :] < prefix_len[:, None])
    owned = (
        (region[None, :] == request[:, None])
        & (offset[None, :] >= prefix_len[:, None])
        & (offset[None, :] < cache_len[:, None])
    )
    return jnp.concatenate([shared | owned, jnp.eye(DEC, dtype=jnp.bool_)], axis=1)


def attention(queries, new_keys, new_values, pool_keys, pool_values, decode_mask, span_start):
    cached = DEC * REG
    span_rows = span_attention(
        queries, pool_keys, pool_values, new_keys, new_values, span_start, cached
    )
    decode_rows = decode_attention(
        queries, new_keys, new_values, pool_keys, pool_values, decode_mask
    )
    return lax.dynamic_update_slice(span_rows, decode_rows, (0, 0))


def finish(attn_rows, resid_rows, out_weight, norm_gain, gate_weight, up_weight, down_weight):
    partial_value = jnp.dot(attn_rows, out_weight, preferred_element_type=jnp.float32)
    proj_cols = lax.psum_scatter(
        partial_value.astype(jnp.bfloat16), "grp", scatter_dimension=1, tiled=True
    ).astype(jnp.float32)
    state_cols = (resid_rows.astype(jnp.float32) + proj_cols).astype(jnp.bfloat16)
    state_full = lax.all_gather(state_cols, "grp", axis=1, tiled=True)
    state32 = state_full.astype(jnp.float32)
    normed = (
        state32 * lax.rsqrt(jnp.mean(state32 * state32, axis=1, keepdims=True) + 1e-05) * norm_gain
    ).astype(jnp.bfloat16)
    gate = jnp.dot(normed, gate_weight, preferred_element_type=jnp.float32)
    upval = jnp.dot(normed, up_weight, preferred_element_type=jnp.float32)
    inner = (jax.nn.silu(gate) * upval).astype(jnp.bfloat16)
    down_cols = lax.psum_scatter(
        jnp.dot(inner, down_weight, preferred_element_type=jnp.float32).astype(jnp.bfloat16),
        "grp",
        scatter_dimension=1,
        tiled=True,
    ).astype(jnp.float32)
    return (state_cols.astype(jnp.float32) + down_cols).astype(jnp.bfloat16)


def shards(
    residual,
    queries,
    new_keys,
    new_values,
    pool_keys,
    pool_values,
    cache_len,
    prefix_group,
    prefix_len,
    span_rows,
    span_offset,
    out_weight,
    norm_gain,
    gate_weight,
    up_weight,
    down_weight,
):
    total_rows = residual.shape[0]
    width = residual.shape[1]
    device = lax.axis_index("req")
    devices = lax.axis_size("req")
    bucket = (total_rows - DEC + devices - 1) // devices
    spread = bucket * devices
    bal = total_rows // 2
    counts = DEC + span_rows
    ends = jnp.cumsum(counts)
    firsts = ends - counts
    first = firsts[device]
    own_count = counts[device]
    shift = first % devices

    def outbound(rows):
        grid = rows[:spread].reshape(bucket, devices, rows.shape[1])
        return jnp.transpose(jnp.roll(grid, shift, axis=1), (1, 0, 2))

    send_resid = outbound(residual)
    got_resid = lax.all_to_all(send_resid, "req", split_axis=0, concat_axis=0, tiled=True)
    decode_mask = build_decode_mask(cache_len, prefix_group, prefix_len)
    attn = attention(
        queries, new_keys, new_values, pool_keys, pool_values, decode_mask, span_offset[0]
    )
    got_attn = lax.all_to_all(outbound(attn), "req", split_axis=0, concat_axis=0, tiled=True)

    slots = jnp.arange(bal, dtype=jnp.int32)
    wanted = slots * devices + device
    src_dev = jnp.sum((ends[None, :] <= wanted[:, None]).astype(jnp.int32), axis=1)
    src_dev = jnp.minimum(src_dev, devices - 1)
    src_pos = jnp.clip((wanted - firsts[src_dev]) // devices, 0, bucket - 1)
    flat_idx = src_dev * bucket + src_pos
    dense_attn = got_attn.reshape(spread, width)[flat_idx]
    dense_resid = got_resid.reshape(spread, width)[flat_idx]
    mixed = finish(
        dense_attn, dense_resid, out_weight, norm_gain, gate_weight, up_weight, down_weight
    )
    lane = (device - firsts) % devices
    row_of = jnp.arange(bucket, dtype=jnp.int32)[None, :] * devices + lane[:, None]
    back_valid = row_of < counts[:, None]
    back_slot = jnp.clip((firsts[:, None] + row_of) // devices, 0, bal - 1)
    picked = jnp.where(
        back_valid[:, :, None], mixed[back_slot.reshape(-1)].reshape(devices, bucket, width), 0
    ).astype(jnp.bfloat16)
    returned = lax.all_to_all(picked, "req", split_axis=0, concat_axis=0, tiled=True)
    restored = jnp.roll(jnp.transpose(returned, (1, 0, 2)), -shift, axis=1).reshape(spread, width)
    if spread < total_rows:
        restored = jnp.concatenate(
            [restored, jnp.zeros((total_rows - spread, width), restored.dtype)], axis=0
        )
    is_live = jnp.arange(total_rows, dtype=jnp.int32) < own_count
    return jnp.where(is_live[:, None], restored, jnp.zeros((), jnp.bfloat16))


def solution(mesh):
    placed = (
        P("req", "grp"),
        P("req", "grp"),
        P("req", "grp"),
        P("req", "grp"),
        P("req", "grp"),
        P("req", "grp"),
        P("req"),
        P("req"),
        P("req"),
        P(),
        P("req"),
        P("grp", None),
        P(),
        P(None, "grp"),
        P(None, "grp"),
        P("grp", None),
    )
    return jax.shard_map(
        shards, mesh=mesh, in_specs=placed, out_specs=P("req", "grp"), check_vma=False
    )
```

time: 315 us -> 253 us (0.80)
  local copies, waits for them, and re-layouts: 77.8 us -> 27 us
  starting transfers between devices: 19.3 us -> 12.9 us
  waiting for transfers between devices: 102 us -> 98.3 us
  other arithmetic: 21.6 us -> 18.3 us
    scatter x4 -> x0, local copies, waits for them, and re-layouts: 14.3 us -> none  [the longest x1 6.35 us: shards(): dense_resid = jnp.zeros((BAL, width), jnp.bfloat16).at[bal_slot].set(got_...]
    unnamed x35 -> x16, local copies, waits for them, and re-layouts: 15.3 us -> 1.18 us
    unnamed x4 -> x0, other arithmetic: 7.94 us -> none
    gather x3 -> x4, local copies, waits for them, and re-layouts: 18.6 us -> 11 us  [the longest x1 5.08 us: shards(): mixed[back_slot.reshape(-1)].reshape(devices, bucket, width)]
    slice x7 -> x0, local copies, waits for them, and re-layouts: 6.27 us -> none  [the longest x3 6.27 us: attention(): return jnp.concatenate([decode_rows, span_rows[DEC:]], axis=0)]
    all_to_all x3 -> x2, starting transfers between devices: 18.8 us -> 12.8 us  [the longest x1 7.25 us: shards(): lax.all_to_all(outbound(attn), 'req', split_axis=0, concat_axis=0, tiled=...]
    gather x1 -> x5, other arithmetic: 0.01 us -> 5.11 us  [the longest x3 5.1 us: shards(): src_pos = jnp.clip((wanted - firsts[src_dev]) // devices, 0, bucket - 1)]
    all_to_all x3 -> x2, waiting for transfers between devices: 49.1 us -> 45.2 us  [the longest x1 24.6 us: shards(): lax.all_to_all(picked, 'req', split_axis=0, concat_axis=0, tiled=True)]
  transfers between devices with their start and end apart: 6 -> 5, of which waited for: 4 -> 4; matrix products, arithmetic and copies ran while one was open for 17% -> 5% of each run, Pallas kernels for 8% -> 0%
where the time goes in v2:
time: 253 us; the launch traced here: 252 us
  waiting for transfers between devices  98.3 us (39%)
  blocking collectives  29.6 us (12%)
  local copies, waits for them, and re-layouts  27 us (11%)
  Pallas kernels  26.4 us (10%)
  matrix products  23.8 us (9%)
  other arithmetic  18.3 us (7%)
  between operations  16 us (6%)
  starting transfers between devices  12.9 us (5%)
    reduce_scatter x1, waiting for transfers between devices, finish(): lax.psum_scatter(jnp.dot(inner, down_weight, preferred_element_type=jnp.f...  31.3 us
    all_to_all x1, blocking collectives, shards(): lax.all_to_all(send_resid, 'req', split_axis=0, concat_axis=0, tiled=True)  29.6 us
    pallas_call x1, Pallas kernels, span_attention(): pl.pallas_call(span_kernel, out_shape=jax.ShapeDtypeStruct((rows, width),...  26.4 us
    all_to_all x1, waiting for transfers between devices, shards(): lax.all_to_all(picked, 'req', split_axis=0, concat_axis=0, tiled=True)  24.6 us
    all_gather x1, waiting for transfers between devices, finish(): state_full = lax.all_gather(state_cols, 'grp', axis=1, tiled=True)  21.8 us
    all_to_all x1, waiting for transfers between devices, shards(): lax.all_to_all(outbound(attn), 'req', split_axis=0, concat_axis=0, tiled=...  20.6 us
    dot_general x1, matrix products, finish(): jnp.dot(inner, down_weight, preferred_element_type=jnp.float32)  10.6 us
    all_to_all x1, starting transfers between devices, shards(): lax.all_to_all(outbound(attn), 'req', split_axis=0, concat_axis=0, tiled=...  7.25 us
  transfers between devices with their start and end apart: 5, of which 4 were waited for; matrix products, arithmetic and copies ran while one was open for 5% of the time, Pallas kernels for 0%

profile of v2, /device:TPU:0, one launch (start us, length us, event | category | flops | bytes accessed | tf_op | source)
XLA Modules:
  0.0 252.2 jit_solution(7629798635754029841)
XLA Ops:
  6.5 0.8 broadcast_add_fusion
  11.5 2.3 slice.25
  13.8 26.4 %shard_map.154 = bf16[1024,512]{1,0:T(8,128)(2,1)} custom-call(s32[1]{0:T(128)S(6)} %copy.89.start_ref, bf16[1024,512]{1,0:T(8,128)(2,1)} %q_ref.1, bf16[4608,128]{1,0:T(8,128)(2,1)} %kp_ref.1, bf16[4608,128]{1,0:T(8,128)(2,1)} %vp_ref.1, bf16[1024,128]{1,0:T(8,128)(2,1)} %kf_ref.1, bf16[1024,128]{1,0:T(8,128)(2,1)} %vf_ref.1), custom_call_target="tpu_custom_call" | custom-call | flops 2147483648 | bytes 2883584 | tf_op jit(solution)/shard_map/pallas_call | solution.py:83
  40.3 2.3 copy.56
  42.6 1.3 copy.52
  44.3 1.6 fusion.41
  46.5 1.7 fusion.19
  49.1 1.3 slice_bitcast_fusion
  50.7 1.4 fusion.11
  52.1 7.3 %all-to-all-start.1 = ((bf16[8,127,512]{2,1,0:T(8,128)(2,1)}), bf16[8,127,512]{2,1,0:T(8,128)(2,1)}, u32[]{:S(2)}, u32[]{:S(2)}) async-start(bf16[8,127,512]{2,1,0:T(8,128)(2,1)} %fusion.11), calls=%async_computation.1 | async-start | bytes 2097152 | tf_op jit(solution)/shard_map/all_to_all | solution.py:213
  59.5 4.5 %compare_select_fusion.6 = s32[512,1]{0,1:T(1,128)S(1)} fusion(s32[]{:T(128)} %bitcast.8, s32[]{:T(128)} %bitcast.9, s32[]{:T(128)} %bitcast.10, s32[]{:T(128)} %bitcast.11, s32[]{:T(128)} %bitcast.12, s32[]{:T(128)} %bitcast.14, s32[]{:T(128)} %bitcast.13, s32[512,1]{0,1:T(1,128)S(1)} %bitcast.66), kind=kLoop, calls=%fused_computation.74 | loop fusion | flops 7680 | bytes 4124 | tf_op jit(solution)/shard_map/gather | solution.py:219
  64.7 20.6 %all-to-all-done.1 = bf16[8,127,512]{2,1,0:T(8,128)(2,1)} async-done(((bf16[8,127,512]{2,1,0:T(8,128)(2,1)}), bf16[8,127,512]{2,1,0:T(8,128)(2,1)}, u32[]{:S(2)}, u32[]{:S(2)}) %all-to-all-start.1) | async-done | bytes 1040416 | tf_op jit(solution)/shard_map/all_to_all | solution.py:213
  85.2 1.5 reshape.479
  86.8 2.6 %gather_fusion.1 = bf16[512,512]{1,0:T(8,128)(2,1)} fusion(bf16[1016,512]{1,0:T(8,128)(2,1)S(1)} %reshape.479, s32[1024]{0:T(1024)S(1)} %pad_clamp_fusion.1), kind=kCustom, calls=%fused_computation.1 | custom fusion | bytes 1050624 | tf_op jit(solution)/shard_map/gather | solution.py:221
  89.4 3.6 %convolution_convert_fusion.1 = bf16[512,2048]{1,0:T(8,128)(2,1)} fusion(bf16[512,512]{1,0:T(8,128)(2,1)} %gather_fusion.1, bf16[512,2048]{1,0:T(8,128)(2,1)S(1)} %copy-done), kind=kOutput, calls=%fused_computation.12 | convolution fusion | flops 1074790400 | bytes 4718592 | tf_op jit(solution)/shard_map/dot_general | solution.py:149
  93.1 1.1 copy-done.3
  95.0 29.6 %all_to_all.15 = bf16[8,127,512]{2,1,0:T(8,128)(2,1)} all-to-all(bf16[8,127,512]{2,1,0:T(8,128)(2,1)S(1)} %fusion.13), channel_id=1, replica_groups=mesh['req'=8,'grp'=4] {'req'}, dimensions={0} | all-to-all | bytes 2080768 | tf_op jit(solution)/shard_map/all_to_all | solution.py:208
  124.6 1.5 reshape.471
  126.2 2.6 %gather_fusion = bf16[512,512]{1,0:T(8,128)(2,1)} fusion(bf16[1016,512]{1,0:T(8,128)(2,1)S(1)} %reshape.471, s32[1024]{0:T(1024)S(1)} %pad_clamp_fusion.1), kind=kCustom, calls=%fused_computation | custom fusion | bytes 1050624 | tf_op jit(solution)/shard_map/gather | solution.py:222
  128.8 2.1 add_convert_fusion.1
  131.0 21.8 %all-gather.2.cloned.1.call-done = bf16[512,2048]{1,0:T(8,128)(2,1)} async-done(((bf16[512,512]{1,0:T(8,128)(2,1)}), bf16[512,2048]{1,0:T(8,128)(2,1)}) %all-gather.2.cloned.1.call-update) | async-done | bytes 2097168 | tf_op jit(solution)/shard_map/all_gather | solution.py:154
  152.8 2.2 fusion.2
  155.0 5.9 %fusion.17 = f32[512,1024]{1,0:T(8,128)} fusion(bf16[2048,1024]{1,0:T(8,128)(2,1)} %param.31, bf16[512,2048]{1,0:T(8,128)(2,1)S(1)} %copy-done.2, f32[2048]{0:T(1024)S(1)} %copy-done.7, f32[512]{0:T(512)S(1)} %add_rsqrt_fusion), kind=kOutput, calls=%fused_computation.41 | convolution fusion | flops 2151677952 | bytes 8398848 | tf_op jit(solution)/shard_map/dot_general | solution.py:159
  160.9 10.6 %convolution_convert_fusion = bf16[512,2048]{1,0:T(8,128)(2,1)} fusion(bf16[1024,2048]{1,0:T(8,128)(2,1)} %param.33, f32[512,1024]{1,0:T(8,128)} %fusion.17, bf16[2048,1024]{1,0:T(8,128)(2,1)} %param.32, bf16[512,2048]{1,0:T(8,128)(2,1)} %all-gather.2.cloned.1.call-done, f32[2048]{0:T(1024)S(1)} %copy-done.7, f32[512]{0:T(512)S(1)} %add_rsqrt_fusion), kind=kOutput, calls=%fused_computation.11 | convolution fusion | flops 4303355904 | bytes 14690304 | tf_op jit(solution)/shard_map/dot_general | solution.py:163
  171.9 31.3 %reduce-scatter.5.cloned.1.call-done = bf16[512,512]{1,0:T(8,128)(2,1)} async-done(((bf16[512,2048]{1,0:T(8,128)(2,1)}), bf16[512,512]{1,0:T(8,128)(2,1)}) %reduce-scatter.5.cloned.1.call-update) | async-done | bytes 524304 | tf_op jit(solution)/shard_map/reduce_scatter | solution.py:162
  203.2 1.2 add_convert_fusion
  204.4 5.1 %gather_fusion.2 = bf16[1016,512]{1,0:T(8,128)(2,1)} fusion(bf16[512,512]{1,0:T(8,128)(2,1)S(1)} %add_convert_fusion, s32[1024]{0:T(1024)S(1)} %pad_clamp_fusion), kind=kCustom, calls=%fused_computation.2 | custom fusion | bytes 2084832 | tf_op jit(solution)/shard_map/gather | solution.py:231
  209.5 1.5 reshape.480
  211.0 1.2 broadcast_select_fusion
  212.2 5.5 %all-to-all-start.2 = ((bf16[8,127,512]{2,1,0:T(8,128)(2,1)}), bf16[8,127,512]{2,1,0:T(8,128)(2,1)S(1)}, u32[]{:S(2)}, u32[]{:S(2)}) async-start(bf16[8,127,512]{2,1,0:T(8,128)(2,1)} %broadcast_select_fusion), calls=%async_computation.4 | async-start | bytes 2097152 | tf_op jit(solution)/shard_map/all_to_all | solution.py:233
  218.8 24.6 %all-to-all-done.2 = bf16[8,127,512]{2,1,0:T(8,128)(2,1)S(1)} async-done(((bf16[8,127,512]{2,1,0:T(8,128)(2,1)}), bf16[8,127,512]{2,1,0:T(8,128)(2,1)S(1)}, u32[]{:S(2)}, u32[]{:S(2)}) %all-to-all-start.2) | async-done | bytes 1040416 | tf_op jit(solution)/shard_map/all_to_all | solution.py:233
  244.4 1.3 pad_select_fusion
  (70 shorter events, 7.8 us)
Async XLA Ops:
  6.5 82.8 %copy-start = (bf16[512,2048]{1,0:T(8,128)(2,1)S(1)}, bf16[512,2048]{1,0:T(8,128)(2,1)}, u32[]{:S(2)}) copy-start(bf16[512,2048]{1,0:T(8,128)(2,1)} %param.29) | copy-start | bytes 6291460
  40.2 2.4 slice-start
  40.2 3.7 %slice-start.1 = ((bf16[1024,512]{1,0:T(8,128)(2,1)}), bf16[8,512]{1,0:T(8,128)(2,1)S(1)}, s32[]{:S(2)}) async-start(bf16[1024,512]{1,0:T(8,128)(2,1)} %q_ref.1), calls=%async_computation.9 | async-start | bytes 16384 | tf_op jit(solution)/shard_map/slice | solution.py:100
  40.2 3.8 %slice-start.3 = ((bf16[1024,128]{1,0:T(8,128)(2,1)}), bf16[8,128]{1,0:T(8,128)(2,1)S(1)}, s32[]{:S(2)}) async-start(bf16[1024,128]{1,0:T(8,128)(2,1)} %kf_ref.1), calls=%async_computation.11 | async-start | bytes 4096 | tf_op jit(solution)/shard_map/slice | solution.py:103
  40.2 3.9 %copy-start.4 = (s32[8]{0:T(128)S(1)}, s32[8]{0:T(128)}, u32[]{:S(2)}) copy-start(s32[8]{0:T(128)} %param.24) | copy-start | bytes 100
  40.2 3.9 %copy-start.5 = (s32[8]{0:T(128)S(1)}, s32[8]{0:T(128)}, u32[]{:S(2)}) copy-start(s32[8]{0:T(128)} %param.25) | copy-start | bytes 100
  40.3 3.9 %copy-start.6 = (s32[8]{0:T(128)S(1)}, s32[8]{0:T(128)}, u32[]{:S(2)}) copy-start(s32[8]{0:T(128)} %param.26) | copy-start | bytes 100
  43.9 2.5 slice-start.2
  52.1 33.1 %all-to-all-start.1 = ((bf16[8,127,512]{2,1,0:T(8,128)(2,1)}), bf16[8,127,512]{2,1,0:T(8,128)(2,1)}, u32[]{:S(2)}, u32[]{:S(2)}) async-start(bf16[8,127,512]{2,1,0:T(8,128)(2,1)} %fusion.11), calls=%async_computation.1 | async-start | bytes 2097152 | tf_op jit(solution)/shard_map/all_to_all | solution.py:213
  59.3 69.5 %reduce-scatter.3.cloned.1.call-start = ((), (), s32[]{:S(2)}) async-start(), calls=%async_computation.5 | async-start | bytes 2621440 | tf_op jit(solution)/shard_map/reduce_scatter | solution.py:150
  93.0 1.2 copy-start.3
  93.1 59.7 %all-gather.2.cloned.1.call-start = ((), (), s32[]{:S(2)}) async-start(), calls=%async_computation.6 | async-start | bytes 2621440 | tf_op jit(solution)/shard_map/all_gather | solution.py:154
  128.8 26.2 %copy-start.7 = (f32[2048]{0:T(1024)S(1)}, f32[2048]{0:T(1024)}, u32[]{:S(2)}) copy-start(f32[2048]{0:T(1024)} %param.30) | copy-start | bytes 24580
  131.0 72.2 %reduce-scatter.5.cloned.1.call-start = ((), (), s32[]{:S(2)}) async-start(), calls=%async_computation.7 | async-start | bytes 2621440 | tf_op jit(solution)/shard_map/reduce_scatter | solution.py:162
  152.8 2.2 copy-start.2
  171.6 31.6 %copy-start.1 = (bf16[512,512]{1,0:T(8,128)(2,1)S(1)}, bf16[512,512]{1,0:T(8,128)(2,1)}, u32[]{:S(2)}) copy-start(bf16[512,512]{1,0:T(8,128)(2,1)} %add_convert_fusion.1) | copy-start | bytes 1572868
  212.2 31.3 %all-to-all-start.2 = ((bf16[8,127,512]{2,1,0:T(8,128)(2,1)}), bf16[8,127,512]{2,1,0:T(8,128)(2,1)S(1)}, u32[]{:S(2)}, u32[]{:S(2)}) async-start(bf16[8,127,512]{2,1,0:T(8,128)(2,1)} %broadcast_select_fusion), calls=%async_computation.4 | async-start | bytes 2097152 | tf_op jit(solution)/shard_map/all_to_all | solution.py:233
Sparse Core Ops, SparseCore 0:
  93.2 30.4 reduce-scatter.2
  131.1 21.6 all-gather.1
  171.7 31.4 reduce-scatter.4

commit v3 on v2

--- a/solution.py
+++ b/solution.py
@@ -145,13 +145,49 @@
     return lax.dynamic_update_slice(span_rows, decode_rows, (0, 0))
 
 
+def grp_block(x, index, width):
+    return lax.dynamic_slice_in_dim(x, index * width, width, 1)
+
+
+def grp_reduce_scatter(partial):
+    parts = lax.axis_size("grp")
+    width = partial.shape[1] // parts
+    if parts != 4:
+        return lax.psum_scatter(partial, "grp", scatter_dimension=1, tiled=True).astype(
+            jnp.float32
+        )
+    me = lax.axis_index("grp")
+    near = [(i, i ^ 1) for i in range(parts)]
+    far = [(i, i ^ 2) for i in range(parts)]
+    outgoing = jnp.stack([grp_block(partial, me ^ 1, width), grp_block(partial, me ^ 3, width)])
+    incoming = lax.ppermute(outgoing, "grp", near)
+    own = grp_block(partial, me, width).astype(jnp.float32) + incoming[0].astype(jnp.float32)
+    other = grp_block(partial, me ^ 2, width).astype(jnp.float32) + incoming[1].astype(
+        jnp.float32
+    )
+    arrived = lax.ppermute(other.astype(jnp.bfloat16), "grp", far)
+    return own + arrived.astype(jnp.float32)
+
+
+def grp_all_gather(block):
+    parts = lax.axis_size("grp")
+    if parts != 4:
+        return lax.all_gather(block, "grp", axis=1, tiled=True)
+    me = lax.axis_index("grp")
+    near = [(i, i ^ 1) for i in range(parts)]
+    far = [(i, i ^ 2) for i in range(parts)]
+    across = lax.ppermute(block, "grp", far)
+    pair = lax.ppermute(jnp.stack([block, across]), "grp", near)
+    held = jnp.stack([block, pair[0], across, pair[1]])
+    pieces = [lax.dynamic_index_in_dim(held, k ^ me, 0, keepdims=False) for k in range(parts)]
+    return jnp.concatenate(pieces, axis=1)
+
+
 def finish(attn_rows, resid_rows, out_weight, norm_gain, gate_weight, up_weight, down_weight):
     partial_value = jnp.dot(attn_rows, out_weight, preferred_element_type=jnp.float32)
-    proj_cols = lax.psum_scatter(
-        partial_value.astype(jnp.bfloat16), "grp", scatter_dimension=1, tiled=True
-    ).astype(jnp.float32)
+    proj_cols = grp_reduce_scatter(partial_value.astype(jnp.bfloat16))
     state_cols = (resid_rows.astype(jnp.float32) + proj_cols).astype(jnp.bfloat16)
-    state_full = lax.all_gather(state_cols, "grp", axis=1, tiled=True)
+    state_full = grp_all_gather(state_cols)
     state32 = state_full.astype(jnp.float32)
     normed = (
         state32 * lax.rsqrt(jnp.mean(state32 * state32, axis=1, keepdims=True) + 1e-05) * norm_gain
@@ -159,12 +195,9 @@
     gate = jnp.dot(normed, gate_weight, preferred_element_type=jnp.float32)
     upval = jnp.dot(normed, up_weight, preferred_element_type=jnp.float32)
     inner = (jax.nn.silu(gate) * upval).astype(jnp.bfloat16)
-    down_cols = lax.psum_scatter(
-        jnp.dot(inner, down_weight, preferred_element_type=jnp.float32).astype(jnp.bfloat16),
-        "grp",
-        scatter_dimension=1,
-        tiled=True,
-    ).astype(jnp.float32)
+    down_cols = grp_reduce_scatter(
+        jnp.dot(inner, down_weight, preferred_element_type=jnp.float32).astype(jnp.bfloat16)
+    )
     return (state_cols.astype(jnp.float32) + down_cols).astype(jnp.bfloat16)
 
 

time: 253 us -> 214 us (0.85)
  blocking collectives: 29.6 us -> 0 us
  between operations: 16 us -> 3.02 us
  starting transfers between devices: 12.9 us -> 20.7 us
  matrix products: 23.8 us -> 19.7 us
  waiting for transfers between devices: 98.3 us -> 94.2 us
  other arithmetic: 18.3 us -> 21 us
    reduce_scatter x2 -> x0, waiting for transfers between devices: 31.3 us -> none  [the longest x1 31.3 us: finish(): lax.psum_scatter(jnp.dot(inner, down_weight, preferred_element_type=jnp.f...]
    all_to_all x1 -> x0, blocking collectives: 29.6 us -> none  [shards(): lax.all_to_all(send_resid, 'req', split_axis=0, concat_axis=0, tiled=True)]
    ppermute x0 -> x6, waiting for transfers between devices: none -> 28.5 us  [the longest x2 12.3 us: grp_reduce_scatter(): arrived = lax.ppermute(other.astype(jnp.bfloat16), 'grp', far)]
    all_to_all x0 -> x1, waiting for transfers between devices: none -> 22.1 us  [shards(): lax.all_to_all(send_resid, 'req', split_axis=0, concat_axis=0, tiled=True)]
    all_gather x1 -> x0, waiting for transfers between devices: 21.8 us -> none  [finish(): state_full = lax.all_gather(state_cols, 'grp', axis=1, tiled=True)]
    ppermute x0 -> x6, starting transfers between devices: none -> 5 us  [the longest x2 3.12 us: grp_reduce_scatter(): arrived = lax.ppermute(other.astype(jnp.bfloat16), 'grp', far)]
    all_to_all x0 -> x1, starting transfers between devices: none -> 3.59 us  [shards(): lax.all_to_all(send_resid, 'req', split_axis=0, concat_axis=0, tiled=True)]
    convert_element_type x0 -> x2, other arithmetic: none -> 3.53 us  [grp_reduce_scatter(): arrived = lax.ppermute(other.astype(jnp.bfloat16), 'grp', far)]
  transfers between devices with their start and end apart: 5 -> 9, of which waited for: 4 -> 7; matrix products, arithmetic and copies ran while one was open for 5% -> 7% of each run, Pallas kernels for 0% -> 0%
where the time goes in v3:
time: 214 us; the launch traced here: 213 us
  waiting for transfers between devices  94.2 us (44%)
  local copies, waits for them, and re-layouts  27.7 us (13%)
  Pallas kernels  26.4 us (12%)
  other arithmetic  21 us (10%)
  starting transfers between devices  20.7 us (10%)
  matrix products  19.7 us (9%)
  between operations  3.02 us (1%)
    pallas_call x1, Pallas kernels, span_attention(): pl.pallas_call(span_kernel, out_shape=jax.ShapeDtypeStruct((rows, width),...  26.4 us
    all_to_all x1, waiting for transfers between devices, shards(): lax.all_to_all(picked, 'req', split_axis=0, concat_axis=0, tiled=True)  24.1 us
    all_to_all x1, waiting for transfers between devices, shards(): lax.all_to_all(send_resid, 'req', split_axis=0, concat_axis=0, tiled=True)  22.1 us
    all_to_all x1, waiting for transfers between devices, shards(): lax.all_to_all(outbound(attn), 'req', split_axis=0, concat_axis=0, tiled=...  19.5 us
    ppermute x2, waiting for transfers between devices, grp_reduce_scatter(): arrived = lax.ppermute(other.astype(jnp.bfloat16), 'grp', far)  12.3 us
    ppermute x1, waiting for transfers between devices, grp_all_gather(): across = lax.ppermute(block, 'grp', far)  11.2 us
    dot_general x1, matrix products, finish(): jnp.dot(inner, down_weight, preferred_element_type=jnp.float32)  9.95 us
    all_to_all x1, starting transfers between devices, shards(): lax.all_to_all(outbound(attn), 'req', split_axis=0, concat_axis=0, tiled=...  7.38 us
  transfers between devices with their start and end apart: 9, of which 7 were waited for; matrix products, arithmetic and copies ran while one was open for 7% of the time, Pallas kernels for 0%

profile of v3, /device:TPU:0, one launch (start us, length us, event | category | flops | bytes accessed | tf_op | source)
XLA Modules:
  0.0 212.6 jit_solution(15340244856816741498)
XLA Ops:
  5.0 2.3 %slice.43 = bf16[4096,128]{1,0:T(8,128)(2,1)} slice(bf16[4608,128]{1,0:T(8,128)(2,1)} %vp_ref.1), slice={[0:4096], [0:128]} | slice | bytes 2097152 | tf_op jit(solution)/shard_map/slice | solution.py:102
  7.3 26.4 %shard_map.154 = bf16[1024,512]{1,0:T(8,128)(2,1)} custom-call(s32[1]{0:T(128)S(6)} %copy.89.start_ref, bf16[1024,512]{1,0:T(8,128)(2,1)} %q_ref.1, bf16[4608,128]{1,0:T(8,128)(2,1)} %kp_ref.1, bf16[4608,128]{1,0:T(8,128)(2,1)} %vp_ref.1, bf16[1024,128]{1,0:T(8,128)(2,1)} %kf_ref.1, bf16[1024,128]{1,0:T(8,128)(2,1)} %vf_ref.1), custom_call_target="tpu_custom_call" | custom-call | flops 2147483648 | bytes 2883584 | tf_op jit(solution)/shard_map/pallas_call | solution.py:83
  33.7 2.4 %copy.56 = bf16[4096,128]{0,1:T(8,128)(2,1)} copy(bf16[4096,128]{1,0:T(8,128)(2,1)} %slice.43) | data formatting | bytes 2097152 | tf_op jit(solution)/shard_map/slice | solution.py:102
  36.1 1.3 copy.52
  37.8 1.6 fusion.50
  40.0 1.7 fusion.27
  44.2 1.4 fusion.11
  45.6 7.4 %all-to-all-start.1 = ((bf16[8,127,512]{2,1,0:T(8,128)(2,1)}), bf16[8,127,512]{2,1,0:T(8,128)(2,1)}, u32[]{:S(2)}, u32[]{:S(2)}) async-start(bf16[8,127,512]{2,1,0:T(8,128)(2,1)} %fusion.11), calls=%async_computation.1 | async-start | bytes 2097152 | tf_op jit(solution)/shard_map/all_to_all | solution.py:246
  54.5 4.2 %compare_select_fusion.6 = s32[512,1]{0,1:T(1,128)S(1)} fusion(s32[]{:T(128)} %bitcast.8, s32[]{:T(128)} %bitcast.9, s32[]{:T(128)} %bitcast.10, s32[]{:T(128)} %bitcast.11, s32[]{:T(128)} %bitcast.12, s32[]{:T(128)} %bitcast.14, s32[]{:T(128)} %bitcast.13, s32[512,1]{0,1:T(1,128)S(1)} %bitcast.108), kind=kLoop, calls=%fused_computation.101 | loop fusion | flops 7680 | bytes 4124 | tf_op jit(solution)/shard_map/gather | solution.py:252
  59.3 19.5 %all-to-all-done.1 = bf16[8,127,512]{2,1,0:T(8,128)(2,1)} async-done(((bf16[8,127,512]{2,1,0:T(8,128)(2,1)}), bf16[8,127,512]{2,1,0:T(8,128)(2,1)}, u32[]{:S(2)}, u32[]{:S(2)}) %all-to-all-start.1) | async-done | bytes 1040416 | tf_op jit(solution)/shard_map/all_to_all | solution.py:246
  78.8 1.5 reshape.487
  80.4 2.6 %gather_fusion.1 = bf16[512,512]{1,0:T(8,128)(2,1)} fusion(bf16[1016,512]{1,0:T(8,128)(2,1)S(1)} %reshape.487, s32[1024]{0:T(1024)S(1)} %pad_clamp_fusion.1), kind=kCustom, calls=%fused_computation.1 | custom fusion | bytes 1050624 | tf_op jit(solution)/shard_map/gather | solution.py:254
  83.0 2.3 %convolution_convert_fusion.1 = bf16[512,2048]{1,0:T(8,128)(2,1)S(1)} fusion(bf16[512,512]{1,0:T(8,128)(2,1)} %gather_fusion.1, bf16[512,2048]{1,0:T(8,128)(2,1)S(1)} %copy-done), kind=kOutput, calls=%fused_computation.12 | convolution fusion | flops 1074790400 | bytes 4718592 | tf_op jit(solution)/shard_map/dot_general | solution.py:187
  87.3 1.4 fusion.13
  88.7 3.6 %all-to-all-start = ((bf16[8,127,512]{2,1,0:T(8,128)(2,1)}), bf16[8,127,512]{2,1,0:T(8,128)(2,1)S(1)}, u32[]{:S(2)}, u32[]{:S(2)}) async-start(bf16[8,127,512]{2,1,0:T(8,128)(2,1)} %fusion.13), calls=%async_computation | async-start | bytes 2097152 | tf_op jit(solution)/shard_map/all_to_all | solution.py:241
  92.3 2.4 %fusion.18 = bf16[512,512]{1,0:T(8,128)(2,1)} fusion(bf16[2,512,512]{2,1,0:T(8,128)(2,1)S(1)} %collective-permute-done, bf16[512,2048]{1,0:T(8,128)(2,1)} %copy-done.3, s32[]{:T(128)S(6)} %select_n.165), kind=kLoop, calls=%fused_computation.43 | loop fusion | flops 1048576 | bytes 1572868 | tf_op jit(solution)/shard_map/convert_element_type | solution.py:168
  94.6 1.5 collective-permute-start.1
  96.2 22.1 %all-to-all-done = bf16[8,127,512]{2,1,0:T(8,128)(2,1)S(1)} async-done(((bf16[8,127,512]{2,1,0:T(8,128)(2,1)}), bf16[8,127,512]{2,1,0:T(8,128)(2,1)S(1)}, u32[]{:S(2)}, u32[]{:S(2)}) %all-to-all-start) | async-done | bytes 1040416 | tf_op jit(solution)/shard_map/all_to_all | solution.py:241
  118.6 2.0 gather_fusion
  120.6 1.5 fusion.21
  122.0 1.6 collective-permute-start.2
  123.6 11.2 %collective-permute-done.2 = bf16[512,512]{1,0:T(8,128)(2,1)S(1)} collective-permute-done((bf16[512,512]{1,0:T(8,128)(2,1)S(1)}, bf16[512,512]{1,0:T(8,128)(2,1)S(1)}, u32[]{:S(2)}, u32[]{:S(2)}) %collective-permute-start.2) | collective-permute-done | bytes 524320 | tf_op jit(solution)/shard_map/ppermute | solution.py:179
  135.1 2.6 %collective-permute-done.3 = bf16[2,512,512]{2,1,0:T(8,128)(2,1)S(1)} collective-permute-done((bf16[2,512,512]{2,1,0:T(8,128)(2,1)S(1)}, bf16[2,512,512]{2,1,0:T(8,128)(2,1)S(1)}, u32[]{:S(2)}, u32[]{:S(2)}) %collective-permute-start.3) | collective-permute-done | bytes 1048608 | tf_op jit(solution)/shard_map/ppermute | solution.py:180
  138.7 1.5 copy-done.10
  140.2 3.8 %fusion.25 = f32[512,1024]{1,0:T(8,128)} fusion(bf16[2048,1024]{1,0:T(8,128)(2,1)S(1)} %copy-done.10, f32[2048]{0:T(1024)S(1)} %copy-done.11, f32[512]{0:T(512)S(1)} %add_rsqrt_fusion, bf16[512,512]{1,0:T(8,128)(2,1)S(1)} %get-tuple-element.11, bf16[512,512]{1,0:T(8,128)(2,1)S(1)} %get-tuple-element.12, bf16[512,512]{1,0:T(8,128)(2,1)S(1)} %get-tuple-element.13, ...), kind=kOutput, calls=%fused_computation.56 | convolution fusion | flops 2159017984 | bytes 8398848 | tf_op jit(solution)/shard_map/dot_general | solution.py:195
  144.0 10.0 %convolution_convert_fusion = bf16[512,2048]{1,0:T(8,128)(2,1)} fusion(bf16[1024,2048]{1,0:T(8,128)(2,1)} %param.33, f32[512,1024]{1,0:T(8,128)} %fusion.25, bf16[2048,1024]{1,0:T(8,128)(2,1)} %param.32, f32[2048]{0:T(1024)S(1)} %copy-done.11, f32[512]{0:T(512)S(1)} %add_rsqrt_fusion, bf16[512,512]{1,0:T(8,128)(2,1)S(1)} %get-tuple-element.11, ...), kind=kOutput, calls=%fused_computation.11 | convolution fusion | flops 4310695936 | bytes 14690304 | tf_op jit(solution)/shard_map/dot_general | solution.py:199
  155.7 2.3 %collective-permute-done.4 = bf16[2,512,512]{2,1,0:T(8,128)(2,1)S(1)} collective-permute-done((bf16[2,512,512]{2,1,0:T(8,128)(2,1)S(1)}, bf16[2,512,512]{2,1,0:T(8,128)(2,1)S(1)}, u32[]{:S(2)}, u32[]{:S(2)}) %collective-permute-start.4) | collective-permute-done | bytes 1048608 | tf_op jit(solution)/shard_map/ppermute | solution.py:163
  159.2 1.6 collective-permute-start.5
  160.9 12.3 %collective-permute-done.5 = bf16[512,512]{1,0:T(8,128)(2,1)S(1)} collective-permute-done((bf16[512,512]{1,0:T(8,128)(2,1)S(1)}, bf16[512,512]{1,0:T(8,128)(2,1)S(1)}, u32[]{:S(2)}, u32[]{:S(2)}) %collective-permute-start.5) | collective-permute-done | bytes 524320 | tf_op jit(solution)/shard_map/ppermute | solution.py:168
  174.6 4.1 %gather_fusion.2 = bf16[1016,512]{1,0:T(8,128)(2,1)S(1)} fusion(bf16[512,512]{1,0:T(8,128)(2,1)S(1)} %fusion.17, s32[1024]{0:T(1024)S(1)} %pad_clamp_fusion), kind=kCustom, calls=%fused_computation.2 | custom fusion | bytes 2084832 | tf_op jit(solution)/shard_map/gather | solution.py:264
  180.2 4.7 %all-to-all-start.2 = ((bf16[8,127,512]{2,1,0:T(8,128)(2,1)}), bf16[8,127,512]{2,1,0:T(8,128)(2,1)S(1)}, u32[]{:S(2)}, u32[]{:S(2)}) async-start(bf16[8,127,512]{2,1,0:T(8,128)(2,1)} %broadcast_select_fusion), calls=%async_computation.2 | async-start | bytes 2097152 | tf_op jit(solution)/shard_map/all_to_all | solution.py:266
  186.3 24.1 %all-to-all-done.2 = bf16[8,127,512]{2,1,0:T(8,128)(2,1)S(1)} async-done(((bf16[8,127,512]{2,1,0:T(8,128)(2,1)}), bf16[8,127,512]{2,1,0:T(8,128)(2,1)S(1)}, u32[]{:S(2)}, u32[]{:S(2)}) %all-to-all-start.2) | async-done | bytes 1040416 | tf_op jit(solution)/shard_map/all_to_all | solution.py:266
  (92 shorter events, 20.9 us)
Async XLA Ops:
  0.0 83.0 %copy-start = (bf16[512,2048]{1,0:T(8,128)(2,1)S(1)}, bf16[512,2048]{1,0:T(8,128)(2,1)}, u32[]{:S(2)}) copy-start(bf16[512,2048]{1,0:T(8,128)(2,1)} %param.29) | copy-start | bytes 6291460
  33.7 2.4 %slice-start = ((bf16[4608,128]{1,0:T(8,128)(2,1)}), bf16[4096,128]{1,0:T(8,128)(2,1)S(1)}, s32[]{:S(2)}) async-start(bf16[4608,128]{1,0:T(8,128)(2,1)} %kp_ref.1), calls=%async_computation.3 | async-start | bytes 2097152 | tf_op jit(solution)/shard_map/slice | solution.py:101
  33.7 3.8 %slice-start.1 = ((bf16[1024,512]{1,0:T(8,128)(2,1)}), bf16[8,512]{1,0:T(8,128)(2,1)S(1)}, s32[]{:S(2)}) async-start(bf16[1024,512]{1,0:T(8,128)(2,1)} %q_ref.1), calls=%async_computation.4 | async-start | bytes 16384 | tf_op jit(solution)/shard_map/slice | solution.py:100
  33.7 3.9 %slice-start.3 = ((bf16[1024,128]{1,0:T(8,128)(2,1)}), bf16[8,128]{1,0:T(8,128)(2,1)S(1)}, s32[]{:S(2)}) async-start(bf16[1024,128]{1,0:T(8,128)(2,1)} %kf_ref.1), calls=%async_computation.6 | async-start | bytes 4096 | tf_op jit(solution)/shard_map/slice | solution.py:103
  33.7 3.9 %copy-start.7 = (s32[8]{0:T(128)S(1)}, s32[8]{0:T(128)}, u32[]{:S(2)}) copy-start(s32[8]{0:T(128)} %param.24) | copy-start | bytes 100
  33.7 3.9 %copy-start.8 = (s32[8]{0:T(128)S(1)}, s32[8]{0:T(128)}, u32[]{:S(2)}) copy-start(s32[8]{0:T(128)} %param.25) | copy-start | bytes 100
  33.7 3.9 %copy-start.9 = (s32[8]{0:T(128)S(1)}, s32[8]{0:T(128)}, u32[]{:S(2)}) copy-start(s32[8]{0:T(128)} %param.26) | copy-start | bytes 100
  37.4 2.5 %slice-start.2 = ((bf16[1024,128]{1,0:T(8,128)(2,1)}), bf16[8,128]{1,0:T(8,128)(2,1)S(1)}, s32[]{:S(2)}) async-start(bf16[1024,128]{1,0:T(8,128)(2,1)} %vf_ref.1), calls=%async_computation.5 | async-start | bytes 4096 | tf_op jit(solution)/shard_map/slice | solution.py:104
  45.6 7.4 %copy-start.6 = (bf16[1024,512]{1,0:T(8,128)(2,1)S(1)}, bf16[1024,512]{1,0:T(8,128)(2,1)}, u32[]{:S(2)}) copy-start(bf16[1024,512]{1,0:T(8,128)(2,1)} %param.18) | copy-start | bytes 3145732
  45.6 33.3 %all-to-all-start.1 = ((bf16[8,127,512]{2,1,0:T(8,128)(2,1)}), bf16[8,127,512]{2,1,0:T(8,128)(2,1)}, u32[]{:S(2)}, u32[]{:S(2)}) async-start(bf16[8,127,512]{2,1,0:T(8,128)(2,1)} %fusion.11), calls=%async_computation.1 | async-start | bytes 2097152 | tf_op jit(solution)/shard_map/all_to_all | solution.py:246
  85.3 1.3 copy-start.3
  85.3 2.0 copy-start.2
  86.7 5.6 %collective-permute-start = (bf16[2,512,512]{2,1,0:T(8,128)(2,1)S(1)}, bf16[2,512,512]{2,1,0:T(8,128)(2,1)S(1)}, u32[]{:S(2)}, u32[]{:S(2)}) collective-permute-start(bf16[2,512,512]{2,1,0:T(8,128)(2,1)S(1)} %pad_maximum_fusion.2), channel_id=1, source_target_pairs={{0,1},{1,0},{2,3},{3,2},{4,5},{5,4},{6,7},{7,6},{8,9},{9,8},{10,11... | collective-permute-start | bytes 3145736 | tf_op jit(solution)/shard_map/ppermute | solution.py:163
  88.7 29.6 %all-to-all-start = ((bf16[8,127,512]{2,1,0:T(8,128)(2,1)}), bf16[8,127,512]{2,1,0:T(8,128)(2,1)S(1)}, u32[]{:S(2)}, u32[]{:S(2)}) async-start(bf16[8,127,512]{2,1,0:T(8,128)(2,1)} %fusion.13), calls=%async_computation | async-start | bytes 2097152 | tf_op jit(solution)/shard_map/all_to_all | solution.py:241
  92.3 3.9 %copy-start.4 = (bf16[2,512,512]{2,1,0:T(8,128)(2,1)}, bf16[2,512,512]{2,1,0:T(8,128)(2,1)S(1)}, u32[]{:S(2)}) copy-start(bf16[2,512,512]{2,1,0:T(8,128)(2,1)S(1)} %collective-permute-done) | copy-start | bytes 3145732
  94.6 25.9 %collective-permute-start.1 = (bf16[512,512]{1,0:T(8,128)(2,1)}, bf16[512,512]{1,0:T(8,128)(2,1)}, u32[]{:S(2)}, u32[]{:S(2)}) collective-permute-start(bf16[512,512]{1,0:T(8,128)(2,1)} %fusion.18), channel_id=1, source_target_pairs={{0,2},{1,3},{2,0},{3,1},{4,6},{5,7},{6,4},{7,5},{8,10},{9,11},{10,... | collective-permute-start | bytes 1572872 | tf_op jit(solution)/shard_map/ppermute | solution.py:168
  118.5 2.0 copy-start.5
  122.0 12.8 %collective-permute-start.2 = (bf16[512,512]{1,0:T(8,128)(2,1)S(1)}, bf16[512,512]{1,0:T(8,128)(2,1)S(1)}, u32[]{:S(2)}, u32[]{:S(2)}) collective-permute-start(bf16[512,512]{1,0:T(8,128)(2,1)S(1)} %fusion.21), channel_id=1, source_target_pairs={{0,2},{1,3},{2,0},{3,1},{4,6},{5,7},{6,4},{7,5},{8,10},{9,11},{10,... | collective-permute-start | bytes 1572872 | tf_op jit(solution)/shard_map/ppermute | solution.py:179
  134.9 2.7 %collective-permute-start.3 = (bf16[2,512,512]{2,1,0:T(8,128)(2,1)S(1)}, bf16[2,512,512]{2,1,0:T(8,128)(2,1)S(1)}, u32[]{:S(2)}, u32[]{:S(2)}) collective-permute-start(bf16[2,512,512]{2,1,0:T(8,128)(2,1)S(1)} %pad_maximum_fusion.3), channel_id=1, source_target_pairs={{0,1},{1,0},{2,3},{3,2},{4,5},{5,4},{6,7},{7,6},{8,9},{9,8},{10,11... | collective-permute-start | bytes 3145736 | tf_op jit(solution)/shard_map/ppermute | solution.py:180
  138.0 2.2 %copy-start.10 = (bf16[2048,1024]{1,0:T(8,128)(2,1)S(1)}, bf16[2048,1024]{1,0:T(8,128)(2,1)}, u32[]{:S(2)}) copy-start(bf16[2048,1024]{1,0:T(8,128)(2,1)} %param.31) | copy-start | bytes 12582916
  138.2 2.0 copy-start.11
  155.3 2.7 %collective-permute-start.4 = (bf16[2,512,512]{2,1,0:T(8,128)(2,1)S(1)}, bf16[2,512,512]{2,1,0:T(8,128)(2,1)S(1)}, u32[]{:S(2)}, u32[]{:S(2)}) collective-permute-start(bf16[2,512,512]{2,1,0:T(8,128)(2,1)S(1)} %pad_maximum_fusion.4), channel_id=1, source_target_pairs={{0,1},{1,0},{2,3},{3,2},{4,5},{5,4},{6,7},{7,6},{8,9},{9,8},{10,11... | collective-permute-start | bytes 3145736 | tf_op jit(solution)/shard_map/ppermute | solution.py:163
  159.2 14.0 %collective-permute-start.5 = (bf16[512,512]{1,0:T(8,128)(2,1)S(1)}, bf16[512,512]{1,0:T(8,128)(2,1)S(1)}, u32[]{:S(2)}, u32[]{:S(2)}) collective-permute-start(bf16[512,512]{1,0:T(8,128)(2,1)S(1)} %fusion.14), channel_id=1, source_target_pairs={{0,2},{1,3},{2,0},{3,1},{4,6},{5,7},{6,4},{7,5},{8,10},{9,11},{10,... | collective-permute-start | bytes 1572872 | tf_op jit(solution)/shard_map/ppermute | solution.py:168
  180.2 30.2 %all-to-all-start.2 = ((bf16[8,127,512]{2,1,0:T(8,128)(2,1)}), bf16[8,127,512]{2,1,0:T(8,128)(2,1)S(1)}, u32[]{:S(2)}, u32[]{:S(2)}) async-start(bf16[8,127,512]{2,1,0:T(8,128)(2,1)} %broadcast_select_fusion), calls=%async_computation.2 | async-start | bytes 2097152 | tf_op jit(solution)/shard_map/all_to_all | solution.py:266
  210.4 2.3 %copy-start.1 = (bf16[512,2048]{1,0:T(8,128)(2,1)S(1)}, bf16[512,2048]{1,0:T(8,128)(2,1)}, u32[]{:S(2)}) copy-start(bf16[512,2048]{1,0:T(8,128)(2,1)} %param.29) | copy-start | bytes 6291460

commit v4 on v3

--- a/solution.py
+++ b/solution.py
@@ -76,7 +76,7 @@
     f_spec = pl.BlockSpec((rows, kv_width), lambda c, s: (0, 0))
     flops = 4 * heads * rows * (prior + rows // 2) * HEAD_DIM
     cost = pl.CostEstimate(
-        flops=flops,
+        flops=16 * flops,
         transcendentals=heads * rows * (prior + rows // 2),
         bytes_accessed=2 * (2 * rows * width + 2 * (prior + rows) * kv_width),
     )
@@ -243,6 +243,7 @@
     attn = attention(
         queries, new_keys, new_values, pool_keys, pool_values, decode_mask, span_offset[0]
     )
+    got_resid, attn = lax.optimization_barrier((got_resid, attn))
     got_attn = lax.all_to_all(outbound(attn), "req", split_axis=0, concat_axis=0, tiled=True)
 
     slots = jnp.arange(bal, dtype=jnp.int32)

time: 214 us -> 211 us (0.986)
  waiting for transfers between devices: 94.2 us -> 86.8 us
  local copies, waits for them, and re-layouts: 27.7 us -> 31.4 us
    all_to_all x1, waiting for transfers between devices: 22.1 us -> 0.01 us  [shards(): lax.all_to_all(send_resid, 'req', split_axis=0, concat_axis=0, tiled=True)]
    ppermute x2, waiting for transfers between devices: 12.3 us -> 22.8 us  [grp_reduce_scatter(): arrived = lax.ppermute(other.astype(jnp.bfloat16), 'grp', far)]
    all_to_all x1, starting transfers between devices: 3.59 us -> 7.25 us  [shards(): lax.all_to_all(send_resid, 'req', split_axis=0, concat_axis=0, tiled=True)]
    slice x3 -> x2, local copies, waits for them, and re-layouts: 1.34 us -> 4.58 us  [decode_attention(): kc = pool_keys[:cached].reshape(cached, kv, HEAD_DIM)]
    ppermute x2, waiting for transfers between devices: 2.35 us -> 5.01 us  [grp_reduce_scatter(): incoming = lax.ppermute(outgoing, 'grp', near)]
  transfers between devices with their start and end apart: 9 -> 9, of which waited for: 7 -> 8; matrix products, arithmetic and copies ran while one was open for 7% -> 11% of each run, Pallas kernels for 0% -> 13%
where the time goes in v4:
time: 211 us; the launch traced here: 210 us
  waiting for transfers between devices  86.8 us (41%)
  local copies, waits for them, and re-layouts  31.4 us (15%)
  Pallas kernels  26.4 us (13%)
  starting transfers between devices  21.8 us (10%)
  other arithmetic  21 us (10%)
  matrix products  20 us (9%)
  between operations  3 us (1%)
    pallas_call x1, Pallas kernels, span_attention(): pl.pallas_call(span_kernel, out_shape=jax.ShapeDtypeStruct((rows, width),...  26.4 us
    all_to_all x1, waiting for transfers between devices, shards(): lax.all_to_all(picked, 'req', split_axis=0, concat_axis=0, tiled=True)  24.4 us
    ppermute x2, waiting for transfers between devices, grp_reduce_scatter(): arrived = lax.ppermute(other.astype(jnp.bfloat16), 'grp', far)  22.8 us
    all_to_all x1, waiting for transfers between devices, shards(): lax.all_to_all(outbound(attn), 'req', split_axis=0, concat_axis=0, tiled=...  20.4 us
    ppermute x1, waiting for transfers between devices, grp_all_gather(): across = lax.ppermute(block, 'grp', far)  11.6 us
    dot_general x1, matrix products, finish(): jnp.dot(inner, down_weight, preferred_element_type=jnp.float32)  9.96 us
    all_to_all x1, starting transfers between devices, shards(): lax.all_to_all(send_resid, 'req', split_axis=0, concat_axis=0, tiled=True)  7.25 us
    all_to_all x1, starting transfers between devices, shards(): lax.all_to_all(outbound(attn), 'req', split_axis=0, concat_axis=0, tiled=...  6 us
  transfers between devices with their start and end apart: 9, of which 8 were waited for; matrix products, arithmetic and copies ran while one was open for 11% of the time, Pallas kernels for 13%

profile of v4, /device:TPU:0, one launch (start us, length us, event | category | flops | bytes accessed | tf_op | source)
XLA Modules:
  0.0 210.4 jit_solution(8190132463680792287)
XLA Ops:
  7.3 7.3 %all-to-all-start = ((bf16[8,127,512]{2,1,0:T(8,128)(2,1)}), bf16[8,127,512]{2,1,0:T(8,128)(2,1)S(1)}, u32[]{:S(2)}, u32[]{:S(2)}) async-start(bf16[8,127,512]{2,1,0:T(8,128)(2,1)} %fusion.13), calls=%async_computation | async-start | bytes 2097152 | tf_op jit(solution)/shard_map/all_to_all | solution.py:241
  15.2 2.3 %slice.43 = bf16[4096,128]{1,0:T(8,128)(2,1)} slice(bf16[4608,128]{1,0:T(8,128)(2,1)} %vp_ref.1), slice={[0:4096], [0:128]} | slice | bytes 2097152 | tf_op jit(solution)/shard_map/slice | solution.py:102
  17.5 2.3 %copy.56 = bf16[4096,128]{0,1:T(8,128)(2,1)} copy(bf16[4096,128]{1,0:T(8,128)(2,1)} %slice.43) | data formatting | bytes 2097152 | tf_op jit(solution)/shard_map/slice | solution.py:102
  19.8 2.3 %slice.40 = bf16[4096,128]{1,0:T(8,128)(2,1)} slice(bf16[4608,128]{1,0:T(8,128)(2,1)} %kp_ref.1), slice={[0:4096], [0:128]} | slice | bytes 2097152 | tf_op jit(solution)/shard_map/slice | solution.py:101
  22.1 2.3 %copy.52 = bf16[4096,128]{0,1:T(8,128)(2,1)} copy(bf16[4096,128]{1,0:T(8,128)(2,1)} %slice.40) | data formatting | bytes 2097152 | tf_op jit(solution)/shard_map/slice | solution.py:101
  24.7 1.6 fusion.50
  27.7 2.0 fusion.27
  30.0 26.4 %shard_map.154 = bf16[1024,512]{1,0:T(8,128)(2,1)} custom-call(s32[1]{0:T(128)S(6)} %copy.89.start_ref, bf16[1024,512]{1,0:T(8,128)(2,1)} %q_ref.1, bf16[4608,128]{1,0:T(8,128)(2,1)} %kp_ref.1, bf16[4608,128]{1,0:T(8,128)(2,1)} %vp_ref.1, bf16[1024,128]{1,0:T(8,128)(2,1)} %kf_ref.1, bf16[1024,128]{1,0:T(8,128)(2,1)} %vf_ref.1), custom_call_target="tpu_custom_call" | custom-call | flops 34359738368 | bytes 2883584 | tf_op jit(solution)/shard_map/pallas_call | solution.py:83
  57.0 1.7 slice_bitcast_fusion
  60.4 6.0 %all-to-all-start.1 = ((bf16[8,127,512]{2,1,0:T(8,128)(2,1)}), bf16[8,127,512]{2,1,0:T(8,128)(2,1)}, u32[]{:S(2)}, u32[]{:S(2)}) async-start(bf16[8,127,512]{2,1,0:T(8,128)(2,1)} %fusion.11), calls=%async_computation.1 | async-start | bytes 2097152 | tf_op jit(solution)/shard_map/all_to_all | solution.py:247
  66.5 4.3 %compare_select_fusion.6 = s32[512,1]{0,1:T(1,128)S(1)} fusion(s32[]{:T(128)} %bitcast.19, s32[]{:T(128)} %bitcast.20, s32[]{:T(128)} %bitcast.21, s32[]{:T(128)} %bitcast.22, s32[]{:T(128)} %bitcast.23, s32[]{:T(128)} %bitcast.25, s32[]{:T(128)} %bitcast.24, s32[512,1]{0,1:T(1,128)S(1)} %bitcast.108), kind=kLoop, calls=%fused_computation.101 | loop fusion | flops 7680 | bytes 4124 | tf_op jit(solution)/shard_map/gather | solution.py:253
  71.5 20.4 %all-to-all-done.1 = bf16[8,127,512]{2,1,0:T(8,128)(2,1)} async-done(((bf16[8,127,512]{2,1,0:T(8,128)(2,1)}), bf16[8,127,512]{2,1,0:T(8,128)(2,1)}, u32[]{:S(2)}, u32[]{:S(2)}) %all-to-all-start.1) | async-done | bytes 1040416 | tf_op jit(solution)/shard_map/all_to_all | solution.py:247
  91.9 1.5 reshape.487
  93.5 2.6 %gather_fusion.1 = bf16[512,512]{1,0:T(8,128)(2,1)} fusion(bf16[1016,512]{1,0:T(8,128)(2,1)S(1)} %reshape.487, s32[1024]{0:T(1024)S(1)} %pad_clamp_fusion.1), kind=kCustom, calls=%fused_computation.1 | custom fusion | bytes 1050624 | tf_op jit(solution)/shard_map/gather | solution.py:255
  96.1 2.3 %convolution_convert_fusion.1 = bf16[512,2048]{1,0:T(8,128)(2,1)S(1)} fusion(bf16[512,512]{1,0:T(8,128)(2,1)} %gather_fusion.1, bf16[512,2048]{1,0:T(8,128)(2,1)S(1)} %copy-done), kind=kOutput, calls=%fused_computation.12 | convolution fusion | flops 1074790400 | bytes 4718592 | tf_op jit(solution)/shard_map/dot_general | solution.py:187
  99.7 2.7 %collective-permute-done = bf16[2,512,512]{2,1,0:T(8,128)(2,1)S(1)} collective-permute-done((bf16[2,512,512]{2,1,0:T(8,128)(2,1)S(1)}, bf16[2,512,512]{2,1,0:T(8,128)(2,1)S(1)}, u32[]{:S(2)}, u32[]{:S(2)}) %collective-permute-start) | collective-permute-done | bytes 1048608 | tf_op jit(solution)/shard_map/ppermute | solution.py:163
  102.4 2.4 %fusion.18 = bf16[512,512]{1,0:T(8,128)(2,1)} fusion(bf16[2,512,512]{2,1,0:T(8,128)(2,1)S(1)} %collective-permute-done, bf16[512,2048]{1,0:T(8,128)(2,1)} %copy-done.5, s32[]{:T(128)S(6)} %select_n.165), kind=kLoop, calls=%fused_computation.43 | loop fusion | flops 1048576 | bytes 1572868 | tf_op jit(solution)/shard_map/convert_element_type | solution.py:168
  104.8 1.5 collective-permute-start.1
  106.6 2.0 gather_fusion
  108.6 10.4 %collective-permute-done.1 = bf16[512,512]{1,0:T(8,128)(2,1)} collective-permute-done((bf16[512,512]{1,0:T(8,128)(2,1)}, bf16[512,512]{1,0:T(8,128)(2,1)}, u32[]{:S(2)}, u32[]{:S(2)}) %collective-permute-start.1) | collective-permute-done | bytes 524320 | tf_op jit(solution)/shard_map/ppermute | solution.py:168
  120.5 1.6 collective-permute-start.2
  122.1 11.6 %collective-permute-done.2 = bf16[512,512]{1,0:T(8,128)(2,1)S(1)} collective-permute-done((bf16[512,512]{1,0:T(8,128)(2,1)S(1)}, bf16[512,512]{1,0:T(8,128)(2,1)S(1)}, u32[]{:S(2)}, u32[]{:S(2)}) %collective-permute-start.2) | collective-permute-done | bytes 524320 | tf_op jit(solution)/shard_map/ppermute | solution.py:179
  133.9 2.6 %collective-permute-done.3 = bf16[2,512,512]{2,1,0:T(8,128)(2,1)S(1)} collective-permute-done((bf16[2,512,512]{2,1,0:T(8,128)(2,1)S(1)}, bf16[2,512,512]{2,1,0:T(8,128)(2,1)S(1)}, u32[]{:S(2)}, u32[]{:S(2)}) %collective-permute-start.3) | collective-permute-done | bytes 1048608 | tf_op jit(solution)/shard_map/ppermute | solution.py:180
  137.6 1.5 copy-done.11
  139.1 3.8 %fusion.25 = f32[512,1024]{1,0:T(8,128)} fusion(bf16[2048,1024]{1,0:T(8,128)(2,1)S(1)} %copy-done.11, f32[2048]{0:T(1024)S(1)} %copy-done.12, f32[512]{0:T(512)S(1)} %add_rsqrt_fusion, bf16[512,512]{1,0:T(8,128)(2,1)S(1)} %get-tuple-element.15, bf16[512,512]{1,0:T(8,128)(2,1)S(1)} %get-tuple-element.16, bf16[512,512]{1,0:T(8,128)(2,1)S(1)} %get-tuple-element.17, ...), kind=kOutput, calls=%fused_computation.56 | convolution fusion | flops 2159017984 | bytes 8398848 | tf_op jit(solution)/shard_map/dot_general | solution.py:195
  142.8 10.0 %convolution_convert_fusion = bf16[512,2048]{1,0:T(8,128)(2,1)} fusion(bf16[1024,2048]{1,0:T(8,128)(2,1)} %param.33, f32[512,1024]{1,0:T(8,128)} %fusion.25, bf16[2048,1024]{1,0:T(8,128)(2,1)} %param.32, f32[2048]{0:T(1024)S(1)} %copy-done.12, f32[512]{0:T(512)S(1)} %add_rsqrt_fusion, bf16[512,512]{1,0:T(8,128)(2,1)S(1)} %get-tuple-element.15, ...), kind=kOutput, calls=%fused_computation.11 | convolution fusion | flops 4310695936 | bytes 14690304 | tf_op jit(solution)/shard_map/dot_general | solution.py:199
  154.6 2.4 %collective-permute-done.4 = bf16[2,512,512]{2,1,0:T(8,128)(2,1)S(1)} collective-permute-done((bf16[2,512,512]{2,1,0:T(8,128)(2,1)S(1)}, bf16[2,512,512]{2,1,0:T(8,128)(2,1)S(1)}, u32[]{:S(2)}, u32[]{:S(2)}) %collective-permute-start.4) | collective-permute-done | bytes 1048608 | tf_op jit(solution)/shard_map/ppermute | solution.py:163
  158.1 1.6 collective-permute-start.5
  159.8 12.3 %collective-permute-done.5 = bf16[512,512]{1,0:T(8,128)(2,1)S(1)} collective-permute-done((bf16[512,512]{1,0:T(8,128)(2,1)S(1)}, bf16[512,512]{1,0:T(8,128)(2,1)S(1)}, u32[]{:S(2)}, u32[]{:S(2)}) %collective-permute-start.5) | collective-permute-done | bytes 524320 | tf_op jit(solution)/shard_map/ppermute | solution.py:168
  173.4 4.1 %gather_fusion.2 = bf16[1016,512]{1,0:T(8,128)(2,1)S(1)} fusion(bf16[512,512]{1,0:T(8,128)(2,1)S(1)} %fusion.17, s32[1024]{0:T(1024)S(1)} %pad_clamp_fusion), kind=kCustom, calls=%fused_computation.2 | custom fusion | bytes 2084832 | tf_op jit(solution)/shard_map/gather | solution.py:265
  179.0 3.6 %all-to-all-start.2 = ((bf16[8,127,512]{2,1,0:T(8,128)(2,1)}), bf16[8,127,512]{2,1,0:T(8,128)(2,1)S(1)}, u32[]{:S(2)}, u32[]{:S(2)}) async-start(bf16[8,127,512]{2,1,0:T(8,128)(2,1)} %broadcast_select_fusion), calls=%async_computation.2 | async-start | bytes 2097152 | tf_op jit(solution)/shard_map/all_to_all | solution.py:267
  183.7 24.4 %all-to-all-done.2 = bf16[8,127,512]{2,1,0:T(8,128)(2,1)S(1)} async-done(((bf16[8,127,512]{2,1,0:T(8,128)(2,1)}), bf16[8,127,512]{2,1,0:T(8,128)(2,1)S(1)}, u32[]{:S(2)}, u32[]{:S(2)}) %all-to-all-start.2) | async-done | bytes 1040416 | tf_op jit(solution)/shard_map/all_to_all | solution.py:267
  (93 shorter events, 24.0 us)
Async XLA Ops:
  0.0 96.1 %copy-start = (bf16[512,2048]{1,0:T(8,128)(2,1)S(1)}, bf16[512,2048]{1,0:T(8,128)(2,1)}, u32[]{:S(2)}) copy-start(bf16[512,2048]{1,0:T(8,128)(2,1)} %param.29) | copy-start | bytes 6291460
  7.3 49.7 %all-to-all-start = ((bf16[8,127,512]{2,1,0:T(8,128)(2,1)}), bf16[8,127,512]{2,1,0:T(8,128)(2,1)S(1)}, u32[]{:S(2)}, u32[]{:S(2)}) async-start(bf16[8,127,512]{2,1,0:T(8,128)(2,1)} %fusion.13), calls=%async_computation | async-start | bytes 2097152 | tf_op jit(solution)/shard_map/all_to_all | solution.py:241
  19.8 4.6 %slice-start = ((bf16[1024,512]{1,0:T(8,128)(2,1)}), bf16[8,512]{1,0:T(8,128)(2,1)S(1)}, s32[]{:S(2)}) async-start(bf16[1024,512]{1,0:T(8,128)(2,1)} %q_ref.1), calls=%async_computation.3 | async-start | bytes 16384 | tf_op jit(solution)/shard_map/slice | solution.py:100
  19.8 4.7 %slice-start.1 = ((bf16[1024,128]{1,0:T(8,128)(2,1)}), bf16[8,128]{1,0:T(8,128)(2,1)S(1)}, s32[]{:S(2)}) async-start(bf16[1024,128]{1,0:T(8,128)(2,1)} %kf_ref.1), calls=%async_computation.4 | async-start | bytes 4096 | tf_op jit(solution)/shard_map/slice | solution.py:103
  19.8 4.8 %copy-start.8 = (s32[8]{0:T(128)S(1)}, s32[8]{0:T(128)}, u32[]{:S(2)}) copy-start(s32[8]{0:T(128)} %param.24) | copy-start | bytes 100
  19.8 4.8 %copy-start.9 = (s32[8]{0:T(128)S(1)}, s32[8]{0:T(128)}, u32[]{:S(2)}) copy-start(s32[8]{0:T(128)} %param.25) | copy-start | bytes 100
  19.8 4.8 %copy-start.10 = (s32[8]{0:T(128)S(1)}, s32[8]{0:T(128)}, u32[]{:S(2)}) copy-start(s32[8]{0:T(128)} %param.26) | copy-start | bytes 100
  24.4 3.2 %slice-start.2 = ((bf16[1024,128]{1,0:T(8,128)(2,1)}), bf16[8,128]{1,0:T(8,128)(2,1)S(1)}, s32[]{:S(2)}) async-start(bf16[1024,128]{1,0:T(8,128)(2,1)} %vf_ref.1), calls=%async_computation.5 | async-start | bytes 4096 | tf_op jit(solution)/shard_map/slice | solution.py:104
  26.3 1.0 copy-start.4
  57.0 3.4 %copy-start.2 = (bf16[8,127,512]{2,1,0:T(8,128)(2,1)}, bf16[8,127,512]{2,1,0:T(8,128)(2,1)S(1)}, u32[]{:S(2)}) copy-start(bf16[8,127,512]{2,1,0:T(8,128)(2,1)S(1)} %all-to-all-done) | copy-start | bytes 3121156
  60.4 31.5 %all-to-all-start.1 = ((bf16[8,127,512]{2,1,0:T(8,128)(2,1)}), bf16[8,127,512]{2,1,0:T(8,128)(2,1)}, u32[]{:S(2)}, u32[]{:S(2)}) async-start(bf16[8,127,512]{2,1,0:T(8,128)(2,1)} %fusion.11), calls=%async_computation.1 | async-start | bytes 2097152 | tf_op jit(solution)/shard_map/all_to_all | solution.py:247
  98.4 1.3 copy-start.5
  98.5 7.8 %copy-start.3 = (bf16[8,127,512]{2,1,0:T(8,128)(2,1)S(1)}, bf16[8,127,512]{2,1,0:T(8,128)(2,1)}, u32[]{:S(2)}) copy-start(bf16[8,127,512]{2,1,0:T(8,128)(2,1)} %copy-done.2) | copy-start | bytes 3121156
  99.7 2.7 %collective-permute-start = (bf16[2,512,512]{2,1,0:T(8,128)(2,1)S(1)}, bf16[2,512,512]{2,1,0:T(8,128)(2,1)S(1)}, u32[]{:S(2)}, u32[]{:S(2)}) collective-permute-start(bf16[2,512,512]{2,1,0:T(8,128)(2,1)S(1)} %pad_maximum_fusion.2), channel_id=1, source_target_pairs={{0,1},{1,0},{2,3},{3,2},{4,5},{5,4},{6,7},{7,6},{8,9},{9,8},{10,11... | collective-permute-start | bytes 3145736 | tf_op jit(solution)/shard_map/ppermute | solution.py:163
  102.4 3.9 %copy-start.6 = (bf16[2,512,512]{2,1,0:T(8,128)(2,1)}, bf16[2,512,512]{2,1,0:T(8,128)(2,1)S(1)}, u32[]{:S(2)}) copy-start(bf16[2,512,512]{2,1,0:T(8,128)(2,1)S(1)} %collective-permute-done) | copy-start | bytes 3145732
  104.8 14.3 %collective-permute-start.1 = (bf16[512,512]{1,0:T(8,128)(2,1)}, bf16[512,512]{1,0:T(8,128)(2,1)}, u32[]{:S(2)}, u32[]{:S(2)}) collective-permute-start(bf16[512,512]{1,0:T(8,128)(2,1)} %fusion.18), channel_id=1, source_target_pairs={{0,2},{1,3},{2,0},{3,1},{4,6},{5,7},{6,4},{7,5},{8,10},{9,11},{10,... | collective-permute-start | bytes 1572872 | tf_op jit(solution)/shard_map/ppermute | solution.py:168
  106.6 12.4 %copy-start.7 = (bf16[2,512,512]{2,1,0:T(8,128)(2,1)S(1)}, bf16[2,512,512]{2,1,0:T(8,128)(2,1)}, u32[]{:S(2)}) copy-start(bf16[2,512,512]{2,1,0:T(8,128)(2,1)} %copy-done.6) | copy-start | bytes 3145732
  120.5 13.2 %collective-permute-start.2 = (bf16[512,512]{1,0:T(8,128)(2,1)S(1)}, bf16[512,512]{1,0:T(8,128)(2,1)S(1)}, u32[]{:S(2)}, u32[]{:S(2)}) collective-permute-start(bf16[512,512]{1,0:T(8,128)(2,1)S(1)} %fusion.21), channel_id=1, source_target_pairs={{0,2},{1,3},{2,0},{3,1},{4,6},{5,7},{6,4},{7,5},{8,10},{9,11},{10,... | collective-permute-start | bytes 1572872 | tf_op jit(solution)/shard_map/ppermute | solution.py:179
  133.8 2.7 %collective-permute-start.3 = (bf16[2,512,512]{2,1,0:T(8,128)(2,1)S(1)}, bf16[2,512,512]{2,1,0:T(8,128)(2,1)S(1)}, u32[]{:S(2)}, u32[]{:S(2)}) collective-permute-start(bf16[2,512,512]{2,1,0:T(8,128)(2,1)S(1)} %pad_maximum_fusion.3), channel_id=1, source_target_pairs={{0,1},{1,0},{2,3},{3,2},{4,5},{5,4},{6,7},{7,6},{8,9},{9,8},{10,11... | collective-permute-start | bytes 3145736 | tf_op jit(solution)/shard_map/ppermute | solution.py:180
  136.9 2.2 %copy-start.11 = (bf16[2048,1024]{1,0:T(8,128)(2,1)S(1)}, bf16[2048,1024]{1,0:T(8,128)(2,1)}, u32[]{:S(2)}) copy-start(bf16[2048,1024]{1,0:T(8,128)(2,1)} %param.31) | copy-start | bytes 12582916
  137.1 2.0 copy-start.12
  154.2 2.7 %collective-permute-start.4 = (bf16[2,512,512]{2,1,0:T(8,128)(2,1)S(1)}, bf16[2,512,512]{2,1,0:T(8,128)(2,1)S(1)}, u32[]{:S(2)}, u32[]{:S(2)}) collective-permute-start(bf16[2,512,512]{2,1,0:T(8,128)(2,1)S(1)} %pad_maximum_fusion.4), channel_id=1, source_target_pairs={{0,1},{1,0},{2,3},{3,2},{4,5},{5,4},{6,7},{7,6},{8,9},{9,8},{10,11... | collective-permute-start | bytes 3145736 | tf_op jit(solution)/shard_map/ppermute | solution.py:163
  158.1 14.0 %collective-permute-start.5 = (bf16[512,512]{1,0:T(8,128)(2,1)S(1)}, bf16[512,512]{1,0:T(8,128)(2,1)S(1)}, u32[]{:S(2)}, u32[]{:S(2)}) collective-permute-start(bf16[512,512]{1,0:T(8,128)(2,1)S(1)} %fusion.14), channel_id=1, source_target_pairs={{0,2},{1,3},{2,0},{3,1},{4,6},{5,7},{6,4},{7,5},{8,10},{9,11},{10,... | collective-permute-start | bytes 1572872 | tf_op jit(solution)/shard_map/ppermute | solution.py:168
  179.0 29.1 %all-to-all-start.2 = ((bf16[8,127,512]{2,1,0:T(8,128)(2,1)}), bf16[8,127,512]{2,1,0:T(8,128)(2,1)S(1)}, u32[]{:S(2)}, u32[]{:S(2)}) async-start(bf16[8,127,512]{2,1,0:T(8,128)(2,1)} %broadcast_select_fusion), calls=%async_computation.2 | async-start | bytes 2097152 | tf_op jit(solution)/shard_map/all_to_all | solution.py:267
  208.2 2.3 %copy-start.1 = (bf16[512,2048]{1,0:T(8,128)(2,1)S(1)}, bf16[512,2048]{1,0:T(8,128)(2,1)}, u32[]{:S(2)}) copy-start(bf16[512,2048]{1,0:T(8,128)(2,1)} %param.29) | copy-start | bytes 6291460

commit v5 on v4

--- a/solution.py
+++ b/solution.py
@@ -95,29 +95,36 @@
 
 def decode_attention(queries, new_keys, new_values, pool_keys, pool_values, decode_mask):
     kv = new_keys.shape[1] // HEAD_DIM
-    per_kv = queries.shape[1] // HEAD_DIM // kv
+    heads = queries.shape[1] // HEAD_DIM
+    per_kv = heads // kv
     cached = DEC * REG
-    q = queries[:DEC].reshape(DEC, kv, per_kv, HEAD_DIM)
-    kc = pool_keys[:cached].reshape(cached, kv, HEAD_DIM)
-    vc = pool_values[:cached].reshape(cached, kv, HEAD_DIM)
-    kn = new_keys[:DEC].reshape(DEC, kv, HEAD_DIM)
-    vn = new_values[:DEC].reshape(DEC, kv, HEAD_DIM)
-    s_c = jnp.einsum("rjhd,tjd->rjht", q, kc, preferred_element_type=jnp.float32) * SCALE
-    s_n = jnp.einsum("rjhd,tjd->rjht", q, kn, preferred_element_type=jnp.float32) * SCALE
-    s_c = jnp.where(decode_mask[:, None, None, :cached], s_c, MASKED_SCORE)
-    s_n = jnp.where(decode_mask[:, None, None, cached:], s_n, MASKED_SCORE)
+    q = queries[:DEC].reshape(DEC, heads, HEAD_DIM)
+    owner = jnp.arange(heads, dtype=jnp.int32) // per_kv
+    lanes = [
+        jnp.where((owner == j)[None, :, None], q, jnp.zeros((), q.dtype)) for j in range(kv)
+    ]
+    q_ext = jnp.concatenate(lanes, axis=2)
+    s_c = jnp.einsum("rhc,tc->rht", q_ext, pool_keys[:cached], preferred_element_type=jnp.float32)
+    s_n = jnp.einsum("rhc,tc->rht", q_ext, new_keys[:DEC], preferred_element_type=jnp.float32)
+    s_c = jnp.where(decode_mask[:, None, :cached], s_c * SCALE, MASKED_SCORE)
+    s_n = jnp.where(decode_mask[:, None, cached:], s_n * SCALE, MASKED_SCORE)
     highest = jnp.maximum(
-        jnp.max(s_c, axis=3, keepdims=True), jnp.max(s_n, axis=3, keepdims=True)
+        jnp.max(s_c, axis=2, keepdims=True), jnp.max(s_n, axis=2, keepdims=True)
     )
     e_c = jnp.exp(s_c - highest)
     e_n = jnp.exp(s_n - highest)
-    totals = jnp.sum(e_c, axis=3, keepdims=True) + jnp.sum(e_n, axis=3, keepdims=True)
+    totals = jnp.sum(e_c, axis=2, keepdims=True) + jnp.sum(e_n, axis=2, keepdims=True)
     p_c = (e_c / totals).astype(jnp.bfloat16)
     p_n = (e_n / totals).astype(jnp.bfloat16)
-    out = jnp.einsum("rjht,tjd->rjhd", p_c, vc, preferred_element_type=jnp.float32) + jnp.einsum(
-        "rjht,tjd->rjhd", p_n, vn, preferred_element_type=jnp.float32
-    )
-    return out.astype(jnp.bfloat16).reshape(DEC, kv * per_kv * HEAD_DIM)
+    full = jnp.einsum(
+        "rht,tc->rhc", p_c, pool_values[:cached], preferred_element_type=jnp.float32
+    ) + jnp.einsum("rht,tc->rhc", p_n, new_values[:DEC], preferred_element_type=jnp.float32)
+    out = full[:, :, 0:HEAD_DIM]
+    for j in range(1, kv):
+        out = jnp.where(
+            (owner == j)[None, :, None], full[:, :, j * HEAD_DIM : (j + 1) * HEAD_DIM], out
+        )
+    return out.astype(jnp.bfloat16).reshape(DEC, heads * HEAD_DIM)
 
 
 def build_decode_mask(cache_len, prefix_group, prefix_len):
@@ -254,8 +261,21 @@
     flat_idx = src_dev * bucket + src_pos
     dense_attn = got_attn.reshape(spread, width)[flat_idx]
     dense_resid = got_resid.reshape(spread, width)[flat_idx]
-    mixed = finish(
-        dense_attn, dense_resid, out_weight, norm_gain, gate_weight, up_weight, down_weight
+    half = bal // 2
+    mixed = jnp.concatenate(
+        [
+            finish(
+                dense_attn[lo : lo + half],
+                dense_resid[lo : lo + half],
+                out_weight,
+                norm_gain,
+                gate_weight,
+                up_weight,
+                down_weight,
+            )
+            for lo in (0, half)
+        ],
+        axis=0,
     )
     lane = (device - firsts) % devices
     row_of = jnp.arange(bucket, dtype=jnp.int32)[None, :] * devices + lane[:, None]

time: 211 us -> 215 us (1.019)
  waiting for transfers between devices: 86.8 us -> 75 us
  other arithmetic: 21 us -> 28.9 us
  matrix products: 20 us -> 25.9 us
  starting transfers between devices: 21.8 us -> 25.4 us
    slice x10 -> x2, local copies, waits for them, and re-layouts: 9.13 us -> 0.01 us  [decode_attention(): q = queries[:DEC].reshape(DEC, heads, HEAD_DIM)]
    ppermute x2 -> x4, waiting for transfers between devices: 22.8 us -> 15.9 us  [grp_reduce_scatter(): arrived = lax.ppermute(other.astype(jnp.bfloat16), 'grp', far)]
    dot_general x1 -> x2, matrix products: 9.96 us -> 14.7 us  [finish(): jnp.dot(inner, down_weight, preferred_element_type=jnp.float32)]
    ppermute x2 -> x4, waiting for transfers between devices: 5.01 us -> 0.88 us  [grp_reduce_scatter(): incoming = lax.ppermute(outgoing, 'grp', near)]
    another operation x2 -> x4, other arithmetic: 0.2 us -> 3.47 us  [grp_reduce_scatter(): jnp.stack([grp_block(partial, me ^ 1, width), grp_block(partial, me ^ 3,...]
    ppermute x1 -> x2, waiting for transfers between devices: 2.62 us -> 0.01 us  [grp_all_gather(): pair = lax.ppermute(jnp.stack([block, across]), 'grp', near)]
    ppermute x1 -> x2, waiting for transfers between devices: 11.6 us -> 13.1 us  [grp_all_gather(): across = lax.ppermute(block, 'grp', far)]
    convert_element_type x2 -> x4, other arithmetic: 3.53 us -> 4.93 us  [grp_reduce_scatter(): arrived = lax.ppermute(other.astype(jnp.bfloat16), 'grp', far)]
  transfers between devices with their start and end apart: 9 -> 15, of which waited for: 8 -> 9; matrix products, arithmetic and copies ran while one was open for 11% -> 24% of each run, Pallas kernels for 13% -> 12%
where the time goes in v5:
time: 215 us; the launch traced here: 214 us
  waiting for transfers between devices  75 us (35%)
  local copies, waits for them, and re-layouts  29.3 us (14%)
  other arithmetic  28.9 us (13%)
  Pallas kernels  26.4 us (12%)
  matrix products  25.9 us (12%)
  starting transfers between devices  25.4 us (12%)
  between operations  3.1 us (1%)
    pallas_call x1, Pallas kernels, span_attention(): pl.pallas_call(span_kernel, out_shape=jax.ShapeDtypeStruct((rows, width),...  26.4 us
    all_to_all x1, waiting for transfers between devices, shards(): lax.all_to_all(picked, 'req', split_axis=0, concat_axis=0, tiled=True)  24.7 us
    all_to_all x1, waiting for transfers between devices, shards(): lax.all_to_all(outbound(attn), 'req', split_axis=0, concat_axis=0, tiled=...  20.4 us
    ppermute x4, waiting for transfers between devices, grp_reduce_scatter(): arrived = lax.ppermute(other.astype(jnp.bfloat16), 'grp', far)  15.9 us
    dot_general x2, matrix products, finish(): jnp.dot(inner, down_weight, preferred_element_type=jnp.float32)  14.7 us
    ppermute x2, waiting for transfers between devices, grp_all_gather(): across = lax.ppermute(block, 'grp', far)  13.1 us
    all_to_all x1, starting transfers between devices, shards(): lax.all_to_all(send_resid, 'req', split_axis=0, concat_axis=0, tiled=True)  7.25 us
    all_to_all x1, starting transfers between devices, shards(): lax.all_to_all(outbound(attn), 'req', split_axis=0, concat_axis=0, tiled=...  5.98 us
  transfers between devices with their start and end apart: 15, of which 9 were waited for; matrix products, arithmetic and copies ran while one was open for 24% of the time, Pallas kernels for 12%

profile of v5, /device:TPU:0, one launch (start us, length us, event | category | flops | bytes accessed | tf_op | source)
XLA Modules:
  0.0 214.0 jit_solution(10619328337795151499)
XLA Ops:
  6.0 1.4 fusion.14
  7.4 7.3 %all-to-all-start = ((bf16[8,127,512]{2,1,0:T(8,128)(2,1)}), bf16[8,127,512]{2,1,0:T(8,128)(2,1)S(1)}, u32[]{:S(2)}, u32[]{:S(2)}) async-start(bf16[8,127,512]{2,1,0:T(8,128)(2,1)} %fusion.14), calls=%async_computation | async-start | bytes 2097152 | tf_op jit(solution)/shard_map/all_to_all | solution.py:248
  15.7 1.9 fusion.78
  20.4 26.4 %shard_map.154 = bf16[1024,512]{1,0:T(8,128)(2,1)} custom-call(s32[1]{0:T(128)S(6)} %copy.43.start_ref, bf16[1024,512]{1,0:T(8,128)(2,1)} %q_ref.1, bf16[4608,128]{1,0:T(8,128)(2,1)} %kp_ref.1, bf16[4608,128]{1,0:T(8,128)(2,1)} %vp_ref.1, bf16[1024,128]{1,0:T(8,128)(2,1)} %kf_ref.1, bf16[1024,128]{1,0:T(8,128)(2,1)} %vf_ref.1), custom_call_target="tpu_custom_call" | custom-call | flops 34359738368 | bytes 2883584 | tf_op jit(solution)/shard_map/pallas_call | solution.py:83
  47.4 1.7 slice_bitcast_fusion
  50.7 6.0 %all-to-all-start.1 = ((bf16[8,127,512]{2,1,0:T(8,128)(2,1)}), bf16[8,127,512]{2,1,0:T(8,128)(2,1)}, u32[]{:S(2)}, u32[]{:S(2)}) async-start(bf16[8,127,512]{2,1,0:T(8,128)(2,1)} %fusion.12), calls=%async_computation.1 | async-start | bytes 2097152 | tf_op jit(solution)/shard_map/all_to_all | solution.py:254
  56.8 4.3 %compare_select_fusion.6 = s32[512,1]{0,1:T(1,128)S(1)} fusion(s32[]{:T(128)} %bitcast.12, s32[]{:T(128)} %bitcast.13, s32[]{:T(128)} %bitcast.14, s32[]{:T(128)} %bitcast.15, s32[]{:T(128)} %bitcast.16, s32[]{:T(128)} %bitcast.18, s32[]{:T(128)} %bitcast.17, s32[512,1]{0,1:T(1,128)S(1)} %bitcast.143), kind=kLoop, calls=%fused_computation.151 | loop fusion | flops 7680 | bytes 4124 | tf_op jit(solution)/shard_map/gather | solution.py:260
  61.8 20.4 %all-to-all-done.1 = bf16[8,127,512]{2,1,0:T(8,128)(2,1)} async-done(((bf16[8,127,512]{2,1,0:T(8,128)(2,1)}), bf16[8,127,512]{2,1,0:T(8,128)(2,1)}, u32[]{:S(2)}, u32[]{:S(2)}) %all-to-all-start.1) | async-done | bytes 1040416 | tf_op jit(solution)/shard_map/all_to_all | solution.py:254
  82.3 1.5 reshape.504
  83.8 2.6 %gather_fusion.1 = bf16[512,512]{1,0:T(8,128)(2,1)} fusion(bf16[1016,512]{1,0:T(8,128)(2,1)S(1)} %reshape.504, s32[1024]{0:T(1024)S(1)} %pad_clamp_fusion.1), kind=kCustom, calls=%fused_computation.1 | custom fusion | bytes 1050624 | tf_op jit(solution)/shard_map/gather | solution.py:262
  86.4 1.7 convolution_convert_fusion.1
  93.2 1.6 collective-permute-start.1
  94.8 1.8 fusion.25
  97.1 1.5 reshape.502
  98.6 2.6 %gather_fusion = bf16[512,512]{1,0:T(8,128)(2,1)} fusion(bf16[1016,512]{1,0:T(8,128)(2,1)S(1)} %reshape.502, s32[1024]{0:T(1024)S(1)} %pad_clamp_fusion.1), kind=kCustom, calls=%fused_computation | custom fusion | bytes 1050624 | tf_op jit(solution)/shard_map/gather | solution.py:263
  102.6 4.8 %collective-permute-done.7 = bf16[256,512]{1,0:T(8,128)(2,1)} collective-permute-done((bf16[256,512]{1,0:T(8,128)(2,1)}, bf16[256,512]{1,0:T(8,128)(2,1)}, u32[]{:S(2)}, u32[]{:S(2)}) %collective-permute-start.7) | collective-permute-done | bytes 262176 | tf_op jit(solution)/shard_map/ppermute | solution.py:175
  107.4 1.8 fusion.36
  109.2 1.6 collective-permute-start.8
  110.7 6.0 %collective-permute-done.8 = bf16[256,512]{1,0:T(8,128)(2,1)S(1)} collective-permute-done((bf16[256,512]{1,0:T(8,128)(2,1)S(1)}, bf16[256,512]{1,0:T(8,128)(2,1)S(1)}, u32[]{:S(2)}, u32[]{:S(2)}) %collective-permute-start.8) | collective-permute-done | bytes 262176 | tf_op jit(solution)/shard_map/ppermute | solution.py:186
  117.6 1.5 collective-permute-start.2
  119.2 7.1 %collective-permute-done.2 = bf16[256,512]{1,0:T(8,128)(2,1)S(1)} collective-permute-done((bf16[256,512]{1,0:T(8,128)(2,1)S(1)}, bf16[256,512]{1,0:T(8,128)(2,1)S(1)}, u32[]{:S(2)}, u32[]{:S(2)}) %collective-permute-start.2) | collective-permute-done | bytes 262176 | tf_op jit(solution)/shard_map/ppermute | solution.py:186
  130.6 2.3 %fusion.43 = f32[256,1024]{1,0:T(8,128)} fusion(bf16[2048,1024]{1,0:T(8,128)(2,1)S(1)} %copy-done.12, f32[256]{0:T(256)S(1)} %add_rsqrt_fusion, f32[2048]{0:T(1024)S(1)} %copy-done.15, bf16[256,512]{1,0:T(8,128)(2,1)S(1)} %get-tuple-element.23, bf16[256,512]{1,0:T(8,128)(2,1)S(1)} %get-tuple-element.24, bf16[256,512]{1,0:T(8,128)(2,1)S(1)} %get-tuple-element.25, ...), kind=kOutput, calls=%fused_computation.89 | convolution fusion | flops 1079508992 | bytes 6300672 | tf_op jit(solution)/shard_map/dot_general | solution.py:202
  132.9 7.4 %convolution_convert_fusion.2 = bf16[256,2048]{1,0:T(8,128)(2,1)} fusion(bf16[1024,2048]{1,0:T(8,128)(2,1)} %param.33, bf16[2048,1024]{1,0:T(8,128)(2,1)} %param.32, f32[256,1024]{1,0:T(8,128)} %fusion.43, f32[256]{0:T(256)S(1)} %add_rsqrt_fusion, f32[2048]{0:T(1024)S(1)} %copy-done.15, bf16[256,512]{1,0:T(8,128)(2,1)S(1)} %get-tuple-element.23, ...), kind=kOutput, calls=%fused_computation.11 | convolution fusion | flops 2155347968 | bytes 11543552 | tf_op jit(solution)/shard_map/dot_general | solution.py:206
  146.1 2.3 %fusion.47 = f32[256,1024]{1,0:T(8,128)} fusion(bf16[2048,1024]{1,0:T(8,128)(2,1)S(1)} %copy-done.13, f32[2048]{0:T(1024)S(1)} %copy-done.15, f32[256]{0:T(256)S(1)} %add_rsqrt_fusion.1, bf16[256,512]{1,0:T(8,128)(2,1)S(1)} %get-tuple-element.15, bf16[256,512]{1,0:T(8,128)(2,1)S(1)} %get-tuple-element.16, bf16[256,512]{1,0:T(8,128)(2,1)S(1)} %get-tuple-element.17, ...), kind=kOutput, calls=%fused_computation.90 | convolution fusion | flops 1079508992 | bytes 6300672 | tf_op jit(solution)/shard_map/dot_general | solution.py:202
  148.4 7.3 %convolution_convert_fusion.3 = bf16[256,2048]{1,0:T(8,128)(2,1)} fusion(bf16[1024,2048]{1,0:T(8,128)(2,1)} %param.33, bf16[2048,1024]{1,0:T(8,128)(2,1)} %param.32, f32[256,1024]{1,0:T(8,128)} %fusion.47, f32[2048]{0:T(1024)S(1)} %copy-done.15, f32[256]{0:T(256)S(1)} %add_rsqrt_fusion.1, bf16[256,512]{1,0:T(8,128)(2,1)S(1)} %get-tuple-element.15, ...), kind=kOutput, calls=%fused_computation.12 | convolution fusion | flops 2155347968 | bytes 11543552 | tf_op jit(solution)/shard_map/dot_general | solution.py:206
  159.0 1.6 collective-permute-start.11
  162.4 5.7 %collective-permute-done.11 = bf16[256,512]{1,0:T(8,128)(2,1)S(1)} collective-permute-done((bf16[256,512]{1,0:T(8,128)(2,1)S(1)}, bf16[256,512]{1,0:T(8,128)(2,1)S(1)}, u32[]{:S(2)}, u32[]{:S(2)}) %collective-permute-start.11) | collective-permute-done | bytes 262176 | tf_op jit(solution)/shard_map/ppermute | solution.py:175
  169.3 4.1 %collective-permute-done.5 = bf16[256,512]{1,0:T(8,128)(2,1)S(1)} collective-permute-done((bf16[256,512]{1,0:T(8,128)(2,1)S(1)}, bf16[256,512]{1,0:T(8,128)(2,1)S(1)}, u32[]{:S(2)}, u32[]{:S(2)}) %collective-permute-start.5) | collective-permute-done | bytes 262176 | tf_op jit(solution)/shard_map/ppermute | solution.py:175
  174.5 5.1 %gather_fusion.2 = bf16[1016,512]{1,0:T(8,128)(2,1)} fusion(bf16[512,512]{1,0:T(8,128)(2,1)S(1)} %pad_maximum_fusion.10, s32[1024]{0:T(1024)S(1)} %pad_clamp_fusion), kind=kCustom, calls=%fused_computation.2 | custom fusion | bytes 2084832 | tf_op jit(solution)/shard_map/gather | solution.py:285
  179.6 1.5 reshape.505
  182.3 3.6 %all-to-all-start.2 = ((bf16[8,127,512]{2,1,0:T(8,128)(2,1)}), bf16[8,127,512]{2,1,0:T(8,128)(2,1)S(1)}, u32[]{:S(2)}, u32[]{:S(2)}) async-start(bf16[8,127,512]{2,1,0:T(8,128)(2,1)} %broadcast_select_fusion), calls=%async_computation.2 | async-start | bytes 2097152 | tf_op jit(solution)/shard_map/all_to_all | solution.py:287
  187.1 24.7 %all-to-all-done.2 = bf16[8,127,512]{2,1,0:T(8,128)(2,1)S(1)} async-done(((bf16[8,127,512]{2,1,0:T(8,128)(2,1)}), bf16[8,127,512]{2,1,0:T(8,128)(2,1)S(1)}, u32[]{:S(2)}, u32[]{:S(2)}) %all-to-all-start.2) | async-done | bytes 1040416 | tf_op jit(solution)/shard_map/all_to_all | solution.py:287
  (120 shorter events, 39.7 us)
Async XLA Ops:
  0.0 86.4 %copy-start = (bf16[512,2048]{1,0:T(8,128)(2,1)S(1)}, bf16[512,2048]{1,0:T(8,128)(2,1)}, u32[]{:S(2)}) copy-start(bf16[512,2048]{1,0:T(8,128)(2,1)} %param.29) | copy-start | bytes 6291460
  5.9 9.4 %slice-start = ((bf16[1024,512]{1,0:T(8,128)(2,1)}), bf16[8,512]{1,0:T(8,128)(2,1)S(1)}, s32[]{:S(2)}) async-start(bf16[1024,512]{1,0:T(8,128)(2,1)} %q_ref.1), calls=%async_computation.3 | async-start | bytes 16384 | tf_op jit(solution)/shard_map/slice | solution.py:101
  5.9 9.6 %copy-start.9 = (s32[8]{0:T(128)S(1)}, s32[8]{0:T(128)}, u32[]{:S(2)}) copy-start(s32[8]{0:T(128)} %param.24) | copy-start | bytes 100
  6.0 9.6 %copy-start.10 = (s32[8]{0:T(128)S(1)}, s32[8]{0:T(128)}, u32[]{:S(2)}) copy-start(s32[8]{0:T(128)} %param.25) | copy-start | bytes 100
  6.0 9.6 %copy-start.11 = (s32[8]{0:T(128)S(1)}, s32[8]{0:T(128)}, u32[]{:S(2)}) copy-start(s32[8]{0:T(128)} %param.26) | copy-start | bytes 100
  7.4 40.0 %all-to-all-start = ((bf16[8,127,512]{2,1,0:T(8,128)(2,1)}), bf16[8,127,512]{2,1,0:T(8,128)(2,1)S(1)}, u32[]{:S(2)}, u32[]{:S(2)}) async-start(bf16[8,127,512]{2,1,0:T(8,128)(2,1)} %fusion.14), calls=%async_computation | async-start | bytes 2097152 | tf_op jit(solution)/shard_map/all_to_all | solution.py:248
  15.4 3.5 %copy-start.14 = (bf16[4608,128]{1,0:T(8,128)(2,1)S(1)}, bf16[4608,128]{1,0:T(8,128)(2,1)}, u32[]{:S(2)}) copy-start(bf16[4608,128]{1,0:T(8,128)(2,1)} %vp_ref.1) | copy-start | bytes 3538948
  47.4 3.4 %copy-start.1 = (bf16[8,127,512]{2,1,0:T(8,128)(2,1)}, bf16[8,127,512]{2,1,0:T(8,128)(2,1)S(1)}, u32[]{:S(2)}) copy-start(bf16[8,127,512]{2,1,0:T(8,128)(2,1)S(1)} %all-to-all-done) | copy-start | bytes 3121156
  50.7 31.5 %all-to-all-start.1 = ((bf16[8,127,512]{2,1,0:T(8,128)(2,1)}), bf16[8,127,512]{2,1,0:T(8,128)(2,1)}, u32[]{:S(2)}, u32[]{:S(2)}) async-start(bf16[8,127,512]{2,1,0:T(8,128)(2,1)} %fusion.12), calls=%async_computation.1 | async-start | bytes 2097152 | tf_op jit(solution)/shard_map/all_to_all | solution.py:254
  86.4 1.7 copy-start.4
  88.2 4.0 %copy-start.2 = (bf16[256,2048]{1,0:T(8,128)(2,1)}, bf16[256,2048]{1,0:T(8,128)(2,1)S(1)}, u32[]{:S(2)}) copy-start(bf16[256,2048]{1,0:T(8,128)(2,1)S(1)} %convolution_convert_fusion.1) | copy-start | bytes 3145732
  88.9 1.9 copy-start.3
  89.9 2.3 %collective-permute-start = (bf16[2,256,512]{2,1,0:T(8,128)(2,1)}, bf16[2,256,512]{2,1,0:T(8,128)(2,1)}, u32[]{:S(2)}, u32[]{:S(2)}) collective-permute-start(bf16[2,256,512]{2,1,0:T(8,128)(2,1)} %pad_maximum_fusion.4), channel_id=1, source_target_pairs={{0,1},{1,0},{2,3},{3,2},{4,5},{5,4},{6,7},{7,6},{8,9},{9,8},{10,11... | collective-permute-start | bytes 1572872 | tf_op jit(solution)/shard_map/ppermute | solution.py:170
  90.8 4.0 %collective-permute-start.6 = (bf16[2,256,512]{2,1,0:T(8,128)(2,1)}, bf16[2,256,512]{2,1,0:T(8,128)(2,1)}, u32[]{:S(2)}, u32[]{:S(2)}) collective-permute-start(bf16[2,256,512]{2,1,0:T(8,128)(2,1)} %pad_maximum_fusion.7), channel_id=1, source_target_pairs={{0,1},{1,0},{2,3},{3,2},{4,5},{5,4},{6,7},{7,6},{8,9},{9,8},{10,11... | collective-permute-start | bytes 1572872 | tf_op jit(solution)/shard_map/ppermute | solution.py:170
  93.2 9.3 %collective-permute-start.1 = (bf16[256,512]{1,0:T(8,128)(2,1)S(1)}, bf16[256,512]{1,0:T(8,128)(2,1)}, u32[]{:S(2)}, u32[]{:S(2)}) collective-permute-start(bf16[256,512]{1,0:T(8,128)(2,1)S(1)} %fusion.33), channel_id=1, source_target_pairs={{0,2},{1,3},{2,0},{3,1},{4,6},{5,7},{6,4},{7,5},{8,10},{9,11},{10,... | collective-permute-start | bytes 786440 | tf_op jit(solution)/shard_map/ppermute | solution.py:175
  96.6 10.8 %collective-permute-start.7 = (bf16[256,512]{1,0:T(8,128)(2,1)}, bf16[256,512]{1,0:T(8,128)(2,1)}, u32[]{:S(2)}, u32[]{:S(2)}) collective-permute-start(bf16[256,512]{1,0:T(8,128)(2,1)} %fusion.25), channel_id=1, source_target_pairs={{0,2},{1,3},{2,0},{3,1},{4,6},{5,7},{6,4},{7,5},{8,10},{9,11},{10,... | collective-permute-start | bytes 786440 | tf_op jit(solution)/shard_map/ppermute | solution.py:175
  109.2 7.6 %collective-permute-start.8 = (bf16[256,512]{1,0:T(8,128)(2,1)S(1)}, bf16[256,512]{1,0:T(8,128)(2,1)S(1)}, u32[]{:S(2)}, u32[]{:S(2)}) collective-permute-start(bf16[256,512]{1,0:T(8,128)(2,1)S(1)} %get-tuple-element.31), channel_id=1, source_target_pairs={{0,2},{1,3},{2,0},{3,1},{4,6},{5,7},{6,4},{7,5},{8,10},{9,11},{10,... | collective-permute-start | bytes 786440 | tf_op jit(solution)/shard_map/ppermute | solution.py:186
  117.6 9.6 %collective-permute-start.9 = (bf16[2,256,512]{2,1,0:T(8,128)(2,1)}, bf16[2,256,512]{2,1,0:T(8,128)(2,1)}, u32[]{:S(2)}, u32[]{:S(2)}) collective-permute-start(bf16[2,256,512]{2,1,0:T(8,128)(2,1)} %pad_maximum_fusion.8), channel_id=1, source_target_pairs={{0,1},{1,0},{2,3},{3,2},{4,5},{5,4},{6,7},{7,6},{8,9},{9,8},{10,11... | collective-permute-start | bytes 1572872 | tf_op jit(solution)/shard_map/ppermute | solution.py:187
  117.6 8.7 %collective-permute-start.2 = (bf16[256,512]{1,0:T(8,128)(2,1)S(1)}, bf16[256,512]{1,0:T(8,128)(2,1)S(1)}, u32[]{:S(2)}, u32[]{:S(2)}) collective-permute-start(bf16[256,512]{1,0:T(8,128)(2,1)S(1)} %get-tuple-element.30), channel_id=1, source_target_pairs={{0,2},{1,3},{2,0},{3,1},{4,6},{5,7},{6,4},{7,5},{8,10},{9,11},{10,... | collective-permute-start | bytes 786440 | tf_op jit(solution)/shard_map/ppermute | solution.py:186
  126.3 2.0 copy-start.7
  127.2 15.5 %collective-permute-start.3 = (bf16[2,256,512]{2,1,0:T(8,128)(2,1)}, bf16[2,256,512]{2,1,0:T(8,128)(2,1)}, u32[]{:S(2)}, u32[]{:S(2)}) collective-permute-start(bf16[2,256,512]{2,1,0:T(8,128)(2,1)} %pad_maximum_fusion.5), channel_id=1, source_target_pairs={{0,1},{1,0},{2,3},{3,2},{4,5},{5,4},{6,7},{7,6},{8,9},{9,8},{10,11... | collective-permute-start | bytes 1572872 | tf_op jit(solution)/shard_map/ppermute | solution.py:187
  128.3 2.3 %copy-start.12 = (bf16[2048,1024]{1,0:T(8,128)(2,1)S(1)}, bf16[2048,1024]{1,0:T(8,128)(2,1)}, u32[]{:S(2)}) copy-start(bf16[2048,1024]{1,0:T(8,128)(2,1)} %param.31) | copy-start | bytes 12582916
  128.4 2.1 copy-start.15
  128.6 0.7 copy-start.6
  140.3 3.6 %copy-start.8 = (bf16[256,512]{1,0:T(8,128)(2,1)S(1)}, bf16[256,512]{1,0:T(8,128)(2,1)}, u32[]{:S(2)}) copy-start(bf16[256,512]{1,0:T(8,128)(2,1)} %copy-done.7) | copy-start | bytes 786436
  142.2 15.6 %collective-permute-start.10 = (bf16[2,256,512]{2,1,0:T(8,128)(2,1)}, bf16[2,256,512]{2,1,0:T(8,128)(2,1)}, u32[]{:S(2)}, u32[]{:S(2)}) collective-permute-start(bf16[2,256,512]{2,1,0:T(8,128)(2,1)} %pad_maximum_fusion.9), channel_id=1, source_target_pairs={{0,1},{1,0},{2,3},{3,2},{4,5},{5,4},{6,7},{7,6},{8,9},{9,8},{10,11... | collective-permute-start | bytes 1572872 | tf_op jit(solution)/shard_map/ppermute | solution.py:170
  143.8 2.3 %copy-start.13 = (bf16[2048,1024]{1,0:T(8,128)(2,1)S(1)}, bf16[2048,1024]{1,0:T(8,128)(2,1)}, u32[]{:S(2)}) copy-start(bf16[2048,1024]{1,0:T(8,128)(2,1)} %param.31) | copy-start | bytes 12582916
  144.1 0.7 copy-start.5
  157.7 2.9 %collective-permute-start.4 = (bf16[2,256,512]{2,1,0:T(8,128)(2,1)}, bf16[2,256,512]{2,1,0:T(8,128)(2,1)S(1)}, u32[]{:S(2)}, u32[]{:S(2)}) collective-permute-start(bf16[2,256,512]{2,1,0:T(8,128)(2,1)} %pad_maximum_fusion.6), channel_id=1, source_target_pairs={{0,1},{1,0},{2,3},{3,2},{4,5},{5,4},{6,7},{7,6},{8,9},{9,8},{10,11... | collective-permute-start | bytes 1572872 | tf_op jit(solution)/shard_map/ppermute | solution.py:170
  159.0 9.2 %collective-permute-start.11 = (bf16[256,512]{1,0:T(8,128)(2,1)S(1)}, bf16[256,512]{1,0:T(8,128)(2,1)S(1)}, u32[]{:S(2)}, u32[]{:S(2)}) collective-permute-start(bf16[256,512]{1,0:T(8,128)(2,1)S(1)} %fusion.21), channel_id=1, source_target_pairs={{0,2},{1,3},{2,0},{3,1},{4,6},{5,7},{6,4},{7,5},{8,10},{9,11},{10,... | collective-permute-start | bytes 786440 | tf_op jit(solution)/shard_map/ppermute | solution.py:175
  161.6 11.8 %collective-permute-start.5 = (bf16[256,512]{1,0:T(8,128)(2,1)S(1)}, bf16[256,512]{1,0:T(8,128)(2,1)S(1)}, u32[]{:S(2)}, u32[]{:S(2)}) collective-permute-start(bf16[256,512]{1,0:T(8,128)(2,1)S(1)} %fusion.29), channel_id=1, source_target_pairs={{0,2},{1,3},{2,0},{3,1},{4,6},{5,7},{6,4},{7,5},{8,10},{9,11},{10,... | collective-permute-start | bytes 786440 | tf_op jit(solution)/shard_map/ppermute | solution.py:175
  182.3 29.4 %all-to-all-start.2 = ((bf16[8,127,512]{2,1,0:T(8,128)(2,1)}), bf16[8,127,512]{2,1,0:T(8,128)(2,1)S(1)}, u32[]{:S(2)}, u32[]{:S(2)}) async-start(bf16[8,127,512]{2,1,0:T(8,128)(2,1)} %broadcast_select_fusion), calls=%async_computation.2 | async-start | bytes 2097152 | tf_op jit(solution)/shard_map/all_to_all | solution.py:287

commit v6 on v5

--- a/solution.py
+++ b/solution.py
@@ -1,3 +1,5 @@
+import functools
+
 import jax
 import jax.numpy as jnp
 from jax import lax
@@ -19,13 +21,12 @@
 QBLK = 256
 
 
-def span_kernel(start_ref, q_ref, kp_ref, vp_ref, kf_ref, vf_ref, o_ref):
+def span_kernel(kv_index, start_ref, q_ref, kp_ref, vp_ref, kf_ref, vf_ref, o_ref):
     span_start = start_ref[0]
-    first_kv = (pl.program_id(0) * 2 // (HEADS // KV_HEADS)) % 2 == 0
     half = HEAD_DIM
 
     def pick(ref, lo, hi):
-        return jnp.where(first_kv, ref[lo:hi, 0:half], ref[lo:hi, half : 2 * half])
+        return ref[lo:hi, kv_index * half : (kv_index + 1) * half]
 
     rows = q_ref.shape[0]
     prior = kp_ref.shape[0]
@@ -65,29 +66,33 @@
             o_ref[lo:hi, hh * half : (hh + 1) * half] = out.astype(o_ref.dtype)
 
 
-def span_attention(queries, pool_keys, pool_values, new_keys, new_values, span_start, cached):
+def span_attention(queries, pool_keys, pool_values, new_keys, new_values, span_start, cached, kv_index):
     rows, width = queries.shape
     kv_width = new_keys.shape[1]
     prior = REG
     lanes = 2 * HEAD_DIM
     heads = width // HEAD_DIM
-    q_spec = pl.BlockSpec((rows, lanes), lambda c, s: (0, c))
+    kv = kv_width // HEAD_DIM
+    steps = width // lanes // kv
+    base = kv_index * steps
+    q_spec = pl.BlockSpec((rows, lanes), lambda c, s: (0, base + c))
+    o_spec = pl.BlockSpec((rows, lanes), lambda c, s: (0, c))
     p_spec = pl.BlockSpec((prior, kv_width), lambda c, s: (cached // prior, 0))
     f_spec = pl.BlockSpec((rows, kv_width), lambda c, s: (0, 0))
-    flops = 4 * heads * rows * (prior + rows // 2) * HEAD_DIM
+    flops = 4 * (heads // kv) * rows * (prior + rows // 2) * HEAD_DIM
     cost = pl.CostEstimate(
         flops=16 * flops,
-        transcendentals=heads * rows * (prior + rows // 2),
-        bytes_accessed=2 * (2 * rows * width + 2 * (prior + rows) * kv_width),
+        transcendentals=(heads // kv) * rows * (prior + rows // 2),
+        bytes_accessed=2 * (2 * rows * width // kv + 2 * (prior + rows) * kv_width),
     )
     return pl.pallas_call(
-        span_kernel,
-        out_shape=jax.ShapeDtypeStruct((rows, width), jnp.bfloat16),
+        functools.partial(span_kernel, kv_index),
+        out_shape=jax.ShapeDtypeStruct((rows, steps * lanes), jnp.bfloat16),
         grid_spec=pltpu.PrefetchScalarGridSpec(
             num_scalar_prefetch=1,
-            grid=(width // lanes,),
+            grid=(steps,),
             in_specs=[q_spec, p_spec, p_spec, f_spec, f_spec],
-            out_specs=q_spec,
+            out_specs=o_spec,
         ),
         cost_estimate=cost,
     )(span_start.reshape(1).astype(jnp.int32), queries, pool_keys, pool_values, new_keys, new_values)
@@ -141,15 +146,24 @@
     return jnp.concatenate([shared | owned, jnp.eye(DEC, dtype=jnp.bool_)], axis=1)
 
 
-def attention(queries, new_keys, new_values, pool_keys, pool_values, decode_mask, span_start):
+def attention_parts(queries, new_keys, new_values, pool_keys, pool_values, decode_mask, span_start, send):
     cached = DEC * REG
-    span_rows = span_attention(
-        queries, pool_keys, pool_values, new_keys, new_values, span_start, cached
-    )
+    kv = new_keys.shape[1] // HEAD_DIM
+    part_width = queries.shape[1] // kv
     decode_rows = decode_attention(
         queries, new_keys, new_values, pool_keys, pool_values, decode_mask
     )
-    return lax.dynamic_update_slice(span_rows, decode_rows, (0, 0))
+    sent = []
+    for j in range(kv):
+        span_rows = span_attention(
+            queries, pool_keys, pool_values, new_keys, new_values, span_start, cached, j
+        )
+        mine = decode_rows[:, j * part_width : (j + 1) * part_width]
+        outgoing = send(lax.dynamic_update_slice(span_rows, mine, (0, 0)))
+        if j + 1 < kv:
+            outgoing, queries = lax.optimization_barrier((outgoing, queries))
+        sent.append(outgoing)
+    return sent
 
 
 def grp_block(x, index, width):
@@ -247,11 +261,14 @@
     send_resid = outbound(residual)
     got_resid = lax.all_to_all(send_resid, "req", split_axis=0, concat_axis=0, tiled=True)
     decode_mask = build_decode_mask(cache_len, prefix_group, prefix_len)
-    attn = attention(
-        queries, new_keys, new_values, pool_keys, pool_values, decode_mask, span_offset[0]
-    )
-    got_resid, attn = lax.optimization_barrier((got_resid, attn))
-    got_attn = lax.all_to_all(outbound(attn), "req", split_axis=0, concat_axis=0, tiled=True)
+    sent_parts = attention_parts(
+        queries, new_keys, new_values, pool_keys, pool_values, decode_mask, span_offset[0], outbound
+    )
+    got_resid, sent_parts[-1] = lax.optimization_barrier((got_resid, sent_parts[-1]))
+    got_parts = [
+        lax.all_to_all(part, "req", split_axis=0, concat_axis=0, tiled=True)
+        for part in sent_parts
+    ]
 
     slots = jnp.arange(bal, dtype=jnp.int32)
     wanted = slots * devices + device
@@ -259,23 +276,12 @@
     src_dev = jnp.minimum(src_dev, devices - 1)
     src_pos = jnp.clip((wanted - firsts[src_dev]) // devices, 0, bucket - 1)
     flat_idx = src_dev * bucket + src_pos
-    dense_attn = got_attn.reshape(spread, width)[flat_idx]
+    dense_attn = jnp.concatenate(
+        [got.reshape(spread, got.shape[2])[flat_idx] for got in got_parts], axis=1
+    )
     dense_resid = got_resid.reshape(spread, width)[flat_idx]
-    half = bal // 2
-    mixed = jnp.concatenate(
-        [
-            finish(
-                dense_attn[lo : lo + half],
-                dense_resid[lo : lo + half],
-                out_weight,
-                norm_gain,
-                gate_weight,
-                up_weight,
-                down_weight,
-            )
-            for lo in (0, half)
-        ],
-        axis=0,
+    mixed = finish(
+        dense_attn, dense_resid, out_weight, norm_gain, gate_weight, up_weight, down_weight
     )
     lane = (device - firsts) % devices
     row_of = jnp.arange(bucket, dtype=jnp.int32)[None, :] * devices + lane[:, None]

time: 215 us -> 205 us (0.953)
  matrix products: 25.9 us -> 19.6 us
  other arithmetic: 28.9 us -> 24.4 us
    all_to_all x1 -> x2, waiting for transfers between devices: 20.4 us -> 5.3 us  [shards(): lax.all_to_all(part, 'req', split_axis=0, concat_axis=0, tiled=True)]
    ppermute x4 -> x2, waiting for transfers between devices: 15.9 us -> 20.9 us  [grp_reduce_scatter(): arrived = lax.ppermute(other.astype(jnp.bfloat16), 'grp', far)]
    ppermute x4 -> x2, waiting for transfers between devices: 0.88 us -> 5.49 us  [grp_reduce_scatter(): incoming = lax.ppermute(outgoing, 'grp', near)]
    dot_general x2 -> x1, matrix products: 14.7 us -> 10.5 us  [finish(): jnp.dot(inner, down_weight, preferred_element_type=jnp.float32)]
    all_to_all x1 -> x2, starting transfers between devices: 5.98 us -> 10 us  [shards(): lax.all_to_all(part, 'req', split_axis=0, concat_axis=0, tiled=True)]
    all_to_all x1, waiting for transfers between devices: 0.01 us -> 3.85 us  [shards(): lax.all_to_all(send_resid, 'req', split_axis=0, concat_axis=0, tiled=True)]
    ppermute x2 -> x1, waiting for transfers between devices: 0.01 us -> 3 us  [grp_all_gather(): pair = lax.ppermute(jnp.stack([block, across]), 'grp', near)]
    another operation x4 -> x2, other arithmetic: 3.47 us -> 1.16 us  [grp_reduce_scatter(): jnp.stack([grp_block(partial, me ^ 1, width), grp_block(partial, me ^ 3,...]
  transfers between devices with their start and end apart: 15 -> 10, of which waited for: 9 -> 9; matrix products, arithmetic and copies ran while one was open for 24% -> 12% of each run, Pallas kernels for 12% -> 13%
where the time goes in v6:
time: 205 us; the launch traced here: 204 us
  waiting for transfers between devices  74.5 us (36%)
  local copies, waits for them, and re-layouts  29.3 us (14%)
  Pallas kernels  27.1 us (13%)
  starting transfers between devices  25.7 us (13%)
  other arithmetic  24.4 us (12%)
  matrix products  19.6 us (10%)
  between operations  3.05 us (1%)
    pallas_call x2, Pallas kernels, span_attention(): pl.pallas_call(functools.partial(span_kernel, kv_index), out_shape=jax.Sh...  27.1 us
    all_to_all x1, waiting for transfers between devices, shards(): lax.all_to_all(picked, 'req', split_axis=0, concat_axis=0, tiled=True)  24.3 us
    ppermute x2, waiting for transfers between devices, grp_reduce_scatter(): arrived = lax.ppermute(other.astype(jnp.bfloat16), 'grp', far)  20.9 us
    ppermute x1, waiting for transfers between devices, grp_all_gather(): across = lax.ppermute(block, 'grp', far)  11.6 us
    dot_general x1, matrix products, finish(): jnp.dot(inner, down_weight, preferred_element_type=jnp.float32)  10.5 us
    all_to_all x2, starting transfers between devices, shards(): lax.all_to_all(part, 'req', split_axis=0, concat_axis=0, tiled=True)  10 us
    all_to_all x1, starting transfers between devices, shards(): lax.all_to_all(send_resid, 'req', split_axis=0, concat_axis=0, tiled=True)  7.25 us
    ppermute x2, waiting for transfers between devices, grp_reduce_scatter(): incoming = lax.ppermute(outgoing, 'grp', near)  5.49 us
  transfers between devices with their start and end apart: 10, of which 9 were waited for; matrix products, arithmetic and copies ran while one was open for 12% of the time, Pallas kernels for 13%

profile of v6, /device:TPU:0, one launch (start us, length us, event | category | flops | bytes accessed | tf_op | source)
XLA Modules:
  0.0 203.7 jit_solution(3249799957502022668)
XLA Ops:
  7.4 7.3 %all-to-all-start = ((bf16[8,127,512]{2,1,0:T(8,128)(2,1)}), bf16[8,127,512]{2,1,0:T(8,128)(2,1)S(1)}, u32[]{:S(2)}, u32[]{:S(2)}) async-start(bf16[8,127,512]{2,1,0:T(8,128)(2,1)} %fusion.7), calls=%async_computation | async-start | bytes 2097152 | tf_op jit(solution)/shard_map/all_to_all | solution.py:262
  15.6 1.9 fusion.61
  20.3 13.4 %shard_map.154 = bf16[1024,256]{1,0:T(8,128)(2,1)} custom-call(s32[1]{0:T(128)S(6)} %copy.51.start_ref, bf16[1024,512]{1,0:T(8,128)(2,1)} %q_ref.2, bf16[4608,128]{1,0:T(8,128)(2,1)} %kp_ref.3, bf16[4608,128]{1,0:T(8,128)(2,1)} %vp_ref.3, bf16[1024,128]{1,0:T(8,128)(2,1)} %kf_ref.3, bf16[1024,128]{1,0:T(8,128)(2,1)} %vf_ref.3), custom_call_target="tpu_custom_call" | custom-call | flops 17179869184 | bytes 1835008 | tf_op jit(solution)/shard_map/pallas_call | solution.py:88
  36.5 3.8 %all-to-all-done = bf16[8,127,512]{2,1,0:T(8,128)(2,1)S(1)} async-done(((bf16[8,127,512]{2,1,0:T(8,128)(2,1)}), bf16[8,127,512]{2,1,0:T(8,128)(2,1)S(1)}, u32[]{:S(2)}, u32[]{:S(2)}) %all-to-all-start) | async-done | bytes 1040416 | tf_op jit(solution)/shard_map/all_to_all | solution.py:262
  40.4 4.3 %all-to-all-start.1 = ((bf16[8,127,256]{2,1,0:T(8,128)(2,1)}), bf16[8,127,256]{2,1,0:T(8,128)(2,1)}, u32[]{:S(2)}, u32[]{:S(2)}) async-start(bf16[8,127,256]{2,1,0:T(8,128)(2,1)} %fusion.29), calls=%async_computation.1 | async-start | bytes 1048576 | tf_op jit(solution)/shard_map/all_to_all | solution.py:269
  44.7 13.7 %shard_map.155 = bf16[1024,256]{1,0:T(8,128)(2,1)} custom-call(s32[1]{0:T(128)S(6)} %copy.51.start_ref, bf16[1024,512]{1,0:T(8,128)(2,1)} %q_ref.2, bf16[4608,128]{1,0:T(8,128)(2,1)} %kp_ref.3, bf16[4608,128]{1,0:T(8,128)(2,1)} %vp_ref.3, bf16[1024,128]{1,0:T(8,128)(2,1)} %kf_ref.3, bf16[1024,128]{1,0:T(8,128)(2,1)} %vf_ref.3), custom_call_target="tpu_custom_call" | custom-call | flops 17179869184 | bytes 1835008 | tf_op jit(solution)/shard_map/pallas_call | solution.py:88
  61.3 5.7 %all-to-all-start.2 = ((bf16[8,127,256]{2,1,0:T(8,128)(2,1)}), bf16[8,127,256]{2,1,0:T(8,128)(2,1)S(1)}, u32[]{:S(2)}, u32[]{:S(2)}) async-start(bf16[8,127,256]{2,1,0:T(8,128)(2,1)} %fusion.27), calls=%async_computation.2 | async-start | bytes 1048576 | tf_op jit(solution)/shard_map/all_to_all | solution.py:269
  67.1 4.4 %compare_select_fusion.6 = s32[512,1]{0,1:T(1,128)S(1)} fusion(s32[]{:T(128)} %bitcast.16, s32[]{:T(128)} %bitcast.17, s32[]{:T(128)} %bitcast.18, s32[]{:T(128)} %bitcast.19, s32[]{:T(128)} %bitcast.20, s32[]{:T(128)} %bitcast.22, s32[]{:T(128)} %bitcast.21, s32[512,1]{0,1:T(1,128)S(1)} %bitcast.101), kind=kLoop, calls=%fused_computation.115 | loop fusion | flops 7680 | bytes 4124 | tf_op jit(solution)/shard_map/gather | solution.py:277
  73.4 2.0 gather_fusion.1
  75.4 5.3 %all-to-all-done.2 = bf16[8,127,256]{2,1,0:T(8,128)(2,1)S(1)} async-done(((bf16[8,127,256]{2,1,0:T(8,128)(2,1)}), bf16[8,127,256]{2,1,0:T(8,128)(2,1)S(1)}, u32[]{:S(2)}, u32[]{:S(2)}) %all-to-all-start.2) | async-done | bytes 520224 | tf_op jit(solution)/shard_map/all_to_all | solution.py:269
  80.9 2.0 gather_fusion.2
  85.4 2.8 %collective-permute-done = bf16[2,512,512]{2,1,0:T(8,128)(2,1)} collective-permute-done((bf16[2,512,512]{2,1,0:T(8,128)(2,1)S(1)}, bf16[2,512,512]{2,1,0:T(8,128)(2,1)}, u32[]{:S(2)}, u32[]{:S(2)}) %collective-permute-start) | collective-permute-done | bytes 1048608 | tf_op jit(solution)/shard_map/ppermute | solution.py:184
  88.2 2.1 %fusion.12 = bf16[512,512]{1,0:T(8,128)(2,1)} fusion(bf16[2,512,512]{2,1,0:T(8,128)(2,1)} %collective-permute-done, bf16[512,2048]{1,0:T(8,128)(2,1)} %copy-done.2, s32[]{:T(128)S(6)} %select_n.204), kind=kLoop, calls=%fused_computation.40 | loop fusion | flops 1048576 | bytes 1572868 | tf_op jit(solution)/shard_map/convert_element_type | solution.py:189
  90.4 1.5 collective-permute-start.1
  91.9 1.5 reshape.494
  93.4 2.6 %gather_fusion = bf16[512,512]{1,0:T(8,128)(2,1)} fusion(bf16[1016,512]{1,0:T(8,128)(2,1)S(1)} %reshape.494, s32[1024]{0:T(1024)S(1)} %pad_clamp_fusion.1), kind=kCustom, calls=%fused_computation | custom fusion | bytes 1050624 | tf_op jit(solution)/shard_map/gather | solution.py:282
  96.1 8.6 %collective-permute-done.1 = bf16[512,512]{1,0:T(8,128)(2,1)} collective-permute-done((bf16[512,512]{1,0:T(8,128)(2,1)}, bf16[512,512]{1,0:T(8,128)(2,1)}, u32[]{:S(2)}, u32[]{:S(2)}) %collective-permute-start.1) | collective-permute-done | bytes 524320 | tf_op jit(solution)/shard_map/ppermute | solution.py:189
  104.6 1.8 fusion.15
  106.4 1.6 collective-permute-start.2
  108.0 11.6 %collective-permute-done.2 = bf16[512,512]{1,0:T(8,128)(2,1)S(1)} collective-permute-done((bf16[512,512]{1,0:T(8,128)(2,1)S(1)}, bf16[512,512]{1,0:T(8,128)(2,1)S(1)}, u32[]{:S(2)}, u32[]{:S(2)}) %collective-permute-start.2) | collective-permute-done | bytes 524320 | tf_op jit(solution)/shard_map/ppermute | solution.py:200
  120.7 3.0 %collective-permute-done.3 = bf16[2,512,512]{2,1,0:T(8,128)(2,1)} collective-permute-done((bf16[2,512,512]{2,1,0:T(8,128)(2,1)}, bf16[2,512,512]{2,1,0:T(8,128)(2,1)}, u32[]{:S(2)}, u32[]{:S(2)}) %collective-permute-start.3) | collective-permute-done | bytes 1048608 | tf_op jit(solution)/shard_map/ppermute | solution.py:201
  126.6 1.4 copy-done.9
  128.0 3.7 %fusion.24 = f32[512,1024]{1,0:T(8,128)} fusion(bf16[2048,1024]{1,0:T(8,128)(2,1)S(1)} %copy-done.9, f32[2048]{0:T(1024)S(1)} %copy-done.11, f32[512]{0:T(512)S(1)} %add_rsqrt_fusion, bf16[512,512]{1,0:T(8,128)(2,1)S(1)} %get-tuple-element.20, bf16[512,512]{1,0:T(8,128)(2,1)S(1)} %get-tuple-element.21, bf16[512,512]{1,0:T(8,128)(2,1)S(1)} %get-tuple-element.22, ...), kind=kOutput, calls=%fused_computation.57 | convolution fusion | flops 2159017984 | bytes 8398848 | tf_op jit(solution)/shard_map/dot_general | solution.py:216
  131.7 10.5 %convolution_convert_fusion = bf16[512,2048]{1,0:T(8,128)(2,1)} fusion(bf16[1024,2048]{1,0:T(8,128)(2,1)} %param.35, f32[512,1024]{1,0:T(8,128)} %fusion.24, bf16[2048,1024]{1,0:T(8,128)(2,1)} %param.34, f32[2048]{0:T(1024)S(1)} %copy-done.11, f32[512]{0:T(512)S(1)} %add_rsqrt_fusion, bf16[512,512]{1,0:T(8,128)(2,1)} %copy-done.3, ...), kind=kOutput, calls=%fused_computation.11 | convolution fusion | flops 4310695936 | bytes 14690304 | tf_op jit(solution)/shard_map/dot_general | solution.py:220
  144.9 2.7 %collective-permute-done.4 = bf16[2,512,512]{2,1,0:T(8,128)(2,1)} collective-permute-done((bf16[2,512,512]{2,1,0:T(8,128)(2,1)}, bf16[2,512,512]{2,1,0:T(8,128)(2,1)}, u32[]{:S(2)}, u32[]{:S(2)}) %collective-permute-start.4) | collective-permute-done | bytes 1048608 | tf_op jit(solution)/shard_map/ppermute | solution.py:184
  148.9 1.6 collective-permute-start.5
  150.6 12.3 %collective-permute-done.5 = bf16[512,512]{1,0:T(8,128)(2,1)S(1)} collective-permute-done((bf16[512,512]{1,0:T(8,128)(2,1)S(1)}, bf16[512,512]{1,0:T(8,128)(2,1)S(1)}, u32[]{:S(2)}, u32[]{:S(2)}) %collective-permute-start.5) | collective-permute-done | bytes 524320 | tf_op jit(solution)/shard_map/ppermute | solution.py:189
  162.9 1.5 fusion.11
  164.4 5.1 %gather_fusion.3 = bf16[1016,512]{1,0:T(8,128)(2,1)} fusion(bf16[512,512]{1,0:T(8,128)(2,1)S(1)} %fusion.11, s32[1024]{0:T(1024)S(1)} %pad_clamp_fusion), kind=kCustom, calls=%fused_computation.3 | custom fusion | bytes 2084832 | tf_op jit(solution)/shard_map/gather | solution.py:291
  169.5 1.5 reshape.497
  172.2 3.6 %all-to-all-start.3 = ((bf16[8,127,512]{2,1,0:T(8,128)(2,1)}), bf16[8,127,512]{2,1,0:T(8,128)(2,1)S(1)}, u32[]{:S(2)}, u32[]{:S(2)}) async-start(bf16[8,127,512]{2,1,0:T(8,128)(2,1)} %broadcast_select_fusion), calls=%async_computation.3 | async-start | bytes 2097152 | tf_op jit(solution)/shard_map/all_to_all | solution.py:293
  177.1 24.3 %all-to-all-done.3 = bf16[8,127,512]{2,1,0:T(8,128)(2,1)S(1)} async-done(((bf16[8,127,512]{2,1,0:T(8,128)(2,1)}), bf16[8,127,512]{2,1,0:T(8,128)(2,1)S(1)}, u32[]{:S(2)}, u32[]{:S(2)}) %all-to-all-start.3) | async-done | bytes 1040416 | tf_op jit(solution)/shard_map/all_to_all | solution.py:293
  (92 shorter events, 31.4 us)
Async XLA Ops:
  0.0 82.8 %copy-start = (bf16[512,2048]{1,0:T(8,128)(2,1)S(1)}, bf16[512,2048]{1,0:T(8,128)(2,1)}, u32[]{:S(2)}) copy-start(bf16[512,2048]{1,0:T(8,128)(2,1)} %param.31) | copy-start | bytes 6291460
  5.9 9.4 %slice-start = ((bf16[1024,512]{1,0:T(8,128)(2,1)}), bf16[8,512]{1,0:T(8,128)(2,1)S(1)}, s32[]{:S(2)}) async-start(bf16[1024,512]{1,0:T(8,128)(2,1)} %q_ref.2), calls=%async_computation.4 | async-start | bytes 16384 | tf_op jit(solution)/shard_map/slice | solution.py:106
  5.9 9.5 %copy-start.6 = (s32[8]{0:T(128)S(1)}, s32[8]{0:T(128)}, u32[]{:S(2)}) copy-start(s32[8]{0:T(128)} %param.26) | copy-start | bytes 100
  6.0 9.5 %copy-start.7 = (s32[8]{0:T(128)S(1)}, s32[8]{0:T(128)}, u32[]{:S(2)}) copy-start(s32[8]{0:T(128)} %param.27) | copy-start | bytes 100
  6.0 9.5 %copy-start.8 = (s32[8]{0:T(128)S(1)}, s32[8]{0:T(128)}, u32[]{:S(2)}) copy-start(s32[8]{0:T(128)} %param.28) | copy-start | bytes 100
  7.4 33.0 %all-to-all-start = ((bf16[8,127,512]{2,1,0:T(8,128)(2,1)}), bf16[8,127,512]{2,1,0:T(8,128)(2,1)S(1)}, u32[]{:S(2)}, u32[]{:S(2)}) async-start(bf16[8,127,512]{2,1,0:T(8,128)(2,1)} %fusion.7), calls=%async_computation | async-start | bytes 2097152 | tf_op jit(solution)/shard_map/all_to_all | solution.py:262
  15.4 3.5 %copy-start.10 = (bf16[4608,128]{1,0:T(8,128)(2,1)S(1)}, bf16[4608,128]{1,0:T(8,128)(2,1)}, u32[]{:S(2)}) copy-start(bf16[4608,128]{1,0:T(8,128)(2,1)} %vp_ref.3) | copy-start | bytes 3538948
  40.4 18.1 %copy-start.1 = (bf16[8,127,512]{2,1,0:T(8,128)(2,1)}, bf16[8,127,512]{2,1,0:T(8,128)(2,1)S(1)}, u32[]{:S(2)}) copy-start(bf16[8,127,512]{2,1,0:T(8,128)(2,1)S(1)} %all-to-all-done) | copy-start | bytes 3121156
  40.4 20.9 %all-to-all-start.1 = ((bf16[8,127,256]{2,1,0:T(8,128)(2,1)}), bf16[8,127,256]{2,1,0:T(8,128)(2,1)}, u32[]{:S(2)}, u32[]{:S(2)}) async-start(bf16[8,127,256]{2,1,0:T(8,128)(2,1)} %fusion.29), calls=%async_computation.1 | async-start | bytes 1048576 | tf_op jit(solution)/shard_map/all_to_all | solution.py:269
  61.3 19.4 %all-to-all-start.2 = ((bf16[8,127,256]{2,1,0:T(8,128)(2,1)}), bf16[8,127,256]{2,1,0:T(8,128)(2,1)S(1)}, u32[]{:S(2)}, u32[]{:S(2)}) async-start(bf16[8,127,256]{2,1,0:T(8,128)(2,1)} %fusion.27), calls=%async_computation.2 | async-start | bytes 1048576 | tf_op jit(solution)/shard_map/all_to_all | solution.py:269
  84.1 1.3 copy-start.2
  85.4 2.8 %collective-permute-start = (bf16[2,512,512]{2,1,0:T(8,128)(2,1)S(1)}, bf16[2,512,512]{2,1,0:T(8,128)(2,1)}, u32[]{:S(2)}, u32[]{:S(2)}) collective-permute-start(bf16[2,512,512]{2,1,0:T(8,128)(2,1)S(1)} %pad_maximum_fusion.2), channel_id=1, source_target_pairs={{0,1},{1,0},{2,3},{3,2},{4,5},{5,4},{6,7},{7,6},{8,9},{9,8},{10,11... | collective-permute-start | bytes 3145736 | tf_op jit(solution)/shard_map/ppermute | solution.py:184
  90.4 14.3 %collective-permute-start.1 = (bf16[512,512]{1,0:T(8,128)(2,1)}, bf16[512,512]{1,0:T(8,128)(2,1)}, u32[]{:S(2)}, u32[]{:S(2)}) collective-permute-start(bf16[512,512]{1,0:T(8,128)(2,1)} %fusion.12), channel_id=1, source_target_pairs={{0,2},{1,3},{2,0},{3,1},{4,6},{5,7},{6,4},{7,5},{8,10},{9,11},{10,... | collective-permute-start | bytes 1572872 | tf_op jit(solution)/shard_map/ppermute | solution.py:189
  106.4 13.2 %collective-permute-start.2 = (bf16[512,512]{1,0:T(8,128)(2,1)S(1)}, bf16[512,512]{1,0:T(8,128)(2,1)S(1)}, u32[]{:S(2)}, u32[]{:S(2)}) collective-permute-start(bf16[512,512]{1,0:T(8,128)(2,1)S(1)} %fusion.15), channel_id=1, source_target_pairs={{0,2},{1,3},{2,0},{3,1},{4,6},{5,7},{6,4},{7,5},{8,10},{9,11},{10,... | collective-permute-start | bytes 1572872 | tf_op jit(solution)/shard_map/ppermute | solution.py:200
  120.7 3.0 %collective-permute-start.3 = (bf16[2,512,512]{2,1,0:T(8,128)(2,1)}, bf16[2,512,512]{2,1,0:T(8,128)(2,1)}, u32[]{:S(2)}, u32[]{:S(2)}) collective-permute-start(bf16[2,512,512]{2,1,0:T(8,128)(2,1)} %pad_maximum_fusion.3), channel_id=1, source_target_pairs={{0,1},{1,0},{2,3},{3,2},{4,5},{5,4},{6,7},{7,6},{8,9},{9,8},{10,11... | collective-permute-start | bytes 3145736 | tf_op jit(solution)/shard_map/ppermute | solution.py:201
  125.2 2.8 %copy-start.9 = (bf16[2048,1024]{1,0:T(8,128)(2,1)S(1)}, bf16[2048,1024]{1,0:T(8,128)(2,1)}, u32[]{:S(2)}) copy-start(bf16[2048,1024]{1,0:T(8,128)(2,1)} %param.33) | copy-start | bytes 12582916
  125.4 0.8 copy-start.3
  125.4 1.0 copy-start.4
  125.4 1.1 copy-start.5
  125.4 2.6 %copy-start.11 = (f32[2048]{0:T(1024)S(1)}, f32[2048]{0:T(1024)}, u32[]{:S(2)}) copy-start(f32[2048]{0:T(1024)} %param.32) | copy-start | bytes 24580
  144.6 3.0 %collective-permute-start.4 = (bf16[2,512,512]{2,1,0:T(8,128)(2,1)}, bf16[2,512,512]{2,1,0:T(8,128)(2,1)}, u32[]{:S(2)}, u32[]{:S(2)}) collective-permute-start(bf16[2,512,512]{2,1,0:T(8,128)(2,1)} %pad_maximum_fusion.4), channel_id=1, source_target_pairs={{0,1},{1,0},{2,3},{3,2},{4,5},{5,4},{6,7},{7,6},{8,9},{9,8},{10,11... | collective-permute-start | bytes 3145736 | tf_op jit(solution)/shard_map/ppermute | solution.py:184
  148.9 14.0 %collective-permute-start.5 = (bf16[512,512]{1,0:T(8,128)(2,1)S(1)}, bf16[512,512]{1,0:T(8,128)(2,1)S(1)}, u32[]{:S(2)}, u32[]{:S(2)}) collective-permute-start(bf16[512,512]{1,0:T(8,128)(2,1)S(1)} %fusion.8), channel_id=1, source_target_pairs={{0,2},{1,3},{2,0},{3,1},{4,6},{5,7},{6,4},{7,5},{8,10},{9,11},{10,... | collective-permute-start | bytes 1572872 | tf_op jit(solution)/shard_map/ppermute | solution.py:189
  172.2 29.2 %all-to-all-start.3 = ((bf16[8,127,512]{2,1,0:T(8,128)(2,1)}), bf16[8,127,512]{2,1,0:T(8,128)(2,1)S(1)}, u32[]{:S(2)}, u32[]{:S(2)}) async-start(bf16[8,127,512]{2,1,0:T(8,128)(2,1)} %broadcast_select_fusion), calls=%async_computation.3 | async-start | bytes 2097152 | tf_op jit(solution)/shard_map/all_to_all | solution.py:293

commit v7 on v6

--- a/solution.py
+++ b/solution.py
@@ -170,13 +170,12 @@
     return lax.dynamic_slice_in_dim(x, index * width, width, 1)
 
 
-def grp_reduce_scatter(partial):
+def grp_reduce_scatter(partial, tie=None):
     parts = lax.axis_size("grp")
     width = partial.shape[1] // parts
     if parts != 4:
-        return lax.psum_scatter(partial, "grp", scatter_dimension=1, tiled=True).astype(
-            jnp.float32
-        )
+        summed = lax.psum_scatter(partial, "grp", scatter_dimension=1, tiled=True)
+        return summed.astype(jnp.float32) if tie is None else (summed.astype(jnp.float32), tie)
     me = lax.axis_index("grp")
     near = [(i, i ^ 1) for i in range(parts)]
     far = [(i, i ^ 2) for i in range(parts)]
@@ -186,8 +185,13 @@
     other = grp_block(partial, me ^ 2, width).astype(jnp.float32) + incoming[1].astype(
         jnp.float32
     )
-    arrived = lax.ppermute(other.astype(jnp.bfloat16), "grp", far)
-    return own + arrived.astype(jnp.float32)
+    leaving = other.astype(jnp.bfloat16)
+    if tie is not None:
+        leaving, tie = lax.optimization_barrier((leaving, tie))
+    arrived = lax.ppermute(leaving, "grp", far)
+    if tie is None:
+        return own + arrived.astype(jnp.float32)
+    return own + arrived.astype(jnp.float32), tie
 
 
 def grp_all_gather(block):
@@ -216,10 +220,10 @@
     gate = jnp.dot(normed, gate_weight, preferred_element_type=jnp.float32)
     upval = jnp.dot(normed, up_weight, preferred_element_type=jnp.float32)
     inner = (jax.nn.silu(gate) * upval).astype(jnp.bfloat16)
-    down_cols = grp_reduce_scatter(
-        jnp.dot(inner, down_weight, preferred_element_type=jnp.float32).astype(jnp.bfloat16)
-    )
-    return (state_cols.astype(jnp.float32) + down_cols).astype(jnp.bfloat16)
+    down_partial = jnp.dot(inner, down_weight, preferred_element_type=jnp.float32).astype(
+        jnp.bfloat16
+    )
+    return state_cols, down_partial
 
 
 def shards(
@@ -287,11 +291,33 @@
     row_of = jnp.arange(bucket, dtype=jnp.int32)[None, :] * devices + lane[:, None]
     back_valid = row_of < counts[:, None]
     back_slot = jnp.clip((firsts[:, None] + row_of) // devices, 0, bal - 1)
-    picked = jnp.where(
-        back_valid[:, :, None], mixed[back_slot.reshape(-1)].reshape(devices, bucket, width), 0
-    ).astype(jnp.bfloat16)
-    returned = lax.all_to_all(picked, "req", split_axis=0, concat_axis=0, tiled=True)
-    restored = jnp.roll(jnp.transpose(returned, (1, 0, 2)), -shift, axis=1).reshape(spread, width)
+    state_cols, down_partial = mixed
+    rows = down_partial.shape[0]
+    parts = lax.axis_size("grp")
+    piece = down_partial.shape[1] // parts // 2
+    quads = down_partial.reshape(rows, parts, 2, piece)
+
+    def pick_back(k, down_cols):
+        own = state_cols[:, k * piece : (k + 1) * piece].astype(jnp.float32)
+        half_rows = (own + down_cols).astype(jnp.bfloat16)
+        return jnp.where(
+            back_valid[:, :, None],
+            half_rows[back_slot.reshape(-1)].reshape(devices, bucket, piece),
+            0,
+        ).astype(jnp.bfloat16)
+
+    picked_a = pick_back(0, grp_reduce_scatter(quads[:, :, 0, :].reshape(rows, parts * piece)))
+    down_b, picked_a = grp_reduce_scatter(
+        quads[:, :, 1, :].reshape(rows, parts * piece), tie=picked_a
+    )
+    picked_b = pick_back(1, down_b)
+    restored_halves = []
+    for picked in (picked_a, picked_b):
+        returned = lax.all_to_all(picked, "req", split_axis=0, concat_axis=0, tiled=True)
+        restored_halves.append(
+            jnp.roll(jnp.transpose(returned, (1, 0, 2)), -shift, axis=1).reshape(spread, piece)
+        )
+    restored = jnp.concatenate(restored_halves, axis=1)
     if spread < total_rows:
         restored = jnp.concatenate(
             [restored, jnp.zeros((total_rows - spread, width), restored.dtype)], axis=0

time: 205 us -> 211 us (1.029)
  local copies, waits for them, and re-layouts: 29.3 us -> 45.3 us
  waiting for transfers between devices: 74.5 us -> 59.1 us
  starting transfers between devices: 25.7 us -> 33.1 us
    all_to_all x1 -> x2, waiting for transfers between devices: 24.3 us -> 11.1 us  [shards(): lax.all_to_all(picked, 'req', split_axis=0, concat_axis=0, tiled=True)]
    slice x0 -> x1, local copies, waits for them, and re-layouts: none -> 10.4 us  [shards(): quads[:, :, 0, :].reshape(rows, parts * piece)]
    all_to_all x1 -> x2, starting transfers between devices: 3.64 us -> 8.95 us  [shards(): lax.all_to_all(picked, 'req', split_axis=0, concat_axis=0, tiled=True)]
    gather x1 -> x2, local copies, waits for them, and re-layouts: 5.08 us -> 8.18 us  [pick_back(): half_rows[back_slot.reshape(-1)].reshape(devices, bucket, piece)]
    ppermute x2 -> x3, waiting for transfers between devices: 5.49 us -> 2.8 us  [grp_reduce_scatter(): incoming = lax.ppermute(outgoing, 'grp', near)]
    reshape x1 -> x3, local copies, waits for them, and re-layouts: 1.53 us -> 3.87 us  [the longest x1 3.55 us: shards(): quads = down_partial.reshape(rows, parts, 2, piece)]
    ppermute x2 -> x3, starting transfers between devices: 3.1 us -> 4.7 us  [grp_reduce_scatter(): arrived = lax.ppermute(leaving, 'grp', far)]
    convert_element_type x3 -> x5, other arithmetic: 4.95 us -> 3.66 us  [the longest x3 2.44 us: grp_reduce_scatter(): leaving = other.astype(jnp.bfloat16)]
  transfers between devices with their start and end apart: 10 -> 13, of which waited for: 9 -> 10; matrix products, arithmetic and copies ran while one was open for 12% -> 17% of each run, Pallas kernels for 13% -> 13%
where the time goes in v7:
time: 211 us; the launch traced here: 210 us
  waiting for transfers between devices  59.1 us (28%)
  local copies, waits for them, and re-layouts  45.3 us (21%)
  starting transfers between devices  33.1 us (16%)
  Pallas kernels  27.1 us (13%)
  other arithmetic  23.3 us (11%)
  matrix products  19.1 us (9%)
  between operations  3.2 us (2%)
    pallas_call x2, Pallas kernels, span_attention(): pl.pallas_call(functools.partial(span_kernel, kv_index), out_shape=jax.Sh...  27.1 us
    ppermute x3, waiting for transfers between devices, grp_reduce_scatter(): arrived = lax.ppermute(leaving, 'grp', far)  21.9 us
    ppermute x1, waiting for transfers between devices, grp_all_gather(): across = lax.ppermute(block, 'grp', far)  11.6 us
    all_to_all x2, waiting for transfers between devices, shards(): lax.all_to_all(picked, 'req', split_axis=0, concat_axis=0, tiled=True)  11.1 us
    slice x1, local copies, waits for them, and re-layouts, shards(): quads[:, :, 0, :].reshape(rows, parts * piece)  10.4 us
    all_to_all x2, starting transfers between devices, shards(): lax.all_to_all(part, 'req', split_axis=0, concat_axis=0, tiled=True)  10 us
    dot_general x1, matrix products, finish(): jnp.dot(inner, down_weight, preferred_element_type=jnp.float32)  9.95 us
    all_to_all x2, starting transfers between devices, shards(): lax.all_to_all(picked, 'req', split_axis=0, concat_axis=0, tiled=True)  8.95 us
  transfers between devices with their start and end apart: 13, of which 10 were waited for; matrix products, arithmetic and copies ran while one was open for 17% of the time, Pallas kernels for 13%

profile of v7, /device:TPU:0, one launch (start us, length us, event | category | flops | bytes accessed | tf_op | source)
XLA Modules:
  0.0 210.2 jit_solution(12316362302248396123)
XLA Ops:
  7.4 7.3 %all-to-all-start = ((bf16[8,127,512]{2,1,0:T(8,128)(2,1)}), bf16[8,127,512]{2,1,0:T(8,128)(2,1)S(1)}, u32[]{:S(2)}, u32[]{:S(2)}) async-start(bf16[8,127,512]{2,1,0:T(8,128)(2,1)} %fusion.8), calls=%async_computation | async-start | bytes 2097152 | tf_op jit(solution)/shard_map/all_to_all | solution.py:266
  15.6 1.9 fusion.70
  20.3 13.4 %shard_map.154 = bf16[1024,256]{1,0:T(8,128)(2,1)} custom-call(s32[1]{0:T(128)S(6)} %copy.68.start_ref, bf16[1024,512]{1,0:T(8,128)(2,1)} %q_ref.2, bf16[4608,128]{1,0:T(8,128)(2,1)} %kp_ref.3, bf16[4608,128]{1,0:T(8,128)(2,1)} %vp_ref.3, bf16[1024,128]{1,0:T(8,128)(2,1)} %kf_ref.3, bf16[1024,128]{1,0:T(8,128)(2,1)} %vf_ref.3), custom_call_target="tpu_custom_call" | custom-call | flops 17179869184 | bytes 1835008 | tf_op jit(solution)/shard_map/pallas_call | solution.py:88
  36.5 3.8 %all-to-all-done = bf16[8,127,512]{2,1,0:T(8,128)(2,1)S(1)} async-done(((bf16[8,127,512]{2,1,0:T(8,128)(2,1)}), bf16[8,127,512]{2,1,0:T(8,128)(2,1)S(1)}, u32[]{:S(2)}, u32[]{:S(2)}) %all-to-all-start) | async-done | bytes 1040416 | tf_op jit(solution)/shard_map/all_to_all | solution.py:266
  40.4 4.3 %all-to-all-start.1 = ((bf16[8,127,256]{2,1,0:T(8,128)(2,1)}), bf16[8,127,256]{2,1,0:T(8,128)(2,1)}, u32[]{:S(2)}, u32[]{:S(2)}) async-start(bf16[8,127,256]{2,1,0:T(8,128)(2,1)} %fusion.30), calls=%async_computation.1 | async-start | bytes 1048576 | tf_op jit(solution)/shard_map/all_to_all | solution.py:273
  44.7 13.7 %shard_map.155 = bf16[1024,256]{1,0:T(8,128)(2,1)} custom-call(s32[1]{0:T(128)S(6)} %copy.68.start_ref, bf16[1024,512]{1,0:T(8,128)(2,1)} %q_ref.2, bf16[4608,128]{1,0:T(8,128)(2,1)} %kp_ref.3, bf16[4608,128]{1,0:T(8,128)(2,1)} %vp_ref.3, bf16[1024,128]{1,0:T(8,128)(2,1)} %kf_ref.3, bf16[1024,128]{1,0:T(8,128)(2,1)} %vf_ref.3), custom_call_target="tpu_custom_call" | custom-call | flops 17179869184 | bytes 1835008 | tf_op jit(solution)/shard_map/pallas_call | solution.py:88
  61.3 5.7 %all-to-all-start.2 = ((bf16[8,127,256]{2,1,0:T(8,128)(2,1)}), bf16[8,127,256]{2,1,0:T(8,128)(2,1)S(1)}, u32[]{:S(2)}, u32[]{:S(2)}) async-start(bf16[8,127,256]{2,1,0:T(8,128)(2,1)} %fusion.28), calls=%async_computation.2 | async-start | bytes 1048576 | tf_op jit(solution)/shard_map/all_to_all | solution.py:273
  67.1 4.5 %compare_select_fusion.6 = s32[512,1]{0,1:T(1,128)S(1)} fusion(s32[]{:T(128)} %bitcast.16, s32[]{:T(128)} %bitcast.17, s32[]{:T(128)} %bitcast.18, s32[]{:T(128)} %bitcast.19, s32[]{:T(128)} %bitcast.20, s32[]{:T(128)} %bitcast.22, s32[]{:T(128)} %bitcast.21, s32[512,1]{0,1:T(1,128)S(1)} %bitcast.130), kind=kLoop, calls=%fused_computation.138 | loop fusion | flops 7680 | bytes 4124 | tf_op jit(solution)/shard_map/gather | solution.py:281
  73.4 2.0 gather_fusion.1
  75.3 5.4 %all-to-all-done.2 = bf16[8,127,256]{2,1,0:T(8,128)(2,1)S(1)} async-done(((bf16[8,127,256]{2,1,0:T(8,128)(2,1)}), bf16[8,127,256]{2,1,0:T(8,128)(2,1)S(1)}, u32[]{:S(2)}, u32[]{:S(2)}) %all-to-all-start.2) | async-done | bytes 520224 | tf_op jit(solution)/shard_map/all_to_all | solution.py:273
  80.9 2.0 gather_fusion.2
  85.4 2.8 %collective-permute-done = bf16[2,512,512]{2,1,0:T(8,128)(2,1)} collective-permute-done((bf16[2,512,512]{2,1,0:T(8,128)(2,1)S(1)}, bf16[2,512,512]{2,1,0:T(8,128)(2,1)}, u32[]{:S(2)}, u32[]{:S(2)}) %collective-permute-start) | collective-permute-done | bytes 1048608 | tf_op jit(solution)/shard_map/ppermute | solution.py:183
  89.6 1.6 collective-permute-start.1
  91.5 2.0 gather_fusion
  93.5 10.1 %collective-permute-done.1 = bf16[512,512]{1,0:T(8,128)(2,1)S(1)} collective-permute-done((bf16[512,512]{1,0:T(8,128)(2,1)S(1)}, bf16[512,512]{1,0:T(8,128)(2,1)S(1)}, u32[]{:S(2)}, u32[]{:S(2)}) %collective-permute-start.1) | collective-permute-done | bytes 524320 | tf_op jit(solution)/shard_map/ppermute | solution.py:191
  105.1 1.6 collective-permute-start.2
  106.7 11.6 %collective-permute-done.2 = bf16[512,512]{1,0:T(8,128)(2,1)S(1)} collective-permute-done((bf16[512,512]{1,0:T(8,128)(2,1)S(1)}, bf16[512,512]{1,0:T(8,128)(2,1)S(1)}, u32[]{:S(2)}, u32[]{:S(2)}) %collective-permute-start.2) | collective-permute-done | bytes 524320 | tf_op jit(solution)/shard_map/ppermute | solution.py:204
  118.7 2.6 %collective-permute-done.3 = bf16[2,512,512]{2,1,0:T(8,128)(2,1)} collective-permute-done((bf16[2,512,512]{2,1,0:T(8,128)(2,1)S(1)}, bf16[2,512,512]{2,1,0:T(8,128)(2,1)}, u32[]{:S(2)}, u32[]{:S(2)}) %collective-permute-start.3) | collective-permute-done | bytes 1048608 | tf_op jit(solution)/shard_map/ppermute | solution.py:205
  125.0 3.8 %fusion.23 = f32[512,1024]{1,0:T(8,128)} fusion(bf16[2048,1024]{1,0:T(8,128)(2,1)S(1)} %copy-done.8, f32[2048]{0:T(1024)S(1)} %copy-done.10, f32[512]{0:T(512)S(1)} %add_rsqrt_fusion, bf16[512,512]{1,0:T(8,128)(2,1)S(1)} %get-tuple-element.23, bf16[512,512]{1,0:T(8,128)(2,1)S(1)} %get-tuple-element.24, bf16[512,512]{1,0:T(8,128)(2,1)S(1)} %get-tuple-element.25, ...), kind=kOutput, calls=%fused_computation.56 | convolution fusion | flops 2159017984 | bytes 8398848 | tf_op jit(solution)/shard_map/dot_general | solution.py:220
  128.7 9.9 %convolution_convert_fusion = bf16[512,2048]{1,0:T(8,128)(2,1)} fusion(bf16[1024,2048]{1,0:T(8,128)(2,1)} %param.33, f32[512,1024]{1,0:T(8,128)} %fusion.23, bf16[2048,1024]{1,0:T(8,128)(2,1)} %param.32, f32[2048]{0:T(1024)S(1)} %copy-done.10, f32[512]{0:T(512)S(1)} %add_rsqrt_fusion, bf16[512,512]{1,0:T(8,128)(2,1)S(1)} %get-tuple-element.23, ...), kind=kOutput, calls=%fused_computation.12 | convolution fusion | flops 4310695936 | bytes 14690304 | tf_op jit(solution)/shard_map/dot_general | solution.py:223
  138.7 3.5 %reshape.511 = bf16[512,4,2,256]{3,2,1,0:T(2,128)(2,1)S(1)} reshape(bf16[512,2048]{1,0:T(8,128)(2,1)} %convolution_convert_fusion) | data formatting | bytes 4194304 | tf_op jit(solution)/shard_map/reshape | solution.py:298
  142.2 10.4 %slice_reduce_fusion = (bf16[512,4,256]{2,1,0:T(4,128)(2,1)S(1)}, bf16[512,4,256]{2,1,0:T(4,128)(2,1)}) fusion(bf16[512,4,2,256]{3,2,1,0:T(2,128)(2,1)S(1)} %reshape.511), kind=kLoop, calls=%fused_computation.17 | loop fusion | bytes 4194304 | tf_op jit(solution)/shard_map/slice | solution.py:309
  154.0 2.4 %copy.60 = bf16[64,8,4,256]{3,1,2,0:T(8,128)(2,1)} copy(bf16[64,8,4,256]{3,2,1,0:T(4,128)(2,1)} %bitcast.121) | data formatting | bytes 2097152
  158.9 1.6 collective-permute-start.6
  161.5 5.8 %collective-permute-done.6 = bf16[512,256]{1,0:T(8,128)(2,1)S(1)} collective-permute-done((bf16[512,256]{1,0:T(8,128)(2,1)S(1)}, bf16[512,256]{1,0:T(8,128)(2,1)S(1)}, u32[]{:S(2)}, u32[]{:S(2)}) %collective-permute-start.6) | collective-permute-done | bytes 262176 | tf_op jit(solution)/shard_map/ppermute | solution.py:191
  167.4 4.1 %gather_fusion.3 = bf16[1016,256]{1,0:T(8,128)(2,1)S(1)} fusion(bf16[512,256]{1,0:T(8,128)(2,1)S(1)} %fusion.40, s32[1024]{0:T(1024)S(1)} %pad_clamp_fusion), kind=kCustom, calls=%fused_computation.3 | custom fusion | bytes 1044448 | tf_op jit(solution)/shard_map/gather | solution.py:305
  172.8 3.6 %all-to-all-start.3 = ((bf16[8,127,256]{2,1,0:T(8,128)(2,1)}), bf16[8,127,256]{2,1,0:T(8,128)(2,1)S(1)}, u32[]{:S(2)}, u32[]{:S(2)}) async-start(bf16[8,127,256]{2,1,0:T(8,128)(2,1)} %broadcast_select_fusion.1), calls=%async_computation.3 | async-start | bytes 1048576 | tf_op jit(solution)/shard_map/all_to_all | solution.py:316
  176.4 1.5 collective-permute-start.7
  177.9 5.9 %collective-permute-done.7 = bf16[512,256]{1,0:T(8,128)(2,1)S(1)} collective-permute-done((bf16[512,256]{1,0:T(8,128)(2,1)S(1)}, bf16[512,256]{1,0:T(8,128)(2,1)S(1)}, u32[]{:S(2)}, u32[]{:S(2)}) %collective-permute-start.7) | collective-permute-done | bytes 262176 | tf_op jit(solution)/shard_map/ppermute | solution.py:191
  184.9 4.1 %gather_fusion.4 = bf16[1016,256]{1,0:T(8,128)(2,1)S(1)} fusion(bf16[512,256]{1,0:T(8,128)(2,1)S(1)} %fusion.36, s32[1024]{0:T(1024)S(1)} %pad_clamp_fusion), kind=kCustom, calls=%fused_computation.4 | custom fusion | bytes 1044448 | tf_op jit(solution)/shard_map/gather | solution.py:305
  190.5 5.3 %all-to-all-start.4 = ((bf16[8,127,256]{2,1,0:T(8,128)(2,1)}), bf16[8,127,256]{2,1,0:T(8,128)(2,1)S(1)}, u32[]{:S(2)}, u32[]{:S(2)}) async-start(bf16[8,127,256]{2,1,0:T(8,128)(2,1)} %broadcast_select_fusion), calls=%async_computation.4 | async-start | bytes 1048576 | tf_op jit(solution)/shard_map/all_to_all | solution.py:316
  197.6 10.8 %all-to-all-done.4 = bf16[8,127,256]{2,1,0:T(8,128)(2,1)S(1)} async-done(((bf16[8,127,256]{2,1,0:T(8,128)(2,1)}), bf16[8,127,256]{2,1,0:T(8,128)(2,1)S(1)}, u32[]{:S(2)}, u32[]{:S(2)}) %all-to-all-start.4) | async-done | bytes 520224 | tf_op jit(solution)/shard_map/all_to_all | solution.py:316
  (109 shorter events, 38.0 us)
Async XLA Ops:
  0.0 82.8 %copy-start = (bf16[512,2048]{1,0:T(8,128)(2,1)S(1)}, bf16[512,2048]{1,0:T(8,128)(2,1)}, u32[]{:S(2)}) copy-start(bf16[512,2048]{1,0:T(8,128)(2,1)} %param.29) | copy-start | bytes 6291460
  5.9 9.4 %slice-start = ((bf16[1024,512]{1,0:T(8,128)(2,1)}), bf16[8,512]{1,0:T(8,128)(2,1)S(1)}, s32[]{:S(2)}) async-start(bf16[1024,512]{1,0:T(8,128)(2,1)} %q_ref.2), calls=%async_computation.5 | async-start | bytes 16384 | tf_op jit(solution)/shard_map/slice | solution.py:106
  6.0 9.5 %copy-start.5 = (s32[8]{0:T(128)S(1)}, s32[8]{0:T(128)}, u32[]{:S(2)}) copy-start(s32[8]{0:T(128)} %param.24) | copy-start | bytes 100
  6.0 9.5 %copy-start.6 = (s32[8]{0:T(128)S(1)}, s32[8]{0:T(128)}, u32[]{:S(2)}) copy-start(s32[8]{0:T(128)} %param.25) | copy-start | bytes 100
  6.0 9.5 %copy-start.7 = (s32[8]{0:T(128)S(1)}, s32[8]{0:T(128)}, u32[]{:S(2)}) copy-start(s32[8]{0:T(128)} %param.26) | copy-start | bytes 100
  7.4 33.0 %all-to-all-start = ((bf16[8,127,512]{2,1,0:T(8,128)(2,1)}), bf16[8,127,512]{2,1,0:T(8,128)(2,1)S(1)}, u32[]{:S(2)}, u32[]{:S(2)}) async-start(bf16[8,127,512]{2,1,0:T(8,128)(2,1)} %fusion.8), calls=%async_computation | async-start | bytes 2097152 | tf_op jit(solution)/shard_map/all_to_all | solution.py:266
  15.4 3.5 %copy-start.9 = (bf16[4608,128]{1,0:T(8,128)(2,1)S(1)}, bf16[4608,128]{1,0:T(8,128)(2,1)}, u32[]{:S(2)}) copy-start(bf16[4608,128]{1,0:T(8,128)(2,1)} %vp_ref.3) | copy-start | bytes 3538948
  40.4 18.0 %copy-start.2 = (bf16[8,127,512]{2,1,0:T(8,128)(2,1)}, bf16[8,127,512]{2,1,0:T(8,128)(2,1)S(1)}, u32[]{:S(2)}) copy-start(bf16[8,127,512]{2,1,0:T(8,128)(2,1)S(1)} %all-to-all-done) | copy-start | bytes 3121156
  40.4 20.9 %all-to-all-start.1 = ((bf16[8,127,256]{2,1,0:T(8,128)(2,1)}), bf16[8,127,256]{2,1,0:T(8,128)(2,1)}, u32[]{:S(2)}, u32[]{:S(2)}) async-start(bf16[8,127,256]{2,1,0:T(8,128)(2,1)} %fusion.30), calls=%async_computation.1 | async-start | bytes 1048576 | tf_op jit(solution)/shard_map/all_to_all | solution.py:273
  61.3 19.4 %all-to-all-start.2 = ((bf16[8,127,256]{2,1,0:T(8,128)(2,1)}), bf16[8,127,256]{2,1,0:T(8,128)(2,1)S(1)}, u32[]{:S(2)}, u32[]{:S(2)}) async-start(bf16[8,127,256]{2,1,0:T(8,128)(2,1)} %fusion.28), calls=%async_computation.2 | async-start | bytes 1048576 | tf_op jit(solution)/shard_map/all_to_all | solution.py:273
  84.1 1.3 copy-start.4
  84.2 6.9 %copy-start.3 = (bf16[8,127,512]{2,1,0:T(8,128)(2,1)S(1)}, bf16[8,127,512]{2,1,0:T(8,128)(2,1)}, u32[]{:S(2)}) copy-start(bf16[8,127,512]{2,1,0:T(8,128)(2,1)} %copy-done.2) | copy-start | bytes 3121156
  85.4 2.8 %collective-permute-start = (bf16[2,512,512]{2,1,0:T(8,128)(2,1)S(1)}, bf16[2,512,512]{2,1,0:T(8,128)(2,1)}, u32[]{:S(2)}, u32[]{:S(2)}) collective-permute-start(bf16[2,512,512]{2,1,0:T(8,128)(2,1)S(1)} %pad_maximum_fusion.2), channel_id=1, source_target_pairs={{0,1},{1,0},{2,3},{3,2},{4,5},{5,4},{6,7},{7,6},{8,9},{9,8},{10,11... | collective-permute-start | bytes 3145736 | tf_op jit(solution)/shard_map/ppermute | solution.py:183
  89.6 14.0 %collective-permute-start.1 = (bf16[512,512]{1,0:T(8,128)(2,1)S(1)}, bf16[512,512]{1,0:T(8,128)(2,1)S(1)}, u32[]{:S(2)}, u32[]{:S(2)}) collective-permute-start(bf16[512,512]{1,0:T(8,128)(2,1)S(1)} %fusion.11), channel_id=1, source_target_pairs={{0,2},{1,3},{2,0},{3,1},{4,6},{5,7},{6,4},{7,5},{8,10},{9,11},{10,... | collective-permute-start | bytes 1572872 | tf_op jit(solution)/shard_map/ppermute | solution.py:191
  105.1 13.2 %collective-permute-start.2 = (bf16[512,512]{1,0:T(8,128)(2,1)S(1)}, bf16[512,512]{1,0:T(8,128)(2,1)S(1)}, u32[]{:S(2)}, u32[]{:S(2)}) collective-permute-start(bf16[512,512]{1,0:T(8,128)(2,1)S(1)} %fusion.14), channel_id=1, source_target_pairs={{0,2},{1,3},{2,0},{3,1},{4,6},{5,7},{6,4},{7,5},{8,10},{9,11},{10,... | collective-permute-start | bytes 1572872 | tf_op jit(solution)/shard_map/ppermute | solution.py:204
  118.4 2.9 %collective-permute-start.3 = (bf16[2,512,512]{2,1,0:T(8,128)(2,1)S(1)}, bf16[2,512,512]{2,1,0:T(8,128)(2,1)}, u32[]{:S(2)}, u32[]{:S(2)}) collective-permute-start(bf16[2,512,512]{2,1,0:T(8,128)(2,1)S(1)} %pad_maximum_fusion.3), channel_id=1, source_target_pairs={{0,1},{1,0},{2,3},{3,2},{4,5},{5,4},{6,7},{7,6},{8,9},{9,8},{10,11... | collective-permute-start | bytes 3145736 | tf_op jit(solution)/shard_map/ppermute | solution.py:205
  122.8 2.2 %copy-start.8 = (bf16[2048,1024]{1,0:T(8,128)(2,1)S(1)}, bf16[2048,1024]{1,0:T(8,128)(2,1)}, u32[]{:S(2)}) copy-start(bf16[2048,1024]{1,0:T(8,128)(2,1)} %param.31) | copy-start | bytes 12582916
  123.0 2.0 copy-start.10
  153.8 5.0 %collective-permute-start.5 = (bf16[2,512,256]{2,1,0:T(8,128)(2,1)}, bf16[2,512,256]{2,1,0:T(8,128)(2,1)S(1)}, u32[]{:S(2)}, u32[]{:S(2)}) collective-permute-start(bf16[2,512,256]{2,1,0:T(8,128)(2,1)} %pad_maximum_fusion.5), channel_id=1, source_target_pairs={{0,1},{1,0},{2,3},{3,2},{4,5},{5,4},{6,7},{7,6},{8,9},{9,8},{10,11... | collective-permute-start | bytes 1572872 | tf_op jit(solution)/shard_map/ppermute | solution.py:183
  158.3 2.1 %collective-permute-start.4 = (bf16[2,512,256]{2,1,0:T(8,128)(2,1)}, bf16[2,512,256]{2,1,0:T(8,128)(2,1)S(1)}, u32[]{:S(2)}, u32[]{:S(2)}) collective-permute-start(bf16[2,512,256]{2,1,0:T(8,128)(2,1)} %pad_maximum_fusion.4), channel_id=1, source_target_pairs={{0,1},{1,0},{2,3},{3,2},{4,5},{5,4},{6,7},{7,6},{8,9},{9,8},{10,11... | collective-permute-start | bytes 1572872 | tf_op jit(solution)/shard_map/ppermute | solution.py:183
  158.9 8.4 %collective-permute-start.6 = (bf16[512,256]{1,0:T(8,128)(2,1)S(1)}, bf16[512,256]{1,0:T(8,128)(2,1)S(1)}, u32[]{:S(2)}, u32[]{:S(2)}) collective-permute-start(bf16[512,256]{1,0:T(8,128)(2,1)S(1)} %fusion.37), channel_id=1, source_target_pairs={{0,2},{1,3},{2,0},{3,1},{4,6},{5,7},{6,4},{7,5},{8,10},{9,11},{10,... | collective-permute-start | bytes 786440 | tf_op jit(solution)/shard_map/ppermute | solution.py:191
  172.8 17.7 %all-to-all-start.3 = ((bf16[8,127,256]{2,1,0:T(8,128)(2,1)}), bf16[8,127,256]{2,1,0:T(8,128)(2,1)S(1)}, u32[]{:S(2)}, u32[]{:S(2)}) async-start(bf16[8,127,256]{2,1,0:T(8,128)(2,1)} %broadcast_select_fusion.1), calls=%async_computation.3 | async-start | bytes 1048576 | tf_op jit(solution)/shard_map/all_to_all | solution.py:316
  176.4 7.5 %collective-permute-start.7 = (bf16[512,256]{1,0:T(8,128)(2,1)S(1)}, bf16[512,256]{1,0:T(8,128)(2,1)S(1)}, u32[]{:S(2)}, u32[]{:S(2)}) collective-permute-start(bf16[512,256]{1,0:T(8,128)(2,1)S(1)} %fusion.41), channel_id=1, source_target_pairs={{0,2},{1,3},{2,0},{3,1},{4,6},{5,7},{6,4},{7,5},{8,10},{9,11},{10,... | collective-permute-start | bytes 786440 | tf_op jit(solution)/shard_map/ppermute | solution.py:191
  190.5 18.0 %all-to-all-start.4 = ((bf16[8,127,256]{2,1,0:T(8,128)(2,1)}), bf16[8,127,256]{2,1,0:T(8,128)(2,1)S(1)}, u32[]{:S(2)}, u32[]{:S(2)}) async-start(bf16[8,127,256]{2,1,0:T(8,128)(2,1)} %broadcast_select_fusion), calls=%async_computation.4 | async-start | bytes 1048576 | tf_op jit(solution)/shard_map/all_to_all | solution.py:316
  197.3 12.9 %copy-start.1 = (bf16[512,2048]{1,0:T(8,128)(2,1)S(1)}, bf16[512,2048]{1,0:T(8,128)(2,1)}, u32[]{:S(2)}) copy-start(bf16[512,2048]{1,0:T(8,128)(2,1)} %param.29) | copy-start | bytes 6291460

commit v8 on v6

--- a/solution.py
+++ b/solution.py
@@ -58,8 +58,9 @@
             e_p = jnp.exp(s_p - highest)
             e_f = jnp.exp(s_f - highest)
             totals = jnp.sum(e_p, axis=1, keepdims=True) + jnp.sum(e_f, axis=1, keepdims=True)
-            p_p = (e_p / totals).astype(jnp.bfloat16)
-            p_f = (e_f / totals).astype(jnp.bfloat16)
+            inverse = 1.0 / totals
+            p_p = (e_p * inverse).astype(jnp.bfloat16)
+            p_f = (e_f * inverse).astype(jnp.bfloat16)
             out = jnp.dot(p_p, vp, preferred_element_type=jnp.float32) + jnp.dot(
                 p_f, vf, preferred_element_type=jnp.float32
             )
@@ -286,10 +287,12 @@
     lane = (device - firsts) % devices
     row_of = jnp.arange(bucket, dtype=jnp.int32)[None, :] * devices + lane[:, None]
     back_valid = row_of < counts[:, None]
-    back_slot = jnp.clip((firsts[:, None] + row_of) // devices, 0, bal - 1)
-    picked = jnp.where(
-        back_valid[:, :, None], mixed[back_slot.reshape(-1)].reshape(devices, bucket, width), 0
-    ).astype(jnp.bfloat16)
+    back_start = (firsts + lane) // devices
+    padded = jnp.concatenate([mixed, jnp.zeros((bucket, width), mixed.dtype)], axis=0)
+    slabs = jnp.stack(
+        [lax.dynamic_slice_in_dim(padded, back_start[k], bucket, 0) for k in range(devices)]
+    )
+    picked = jnp.where(back_valid[:, :, None], slabs, jnp.zeros((), slabs.dtype))
     returned = lax.all_to_all(picked, "req", split_axis=0, concat_axis=0, tiled=True)
     restored = jnp.roll(jnp.transpose(returned, (1, 0, 2)), -shift, axis=1).reshape(spread, width)
     if spread < total_rows:

time: 205 us -> 202 us (0.985)
  between operations: 3.05 us -> 18.1 us
  waiting for transfers between devices: 74.5 us -> 62.5 us
  local copies, waits for them, and re-layouts: 29.3 us -> 24.2 us
    ppermute x2, waiting for transfers between devices: 20.9 us -> 8.6 us  [grp_reduce_scatter(): arrived = lax.ppermute(other.astype(jnp.bfloat16), 'grp', far)]
    gather x2 -> x0, local copies, waits for them, and re-layouts: 5.76 us -> none  [the longest x1 5.08 us: shards(): mixed[back_slot.reshape(-1)].reshape(devices, bucket, width)]
    unnamed x24 -> x33, local copies, waits for them, and re-layouts: 3.19 us -> 4.74 us
  transfers between devices with their start and end apart: 10 -> 10, of which waited for: 9 -> 8; matrix products, arithmetic and copies ran while one was open for 12% -> 12% of each run, Pallas kernels for 13% -> 14%
where the time goes in v8:
time: 202 us; the launch traced here: 201 us
  waiting for transfers between devices  62.5 us (31%)
  Pallas kernels  27.1 us (13%)
  starting transfers between devices  25.8 us (13%)
  local copies, waits for them, and re-layouts  24.2 us (12%)
  other arithmetic  23.2 us (11%)
  matrix products  19.6 us (10%)
  between operations  18.1 us (9%)
    pallas_call x2, Pallas kernels, span_attention(): pl.pallas_call(functools.partial(span_kernel, kv_index), out_shape=jax.Sh...  27.1 us
    all_to_all x1, waiting for transfers between devices, shards(): lax.all_to_all(picked, 'req', split_axis=0, concat_axis=0, tiled=True)  24.8 us
    ppermute x1, waiting for transfers between devices, grp_all_gather(): across = lax.ppermute(block, 'grp', far)  11.6 us
    dot_general x1, matrix products, finish(): jnp.dot(inner, down_weight, preferred_element_type=jnp.float32)  10.5 us
    all_to_all x2, starting transfers between devices, shards(): lax.all_to_all(part, 'req', split_axis=0, concat_axis=0, tiled=True)  10 us
    ppermute x2, waiting for transfers between devices, grp_reduce_scatter(): arrived = lax.ppermute(other.astype(jnp.bfloat16), 'grp', far)  8.6 us
    all_to_all x1, starting transfers between devices, shards(): lax.all_to_all(send_resid, 'req', split_axis=0, concat_axis=0, tiled=True)  7.25 us
    all_to_all x2, waiting for transfers between devices, shards(): lax.all_to_all(part, 'req', split_axis=0, concat_axis=0, tiled=True)  5.35 us
  transfers between devices with their start and end apart: 10, of which 8 were waited for; matrix products, arithmetic and copies ran while one was open for 12% of the time, Pallas kernels for 14%

profile of v8, /device:TPU:0, one launch (start us, length us, event | category | flops | bytes accessed | tf_op | source)
XLA Modules:
  0.0 200.5 jit_solution(15472817648385611187)
XLA Ops:
  4.4 1.3 slice_bitcast_fusion
  6.0 1.4 fusion.7
  7.4 7.3 %all-to-all-start = ((bf16[8,127,512]{2,1,0:T(8,128)(2,1)}), bf16[8,127,512]{2,1,0:T(8,128)(2,1)S(1)}, u32[]{:S(2)}, u32[]{:S(2)}) async-start(bf16[8,127,512]{2,1,0:T(8,128)(2,1)} %fusion.7), calls=%async_computation | async-start | bytes 2097152 | tf_op jit(solution)/shard_map/all_to_all | solution.py:263
  15.7 1.9 fusion.78
  20.4 13.4 %shard_map.154 = bf16[1024,256]{1,0:T(8,128)(2,1)} custom-call(s32[1]{0:T(128)S(6)} %copy.51.start_ref, bf16[1024,512]{1,0:T(8,128)(2,1)} %q_ref.2, bf16[4608,128]{1,0:T(8,128)(2,1)} %kp_ref.3, bf16[4608,128]{1,0:T(8,128)(2,1)} %vp_ref.3, bf16[1024,128]{1,0:T(8,128)(2,1)} %kf_ref.3, bf16[1024,128]{1,0:T(8,128)(2,1)} %vf_ref.3), custom_call_target="tpu_custom_call" | custom-call | flops 17179869184 | bytes 1835008 | tf_op jit(solution)/shard_map/pallas_call | solution.py:89
  36.6 3.8 %all-to-all-done = bf16[8,127,512]{2,1,0:T(8,128)(2,1)S(1)} async-done(((bf16[8,127,512]{2,1,0:T(8,128)(2,1)}), bf16[8,127,512]{2,1,0:T(8,128)(2,1)S(1)}, u32[]{:S(2)}, u32[]{:S(2)}) %all-to-all-start) | async-done | bytes 1040416 | tf_op jit(solution)/shard_map/all_to_all | solution.py:263
  40.4 4.3 %all-to-all-start.1 = ((bf16[8,127,256]{2,1,0:T(8,128)(2,1)}), bf16[8,127,256]{2,1,0:T(8,128)(2,1)}, u32[]{:S(2)}, u32[]{:S(2)}) async-start(bf16[8,127,256]{2,1,0:T(8,128)(2,1)} %fusion.29), calls=%async_computation.1 | async-start | bytes 1048576 | tf_op jit(solution)/shard_map/all_to_all | solution.py:270
  44.8 13.7 %shard_map.155 = bf16[1024,256]{1,0:T(8,128)(2,1)} custom-call(s32[1]{0:T(128)S(6)} %copy.51.start_ref, bf16[1024,512]{1,0:T(8,128)(2,1)} %q_ref.2, bf16[4608,128]{1,0:T(8,128)(2,1)} %kp_ref.3, bf16[4608,128]{1,0:T(8,128)(2,1)} %vp_ref.3, bf16[1024,128]{1,0:T(8,128)(2,1)} %kf_ref.3, bf16[1024,128]{1,0:T(8,128)(2,1)} %vf_ref.3), custom_call_target="tpu_custom_call" | custom-call | flops 17179869184 | bytes 1835008 | tf_op jit(solution)/shard_map/pallas_call | solution.py:89
  61.4 5.7 %all-to-all-start.2 = ((bf16[8,127,256]{2,1,0:T(8,128)(2,1)}), bf16[8,127,256]{2,1,0:T(8,128)(2,1)S(1)}, u32[]{:S(2)}, u32[]{:S(2)}) async-start(bf16[8,127,256]{2,1,0:T(8,128)(2,1)} %fusion.27), calls=%async_computation.2 | async-start | bytes 1048576 | tf_op jit(solution)/shard_map/all_to_all | solution.py:270
  67.1 4.4 %compare_select_fusion.2 = s32[512,1]{0,1:T(1,128)S(1)} fusion(s32[]{:T(128)} %bitcast.16, s32[]{:T(128)} %bitcast.17, s32[]{:T(128)} %bitcast.18, s32[]{:T(128)} %bitcast.19, s32[]{:T(128)} %bitcast.20, s32[]{:T(128)} %bitcast.22, s32[]{:T(128)} %bitcast.21, s32[512,1]{0,1:T(1,128)S(1)} %bitcast.140), kind=kLoop, calls=%fused_computation.133 | loop fusion | flops 7680 | bytes 4124 | tf_op jit(solution)/shard_map/gather | solution.py:278
  73.4 2.0 gather_fusion.1
  75.4 5.3 %all-to-all-done.2 = bf16[8,127,256]{2,1,0:T(8,128)(2,1)S(1)} async-done(((bf16[8,127,256]{2,1,0:T(8,128)(2,1)}), bf16[8,127,256]{2,1,0:T(8,128)(2,1)S(1)}, u32[]{:S(2)}, u32[]{:S(2)}) %all-to-all-start.2) | async-done | bytes 520224 | tf_op jit(solution)/shard_map/all_to_all | solution.py:270
  80.9 2.0 gather_fusion.2
  85.5 2.8 %collective-permute-done = bf16[2,512,512]{2,1,0:T(8,128)(2,1)} collective-permute-done((bf16[2,512,512]{2,1,0:T(8,128)(2,1)S(1)}, bf16[2,512,512]{2,1,0:T(8,128)(2,1)}, u32[]{:S(2)}, u32[]{:S(2)}) %collective-permute-start) | collective-permute-done | bytes 1048608 | tf_op jit(solution)/shard_map/ppermute | solution.py:185
  88.3 2.1 %fusion.12 = bf16[512,512]{1,0:T(8,128)(2,1)} fusion(bf16[2,512,512]{2,1,0:T(8,128)(2,1)} %collective-permute-done, bf16[512,2048]{1,0:T(8,128)(2,1)} %copy-done.2, s32[]{:T(128)S(6)} %select_n.208), kind=kLoop, calls=%fused_computation.39 | loop fusion | flops 1048576 | bytes 1572868 | tf_op jit(solution)/shard_map/convert_element_type | solution.py:190
  90.4 1.5 collective-permute-start.1
  92.0 1.5 reshape.400
  93.5 2.6 %gather_fusion = bf16[512,512]{1,0:T(8,128)(2,1)} fusion(bf16[1016,512]{1,0:T(8,128)(2,1)S(1)} %reshape.400, s32[1024]{0:T(1024)S(1)} %pad_clamp_fusion), kind=kCustom, calls=%fused_computation | custom fusion | bytes 1050624 | tf_op jit(solution)/shard_map/gather | solution.py:283
  96.1 8.6 %collective-permute-done.1 = bf16[512,512]{1,0:T(8,128)(2,1)} collective-permute-done((bf16[512,512]{1,0:T(8,128)(2,1)}, bf16[512,512]{1,0:T(8,128)(2,1)}, u32[]{:S(2)}, u32[]{:S(2)}) %collective-permute-start.1) | collective-permute-done | bytes 524320 | tf_op jit(solution)/shard_map/ppermute | solution.py:190
  104.7 1.8 fusion.15
  106.5 1.6 collective-permute-start.2
  108.1 11.6 %collective-permute-done.2 = bf16[512,512]{1,0:T(8,128)(2,1)S(1)} collective-permute-done((bf16[512,512]{1,0:T(8,128)(2,1)S(1)}, bf16[512,512]{1,0:T(8,128)(2,1)S(1)}, u32[]{:S(2)}, u32[]{:S(2)}) %collective-permute-start.2) | collective-permute-done | bytes 524320 | tf_op jit(solution)/shard_map/ppermute | solution.py:201
  120.8 3.0 %collective-permute-done.3 = bf16[2,512,512]{2,1,0:T(8,128)(2,1)} collective-permute-done((bf16[2,512,512]{2,1,0:T(8,128)(2,1)}, bf16[2,512,512]{2,1,0:T(8,128)(2,1)}, u32[]{:S(2)}, u32[]{:S(2)}) %collective-permute-start.3) | collective-permute-done | bytes 1048608 | tf_op jit(solution)/shard_map/ppermute | solution.py:202
  126.6 1.4 copy-done.10
  128.1 3.7 %fusion.24 = f32[512,1024]{1,0:T(8,128)} fusion(bf16[2048,1024]{1,0:T(8,128)(2,1)S(1)} %copy-done.10, f32[2048]{0:T(1024)S(1)} %copy-done.12, f32[512]{0:T(512)S(1)} %add_rsqrt_fusion, bf16[512,512]{1,0:T(8,128)(2,1)S(1)} %get-tuple-element.21, bf16[512,512]{1,0:T(8,128)(2,1)S(1)} %get-tuple-element.22, bf16[512,512]{1,0:T(8,128)(2,1)S(1)} %get-tuple-element.23, ...), kind=kOutput, calls=%fused_computation.56 | convolution fusion | flops 2159017984 | bytes 8398848 | tf_op jit(solution)/shard_map/dot_general | solution.py:217
  131.8 10.5 %convolution_convert_fusion = bf16[512,2048]{1,0:T(8,128)(2,1)} fusion(bf16[1024,2048]{1,0:T(8,128)(2,1)} %param.35, f32[512,1024]{1,0:T(8,128)} %fusion.24, bf16[2048,1024]{1,0:T(8,128)(2,1)} %param.34, f32[2048]{0:T(1024)S(1)} %copy-done.12, f32[512]{0:T(512)S(1)} %add_rsqrt_fusion, bf16[512,512]{1,0:T(8,128)(2,1)} %copy-done.3, ...), kind=kOutput, calls=%fused_computation.10 | convolution fusion | flops 4310695936 | bytes 14690304 | tf_op jit(solution)/shard_map/dot_general | solution.py:221
  143.9 2.5 %collective-permute-done.4 = bf16[2,512,512]{2,1,0:T(8,128)(2,1)S(1)} collective-permute-done((bf16[2,512,512]{2,1,0:T(8,128)(2,1)S(1)}, bf16[2,512,512]{2,1,0:T(8,128)(2,1)S(1)}, u32[]{:S(2)}, u32[]{:S(2)}) %collective-permute-start.4) | collective-permute-done | bytes 1048608 | tf_op jit(solution)/shard_map/ppermute | solution.py:185
  148.6 1.6 collective-permute-start.5
  165.2 1.6 fusion.11
  168.7 3.6 %all-to-all-start.3 = ((bf16[8,127,512]{2,1,0:T(8,128)(2,1)}), bf16[8,127,512]{2,1,0:T(8,128)(2,1)S(1)}, u32[]{:S(2)}, u32[]{:S(2)}) async-start(bf16[8,127,512]{2,1,0:T(8,128)(2,1)} %broadcast_select_fusion), calls=%async_computation.3 | async-start | bytes 2097152 | tf_op jit(solution)/shard_map/all_to_all | solution.py:296
  173.5 24.8 %all-to-all-done.3 = bf16[8,127,512]{2,1,0:T(8,128)(2,1)S(1)} async-done(((bf16[8,127,512]{2,1,0:T(8,128)(2,1)}), bf16[8,127,512]{2,1,0:T(8,128)(2,1)S(1)}, u32[]{:S(2)}, u32[]{:S(2)}) %all-to-all-start.3) | async-done | bytes 1040416 | tf_op jit(solution)/shard_map/all_to_all | solution.py:296
  199.3 1.3 pad_select_fusion
  (96 shorter events, 27.7 us)
Async XLA Ops:
  0.0 82.9 %copy-start = (bf16[512,2048]{1,0:T(8,128)(2,1)S(1)}, bf16[512,2048]{1,0:T(8,128)(2,1)}, u32[]{:S(2)}) copy-start(bf16[512,2048]{1,0:T(8,128)(2,1)} %param.31) | copy-start | bytes 6291460
  6.0 9.4 %slice-start = ((bf16[1024,512]{1,0:T(8,128)(2,1)}), bf16[8,512]{1,0:T(8,128)(2,1)S(1)}, s32[]{:S(2)}) async-start(bf16[1024,512]{1,0:T(8,128)(2,1)} %q_ref.2), calls=%async_computation.4 | async-start | bytes 16384 | tf_op jit(solution)/shard_map/slice | solution.py:107
  6.0 9.5 %copy-start.7 = (s32[8]{0:T(128)S(1)}, s32[8]{0:T(128)}, u32[]{:S(2)}) copy-start(s32[8]{0:T(128)} %param.26) | copy-start | bytes 100
  6.0 9.5 %copy-start.8 = (s32[8]{0:T(128)S(1)}, s32[8]{0:T(128)}, u32[]{:S(2)}) copy-start(s32[8]{0:T(128)} %param.27) | copy-start | bytes 100
  6.0 9.5 %copy-start.9 = (s32[8]{0:T(128)S(1)}, s32[8]{0:T(128)}, u32[]{:S(2)}) copy-start(s32[8]{0:T(128)} %param.28) | copy-start | bytes 100
  7.4 33.0 %all-to-all-start = ((bf16[8,127,512]{2,1,0:T(8,128)(2,1)}), bf16[8,127,512]{2,1,0:T(8,128)(2,1)S(1)}, u32[]{:S(2)}, u32[]{:S(2)}) async-start(bf16[8,127,512]{2,1,0:T(8,128)(2,1)} %fusion.7), calls=%async_computation | async-start | bytes 2097152 | tf_op jit(solution)/shard_map/all_to_all | solution.py:263
  15.4 3.5 %copy-start.11 = (bf16[4608,128]{1,0:T(8,128)(2,1)S(1)}, bf16[4608,128]{1,0:T(8,128)(2,1)}, u32[]{:S(2)}) copy-start(bf16[4608,128]{1,0:T(8,128)(2,1)} %vp_ref.3) | copy-start | bytes 3538948
  40.4 18.1 %copy-start.1 = (bf16[8,127,512]{2,1,0:T(8,128)(2,1)}, bf16[8,127,512]{2,1,0:T(8,128)(2,1)S(1)}, u32[]{:S(2)}) copy-start(bf16[8,127,512]{2,1,0:T(8,128)(2,1)S(1)} %all-to-all-done) | copy-start | bytes 3121156
  40.4 20.9 %all-to-all-start.1 = ((bf16[8,127,256]{2,1,0:T(8,128)(2,1)}), bf16[8,127,256]{2,1,0:T(8,128)(2,1)}, u32[]{:S(2)}, u32[]{:S(2)}) async-start(bf16[8,127,256]{2,1,0:T(8,128)(2,1)} %fusion.29), calls=%async_computation.1 | async-start | bytes 1048576 | tf_op jit(solution)/shard_map/all_to_all | solution.py:270
  61.4 19.4 %all-to-all-start.2 = ((bf16[8,127,256]{2,1,0:T(8,128)(2,1)}), bf16[8,127,256]{2,1,0:T(8,128)(2,1)S(1)}, u32[]{:S(2)}, u32[]{:S(2)}) async-start(bf16[8,127,256]{2,1,0:T(8,128)(2,1)} %fusion.27), calls=%async_computation.2 | async-start | bytes 1048576 | tf_op jit(solution)/shard_map/all_to_all | solution.py:270
  84.2 1.3 copy-start.2
  85.5 2.8 %collective-permute-start = (bf16[2,512,512]{2,1,0:T(8,128)(2,1)S(1)}, bf16[2,512,512]{2,1,0:T(8,128)(2,1)}, u32[]{:S(2)}, u32[]{:S(2)}) collective-permute-start(bf16[2,512,512]{2,1,0:T(8,128)(2,1)S(1)} %pad_maximum_fusion.2), channel_id=1, source_target_pairs={{0,1},{1,0},{2,3},{3,2},{4,5},{5,4},{6,7},{7,6},{8,9},{9,8},{10,11... | collective-permute-start | bytes 3145736 | tf_op jit(solution)/shard_map/ppermute | solution.py:185
  90.4 14.3 %collective-permute-start.1 = (bf16[512,512]{1,0:T(8,128)(2,1)}, bf16[512,512]{1,0:T(8,128)(2,1)}, u32[]{:S(2)}, u32[]{:S(2)}) collective-permute-start(bf16[512,512]{1,0:T(8,128)(2,1)} %fusion.12), channel_id=1, source_target_pairs={{0,2},{1,3},{2,0},{3,1},{4,6},{5,7},{6,4},{7,5},{8,10},{9,11},{10,... | collective-permute-start | bytes 1572872 | tf_op jit(solution)/shard_map/ppermute | solution.py:190
  106.5 13.2 %collective-permute-start.2 = (bf16[512,512]{1,0:T(8,128)(2,1)S(1)}, bf16[512,512]{1,0:T(8,128)(2,1)S(1)}, u32[]{:S(2)}, u32[]{:S(2)}) collective-permute-start(bf16[512,512]{1,0:T(8,128)(2,1)S(1)} %fusion.15), channel_id=1, source_target_pairs={{0,2},{1,3},{2,0},{3,1},{4,6},{5,7},{6,4},{7,5},{8,10},{9,11},{10,... | collective-permute-start | bytes 1572872 | tf_op jit(solution)/shard_map/ppermute | solution.py:201
  120.8 3.0 %collective-permute-start.3 = (bf16[2,512,512]{2,1,0:T(8,128)(2,1)}, bf16[2,512,512]{2,1,0:T(8,128)(2,1)}, u32[]{:S(2)}, u32[]{:S(2)}) collective-permute-start(bf16[2,512,512]{2,1,0:T(8,128)(2,1)} %pad_maximum_fusion.3), channel_id=1, source_target_pairs={{0,1},{1,0},{2,3},{3,2},{4,5},{5,4},{6,7},{7,6},{8,9},{9,8},{10,11... | collective-permute-start | bytes 3145736 | tf_op jit(solution)/shard_map/ppermute | solution.py:202
  125.3 2.8 %copy-start.10 = (bf16[2048,1024]{1,0:T(8,128)(2,1)S(1)}, bf16[2048,1024]{1,0:T(8,128)(2,1)}, u32[]{:S(2)}) copy-start(bf16[2048,1024]{1,0:T(8,128)(2,1)} %param.33) | copy-start | bytes 12582916
  125.5 0.8 copy-start.3
  125.5 1.0 copy-start.4
  125.5 1.1 copy-start.5
  125.5 2.6 %copy-start.12 = (f32[2048]{0:T(1024)S(1)}, f32[2048]{0:T(1024)}, u32[]{:S(2)}) copy-start(f32[2048]{0:T(1024)} %param.32) | copy-start | bytes 24580
  143.7 2.7 %collective-permute-start.4 = (bf16[2,512,512]{2,1,0:T(8,128)(2,1)S(1)}, bf16[2,512,512]{2,1,0:T(8,128)(2,1)S(1)}, u32[]{:S(2)}, u32[]{:S(2)}) collective-permute-start(bf16[2,512,512]{2,1,0:T(8,128)(2,1)S(1)} %pad_maximum_fusion.4), channel_id=1, source_target_pairs={{0,1},{1,0},{2,3},{3,2},{4,5},{5,4},{6,7},{7,6},{8,9},{9,8},{10,11... | collective-permute-start | bytes 3145736 | tf_op jit(solution)/shard_map/ppermute | solution.py:185
  146.4 1.0 copy-start.6
  148.6 16.6 %collective-permute-start.5 = (bf16[512,512]{1,0:T(8,128)(2,1)S(1)}, bf16[512,512]{1,0:T(8,128)(2,1)}, u32[]{:S(2)}, u32[]{:S(2)}) collective-permute-start(bf16[512,512]{1,0:T(8,128)(2,1)S(1)} %fusion.8), channel_id=1, source_target_pairs={{0,2},{1,3},{2,0},{3,1},{4,6},{5,7},{6,4},{7,5},{8,10},{9,11},{10,... | collective-permute-start | bytes 1572872 | tf_op jit(solution)/shard_map/ppermute | solution.py:190
  168.7 29.6 %all-to-all-start.3 = ((bf16[8,127,512]{2,1,0:T(8,128)(2,1)}), bf16[8,127,512]{2,1,0:T(8,128)(2,1)S(1)}, u32[]{:S(2)}, u32[]{:S(2)}) async-start(bf16[8,127,512]{2,1,0:T(8,128)(2,1)} %broadcast_select_fusion), calls=%async_computation.3 | async-start | bytes 2097152 | tf_op jit(solution)/shard_map/all_to_all | solution.py:296

commit v9 on v8

--- a/solution.py
+++ b/solution.py
@@ -43,13 +43,13 @@
         k_pos = lax.broadcasted_iota(jnp.int32, (QBLK, hi), 1)
         seen = (k_pos >= DEC) & (k_pos <= q_pos)
         for hh in range(2):
-            q = q_ref[lo:hi, hh * half : (hh + 1) * half]
+            q = q_ref[lo:hi, hh * half : (hh + 1) * half] * jnp.asarray(SCALE, q_ref.dtype)
             s_p = lax.dot_general(
                 q, kp, (((1,), (1,)), ((), ())), preferred_element_type=jnp.float32
-            ) * SCALE
+            )
             s_f = lax.dot_general(
                 q, kf, (((1,), (1,)), ((), ())), preferred_element_type=jnp.float32
-            ) * SCALE
+            )
             s_p = jnp.where(prior_seen, s_p, MASKED_SCORE)
             s_f = jnp.where(seen, s_f, MASKED_SCORE)
             highest = jnp.maximum(
@@ -191,6 +191,23 @@
     return own + arrived.astype(jnp.float32)
 
 
+def grp_reduce_scatter_blocks(block_of, total):
+    parts = lax.axis_size("grp")
+    width = total // parts
+    if parts != 4:
+        whole = jnp.concatenate([block_of(k, width) for k in range(parts)], axis=1)
+        return grp_reduce_scatter(whole)
+    me = lax.axis_index("grp")
+    near = [(i, i ^ 1) for i in range(parts)]
+    far = [(i, i ^ 2) for i in range(parts)]
+    outgoing = jnp.stack([block_of(me ^ 1, width), block_of(me ^ 3, width)])
+    incoming = lax.ppermute(outgoing, "grp", near)
+    other = block_of(me ^ 2, width).astype(jnp.float32) + incoming[1].astype(jnp.float32)
+    arrived = lax.ppermute(other.astype(jnp.bfloat16), "grp", far)
+    own = block_of(me, width).astype(jnp.float32) + incoming[0].astype(jnp.float32)
+    return own + arrived.astype(jnp.float32)
+
+
 def grp_all_gather(block):
     parts = lax.axis_size("grp")
     if parts != 4:
@@ -217,8 +234,11 @@
     gate = jnp.dot(normed, gate_weight, preferred_element_type=jnp.float32)
     upval = jnp.dot(normed, up_weight, preferred_element_type=jnp.float32)
     inner = (jax.nn.silu(gate) * upval).astype(jnp.bfloat16)
-    down_cols = grp_reduce_scatter(
-        jnp.dot(inner, down_weight, preferred_element_type=jnp.float32).astype(jnp.bfloat16)
+    down_cols = grp_reduce_scatter_blocks(
+        lambda index, width: jnp.dot(
+            inner, grp_block(down_weight, index, width), preferred_element_type=jnp.float32
+        ).astype(jnp.bfloat16),
+        down_weight.shape[1],
     )
     return (state_cols.astype(jnp.float32) + down_cols).astype(jnp.bfloat16)
 

time: 202 us -> 193 us (0.955)
  matrix products: 19.6 us -> 16.4 us
  local copies, waits for them, and re-layouts: 24.2 us -> 21.5 us
  other arithmetic: 23.2 us -> 20.7 us
    ppermute x0 -> x2, waiting for transfers between devices: none -> 2.54 us  [the longest x1 2.54 us: grp_reduce_scatter_blocks(): incoming = lax.ppermute(outgoing, 'grp', near)]
    ppermute x2 -> x1, waiting for transfers between devices: 5.31 us -> 2.79 us  [grp_reduce_scatter(): incoming = lax.ppermute(outgoing, 'grp', near)]
    dot_general x1 -> x5, matrix products: 10.5 us -> 8.58 us  [the longest x4 5.32 us: finish(): jnp.dot(inner, grp_block(down_weight, index, width), preferred_element_ty...]
    unnamed x33 -> x35, local copies, waits for them, and re-layouts: 4.74 us -> 3.21 us
    ppermute x2 -> x1, waiting for transfers between devices: 8.6 us -> 8.59 us  [grp_reduce_scatter(): arrived = lax.ppermute(other.astype(jnp.bfloat16), 'grp', far)]
  transfers between devices with their start and end apart: 10 -> 10, of which waited for: 8 -> 8; matrix products, arithmetic and copies ran while one was open for 12% -> 14% of each run, Pallas kernels for 14% -> 14%
where the time goes in v9:
time: 193 us; the launch traced here: 192 us
  waiting for transfers between devices  62.8 us (33%)
  Pallas kernels  26.6 us (14%)
  starting transfers between devices  25.7 us (13%)
  local copies, waits for them, and re-layouts  21.5 us (11%)
  other arithmetic  20.7 us (11%)
  between operations  18.5 us (10%)
  matrix products  16.4 us (8%)
    pallas_call x2, Pallas kernels, span_attention(): pl.pallas_call(functools.partial(span_kernel, kv_index), out_shape=jax.Sh...  26.6 us
    all_to_all x1, waiting for transfers between devices, shards(): lax.all_to_all(picked, 'req', split_axis=0, concat_axis=0, tiled=True)  24.8 us
    ppermute x1, waiting for transfers between devices, grp_all_gather(): across = lax.ppermute(block, 'grp', far)  11.6 us
    all_to_all x2, starting transfers between devices, shards(): lax.all_to_all(part, 'req', split_axis=0, concat_axis=0, tiled=True)  10 us
    ppermute x1, waiting for transfers between devices, grp_reduce_scatter(): arrived = lax.ppermute(other.astype(jnp.bfloat16), 'grp', far)  8.59 us
    all_to_all x1, starting transfers between devices, shards(): lax.all_to_all(send_resid, 'req', split_axis=0, concat_axis=0, tiled=True)  7.25 us
    all_to_all x2, waiting for transfers between devices, shards(): lax.all_to_all(part, 'req', split_axis=0, concat_axis=0, tiled=True)  5.35 us
    dot_general x4, matrix products, finish(): jnp.dot(inner, grp_block(down_weight, index, width), preferred_element_ty...  5.32 us
  transfers between devices with their start and end apart: 10, of which 8 were waited for; matrix products, arithmetic and copies ran while one was open for 14% of the time, Pallas kernels for 14%

profile of v9, /device:TPU:0, one launch (start us, length us, event | category | flops | bytes accessed | tf_op | source)
XLA Modules:
  0.0 192.2 jit_solution(11405385779758471242)
XLA Ops:
  4.4 1.3 slice_bitcast_fusion
  6.0 1.4 fusion.11
  7.4 7.3 %all-to-all-start = ((bf16[8,127,512]{2,1,0:T(8,128)(2,1)}), bf16[8,127,512]{2,1,0:T(8,128)(2,1)S(1)}, u32[]{:S(2)}, u32[]{:S(2)}) async-start(bf16[8,127,512]{2,1,0:T(8,128)(2,1)} %fusion.11), calls=%async_computation | async-start | bytes 2097152 | tf_op jit(solution)/shard_map/all_to_all | solution.py:283
  15.7 1.9 %fusion.90 = (f32[8,8]{1,0:T(8,128)S(1)}, f32[8,8,4096]{2,1,0:T(8,128)S(1)}) fusion(bf16[4608,128]{1,0:T(8,128)(2,1)} %kp_ref.3, bf16[8,8,64]{2,1,0:T(8,128)(2,1)S(1)} %get-tuple-element.27, bf16[8,8,64]{2,1,0:T(8,128)(2,1)S(1)} %get-tuple-element.26, pred[8,4096]{1,0:T(8,128)(4,1)S(1)} %fusion.60), kind=kOutput, calls=%fused_computation.194 | convolution fusion | flops 67928000 | bytes 2146560 | tf_op jit(solution)/shard_map/rhc,tc->rht/dot_general | solution.py:113
  20.4 13.1 %shard_map.154 = bf16[1024,256]{1,0:T(8,128)(2,1)} custom-call(s32[1]{0:T(128)S(6)} %copy.51.start_ref, bf16[1024,512]{1,0:T(8,128)(2,1)} %q_ref.2, bf16[4608,128]{1,0:T(8,128)(2,1)} %kp_ref.3, bf16[4608,128]{1,0:T(8,128)(2,1)} %vp_ref.3, bf16[1024,128]{1,0:T(8,128)(2,1)} %kf_ref.3, bf16[1024,128]{1,0:T(8,128)(2,1)} %vf_ref.3), custom_call_target="tpu_custom_call" | custom-call | flops 17179869184 | bytes 1835008 | tf_op jit(solution)/shard_map/pallas_call | solution.py:89
  36.3 4.1 %all-to-all-done = bf16[8,127,512]{2,1,0:T(8,128)(2,1)S(1)} async-done(((bf16[8,127,512]{2,1,0:T(8,128)(2,1)}), bf16[8,127,512]{2,1,0:T(8,128)(2,1)S(1)}, u32[]{:S(2)}, u32[]{:S(2)}) %all-to-all-start) | async-done | bytes 1040416 | tf_op jit(solution)/shard_map/all_to_all | solution.py:283
  40.4 4.3 %all-to-all-start.1 = ((bf16[8,127,256]{2,1,0:T(8,128)(2,1)}), bf16[8,127,256]{2,1,0:T(8,128)(2,1)}, u32[]{:S(2)}, u32[]{:S(2)}) async-start(bf16[8,127,256]{2,1,0:T(8,128)(2,1)} %fusion.36), calls=%async_computation.1 | async-start | bytes 1048576 | tf_op jit(solution)/shard_map/all_to_all | solution.py:290
  44.8 13.5 %shard_map.155 = bf16[1024,256]{1,0:T(8,128)(2,1)} custom-call(s32[1]{0:T(128)S(6)} %copy.51.start_ref, bf16[1024,512]{1,0:T(8,128)(2,1)} %q_ref.2, bf16[4608,128]{1,0:T(8,128)(2,1)} %kp_ref.3, bf16[4608,128]{1,0:T(8,128)(2,1)} %vp_ref.3, bf16[1024,128]{1,0:T(8,128)(2,1)} %kf_ref.3, bf16[1024,128]{1,0:T(8,128)(2,1)} %vf_ref.3), custom_call_target="tpu_custom_call" | custom-call | flops 17179869184 | bytes 1835008 | tf_op jit(solution)/shard_map/pallas_call | solution.py:89
  61.1 5.7 %all-to-all-start.2 = ((bf16[8,127,256]{2,1,0:T(8,128)(2,1)}), bf16[8,127,256]{2,1,0:T(8,128)(2,1)S(1)}, u32[]{:S(2)}, u32[]{:S(2)}) async-start(bf16[8,127,256]{2,1,0:T(8,128)(2,1)} %fusion.34), calls=%async_computation.2 | async-start | bytes 1048576 | tf_op jit(solution)/shard_map/all_to_all | solution.py:290
  66.9 4.4 %compare_select_fusion.2 = s32[512,1]{0,1:T(1,128)S(1)} fusion(s32[]{:T(128)} %bitcast.16, s32[]{:T(128)} %bitcast.17, s32[]{:T(128)} %bitcast.18, s32[]{:T(128)} %bitcast.19, s32[]{:T(128)} %bitcast.20, s32[]{:T(128)} %bitcast.22, s32[]{:T(128)} %bitcast.21, s32[512,1]{0,1:T(1,128)S(1)} %bitcast.143), kind=kLoop, calls=%fused_computation.142 | loop fusion | flops 7680 | bytes 4124 | tf_op jit(solution)/shard_map/gather | solution.py:298
  73.2 2.0 %gather_fusion.1 = bf16[512,256]{1,0:T(8,128)(2,1)S(1)} fusion(bf16[1016,256]{1,0:T(8,128)(2,1)S(1)} %reshape.401, s32[1024]{0:T(1024)S(1)} %pad_clamp_fusion), kind=kCustom, calls=%fused_computation.1 | custom fusion | bytes 526336 | tf_op jit(solution)/shard_map/gather | solution.py:301
  75.2 5.3 %all-to-all-done.2 = bf16[8,127,256]{2,1,0:T(8,128)(2,1)S(1)} async-done(((bf16[8,127,256]{2,1,0:T(8,128)(2,1)}), bf16[8,127,256]{2,1,0:T(8,128)(2,1)S(1)}, u32[]{:S(2)}, u32[]{:S(2)}) %all-to-all-start.2) | async-done | bytes 520224 | tf_op jit(solution)/shard_map/all_to_all | solution.py:290
  80.7 2.0 %gather_fusion.2 = bf16[512,256]{1,0:T(8,128)(2,1)S(1)} fusion(bf16[1016,256]{1,0:T(8,128)(2,1)S(1)} %reshape.402, s32[1024]{0:T(1024)S(1)} %pad_clamp_fusion), kind=kCustom, calls=%fused_computation.2 | custom fusion | bytes 526336 | tf_op jit(solution)/shard_map/gather | solution.py:301
  85.3 2.8 %collective-permute-done = bf16[2,512,512]{2,1,0:T(8,128)(2,1)} collective-permute-done((bf16[2,512,512]{2,1,0:T(8,128)(2,1)S(1)}, bf16[2,512,512]{2,1,0:T(8,128)(2,1)}, u32[]{:S(2)}, u32[]{:S(2)}) %collective-permute-start) | collective-permute-done | bytes 1048608 | tf_op jit(solution)/shard_map/ppermute | solution.py:185
  88.0 2.1 %fusion.16 = bf16[512,512]{1,0:T(8,128)(2,1)} fusion(bf16[2,512,512]{2,1,0:T(8,128)(2,1)} %collective-permute-done, bf16[512,2048]{1,0:T(8,128)(2,1)} %copy-done.2, s32[]{:T(128)S(6)} %select_n.208), kind=kLoop, calls=%fused_computation.46 | loop fusion | flops 1048576 | bytes 1572868 | tf_op jit(solution)/shard_map/convert_element_type | solution.py:190
  90.2 1.5 collective-permute-start.1
  91.7 1.5 reshape.400
  93.2 2.6 %gather_fusion = bf16[512,512]{1,0:T(8,128)(2,1)} fusion(bf16[1016,512]{1,0:T(8,128)(2,1)S(1)} %reshape.400, s32[1024]{0:T(1024)S(1)} %pad_clamp_fusion), kind=kCustom, calls=%fused_computation | custom fusion | bytes 1050624 | tf_op jit(solution)/shard_map/gather | solution.py:303
  95.9 8.6 %collective-permute-done.1 = bf16[512,512]{1,0:T(8,128)(2,1)} collective-permute-done((bf16[512,512]{1,0:T(8,128)(2,1)}, bf16[512,512]{1,0:T(8,128)(2,1)}, u32[]{:S(2)}, u32[]{:S(2)}) %collective-permute-start.1) | collective-permute-done | bytes 524320 | tf_op jit(solution)/shard_map/ppermute | solution.py:190
  104.5 1.8 fusion.19
  106.3 1.6 collective-permute-start.2
  107.8 11.6 %collective-permute-done.2 = bf16[512,512]{1,0:T(8,128)(2,1)S(1)} collective-permute-done((bf16[512,512]{1,0:T(8,128)(2,1)S(1)}, bf16[512,512]{1,0:T(8,128)(2,1)S(1)}, u32[]{:S(2)}, u32[]{:S(2)}) %collective-permute-start.2) | collective-permute-done | bytes 524320 | tf_op jit(solution)/shard_map/ppermute | solution.py:218
  120.5 3.0 %collective-permute-done.3 = bf16[2,512,512]{2,1,0:T(8,128)(2,1)} collective-permute-done((bf16[2,512,512]{2,1,0:T(8,128)(2,1)}, bf16[2,512,512]{2,1,0:T(8,128)(2,1)}, u32[]{:S(2)}, u32[]{:S(2)}) %collective-permute-start.3) | collective-permute-done | bytes 1048608 | tf_op jit(solution)/shard_map/ppermute | solution.py:219
  125.8 1.5 copy-done.8
  127.3 2.4 %fusion.31 = f32[512,1024]{1,0:T(8,128)S(1)} fusion(bf16[2048,1024]{1,0:T(8,128)(2,1)S(1)} %copy-done.8, f32[2048]{0:T(1024)S(1)} %copy-done.12, f32[512]{0:T(512)S(1)} %add_rsqrt_fusion, bf16[512,512]{1,0:T(8,128)(2,1)S(1)} %get-tuple-element.19, bf16[512,512]{1,0:T(8,128)(2,1)S(1)} %get-tuple-element.20, bf16[512,512]{1,0:T(8,128)(2,1)S(1)} %get-tuple-element.21, ...), kind=kOutput, calls=%fused_computation.67 | convolution fusion | flops 2159017984 | bytes 8398848 | tf_op jit(solution)/shard_map/dot_general | solution.py:234
  129.7 3.3 %multiply_convert_fusion = bf16[512,1024]{1,0:T(8,128)(2,1)S(1)} fusion(f32[512,1024]{1,0:T(8,128)S(1)} %fusion.31, bf16[2048,1024]{1,0:T(8,128)(2,1)S(1)} %copy-done.9, f32[2048]{0:T(1024)S(1)} %copy-done.12, f32[512]{0:T(512)S(1)} %add_rsqrt_fusion, bf16[512,512]{1,0:T(8,128)(2,1)S(1)} %get-tuple-element.19, bf16[512,512]{1,0:T(8,128)(2,1)S(1)} %get-tuple-element.20, ...), kind=kOutput, calls=%fused_computation.17 | convolution fusion | flops 2162163712 | bytes 9447424 | tf_op jit(solution)/shard_map/dot_general | solution.py:235
  134.7 2.5 %collective-permute-done.4 = bf16[2,512,512]{2,1,0:T(8,128)(2,1)S(1)} collective-permute-done((bf16[2,512,512]{2,1,0:T(8,128)(2,1)S(1)}, bf16[2,512,512]{2,1,0:T(8,128)(2,1)S(1)}, u32[]{:S(2)}, u32[]{:S(2)}) %collective-permute-start.4) | collective-permute-done | bytes 1048608 | tf_op jit(solution)/shard_map/ppermute | solution.py:204
  137.3 1.5 fusion.12
  138.8 1.5 collective-permute-start.5
  155.8 2.3 %fusion.5 = f32[512,512]{1,0:T(8,128)S(1)} fusion(bf16[512,1024]{1,0:T(8,128)(2,1)} %copy-done.13, bf16[1024,2048]{1,0:T(8,128)(2,1)} %param.35, s32[]{:T(128)S(6)} %select_n.205), kind=kOutput, calls=%fused_computation.23 | convolution fusion | flops 537395200 | bytes 3145732 | tf_op jit(solution)/shard_map/dot_general | solution.py:238
  160.4 3.6 %all-to-all-start.3 = ((bf16[8,127,512]{2,1,0:T(8,128)(2,1)}), bf16[8,127,512]{2,1,0:T(8,128)(2,1)S(1)}, u32[]{:S(2)}, u32[]{:S(2)}) async-start(bf16[8,127,512]{2,1,0:T(8,128)(2,1)} %broadcast_select_fusion), calls=%async_computation.3 | async-start | bytes 2097152 | tf_op jit(solution)/shard_map/all_to_all | solution.py:316
  165.1 24.8 %all-to-all-done.3 = bf16[8,127,512]{2,1,0:T(8,128)(2,1)S(1)} async-done(((bf16[8,127,512]{2,1,0:T(8,128)(2,1)}), bf16[8,127,512]{2,1,0:T(8,128)(2,1)S(1)}, u32[]{:S(2)}, u32[]{:S(2)}) %all-to-all-start.3) | async-done | bytes 1040416 | tf_op jit(solution)/shard_map/all_to_all | solution.py:316
  (100 shorter events, 26.7 us)
Async XLA Ops:
  0.0 82.6 %copy-start = (bf16[512,2048]{1,0:T(8,128)(2,1)S(1)}, bf16[512,2048]{1,0:T(8,128)(2,1)}, u32[]{:S(2)}) copy-start(bf16[512,2048]{1,0:T(8,128)(2,1)} %param.31) | copy-start | bytes 6291460
  6.0 9.4 %slice-start = ((bf16[1024,512]{1,0:T(8,128)(2,1)}), bf16[8,512]{1,0:T(8,128)(2,1)S(1)}, s32[]{:S(2)}) async-start(bf16[1024,512]{1,0:T(8,128)(2,1)} %q_ref.2), calls=%async_computation.4 | async-start | bytes 16384 | tf_op jit(solution)/shard_map/slice | solution.py:107
  6.0 9.5 %copy-start.5 = (s32[8]{0:T(128)S(1)}, s32[8]{0:T(128)}, u32[]{:S(2)}) copy-start(s32[8]{0:T(128)} %param.26) | copy-start | bytes 100
  6.0 9.5 %copy-start.6 = (s32[8]{0:T(128)S(1)}, s32[8]{0:T(128)}, u32[]{:S(2)}) copy-start(s32[8]{0:T(128)} %param.27) | copy-start | bytes 100
  6.0 9.5 %copy-start.7 = (s32[8]{0:T(128)S(1)}, s32[8]{0:T(128)}, u32[]{:S(2)}) copy-start(s32[8]{0:T(128)} %param.28) | copy-start | bytes 100
  7.4 33.0 %all-to-all-start = ((bf16[8,127,512]{2,1,0:T(8,128)(2,1)}), bf16[8,127,512]{2,1,0:T(8,128)(2,1)S(1)}, u32[]{:S(2)}, u32[]{:S(2)}) async-start(bf16[8,127,512]{2,1,0:T(8,128)(2,1)} %fusion.11), calls=%async_computation | async-start | bytes 2097152 | tf_op jit(solution)/shard_map/all_to_all | solution.py:283
  15.4 3.5 %copy-start.11 = (bf16[4608,128]{1,0:T(8,128)(2,1)S(1)}, bf16[4608,128]{1,0:T(8,128)(2,1)}, u32[]{:S(2)}) copy-start(bf16[4608,128]{1,0:T(8,128)(2,1)} %vp_ref.3) | copy-start | bytes 3538948
  40.4 17.8 %copy-start.1 = (bf16[8,127,512]{2,1,0:T(8,128)(2,1)}, bf16[8,127,512]{2,1,0:T(8,128)(2,1)S(1)}, u32[]{:S(2)}) copy-start(bf16[8,127,512]{2,1,0:T(8,128)(2,1)S(1)} %all-to-all-done) | copy-start | bytes 3121156
  40.4 20.7 %all-to-all-start.1 = ((bf16[8,127,256]{2,1,0:T(8,128)(2,1)}), bf16[8,127,256]{2,1,0:T(8,128)(2,1)}, u32[]{:S(2)}, u32[]{:S(2)}) async-start(bf16[8,127,256]{2,1,0:T(8,128)(2,1)} %fusion.36), calls=%async_computation.1 | async-start | bytes 1048576 | tf_op jit(solution)/shard_map/all_to_all | solution.py:290
  61.1 19.4 %all-to-all-start.2 = ((bf16[8,127,256]{2,1,0:T(8,128)(2,1)}), bf16[8,127,256]{2,1,0:T(8,128)(2,1)S(1)}, u32[]{:S(2)}, u32[]{:S(2)}) async-start(bf16[8,127,256]{2,1,0:T(8,128)(2,1)} %fusion.34), calls=%async_computation.2 | async-start | bytes 1048576 | tf_op jit(solution)/shard_map/all_to_all | solution.py:290
  83.9 1.3 copy-start.2
  85.3 2.8 %collective-permute-start = (bf16[2,512,512]{2,1,0:T(8,128)(2,1)S(1)}, bf16[2,512,512]{2,1,0:T(8,128)(2,1)}, u32[]{:S(2)}, u32[]{:S(2)}) collective-permute-start(bf16[2,512,512]{2,1,0:T(8,128)(2,1)S(1)} %pad_maximum_fusion.2), channel_id=1, source_target_pairs={{0,1},{1,0},{2,3},{3,2},{4,5},{5,4},{6,7},{7,6},{8,9},{9,8},{10,11... | collective-permute-start | bytes 3145736 | tf_op jit(solution)/shard_map/ppermute | solution.py:185
  90.2 14.3 %collective-permute-start.1 = (bf16[512,512]{1,0:T(8,128)(2,1)}, bf16[512,512]{1,0:T(8,128)(2,1)}, u32[]{:S(2)}, u32[]{:S(2)}) collective-permute-start(bf16[512,512]{1,0:T(8,128)(2,1)} %fusion.16), channel_id=1, source_target_pairs={{0,2},{1,3},{2,0},{3,1},{4,6},{5,7},{6,4},{7,5},{8,10},{9,11},{10,... | collective-permute-start | bytes 1572872 | tf_op jit(solution)/shard_map/ppermute | solution.py:190
  106.3 13.2 %collective-permute-start.2 = (bf16[512,512]{1,0:T(8,128)(2,1)S(1)}, bf16[512,512]{1,0:T(8,128)(2,1)S(1)}, u32[]{:S(2)}, u32[]{:S(2)}) collective-permute-start(bf16[512,512]{1,0:T(8,128)(2,1)S(1)} %fusion.19), channel_id=1, source_target_pairs={{0,2},{1,3},{2,0},{3,1},{4,6},{5,7},{6,4},{7,5},{8,10},{9,11},{10,... | collective-permute-start | bytes 1572872 | tf_op jit(solution)/shard_map/ppermute | solution.py:218
  120.5 3.0 %collective-permute-start.3 = (bf16[2,512,512]{2,1,0:T(8,128)(2,1)}, bf16[2,512,512]{2,1,0:T(8,128)(2,1)}, u32[]{:S(2)}, u32[]{:S(2)}) collective-permute-start(bf16[2,512,512]{2,1,0:T(8,128)(2,1)} %pad_maximum_fusion.3), channel_id=1, source_target_pairs={{0,1},{1,0},{2,3},{3,2},{4,5},{5,4},{6,7},{7,6},{8,9},{9,8},{10,11... | collective-permute-start | bytes 3145736 | tf_op jit(solution)/shard_map/ppermute | solution.py:219
  125.1 2.2 %copy-start.8 = (bf16[2048,1024]{1,0:T(8,128)(2,1)S(1)}, bf16[2048,1024]{1,0:T(8,128)(2,1)}, u32[]{:S(2)}) copy-start(bf16[2048,1024]{1,0:T(8,128)(2,1)} %param.33) | copy-start | bytes 12582916
  125.3 2.0 %copy-start.12 = (f32[2048]{0:T(1024)S(1)}, f32[2048]{0:T(1024)}, u32[]{:S(2)}) copy-start(f32[2048]{0:T(1024)} %param.32) | copy-start | bytes 24580
  127.3 2.4 %copy-start.9 = (bf16[2048,1024]{1,0:T(8,128)(2,1)S(1)}, bf16[2048,1024]{1,0:T(8,128)(2,1)}, u32[]{:S(2)}) copy-start(bf16[2048,1024]{1,0:T(8,128)(2,1)} %param.34) | copy-start | bytes 12582916
  129.7 3.3 %copy-start.10 = (bf16[1024,2048]{1,0:T(8,128)(2,1)S(1)}, bf16[1024,2048]{1,0:T(8,128)(2,1)}, u32[]{:S(2)}) copy-start(bf16[1024,2048]{1,0:T(8,128)(2,1)} %param.35) | copy-start | bytes 12582916
  133.0 4.3 %copy-start.13 = (bf16[512,1024]{1,0:T(8,128)(2,1)}, bf16[512,1024]{1,0:T(8,128)(2,1)S(1)}, u32[]{:S(2)}) copy-start(bf16[512,1024]{1,0:T(8,128)(2,1)S(1)} %multiply_convert_fusion) | copy-start | bytes 3145732
  134.6 2.7 %collective-permute-start.4 = (bf16[2,512,512]{2,1,0:T(8,128)(2,1)S(1)}, bf16[2,512,512]{2,1,0:T(8,128)(2,1)S(1)}, u32[]{:S(2)}, u32[]{:S(2)}) collective-permute-start(bf16[2,512,512]{2,1,0:T(8,128)(2,1)S(1)} %pad_maximum_fusion.4), channel_id=1, source_target_pairs={{0,1},{1,0},{2,3},{3,2},{4,5},{5,4},{6,7},{7,6},{8,9},{9,8},{10,11... | collective-permute-start | bytes 3145736 | tf_op jit(solution)/shard_map/ppermute | solution.py:204
  137.3 1.5 copy-start.3
  138.8 19.3 %collective-permute-start.5 = (bf16[512,512]{1,0:T(8,128)(2,1)}, bf16[512,512]{1,0:T(8,128)(2,1)S(1)}, u32[]{:S(2)}, u32[]{:S(2)}) collective-permute-start(bf16[512,512]{1,0:T(8,128)(2,1)} %fusion.12), channel_id=1, source_target_pairs={{0,2},{1,3},{2,0},{3,1},{4,6},{5,7},{6,4},{7,5},{8,10},{9,11},{10,... | collective-permute-start | bytes 1572872 | tf_op jit(solution)/shard_map/ppermute | solution.py:206
  155.8 2.4 %copy-start.4 = (bf16[2,512,512]{2,1,0:T(8,128)(2,1)S(1)}, bf16[2,512,512]{2,1,0:T(8,128)(2,1)}, u32[]{:S(2)}) copy-start(bf16[2,512,512]{2,1,0:T(8,128)(2,1)} %copy-done.3) | copy-start | bytes 3145732
  160.4 29.6 %all-to-all-start.3 = ((bf16[8,127,512]{2,1,0:T(8,128)(2,1)}), bf16[8,127,512]{2,1,0:T(8,128)(2,1)S(1)}, u32[]{:S(2)}, u32[]{:S(2)}) async-start(bf16[8,127,512]{2,1,0:T(8,128)(2,1)} %broadcast_select_fusion), calls=%async_computation.3 | async-start | bytes 2097152 | tf_op jit(solution)/shard_map/all_to_all | solution.py:316

commit v10 on v9

--- a/solution.py
+++ b/solution.py
@@ -215,16 +215,21 @@
     me = lax.axis_index("grp")
     near = [(i, i ^ 1) for i in range(parts)]
     far = [(i, i ^ 2) for i in range(parts)]
+    beside = lax.ppermute(block, "grp", near)
     across = lax.ppermute(block, "grp", far)
-    pair = lax.ppermute(jnp.stack([block, across]), "grp", near)
-    held = jnp.stack([block, pair[0], across, pair[1]])
+    diagonal = lax.ppermute(across, "grp", near)
+    held = jnp.stack([block, beside, across, diagonal])
     pieces = [lax.dynamic_index_in_dim(held, k ^ me, 0, keepdims=False) for k in range(parts)]
     return jnp.concatenate(pieces, axis=1)
 
 
 def finish(attn_rows, resid_rows, out_weight, norm_gain, gate_weight, up_weight, down_weight):
-    partial_value = jnp.dot(attn_rows, out_weight, preferred_element_type=jnp.float32)
-    proj_cols = grp_reduce_scatter(partial_value.astype(jnp.bfloat16))
+    proj_cols = grp_reduce_scatter_blocks(
+        lambda index, width: jnp.dot(
+            attn_rows, grp_block(out_weight, index, width), preferred_element_type=jnp.float32
+        ).astype(jnp.bfloat16),
+        out_weight.shape[1],
+    )
     state_cols = (resid_rows.astype(jnp.float32) + proj_cols).astype(jnp.bfloat16)
     state_full = grp_all_gather(state_cols)
     state32 = state_full.astype(jnp.float32)

time: 193 us -> 203 us (1.052)
  waiting for transfers between devices: 62.8 us -> 66.6 us
  matrix products: 16.4 us -> 19.8 us
  local copies, waits for them, and re-layouts: 21.5 us -> 24.2 us
    ppermute x3 -> x2, waiting for transfers between devices: 14.4 us -> 2.04 us  [the longest x1 2.04 us: grp_all_gather(): diagonal = lax.ppermute(across, 'grp', near)]
    all_to_all x2, waiting for transfers between devices: 5.35 us -> 16.9 us  [shards(): lax.all_to_all(part, 'req', split_axis=0, concat_axis=0, tiled=True)]
    ppermute x1 -> x2, waiting for transfers between devices: 0.01 us -> 5.81 us  [grp_reduce_scatter_blocks(): arrived = lax.ppermute(other.astype(jnp.bfloat16), 'grp', far)]
    all_to_all x1, waiting for transfers between devices: 4.09 us -> 0.01 us  [shards(): lax.all_to_all(send_resid, 'req', split_axis=0, concat_axis=0, tiled=True)]
    dot_general x1 -> x4, matrix products: 1.26 us -> 4.84 us  [finish(): jnp.dot(attn_rows, grp_block(out_weight, index, width), preferred_element...]
    ppermute x1 -> x2, waiting for transfers between devices: 2.54 us -> 5.54 us  [grp_reduce_scatter_blocks(): incoming = lax.ppermute(outgoing, 'grp', near)]
    convert_element_type x1 -> x0, other arithmetic: 2.14 us -> none  [grp_reduce_scatter(): arrived = lax.ppermute(other.astype(jnp.bfloat16), 'grp', far)]
  transfers between devices with their start and end apart: 10 -> 11, of which waited for: 8 -> 8; matrix products, arithmetic and copies ran while one was open for 14% -> 15% of each run, Pallas kernels for 14% -> 13%
where the time goes in v10:
time: 203 us; the launch traced here: 202 us
  waiting for transfers between devices  66.6 us (33%)
  Pallas kernels  26.6 us (13%)
  starting transfers between devices  25.9 us (13%)
  local copies, waits for them, and re-layouts  24.2 us (12%)
  other arithmetic  20.3 us (10%)
  matrix products  19.8 us (10%)
  between operations  18.4 us (9%)
    pallas_call x2, Pallas kernels, span_attention(): pl.pallas_call(functools.partial(span_kernel, kv_index), out_shape=jax.Sh...  26.6 us
    all_to_all x1, waiting for transfers between devices, shards(): lax.all_to_all(picked, 'req', split_axis=0, concat_axis=0, tiled=True)  24.7 us
    all_to_all x2, waiting for transfers between devices, shards(): lax.all_to_all(part, 'req', split_axis=0, concat_axis=0, tiled=True)  16.9 us
    ppermute x1, waiting for transfers between devices, grp_all_gather(): across = lax.ppermute(block, 'grp', far)  11.6 us
    all_to_all x2, starting transfers between devices, shards(): lax.all_to_all(part, 'req', split_axis=0, concat_axis=0, tiled=True)  10.1 us
    all_to_all x1, starting transfers between devices, shards(): lax.all_to_all(send_resid, 'req', split_axis=0, concat_axis=0, tiled=True)  7.25 us
    ppermute x2, waiting for transfers between devices, grp_reduce_scatter_blocks(): arrived = lax.ppermute(other.astype(jnp.bfloat16), 'grp', far)  5.81 us
    ppermute x2, waiting for transfers between devices, grp_reduce_scatter_blocks(): incoming = lax.ppermute(outgoing, 'grp', near)  5.54 us
  transfers between devices with their start and end apart: 11, of which 8 were waited for; matrix products, arithmetic and copies ran while one was open for 15% of the time, Pallas kernels for 13%

profile of v10, /device:TPU:0, one launch (start us, length us, event | category | flops | bytes accessed | tf_op | source)
XLA Modules:
  0.0 201.7 jit_solution(4073633901472103533)
XLA Ops:
  7.4 7.3 %all-to-all-start = ((bf16[8,127,512]{2,1,0:T(8,128)(2,1)}), bf16[8,127,512]{2,1,0:T(8,128)(2,1)S(1)}, u32[]{:S(2)}, u32[]{:S(2)}) async-start(bf16[8,127,512]{2,1,0:T(8,128)(2,1)} %fusion.15), calls=%async_computation | async-start | bytes 2097152 | tf_op jit(solution)/shard_map/all_to_all | solution.py:288
  15.7 1.9 fusion.99
  19.3 13.2 %shard_map.154 = bf16[1024,256]{1,0:T(8,128)(2,1)} custom-call(s32[1]{0:T(128)S(6)} %copy.81.start_ref, bf16[1024,512]{1,0:T(8,128)(2,1)} %q_ref.2, bf16[4608,128]{1,0:T(8,128)(2,1)} %kp_ref.3, bf16[4608,128]{1,0:T(8,128)(2,1)} %vp_ref.3, bf16[1024,128]{1,0:T(8,128)(2,1)} %kf_ref.3, bf16[1024,128]{1,0:T(8,128)(2,1)} %vf_ref.3), custom_call_target="tpu_custom_call" | custom-call | flops 17179869184 | bytes 1835008 | tf_op jit(solution)/shard_map/pallas_call | solution.py:89
  36.4 13.4 %shard_map.155 = bf16[1024,256]{1,0:T(8,128)(2,1)} custom-call(s32[1]{0:T(128)S(6)} %copy.81.start_ref, bf16[1024,512]{1,0:T(8,128)(2,1)} %q_ref.2, bf16[4608,128]{1,0:T(8,128)(2,1)} %kp_ref.3, bf16[4608,128]{1,0:T(8,128)(2,1)} %vp_ref.3, bf16[1024,128]{1,0:T(8,128)(2,1)} %kf_ref.3, bf16[1024,128]{1,0:T(8,128)(2,1)} %vf_ref.3), custom_call_target="tpu_custom_call" | custom-call | flops 17179869184 | bytes 1835008 | tf_op jit(solution)/shard_map/pallas_call | solution.py:89
  49.8 6.0 %all-to-all-start.1 = ((bf16[8,127,256]{2,1,0:T(8,128)(2,1)}), bf16[8,127,256]{2,1,0:T(8,128)(2,1)}, u32[]{:S(2)}, u32[]{:S(2)}) async-start(bf16[8,127,256]{2,1,0:T(8,128)(2,1)} %fusion.40), calls=%async_computation.1 | async-start | bytes 1048576 | tf_op jit(solution)/shard_map/all_to_all | solution.py:295
  58.7 11.2 %all-to-all-done.1 = bf16[8,127,256]{2,1,0:T(8,128)(2,1)} async-done(((bf16[8,127,256]{2,1,0:T(8,128)(2,1)}), bf16[8,127,256]{2,1,0:T(8,128)(2,1)}, u32[]{:S(2)}, u32[]{:S(2)}) %all-to-all-start.1) | async-done | bytes 520224 | tf_op jit(solution)/shard_map/all_to_all | solution.py:295
  69.9 4.1 %all-to-all-start.2 = ((bf16[8,127,256]{2,1,0:T(8,128)(2,1)}), bf16[8,127,256]{2,1,0:T(8,128)(2,1)}, u32[]{:S(2)}, u32[]{:S(2)}) async-start(bf16[8,127,256]{2,1,0:T(8,128)(2,1)} %fusion.38), calls=%async_computation.2 | async-start | bytes 1048576 | tf_op jit(solution)/shard_map/all_to_all | solution.py:295
  74.1 4.2 %compare_select_fusion.2 = s32[512,1]{0,1:T(1,128)S(1)} fusion(s32[]{:T(128)} %bitcast.16, s32[]{:T(128)} %bitcast.17, s32[]{:T(128)} %bitcast.18, s32[]{:T(128)} %bitcast.19, s32[]{:T(128)} %bitcast.20, s32[]{:T(128)} %bitcast.22, s32[]{:T(128)} %bitcast.21, s32[512,1]{0,1:T(1,128)S(1)} %bitcast.144), kind=kLoop, calls=%fused_computation.148 | loop fusion | flops 7680 | bytes 4124 | tf_op jit(solution)/shard_map/gather | solution.py:303
  80.2 2.0 gather_fusion.1
  82.1 5.7 %all-to-all-done.2 = bf16[8,127,256]{2,1,0:T(8,128)(2,1)} async-done(((bf16[8,127,256]{2,1,0:T(8,128)(2,1)}), bf16[8,127,256]{2,1,0:T(8,128)(2,1)}, u32[]{:S(2)}, u32[]{:S(2)}) %all-to-all-start.2) | async-done | bytes 520224 | tf_op jit(solution)/shard_map/all_to_all | solution.py:295
  89.1 2.0 gather_fusion.2
  93.1 3.0 %collective-permute-done = bf16[2,512,512]{1,2,0:T(8,128)(2,1)} collective-permute-done((bf16[2,512,512]{1,2,0:T(8,128)(2,1)}, bf16[2,512,512]{1,2,0:T(8,128)(2,1)}, u32[]{:S(2)}, u32[]{:S(2)}) %collective-permute-start) | collective-permute-done | bytes 1048608 | tf_op jit(solution)/shard_map/ppermute | solution.py:204
  96.1 2.3 %fusion.20 = bf16[512,512]{0,1:T(8,128)(2,1)} fusion(bf16[2,512,512]{1,2,0:T(8,128)(2,1)} %collective-permute-done, bf16[512,512]{1,0:T(8,128)(2,1)S(1)} %constant_dynamic-update-slice_fusion, bf16[512,2048]{1,0:T(8,128)(2,1)S(1)} %copy-done, s32[]{:T(128)S(6)} %select_n.208), kind=kOutput, calls=%fused_computation.52 | convolution fusion | flops 269746176 | bytes 2097156 | tf_op jit(solution)/shard_map/dot_general | solution.py:228
  98.5 1.5 collective-permute-start.1
  100.0 1.5 reshape.400
  101.5 2.6 %gather_fusion = bf16[512,512]{1,0:T(8,128)(2,1)} fusion(bf16[1016,512]{1,0:T(8,128)(2,1)S(1)} %reshape.400, s32[1024]{0:T(1024)S(1)} %pad_clamp_fusion), kind=kCustom, calls=%fused_computation | custom fusion | bytes 1050624 | tf_op jit(solution)/shard_map/gather | solution.py:308
  105.4 1.5 fusion.4
  106.9 5.8 %collective-permute-done.1 = bf16[512,512]{0,1:T(8,128)(2,1)} collective-permute-done((bf16[512,512]{0,1:T(8,128)(2,1)}, bf16[512,512]{0,1:T(8,128)(2,1)}, u32[]{:S(2)}, u32[]{:S(2)}) %collective-permute-start.1) | collective-permute-done | bytes 524320 | tf_op jit(solution)/shard_map/ppermute | solution.py:206
  112.7 1.5 fusion.23
  114.3 1.6 collective-permute-start.3
  115.9 11.6 %collective-permute-done.3 = bf16[512,512]{0,1:T(8,128)(2,1)S(1)} collective-permute-done((bf16[512,512]{0,1:T(8,128)(2,1)S(1)}, bf16[512,512]{0,1:T(8,128)(2,1)S(1)}, u32[]{:S(2)}, u32[]{:S(2)}) %collective-permute-start.3) | collective-permute-done | bytes 524320 | tf_op jit(solution)/shard_map/ppermute | solution.py:219
  127.5 2.0 %collective-permute-done.4 = bf16[512,512]{0,1:T(8,128)(2,1)} collective-permute-done((bf16[512,512]{0,1:T(8,128)(2,1)S(1)}, bf16[512,512]{0,1:T(8,128)(2,1)}, u32[]{:S(2)}, u32[]{:S(2)}) %collective-permute-start.4) | collective-permute-done | bytes 524320 | tf_op jit(solution)/shard_map/ppermute | solution.py:220
  133.2 2.6 %fusion.35 = f32[512,1024]{1,0:T(8,128)S(1)} fusion(bf16[2048,1024]{1,0:T(8,128)(2,1)S(1)} %copy-done.8, f32[2048]{0:T(1024)S(1)} %copy-done.12, f32[512]{0:T(512)S(1)} %add_rsqrt_fusion, bf16[512,512]{0,1:T(8,128)(2,1)S(1)} %get-tuple-element.19, bf16[512,512]{0,1:T(8,128)(2,1)S(1)} %get-tuple-element.20, bf16[512,512]{0,1:T(8,128)(2,1)S(1)} %get-tuple-element.21, ...), kind=kOutput, calls=%fused_computation.72 | convolution fusion | flops 2159017984 | bytes 8398848 | tf_op jit(solution)/shard_map/dot_general | solution.py:239
  135.8 2.8 %multiply_convert_fusion = bf16[512,1024]{1,0:T(8,128)(2,1)S(1)} fusion(f32[512,1024]{1,0:T(8,128)S(1)} %fusion.35, bf16[2048,1024]{1,0:T(8,128)(2,1)S(1)} %copy-done.9, f32[2048]{0:T(1024)S(1)} %copy-done.12, f32[512]{0:T(512)S(1)} %add_rsqrt_fusion, bf16[512,512]{0,1:T(8,128)(2,1)S(1)} %get-tuple-element.19, bf16[512,512]{0,1:T(8,128)(2,1)S(1)} %get-tuple-element.20, ...), kind=kOutput, calls=%fused_computation.16 | convolution fusion | flops 2162163712 | bytes 9447424 | tf_op jit(solution)/shard_map/dot_general | solution.py:240
  140.4 2.5 %collective-permute-done.5 = bf16[2,512,512]{1,2,0:T(8,128)(2,1)S(1)} collective-permute-done((bf16[2,512,512]{1,2,0:T(8,128)(2,1)S(1)}, bf16[2,512,512]{1,2,0:T(8,128)(2,1)S(1)}, u32[]{:S(2)}, u32[]{:S(2)}) %collective-permute-start.5) | collective-permute-done | bytes 1048608 | tf_op jit(solution)/shard_map/ppermute | solution.py:204
  144.0 1.6 fusion.16
  145.5 1.5 collective-permute-start.6
  162.4 2.4 %fusion.7 = f32[512,512]{0,1:T(8,128)S(1)} fusion(bf16[512,1024]{1,0:T(8,128)(2,1)} %copy-done.13, bf16[1024,2048]{1,0:T(8,128)(2,1)} %param.35, s32[]{:T(128)S(6)} %select_n.205), kind=kOutput, calls=%fused_computation.28 | convolution fusion | flops 537395200 | bytes 3145732 | tf_op jit(solution)/shard_map/dot_general | solution.py:243
  167.4 3.7 %all-to-all-start.3 = ((bf16[8,127,512]{1,2,0:T(8,128)(2,1)}), bf16[8,127,512]{1,2,0:T(8,128)(2,1)S(1)}, u32[]{:S(2)}, u32[]{:S(2)}) async-start(bf16[8,127,512]{1,2,0:T(8,128)(2,1)} %broadcast_select_fusion), calls=%async_computation.3 | async-start | bytes 2097152 | tf_op jit(solution)/shard_map/all_to_all | solution.py:321
  172.3 24.7 %all-to-all-done.3 = bf16[8,127,512]{1,2,0:T(8,128)(2,1)S(1)} async-done(((bf16[8,127,512]{1,2,0:T(8,128)(2,1)}), bf16[8,127,512]{1,2,0:T(8,128)(2,1)S(1)}, u32[]{:S(2)}, u32[]{:S(2)}) %all-to-all-start.3) | async-done | bytes 1040416 | tf_op jit(solution)/shard_map/all_to_all | solution.py:321
  197.0 1.5 fusion.13
  198.5 1.9 copy.62
  (104 shorter events, 32.2 us)
Async XLA Ops:
  0.0 91.0 %copy-start = (bf16[512,2048]{1,0:T(8,128)(2,1)S(1)}, bf16[512,2048]{1,0:T(8,128)(2,1)}, u32[]{:S(2)}) copy-start(bf16[512,2048]{1,0:T(8,128)(2,1)} %param.31) | copy-start | bytes 6291460
  6.0 9.4 %slice-start = ((bf16[1024,512]{1,0:T(8,128)(2,1)}), bf16[8,512]{1,0:T(8,128)(2,1)S(1)}, s32[]{:S(2)}) async-start(bf16[1024,512]{1,0:T(8,128)(2,1)} %q_ref.2), calls=%async_computation.4 | async-start | bytes 16384 | tf_op jit(solution)/shard_map/slice | solution.py:107
  6.0 9.5 %copy-start.5 = (s32[8]{0:T(128)S(1)}, s32[8]{0:T(128)}, u32[]{:S(2)}) copy-start(s32[8]{0:T(128)} %param.26) | copy-start | bytes 100
  6.0 9.5 %copy-start.6 = (s32[8]{0:T(128)S(1)}, s32[8]{0:T(128)}, u32[]{:S(2)}) copy-start(s32[8]{0:T(128)} %param.27) | copy-start | bytes 100
  6.0 9.5 %copy-start.7 = (s32[8]{0:T(128)S(1)}, s32[8]{0:T(128)}, u32[]{:S(2)}) copy-start(s32[8]{0:T(128)} %param.28) | copy-start | bytes 100
  7.4 42.4 %all-to-all-start = ((bf16[8,127,512]{2,1,0:T(8,128)(2,1)}), bf16[8,127,512]{2,1,0:T(8,128)(2,1)S(1)}, u32[]{:S(2)}, u32[]{:S(2)}) async-start(bf16[8,127,512]{2,1,0:T(8,128)(2,1)} %fusion.15), calls=%async_computation | async-start | bytes 2097152 | tf_op jit(solution)/shard_map/all_to_all | solution.py:288
  15.4 3.5 %copy-start.11 = (bf16[4608,128]{1,0:T(8,128)(2,1)S(1)}, bf16[4608,128]{1,0:T(8,128)(2,1)}, u32[]{:S(2)}) copy-start(bf16[4608,128]{1,0:T(8,128)(2,1)} %vp_ref.3) | copy-start | bytes 3538948
  49.8 8.9 %copy-start.2 = (bf16[8,127,512]{2,1,0:T(8,128)(2,1)}, bf16[8,127,512]{2,1,0:T(8,128)(2,1)S(1)}, u32[]{:S(2)}) copy-start(bf16[8,127,512]{2,1,0:T(8,128)(2,1)S(1)} %all-to-all-done) | copy-start | bytes 3121156
  49.8 20.1 %all-to-all-start.1 = ((bf16[8,127,256]{2,1,0:T(8,128)(2,1)}), bf16[8,127,256]{2,1,0:T(8,128)(2,1)}, u32[]{:S(2)}, u32[]{:S(2)}) async-start(bf16[8,127,256]{2,1,0:T(8,128)(2,1)} %fusion.40), calls=%async_computation.1 | async-start | bytes 1048576 | tf_op jit(solution)/shard_map/all_to_all | solution.py:295
  69.9 18.0 %all-to-all-start.2 = ((bf16[8,127,256]{2,1,0:T(8,128)(2,1)}), bf16[8,127,256]{2,1,0:T(8,128)(2,1)}, u32[]{:S(2)}, u32[]{:S(2)}) async-start(bf16[8,127,256]{2,1,0:T(8,128)(2,1)} %fusion.38), calls=%async_computation.2 | async-start | bytes 1048576 | tf_op jit(solution)/shard_map/all_to_all | solution.py:295
  91.1 5.1 %copy-start.1 = (bf16[512,512]{1,0:T(8,128)(2,1)}, bf16[512,512]{1,0:T(8,128)(2,1)S(1)}, u32[]{:S(2)}) copy-start(bf16[512,512]{1,0:T(8,128)(2,1)S(1)} %constant_dynamic-update-slice_fusion) | copy-start | bytes 1572868
  93.1 3.0 %collective-permute-start = (bf16[2,512,512]{1,2,0:T(8,128)(2,1)}, bf16[2,512,512]{1,2,0:T(8,128)(2,1)}, u32[]{:S(2)}, u32[]{:S(2)}) collective-permute-start(bf16[2,512,512]{1,2,0:T(8,128)(2,1)} %pad_maximum_fusion.2), channel_id=1, source_target_pairs={{0,1},{1,0},{2,3},{3,2},{4,5},{5,4},{6,7},{7,6},{8,9},{9,8},{10,11... | collective-permute-start | bytes 3145736 | tf_op jit(solution)/shard_map/ppermute | solution.py:204
  98.5 14.3 %collective-permute-start.1 = (bf16[512,512]{0,1:T(8,128)(2,1)}, bf16[512,512]{0,1:T(8,128)(2,1)}, u32[]{:S(2)}, u32[]{:S(2)}) collective-permute-start(bf16[512,512]{0,1:T(8,128)(2,1)} %fusion.20), channel_id=1, source_target_pairs={{0,2},{1,3},{2,0},{3,1},{4,6},{5,7},{6,4},{7,5},{8,10},{9,11},{10,... | collective-permute-start | bytes 1572872 | tf_op jit(solution)/shard_map/ppermute | solution.py:206
  114.3 13.2 %collective-permute-start.3 = (bf16[512,512]{0,1:T(8,128)(2,1)S(1)}, bf16[512,512]{0,1:T(8,128)(2,1)S(1)}, u32[]{:S(2)}, u32[]{:S(2)}) collective-permute-start(bf16[512,512]{0,1:T(8,128)(2,1)S(1)} %fusion.23), channel_id=1, source_target_pairs={{0,2},{1,3},{2,0},{3,1},{4,6},{5,7},{6,4},{7,5},{8,10},{9,11},{10,... | collective-permute-start | bytes 1572872 | tf_op jit(solution)/shard_map/ppermute | solution.py:219
  115.9 11.6 %collective-permute-start.2 = (bf16[512,512]{0,1:T(8,128)(2,1)S(1)}, bf16[512,512]{0,1:T(8,128)(2,1)}, u32[]{:S(2)}, u32[]{:S(2)}) collective-permute-start(bf16[512,512]{0,1:T(8,128)(2,1)S(1)} %fusion.23), channel_id=1, source_target_pairs={{0,1},{1,0},{2,3},{3,2},{4,5},{5,4},{6,7},{7,6},{8,9},{9,8},{10,11... | collective-permute-start | bytes 1572872 | tf_op jit(solution)/shard_map/ppermute | solution.py:218
  127.5 2.0 %collective-permute-start.4 = (bf16[512,512]{0,1:T(8,128)(2,1)S(1)}, bf16[512,512]{0,1:T(8,128)(2,1)}, u32[]{:S(2)}, u32[]{:S(2)}) collective-permute-start(bf16[512,512]{0,1:T(8,128)(2,1)S(1)} %collective-permute-done.3), channel_id=1, source_target_pairs={{0,1},{1,0},{2,3},{3,2},{4,5},{5,4},{6,7},{7,6},{8,9},{9,8},{10,11... | collective-permute-start | bytes 1572872 | tf_op jit(solution)/shard_map/ppermute | solution.py:220
  131.0 2.2 %copy-start.8 = (bf16[2048,1024]{1,0:T(8,128)(2,1)S(1)}, bf16[2048,1024]{1,0:T(8,128)(2,1)}, u32[]{:S(2)}) copy-start(bf16[2048,1024]{1,0:T(8,128)(2,1)} %param.33) | copy-start | bytes 12582916
  131.2 2.0 copy-start.12
  133.2 2.6 %copy-start.9 = (bf16[2048,1024]{1,0:T(8,128)(2,1)S(1)}, bf16[2048,1024]{1,0:T(8,128)(2,1)}, u32[]{:S(2)}) copy-start(bf16[2048,1024]{1,0:T(8,128)(2,1)} %param.34) | copy-start | bytes 12582916
  135.8 2.8 %copy-start.10 = (bf16[1024,2048]{1,0:T(8,128)(2,1)S(1)}, bf16[1024,2048]{1,0:T(8,128)(2,1)}, u32[]{:S(2)}) copy-start(bf16[1024,2048]{1,0:T(8,128)(2,1)} %param.35) | copy-start | bytes 12582916
  138.6 4.4 %copy-start.13 = (bf16[512,1024]{1,0:T(8,128)(2,1)}, bf16[512,1024]{1,0:T(8,128)(2,1)S(1)}, u32[]{:S(2)}) copy-start(bf16[512,1024]{1,0:T(8,128)(2,1)S(1)} %multiply_convert_fusion) | copy-start | bytes 3145732
  140.3 2.7 %collective-permute-start.5 = (bf16[2,512,512]{1,2,0:T(8,128)(2,1)S(1)}, bf16[2,512,512]{1,2,0:T(8,128)(2,1)S(1)}, u32[]{:S(2)}, u32[]{:S(2)}) collective-permute-start(bf16[2,512,512]{1,2,0:T(8,128)(2,1)S(1)} %pad_maximum_fusion.3), channel_id=1, source_target_pairs={{0,1},{1,0},{2,3},{3,2},{4,5},{5,4},{6,7},{7,6},{8,9},{9,8},{10,11... | collective-permute-start | bytes 3145736 | tf_op jit(solution)/shard_map/ppermute | solution.py:204
  143.0 1.0 copy-start.3
  145.5 19.2 %collective-permute-start.6 = (bf16[512,512]{0,1:T(8,128)(2,1)}, bf16[512,512]{0,1:T(8,128)(2,1)S(1)}, u32[]{:S(2)}, u32[]{:S(2)}) collective-permute-start(bf16[512,512]{0,1:T(8,128)(2,1)} %fusion.16), channel_id=1, source_target_pairs={{0,2},{1,3},{2,0},{3,1},{4,6},{5,7},{6,4},{7,5},{8,10},{9,11},{10,... | collective-permute-start | bytes 1572872 | tf_op jit(solution)/shard_map/ppermute | solution.py:206
  162.3 2.5 %copy-start.4 = (bf16[2,512,512]{1,2,0:T(8,128)(2,1)S(1)}, bf16[2,512,512]{1,2,0:T(8,128)(2,1)}, u32[]{:S(2)}) copy-start(bf16[2,512,512]{1,2,0:T(8,128)(2,1)} %copy-done.3) | copy-start | bytes 3145732
  167.4 29.6 %all-to-all-start.3 = ((bf16[8,127,512]{1,2,0:T(8,128)(2,1)}), bf16[8,127,512]{1,2,0:T(8,128)(2,1)S(1)}, u32[]{:S(2)}, u32[]{:S(2)}) async-start(bf16[8,127,512]{1,2,0:T(8,128)(2,1)} %broadcast_select_fusion), calls=%async_computation.3 | async-start | bytes 2097152 | tf_op jit(solution)/shard_map/all_to_all | solution.py:321

commit v11 on v9

--- a/solution.py
+++ b/solution.py
@@ -215,9 +215,10 @@
     me = lax.axis_index("grp")
     near = [(i, i ^ 1) for i in range(parts)]
     far = [(i, i ^ 2) for i in range(parts)]
+    beside = lax.ppermute(block, "grp", near)
     across = lax.ppermute(block, "grp", far)
-    pair = lax.ppermute(jnp.stack([block, across]), "grp", near)
-    held = jnp.stack([block, pair[0], across, pair[1]])
+    diagonal = lax.ppermute(across, "grp", near)
+    held = jnp.stack([block, beside, across, diagonal])
     pieces = [lax.dynamic_index_in_dim(held, k ^ me, 0, keepdims=False) for k in range(parts)]
     return jnp.concatenate(pieces, axis=1)
 

time: 193 us -> 191 us (0.990)
  transfers between devices with their start and end apart: 10 -> 11, of which waited for: 8 -> 8; matrix products, arithmetic and copies ran while one was open for 14% -> 14% of each run, Pallas kernels for 14% -> 14%
where the time goes in v11:
time: 191 us; the launch traced here: 190 us
  waiting for transfers between devices  61.8 us (32%)
  Pallas kernels  26.6 us (14%)
  starting transfers between devices  25.7 us (13%)
  other arithmetic  20.8 us (11%)
  local copies, waits for them, and re-layouts  20.2 us (11%)
  between operations  18.5 us (10%)
  matrix products  16.4 us (9%)
    pallas_call x2, Pallas kernels, span_attention(): pl.pallas_call(functools.partial(span_kernel, kv_index), out_shape=jax.Sh...  26.6 us
    all_to_all x1, waiting for transfers between devices, shards(): lax.all_to_all(picked, 'req', split_axis=0, concat_axis=0, tiled=True)  24.8 us
    ppermute x1, waiting for transfers between devices, grp_all_gather(): across = lax.ppermute(block, 'grp', far)  11.6 us
    all_to_all x2, starting transfers between devices, shards(): lax.all_to_all(part, 'req', split_axis=0, concat_axis=0, tiled=True)  10 us
    ppermute x1, waiting for transfers between devices, grp_reduce_scatter(): arrived = lax.ppermute(other.astype(jnp.bfloat16), 'grp', far)  8.59 us
    all_to_all x1, starting transfers between devices, shards(): lax.all_to_all(send_resid, 'req', split_axis=0, concat_axis=0, tiled=True)  7.25 us
    all_to_all x2, waiting for transfers between devices, shards(): lax.all_to_all(part, 'req', split_axis=0, concat_axis=0, tiled=True)  5.35 us
    dot_general x4, matrix products, finish(): jnp.dot(inner, grp_block(down_weight, index, width), preferred_element_ty...  5.32 us
  transfers between devices with their start and end apart: 11, of which 8 were waited for; matrix products, arithmetic and copies ran while one was open for 14% of the time, Pallas kernels for 14%

profile of v11, /device:TPU:0, one launch (start us, length us, event | category | flops | bytes accessed | tf_op | source)
XLA Modules:
  0.0 190.1 jit_solution(3490551081578639091)
XLA Ops:
  6.0 1.4 fusion.11
  7.4 7.3 %all-to-all-start = ((bf16[8,127,512]{2,1,0:T(8,128)(2,1)}), bf16[8,127,512]{2,1,0:T(8,128)(2,1)S(1)}, u32[]{:S(2)}, u32[]{:S(2)}) async-start(bf16[8,127,512]{2,1,0:T(8,128)(2,1)} %fusion.11), calls=%async_computation | async-start | bytes 2097152 | tf_op jit(solution)/shard_map/all_to_all | solution.py:284
  15.7 1.9 %fusion.89 = (f32[8,8]{1,0:T(8,128)S(1)}, f32[8,8,4096]{2,1,0:T(8,128)S(1)}) fusion(bf16[4608,128]{1,0:T(8,128)(2,1)} %kp_ref.3, bf16[8,8,64]{2,1,0:T(8,128)(2,1)S(1)} %get-tuple-element.25, bf16[8,8,64]{2,1,0:T(8,128)(2,1)S(1)} %get-tuple-element.24, pred[8,4096]{1,0:T(8,128)(4,1)S(1)} %fusion.60), kind=kOutput, calls=%fused_computation.192 | convolution fusion | flops 67928000 | bytes 2146560 | tf_op jit(solution)/shard_map/rhc,tc->rht/dot_general | solution.py:113
  20.4 13.1 %shard_map.154 = bf16[1024,256]{1,0:T(8,128)(2,1)} custom-call(s32[1]{0:T(128)S(6)} %copy.51.start_ref, bf16[1024,512]{1,0:T(8,128)(2,1)} %q_ref.2, bf16[4608,128]{1,0:T(8,128)(2,1)} %kp_ref.3, bf16[4608,128]{1,0:T(8,128)(2,1)} %vp_ref.3, bf16[1024,128]{1,0:T(8,128)(2,1)} %kf_ref.3, bf16[1024,128]{1,0:T(8,128)(2,1)} %vf_ref.3), custom_call_target="tpu_custom_call" | custom-call | flops 17179869184 | bytes 1835008 | tf_op jit(solution)/shard_map/pallas_call | solution.py:89
  36.3 4.1 %all-to-all-done = bf16[8,127,512]{2,1,0:T(8,128)(2,1)S(1)} async-done(((bf16[8,127,512]{2,1,0:T(8,128)(2,1)}), bf16[8,127,512]{2,1,0:T(8,128)(2,1)S(1)}, u32[]{:S(2)}, u32[]{:S(2)}) %all-to-all-start) | async-done | bytes 1040416 | tf_op jit(solution)/shard_map/all_to_all | solution.py:284
  40.4 4.3 %all-to-all-start.1 = ((bf16[8,127,256]{2,1,0:T(8,128)(2,1)}), bf16[8,127,256]{2,1,0:T(8,128)(2,1)}, u32[]{:S(2)}, u32[]{:S(2)}) async-start(bf16[8,127,256]{2,1,0:T(8,128)(2,1)} %fusion.36), calls=%async_computation.1 | async-start | bytes 1048576 | tf_op jit(solution)/shard_map/all_to_all | solution.py:291
  44.8 13.5 %shard_map.155 = bf16[1024,256]{1,0:T(8,128)(2,1)} custom-call(s32[1]{0:T(128)S(6)} %copy.51.start_ref, bf16[1024,512]{1,0:T(8,128)(2,1)} %q_ref.2, bf16[4608,128]{1,0:T(8,128)(2,1)} %kp_ref.3, bf16[4608,128]{1,0:T(8,128)(2,1)} %vp_ref.3, bf16[1024,128]{1,0:T(8,128)(2,1)} %kf_ref.3, bf16[1024,128]{1,0:T(8,128)(2,1)} %vf_ref.3), custom_call_target="tpu_custom_call" | custom-call | flops 17179869184 | bytes 1835008 | tf_op jit(solution)/shard_map/pallas_call | solution.py:89
  61.1 5.7 %all-to-all-start.2 = ((bf16[8,127,256]{2,1,0:T(8,128)(2,1)}), bf16[8,127,256]{2,1,0:T(8,128)(2,1)S(1)}, u32[]{:S(2)}, u32[]{:S(2)}) async-start(bf16[8,127,256]{2,1,0:T(8,128)(2,1)} %fusion.34), calls=%async_computation.2 | async-start | bytes 1048576 | tf_op jit(solution)/shard_map/all_to_all | solution.py:291
  66.9 4.4 %compare_select_fusion.2 = s32[512,1]{0,1:T(1,128)S(1)} fusion(s32[]{:T(128)} %bitcast.16, s32[]{:T(128)} %bitcast.17, s32[]{:T(128)} %bitcast.18, s32[]{:T(128)} %bitcast.19, s32[]{:T(128)} %bitcast.20, s32[]{:T(128)} %bitcast.22, s32[]{:T(128)} %bitcast.21, s32[512,1]{0,1:T(1,128)S(1)} %bitcast.143), kind=kLoop, calls=%fused_computation.141 | loop fusion | flops 7680 | bytes 4124 | tf_op jit(solution)/shard_map/gather | solution.py:299
  73.2 2.0 %gather_fusion.1 = bf16[512,256]{1,0:T(8,128)(2,1)S(1)} fusion(bf16[1016,256]{1,0:T(8,128)(2,1)S(1)} %reshape.401, s32[1024]{0:T(1024)S(1)} %pad_clamp_fusion), kind=kCustom, calls=%fused_computation.1 | custom fusion | bytes 526336 | tf_op jit(solution)/shard_map/gather | solution.py:302
  75.2 5.3 %all-to-all-done.2 = bf16[8,127,256]{2,1,0:T(8,128)(2,1)S(1)} async-done(((bf16[8,127,256]{2,1,0:T(8,128)(2,1)}), bf16[8,127,256]{2,1,0:T(8,128)(2,1)S(1)}, u32[]{:S(2)}, u32[]{:S(2)}) %all-to-all-start.2) | async-done | bytes 520224 | tf_op jit(solution)/shard_map/all_to_all | solution.py:291
  80.7 2.0 %gather_fusion.2 = bf16[512,256]{1,0:T(8,128)(2,1)S(1)} fusion(bf16[1016,256]{1,0:T(8,128)(2,1)S(1)} %reshape.402, s32[1024]{0:T(1024)S(1)} %pad_clamp_fusion), kind=kCustom, calls=%fused_computation.2 | custom fusion | bytes 526336 | tf_op jit(solution)/shard_map/gather | solution.py:302
  85.3 2.8 %collective-permute-done = bf16[2,512,512]{2,1,0:T(8,128)(2,1)} collective-permute-done((bf16[2,512,512]{2,1,0:T(8,128)(2,1)S(1)}, bf16[2,512,512]{2,1,0:T(8,128)(2,1)}, u32[]{:S(2)}, u32[]{:S(2)}) %collective-permute-start) | collective-permute-done | bytes 1048608 | tf_op jit(solution)/shard_map/ppermute | solution.py:185
  88.0 2.1 %fusion.16 = bf16[512,512]{1,0:T(8,128)(2,1)} fusion(bf16[2,512,512]{2,1,0:T(8,128)(2,1)} %collective-permute-done, bf16[512,2048]{1,0:T(8,128)(2,1)} %copy-done.2, s32[]{:T(128)S(6)} %select_n.208), kind=kLoop, calls=%fused_computation.45 | loop fusion | flops 1048576 | bytes 1572868 | tf_op jit(solution)/shard_map/convert_element_type | solution.py:190
  90.2 1.5 collective-permute-start.1
  91.7 1.5 reshape.400
  93.2 2.6 %gather_fusion = bf16[512,512]{1,0:T(8,128)(2,1)} fusion(bf16[1016,512]{1,0:T(8,128)(2,1)S(1)} %reshape.400, s32[1024]{0:T(1024)S(1)} %pad_clamp_fusion), kind=kCustom, calls=%fused_computation | custom fusion | bytes 1050624 | tf_op jit(solution)/shard_map/gather | solution.py:304
  95.9 8.6 %collective-permute-done.1 = bf16[512,512]{1,0:T(8,128)(2,1)} collective-permute-done((bf16[512,512]{1,0:T(8,128)(2,1)}, bf16[512,512]{1,0:T(8,128)(2,1)}, u32[]{:S(2)}, u32[]{:S(2)}) %collective-permute-start.1) | collective-permute-done | bytes 524320 | tf_op jit(solution)/shard_map/ppermute | solution.py:190
  104.5 1.8 fusion.19
  106.3 1.6 collective-permute-start.3
  107.8 11.6 %collective-permute-done.3 = bf16[512,512]{1,0:T(8,128)(2,1)S(1)} collective-permute-done((bf16[512,512]{1,0:T(8,128)(2,1)S(1)}, bf16[512,512]{1,0:T(8,128)(2,1)S(1)}, u32[]{:S(2)}, u32[]{:S(2)}) %collective-permute-start.3) | collective-permute-done | bytes 524320 | tf_op jit(solution)/shard_map/ppermute | solution.py:219
  119.5 2.0 %collective-permute-done.4 = bf16[512,512]{1,0:T(8,128)(2,1)} collective-permute-done((bf16[512,512]{1,0:T(8,128)(2,1)S(1)}, bf16[512,512]{1,0:T(8,128)(2,1)}, u32[]{:S(2)}, u32[]{:S(2)}) %collective-permute-start.4) | collective-permute-done | bytes 524320 | tf_op jit(solution)/shard_map/ppermute | solution.py:220
  121.5 1.5 pad_maximum_fusion
  123.7 1.5 copy-done.8
  125.2 2.4 %fusion.31 = f32[512,1024]{1,0:T(8,128)S(1)} fusion(bf16[2048,1024]{1,0:T(8,128)(2,1)S(1)} %copy-done.8, f32[2048]{0:T(1024)S(1)} %copy-done.12, f32[512]{0:T(512)S(1)} %add_rsqrt_fusion, bf16[512,512]{1,0:T(8,128)(2,1)S(1)} %get-tuple-element.19, bf16[512,512]{1,0:T(8,128)(2,1)S(1)} %get-tuple-element.20, bf16[512,512]{1,0:T(8,128)(2,1)S(1)} %get-tuple-element.21, ...), kind=kOutput, calls=%fused_computation.66 | convolution fusion | flops 2159017984 | bytes 8398848 | tf_op jit(solution)/shard_map/dot_general | solution.py:235
  127.6 3.3 %multiply_convert_fusion = bf16[512,1024]{1,0:T(8,128)(2,1)S(1)} fusion(f32[512,1024]{1,0:T(8,128)S(1)} %fusion.31, bf16[2048,1024]{1,0:T(8,128)(2,1)S(1)} %copy-done.9, f32[2048]{0:T(1024)S(1)} %copy-done.12, f32[512]{0:T(512)S(1)} %add_rsqrt_fusion, bf16[512,512]{1,0:T(8,128)(2,1)S(1)} %get-tuple-element.19, bf16[512,512]{1,0:T(8,128)(2,1)S(1)} %get-tuple-element.20, ...), kind=kOutput, calls=%fused_computation.17 | convolution fusion | flops 2162163712 | bytes 9447424 | tf_op jit(solution)/shard_map/dot_general | solution.py:236
  132.6 2.5 %collective-permute-done.5 = bf16[2,512,512]{2,1,0:T(8,128)(2,1)S(1)} collective-permute-done((bf16[2,512,512]{2,1,0:T(8,128)(2,1)S(1)}, bf16[2,512,512]{2,1,0:T(8,128)(2,1)S(1)}, u32[]{:S(2)}, u32[]{:S(2)}) %collective-permute-start.5) | collective-permute-done | bytes 1048608 | tf_op jit(solution)/shard_map/ppermute | solution.py:204
  135.2 1.5 fusion.12
  136.7 1.5 collective-permute-start.6
  153.7 2.3 %fusion.5 = f32[512,512]{1,0:T(8,128)S(1)} fusion(bf16[512,1024]{1,0:T(8,128)(2,1)} %copy-done.13, bf16[1024,2048]{1,0:T(8,128)(2,1)} %param.35, s32[]{:T(128)S(6)} %select_n.205), kind=kOutput, calls=%fused_computation.23 | convolution fusion | flops 537395200 | bytes 3145732 | tf_op jit(solution)/shard_map/dot_general | solution.py:239
  158.3 3.7 %all-to-all-start.3 = ((bf16[8,127,512]{2,1,0:T(8,128)(2,1)}), bf16[8,127,512]{2,1,0:T(8,128)(2,1)S(1)}, u32[]{:S(2)}, u32[]{:S(2)}) async-start(bf16[8,127,512]{2,1,0:T(8,128)(2,1)} %broadcast_select_fusion), calls=%async_computation.3 | async-start | bytes 2097152 | tf_op jit(solution)/shard_map/all_to_all | solution.py:317
  163.0 24.8 %all-to-all-done.3 = bf16[8,127,512]{2,1,0:T(8,128)(2,1)S(1)} async-done(((bf16[8,127,512]{2,1,0:T(8,128)(2,1)}), bf16[8,127,512]{2,1,0:T(8,128)(2,1)S(1)}, u32[]{:S(2)}, u32[]{:S(2)}) %all-to-all-start.3) | async-done | bytes 1040416 | tf_op jit(solution)/shard_map/all_to_all | solution.py:317
  (100 shorter events, 25.4 us)
Async XLA Ops:
  0.0 82.6 %copy-start = (bf16[512,2048]{1,0:T(8,128)(2,1)S(1)}, bf16[512,2048]{1,0:T(8,128)(2,1)}, u32[]{:S(2)}) copy-start(bf16[512,2048]{1,0:T(8,128)(2,1)} %param.31) | copy-start | bytes 6291460
  6.0 9.4 %slice-start = ((bf16[1024,512]{1,0:T(8,128)(2,1)}), bf16[8,512]{1,0:T(8,128)(2,1)S(1)}, s32[]{:S(2)}) async-start(bf16[1024,512]{1,0:T(8,128)(2,1)} %q_ref.2), calls=%async_computation.4 | async-start | bytes 16384 | tf_op jit(solution)/shard_map/slice | solution.py:107
  6.0 9.5 %copy-start.5 = (s32[8]{0:T(128)S(1)}, s32[8]{0:T(128)}, u32[]{:S(2)}) copy-start(s32[8]{0:T(128)} %param.26) | copy-start | bytes 100
  6.0 9.5 %copy-start.6 = (s32[8]{0:T(128)S(1)}, s32[8]{0:T(128)}, u32[]{:S(2)}) copy-start(s32[8]{0:T(128)} %param.27) | copy-start | bytes 100
  6.0 9.5 %copy-start.7 = (s32[8]{0:T(128)S(1)}, s32[8]{0:T(128)}, u32[]{:S(2)}) copy-start(s32[8]{0:T(128)} %param.28) | copy-start | bytes 100
  7.4 33.0 %all-to-all-start = ((bf16[8,127,512]{2,1,0:T(8,128)(2,1)}), bf16[8,127,512]{2,1,0:T(8,128)(2,1)S(1)}, u32[]{:S(2)}, u32[]{:S(2)}) async-start(bf16[8,127,512]{2,1,0:T(8,128)(2,1)} %fusion.11), calls=%async_computation | async-start | bytes 2097152 | tf_op jit(solution)/shard_map/all_to_all | solution.py:284
  15.4 3.5 %copy-start.11 = (bf16[4608,128]{1,0:T(8,128)(2,1)S(1)}, bf16[4608,128]{1,0:T(8,128)(2,1)}, u32[]{:S(2)}) copy-start(bf16[4608,128]{1,0:T(8,128)(2,1)} %vp_ref.3) | copy-start | bytes 3538948
  40.4 17.8 %copy-start.1 = (bf16[8,127,512]{2,1,0:T(8,128)(2,1)}, bf16[8,127,512]{2,1,0:T(8,128)(2,1)S(1)}, u32[]{:S(2)}) copy-start(bf16[8,127,512]{2,1,0:T(8,128)(2,1)S(1)} %all-to-all-done) | copy-start | bytes 3121156
  40.4 20.7 %all-to-all-start.1 = ((bf16[8,127,256]{2,1,0:T(8,128)(2,1)}), bf16[8,127,256]{2,1,0:T(8,128)(2,1)}, u32[]{:S(2)}, u32[]{:S(2)}) async-start(bf16[8,127,256]{2,1,0:T(8,128)(2,1)} %fusion.36), calls=%async_computation.1 | async-start | bytes 1048576 | tf_op jit(solution)/shard_map/all_to_all | solution.py:291
  61.1 19.4 %all-to-all-start.2 = ((bf16[8,127,256]{2,1,0:T(8,128)(2,1)}), bf16[8,127,256]{2,1,0:T(8,128)(2,1)S(1)}, u32[]{:S(2)}, u32[]{:S(2)}) async-start(bf16[8,127,256]{2,1,0:T(8,128)(2,1)} %fusion.34), calls=%async_computation.2 | async-start | bytes 1048576 | tf_op jit(solution)/shard_map/all_to_all | solution.py:291
  83.9 1.3 copy-start.2
  85.3 2.8 %collective-permute-start = (bf16[2,512,512]{2,1,0:T(8,128)(2,1)S(1)}, bf16[2,512,512]{2,1,0:T(8,128)(2,1)}, u32[]{:S(2)}, u32[]{:S(2)}) collective-permute-start(bf16[2,512,512]{2,1,0:T(8,128)(2,1)S(1)} %pad_maximum_fusion.2), channel_id=1, source_target_pairs={{0,1},{1,0},{2,3},{3,2},{4,5},{5,4},{6,7},{7,6},{8,9},{9,8},{10,11... | collective-permute-start | bytes 3145736 | tf_op jit(solution)/shard_map/ppermute | solution.py:185
  90.2 14.3 %collective-permute-start.1 = (bf16[512,512]{1,0:T(8,128)(2,1)}, bf16[512,512]{1,0:T(8,128)(2,1)}, u32[]{:S(2)}, u32[]{:S(2)}) collective-permute-start(bf16[512,512]{1,0:T(8,128)(2,1)} %fusion.16), channel_id=1, source_target_pairs={{0,2},{1,3},{2,0},{3,1},{4,6},{5,7},{6,4},{7,5},{8,10},{9,11},{10,... | collective-permute-start | bytes 1572872 | tf_op jit(solution)/shard_map/ppermute | solution.py:190
  106.3 13.2 %collective-permute-start.3 = (bf16[512,512]{1,0:T(8,128)(2,1)S(1)}, bf16[512,512]{1,0:T(8,128)(2,1)S(1)}, u32[]{:S(2)}, u32[]{:S(2)}) collective-permute-start(bf16[512,512]{1,0:T(8,128)(2,1)S(1)} %fusion.19), channel_id=1, source_target_pairs={{0,2},{1,3},{2,0},{3,1},{4,6},{5,7},{6,4},{7,5},{8,10},{9,11},{10,... | collective-permute-start | bytes 1572872 | tf_op jit(solution)/shard_map/ppermute | solution.py:219
  107.8 11.6 %collective-permute-start.2 = (bf16[512,512]{1,0:T(8,128)(2,1)S(1)}, bf16[512,512]{1,0:T(8,128)(2,1)}, u32[]{:S(2)}, u32[]{:S(2)}) collective-permute-start(bf16[512,512]{1,0:T(8,128)(2,1)S(1)} %fusion.19), channel_id=1, source_target_pairs={{0,1},{1,0},{2,3},{3,2},{4,5},{5,4},{6,7},{7,6},{8,9},{9,8},{10,11... | collective-permute-start | bytes 1572872 | tf_op jit(solution)/shard_map/ppermute | solution.py:218
  119.5 2.0 %collective-permute-start.4 = (bf16[512,512]{1,0:T(8,128)(2,1)S(1)}, bf16[512,512]{1,0:T(8,128)(2,1)}, u32[]{:S(2)}, u32[]{:S(2)}) collective-permute-start(bf16[512,512]{1,0:T(8,128)(2,1)S(1)} %collective-permute-done.3), channel_id=1, source_target_pairs={{0,1},{1,0},{2,3},{3,2},{4,5},{5,4},{6,7},{7,6},{8,9},{9,8},{10,11... | collective-permute-start | bytes 1572872 | tf_op jit(solution)/shard_map/ppermute | solution.py:220
  123.0 2.2 %copy-start.8 = (bf16[2048,1024]{1,0:T(8,128)(2,1)S(1)}, bf16[2048,1024]{1,0:T(8,128)(2,1)}, u32[]{:S(2)}) copy-start(bf16[2048,1024]{1,0:T(8,128)(2,1)} %param.33) | copy-start | bytes 12582916
  123.2 2.0 %copy-start.12 = (f32[2048]{0:T(1024)S(1)}, f32[2048]{0:T(1024)}, u32[]{:S(2)}) copy-start(f32[2048]{0:T(1024)} %param.32) | copy-start | bytes 24580
  125.2 2.4 %copy-start.9 = (bf16[2048,1024]{1,0:T(8,128)(2,1)S(1)}, bf16[2048,1024]{1,0:T(8,128)(2,1)}, u32[]{:S(2)}) copy-start(bf16[2048,1024]{1,0:T(8,128)(2,1)} %param.34) | copy-start | bytes 12582916
  127.6 3.3 %copy-start.10 = (bf16[1024,2048]{1,0:T(8,128)(2,1)S(1)}, bf16[1024,2048]{1,0:T(8,128)(2,1)}, u32[]{:S(2)}) copy-start(bf16[1024,2048]{1,0:T(8,128)(2,1)} %param.35) | copy-start | bytes 12582916
  130.9 4.3 %copy-start.13 = (bf16[512,1024]{1,0:T(8,128)(2,1)}, bf16[512,1024]{1,0:T(8,128)(2,1)S(1)}, u32[]{:S(2)}) copy-start(bf16[512,1024]{1,0:T(8,128)(2,1)S(1)} %multiply_convert_fusion) | copy-start | bytes 3145732
  132.5 2.7 %collective-permute-start.5 = (bf16[2,512,512]{2,1,0:T(8,128)(2,1)S(1)}, bf16[2,512,512]{2,1,0:T(8,128)(2,1)S(1)}, u32[]{:S(2)}, u32[]{:S(2)}) collective-permute-start(bf16[2,512,512]{2,1,0:T(8,128)(2,1)S(1)} %pad_maximum_fusion.3), channel_id=1, source_target_pairs={{0,1},{1,0},{2,3},{3,2},{4,5},{5,4},{6,7},{7,6},{8,9},{9,8},{10,11... | collective-permute-start | bytes 3145736 | tf_op jit(solution)/shard_map/ppermute | solution.py:204
  135.2 1.5 copy-start.3
  136.7 19.3 %collective-permute-start.6 = (bf16[512,512]{1,0:T(8,128)(2,1)}, bf16[512,512]{1,0:T(8,128)(2,1)S(1)}, u32[]{:S(2)}, u32[]{:S(2)}) collective-permute-start(bf16[512,512]{1,0:T(8,128)(2,1)} %fusion.12), channel_id=1, source_target_pairs={{0,2},{1,3},{2,0},{3,1},{4,6},{5,7},{6,4},{7,5},{8,10},{9,11},{10,... | collective-permute-start | bytes 1572872 | tf_op jit(solution)/shard_map/ppermute | solution.py:206
  153.7 2.4 %copy-start.4 = (bf16[2,512,512]{2,1,0:T(8,128)(2,1)S(1)}, bf16[2,512,512]{2,1,0:T(8,128)(2,1)}, u32[]{:S(2)}) copy-start(bf16[2,512,512]{2,1,0:T(8,128)(2,1)} %copy-done.3) | copy-start | bytes 3145732
  158.3 29.6 %all-to-all-start.3 = ((bf16[8,127,512]{2,1,0:T(8,128)(2,1)}), bf16[8,127,512]{2,1,0:T(8,128)(2,1)S(1)}, u32[]{:S(2)}, u32[]{:S(2)}) async-start(bf16[8,127,512]{2,1,0:T(8,128)(2,1)} %broadcast_select_fusion), calls=%async_computation.3 | async-start | bytes 2097152 | tf_op jit(solution)/shard_map/all_to_all | solution.py:317

commit v12 on v11

--- a/solution.py
+++ b/solution.py
@@ -18,7 +18,7 @@
 
 
 SCALE = HEAD_DIM ** (-0.5)
-QBLK = 256
+QBLK = 128
 
 
 def span_kernel(kv_index, start_ref, q_ref, kp_ref, vp_ref, kf_ref, vf_ref, o_ref):

time: 191 us -> 198 us (1.037)
  Pallas kernels: 26.6 us -> 35.4 us
  waiting for transfers between devices: 61.8 us -> 57.4 us
  starting transfers between devices: 25.7 us -> 27.8 us
    pallas_call x2, Pallas kernels: 26.6 us -> 35.4 us  [span_attention(): pl.pallas_call(functools.partial(span_kernel, kv_index), out_shape=jax.Sh...]
    all_to_all x1, waiting for transfers between devices: 4.09 us -> 0.01 us  [shards(): lax.all_to_all(send_resid, 'req', split_axis=0, concat_axis=0, tiled=True)]
  transfers between devices with their start and end apart: 11 -> 11, of which waited for: 8 -> 7; matrix products, arithmetic and copies ran while one was open for 14% -> 14% of each run, Pallas kernels for 14% -> 18%
where the time goes in v12:
time: 198 us; the launch traced here: 196 us
  waiting for transfers between devices  57.4 us (29%)
  Pallas kernels  35.4 us (18%)
  starting transfers between devices  27.8 us (14%)
  other arithmetic  20.8 us (11%)
  local copies, waits for them, and re-layouts  20.2 us (10%)
  between operations  18.5 us (9%)
  matrix products  16.4 us (8%)
    pallas_call x2, Pallas kernels, span_attention(): pl.pallas_call(functools.partial(span_kernel, kv_index), out_shape=jax.Sh...  35.4 us
    all_to_all x1, waiting for transfers between devices, shards(): lax.all_to_all(picked, 'req', split_axis=0, concat_axis=0, tiled=True)  24.8 us
    all_to_all x2, starting transfers between devices, shards(): lax.all_to_all(part, 'req', split_axis=0, concat_axis=0, tiled=True)  12 us
    ppermute x1, waiting for transfers between devices, grp_all_gather(): across = lax.ppermute(block, 'grp', far)  11.6 us
    ppermute x1, waiting for transfers between devices, grp_reduce_scatter(): arrived = lax.ppermute(other.astype(jnp.bfloat16), 'grp', far)  8.59 us
    all_to_all x1, starting transfers between devices, shards(): lax.all_to_all(send_resid, 'req', split_axis=0, concat_axis=0, tiled=True)  7.25 us
    dot_general x4, matrix products, finish(): jnp.dot(inner, grp_block(down_weight, index, width), preferred_element_ty...  5.32 us
    gather x3, other arithmetic, shards(): src_pos = jnp.clip((wanted - firsts[src_dev]) // devices, 0, bucket - 1)  5.07 us
  transfers between devices with their start and end apart: 11, of which 7 were waited for; matrix products, arithmetic and copies ran while one was open for 14% of the time, Pallas kernels for 18%

profile of v12, /device:TPU:0, one launch (start us, length us, event | category | flops | bytes accessed | tf_op | source)
XLA Modules:
  0.0 196.4 jit_solution(11701791067610122414)
XLA Ops:
  4.4 1.3 slice_bitcast_fusion
  6.0 1.4 fusion.11
  7.4 7.3 %all-to-all-start = ((bf16[8,127,512]{2,1,0:T(8,128)(2,1)}), bf16[8,127,512]{2,1,0:T(8,128)(2,1)S(1)}, u32[]{:S(2)}, u32[]{:S(2)}) async-start(bf16[8,127,512]{2,1,0:T(8,128)(2,1)} %fusion.11), calls=%async_computation | async-start | bytes 2097152 | tf_op jit(solution)/shard_map/all_to_all | solution.py:284
  15.7 1.9 fusion.89
  20.4 17.5 %shard_map.154 = bf16[1024,256]{1,0:T(8,128)(2,1)} custom-call(s32[1]{0:T(128)S(6)} %copy.51.start_ref, bf16[1024,512]{1,0:T(8,128)(2,1)} %q_ref.2, bf16[4608,128]{1,0:T(8,128)(2,1)} %kp_ref.3, bf16[4608,128]{1,0:T(8,128)(2,1)} %vp_ref.3, bf16[1024,128]{1,0:T(8,128)(2,1)} %kf_ref.3, bf16[1024,128]{1,0:T(8,128)(2,1)} %vf_ref.3), custom_call_target="tpu_custom_call" | custom-call | flops 17179869184 | bytes 1835008 | tf_op jit(solution)/shard_map/pallas_call | solution.py:89
  40.7 6.0 %all-to-all-start.1 = ((bf16[8,127,256]{2,1,0:T(8,128)(2,1)}), bf16[8,127,256]{2,1,0:T(8,128)(2,1)}, u32[]{:S(2)}, u32[]{:S(2)}) async-start(bf16[8,127,256]{2,1,0:T(8,128)(2,1)} %fusion.36), calls=%async_computation.1 | async-start | bytes 1048576 | tf_op jit(solution)/shard_map/all_to_all | solution.py:291
  46.7 17.9 %shard_map.155 = bf16[1024,256]{1,0:T(8,128)(2,1)} custom-call(s32[1]{0:T(128)S(6)} %copy.51.start_ref, bf16[1024,512]{1,0:T(8,128)(2,1)} %q_ref.2, bf16[4608,128]{1,0:T(8,128)(2,1)} %kp_ref.3, bf16[4608,128]{1,0:T(8,128)(2,1)} %vp_ref.3, bf16[1024,128]{1,0:T(8,128)(2,1)} %kf_ref.3, bf16[1024,128]{1,0:T(8,128)(2,1)} %vf_ref.3), custom_call_target="tpu_custom_call" | custom-call | flops 17179869184 | bytes 1835008 | tf_op jit(solution)/shard_map/pallas_call | solution.py:89
  67.5 6.0 %all-to-all-start.2 = ((bf16[8,127,256]{2,1,0:T(8,128)(2,1)}), bf16[8,127,256]{2,1,0:T(8,128)(2,1)S(1)}, u32[]{:S(2)}, u32[]{:S(2)}) async-start(bf16[8,127,256]{2,1,0:T(8,128)(2,1)} %fusion.34), calls=%async_computation.2 | async-start | bytes 1048576 | tf_op jit(solution)/shard_map/all_to_all | solution.py:291
  73.5 4.4 %compare_select_fusion.2 = s32[512,1]{0,1:T(1,128)S(1)} fusion(s32[]{:T(128)} %bitcast.16, s32[]{:T(128)} %bitcast.17, s32[]{:T(128)} %bitcast.18, s32[]{:T(128)} %bitcast.19, s32[]{:T(128)} %bitcast.20, s32[]{:T(128)} %bitcast.22, s32[]{:T(128)} %bitcast.21, s32[512,1]{0,1:T(1,128)S(1)} %bitcast.143), kind=kLoop, calls=%fused_computation.141 | loop fusion | flops 7680 | bytes 4124 | tf_op jit(solution)/shard_map/gather | solution.py:299
  79.8 2.0 gather_fusion.1
  81.8 5.0 %all-to-all-done.2 = bf16[8,127,256]{2,1,0:T(8,128)(2,1)S(1)} async-done(((bf16[8,127,256]{2,1,0:T(8,128)(2,1)}), bf16[8,127,256]{2,1,0:T(8,128)(2,1)S(1)}, u32[]{:S(2)}, u32[]{:S(2)}) %all-to-all-start.2) | async-done | bytes 520224 | tf_op jit(solution)/shard_map/all_to_all | solution.py:291
  87.0 2.0 gather_fusion.2
  91.6 2.8 %collective-permute-done = bf16[2,512,512]{2,1,0:T(8,128)(2,1)} collective-permute-done((bf16[2,512,512]{2,1,0:T(8,128)(2,1)S(1)}, bf16[2,512,512]{2,1,0:T(8,128)(2,1)}, u32[]{:S(2)}, u32[]{:S(2)}) %collective-permute-start) | collective-permute-done | bytes 1048608 | tf_op jit(solution)/shard_map/ppermute | solution.py:185
  94.4 2.1 %fusion.16 = bf16[512,512]{1,0:T(8,128)(2,1)} fusion(bf16[2,512,512]{2,1,0:T(8,128)(2,1)} %collective-permute-done, bf16[512,2048]{1,0:T(8,128)(2,1)} %copy-done.2, s32[]{:T(128)S(6)} %select_n.208), kind=kLoop, calls=%fused_computation.45 | loop fusion | flops 1048576 | bytes 1572868 | tf_op jit(solution)/shard_map/convert_element_type | solution.py:190
  96.5 1.5 collective-permute-start.1
  98.0 1.5 reshape.400
  99.6 2.6 %gather_fusion = bf16[512,512]{1,0:T(8,128)(2,1)} fusion(bf16[1016,512]{1,0:T(8,128)(2,1)S(1)} %reshape.400, s32[1024]{0:T(1024)S(1)} %pad_clamp_fusion), kind=kCustom, calls=%fused_computation | custom fusion | bytes 1050624 | tf_op jit(solution)/shard_map/gather | solution.py:304
  102.2 8.6 %collective-permute-done.1 = bf16[512,512]{1,0:T(8,128)(2,1)} collective-permute-done((bf16[512,512]{1,0:T(8,128)(2,1)}, bf16[512,512]{1,0:T(8,128)(2,1)}, u32[]{:S(2)}, u32[]{:S(2)}) %collective-permute-start.1) | collective-permute-done | bytes 524320 | tf_op jit(solution)/shard_map/ppermute | solution.py:190
  110.8 1.8 fusion.19
  112.6 1.6 collective-permute-start.3
  114.2 11.6 %collective-permute-done.3 = bf16[512,512]{1,0:T(8,128)(2,1)S(1)} collective-permute-done((bf16[512,512]{1,0:T(8,128)(2,1)S(1)}, bf16[512,512]{1,0:T(8,128)(2,1)S(1)}, u32[]{:S(2)}, u32[]{:S(2)}) %collective-permute-start.3) | collective-permute-done | bytes 524320 | tf_op jit(solution)/shard_map/ppermute | solution.py:219
  125.8 2.0 %collective-permute-done.4 = bf16[512,512]{1,0:T(8,128)(2,1)} collective-permute-done((bf16[512,512]{1,0:T(8,128)(2,1)S(1)}, bf16[512,512]{1,0:T(8,128)(2,1)}, u32[]{:S(2)}, u32[]{:S(2)}) %collective-permute-start.4) | collective-permute-done | bytes 524320 | tf_op jit(solution)/shard_map/ppermute | solution.py:220
  127.8 1.5 pad_maximum_fusion
  130.0 1.5 copy-done.8
  131.5 2.4 %fusion.31 = f32[512,1024]{1,0:T(8,128)S(1)} fusion(bf16[2048,1024]{1,0:T(8,128)(2,1)S(1)} %copy-done.8, f32[2048]{0:T(1024)S(1)} %copy-done.12, f32[512]{0:T(512)S(1)} %add_rsqrt_fusion, bf16[512,512]{1,0:T(8,128)(2,1)S(1)} %get-tuple-element.19, bf16[512,512]{1,0:T(8,128)(2,1)S(1)} %get-tuple-element.20, bf16[512,512]{1,0:T(8,128)(2,1)S(1)} %get-tuple-element.21, ...), kind=kOutput, calls=%fused_computation.66 | convolution fusion | flops 2159017984 | bytes 8398848 | tf_op jit(solution)/shard_map/dot_general | solution.py:235
  133.9 3.3 %multiply_convert_fusion = bf16[512,1024]{1,0:T(8,128)(2,1)S(1)} fusion(f32[512,1024]{1,0:T(8,128)S(1)} %fusion.31, bf16[2048,1024]{1,0:T(8,128)(2,1)S(1)} %copy-done.9, f32[2048]{0:T(1024)S(1)} %copy-done.12, f32[512]{0:T(512)S(1)} %add_rsqrt_fusion, bf16[512,512]{1,0:T(8,128)(2,1)S(1)} %get-tuple-element.19, bf16[512,512]{1,0:T(8,128)(2,1)S(1)} %get-tuple-element.20, ...), kind=kOutput, calls=%fused_computation.17 | convolution fusion | flops 2162163712 | bytes 9447424 | tf_op jit(solution)/shard_map/dot_general | solution.py:236
  139.0 2.5 %collective-permute-done.5 = bf16[2,512,512]{2,1,0:T(8,128)(2,1)S(1)} collective-permute-done((bf16[2,512,512]{2,1,0:T(8,128)(2,1)S(1)}, bf16[2,512,512]{2,1,0:T(8,128)(2,1)S(1)}, u32[]{:S(2)}, u32[]{:S(2)}) %collective-permute-start.5) | collective-permute-done | bytes 1048608 | tf_op jit(solution)/shard_map/ppermute | solution.py:204
  141.5 1.5 fusion.12
  143.1 1.5 collective-permute-start.6
  160.0 2.3 %fusion.5 = f32[512,512]{1,0:T(8,128)S(1)} fusion(bf16[512,1024]{1,0:T(8,128)(2,1)} %copy-done.13, bf16[1024,2048]{1,0:T(8,128)(2,1)} %param.35, s32[]{:T(128)S(6)} %select_n.205), kind=kOutput, calls=%fused_computation.23 | convolution fusion | flops 537395200 | bytes 3145732 | tf_op jit(solution)/shard_map/dot_general | solution.py:239
  164.6 3.7 %all-to-all-start.3 = ((bf16[8,127,512]{2,1,0:T(8,128)(2,1)}), bf16[8,127,512]{2,1,0:T(8,128)(2,1)S(1)}, u32[]{:S(2)}, u32[]{:S(2)}) async-start(bf16[8,127,512]{2,1,0:T(8,128)(2,1)} %broadcast_select_fusion), calls=%async_computation.3 | async-start | bytes 2097152 | tf_op jit(solution)/shard_map/all_to_all | solution.py:317
  169.4 24.8 %all-to-all-done.3 = bf16[8,127,512]{2,1,0:T(8,128)(2,1)S(1)} async-done(((bf16[8,127,512]{2,1,0:T(8,128)(2,1)}), bf16[8,127,512]{2,1,0:T(8,128)(2,1)S(1)}, u32[]{:S(2)}, u32[]{:S(2)}) %all-to-all-start.3) | async-done | bytes 1040416 | tf_op jit(solution)/shard_map/all_to_all | solution.py:317
  (100 shorter events, 24.2 us)
Async XLA Ops:
  0.0 89.0 %copy-start = (bf16[512,2048]{1,0:T(8,128)(2,1)S(1)}, bf16[512,2048]{1,0:T(8,128)(2,1)}, u32[]{:S(2)}) copy-start(bf16[512,2048]{1,0:T(8,128)(2,1)} %param.31) | copy-start | bytes 6291460
  6.0 9.4 %slice-start = ((bf16[1024,512]{1,0:T(8,128)(2,1)}), bf16[8,512]{1,0:T(8,128)(2,1)S(1)}, s32[]{:S(2)}) async-start(bf16[1024,512]{1,0:T(8,128)(2,1)} %q_ref.2), calls=%async_computation.4 | async-start | bytes 16384 | tf_op jit(solution)/shard_map/slice | solution.py:107
  6.0 9.5 %copy-start.5 = (s32[8]{0:T(128)S(1)}, s32[8]{0:T(128)}, u32[]{:S(2)}) copy-start(s32[8]{0:T(128)} %param.26) | copy-start | bytes 100
  6.0 9.5 %copy-start.6 = (s32[8]{0:T(128)S(1)}, s32[8]{0:T(128)}, u32[]{:S(2)}) copy-start(s32[8]{0:T(128)} %param.27) | copy-start | bytes 100
  6.0 9.5 %copy-start.7 = (s32[8]{0:T(128)S(1)}, s32[8]{0:T(128)}, u32[]{:S(2)}) copy-start(s32[8]{0:T(128)} %param.28) | copy-start | bytes 100
  7.4 33.3 %all-to-all-start = ((bf16[8,127,512]{2,1,0:T(8,128)(2,1)}), bf16[8,127,512]{2,1,0:T(8,128)(2,1)S(1)}, u32[]{:S(2)}, u32[]{:S(2)}) async-start(bf16[8,127,512]{2,1,0:T(8,128)(2,1)} %fusion.11), calls=%async_computation | async-start | bytes 2097152 | tf_op jit(solution)/shard_map/all_to_all | solution.py:284
  15.4 3.5 %copy-start.11 = (bf16[4608,128]{1,0:T(8,128)(2,1)S(1)}, bf16[4608,128]{1,0:T(8,128)(2,1)}, u32[]{:S(2)}) copy-start(bf16[4608,128]{1,0:T(8,128)(2,1)} %vp_ref.3) | copy-start | bytes 3538948
  40.7 23.9 %copy-start.1 = (bf16[8,127,512]{2,1,0:T(8,128)(2,1)}, bf16[8,127,512]{2,1,0:T(8,128)(2,1)S(1)}, u32[]{:S(2)}) copy-start(bf16[8,127,512]{2,1,0:T(8,128)(2,1)S(1)} %all-to-all-done) | copy-start | bytes 3121156
  40.7 26.8 %all-to-all-start.1 = ((bf16[8,127,256]{2,1,0:T(8,128)(2,1)}), bf16[8,127,256]{2,1,0:T(8,128)(2,1)}, u32[]{:S(2)}, u32[]{:S(2)}) async-start(bf16[8,127,256]{2,1,0:T(8,128)(2,1)} %fusion.36), calls=%async_computation.1 | async-start | bytes 1048576 | tf_op jit(solution)/shard_map/all_to_all | solution.py:291
  67.5 19.4 %all-to-all-start.2 = ((bf16[8,127,256]{2,1,0:T(8,128)(2,1)}), bf16[8,127,256]{2,1,0:T(8,128)(2,1)S(1)}, u32[]{:S(2)}, u32[]{:S(2)}) async-start(bf16[8,127,256]{2,1,0:T(8,128)(2,1)} %fusion.34), calls=%async_computation.2 | async-start | bytes 1048576 | tf_op jit(solution)/shard_map/all_to_all | solution.py:291
  90.2 1.3 copy-start.2
  91.6 2.8 %collective-permute-start = (bf16[2,512,512]{2,1,0:T(8,128)(2,1)S(1)}, bf16[2,512,512]{2,1,0:T(8,128)(2,1)}, u32[]{:S(2)}, u32[]{:S(2)}) collective-permute-start(bf16[2,512,512]{2,1,0:T(8,128)(2,1)S(1)} %pad_maximum_fusion.2), channel_id=1, source_target_pairs={{0,1},{1,0},{2,3},{3,2},{4,5},{5,4},{6,7},{7,6},{8,9},{9,8},{10,11... | collective-permute-start | bytes 3145736 | tf_op jit(solution)/shard_map/ppermute | solution.py:185
  96.5 14.3 %collective-permute-start.1 = (bf16[512,512]{1,0:T(8,128)(2,1)}, bf16[512,512]{1,0:T(8,128)(2,1)}, u32[]{:S(2)}, u32[]{:S(2)}) collective-permute-start(bf16[512,512]{1,0:T(8,128)(2,1)} %fusion.16), channel_id=1, source_target_pairs={{0,2},{1,3},{2,0},{3,1},{4,6},{5,7},{6,4},{7,5},{8,10},{9,11},{10,... | collective-permute-start | bytes 1572872 | tf_op jit(solution)/shard_map/ppermute | solution.py:190
  112.6 13.2 %collective-permute-start.3 = (bf16[512,512]{1,0:T(8,128)(2,1)S(1)}, bf16[512,512]{1,0:T(8,128)(2,1)S(1)}, u32[]{:S(2)}, u32[]{:S(2)}) collective-permute-start(bf16[512,512]{1,0:T(8,128)(2,1)S(1)} %fusion.19), channel_id=1, source_target_pairs={{0,2},{1,3},{2,0},{3,1},{4,6},{5,7},{6,4},{7,5},{8,10},{9,11},{10,... | collective-permute-start | bytes 1572872 | tf_op jit(solution)/shard_map/ppermute | solution.py:219
  114.2 11.6 %collective-permute-start.2 = (bf16[512,512]{1,0:T(8,128)(2,1)S(1)}, bf16[512,512]{1,0:T(8,128)(2,1)}, u32[]{:S(2)}, u32[]{:S(2)}) collective-permute-start(bf16[512,512]{1,0:T(8,128)(2,1)S(1)} %fusion.19), channel_id=1, source_target_pairs={{0,1},{1,0},{2,3},{3,2},{4,5},{5,4},{6,7},{7,6},{8,9},{9,8},{10,11... | collective-permute-start | bytes 1572872 | tf_op jit(solution)/shard_map/ppermute | solution.py:218
  125.8 2.0 %collective-permute-start.4 = (bf16[512,512]{1,0:T(8,128)(2,1)S(1)}, bf16[512,512]{1,0:T(8,128)(2,1)}, u32[]{:S(2)}, u32[]{:S(2)}) collective-permute-start(bf16[512,512]{1,0:T(8,128)(2,1)S(1)} %collective-permute-done.3), channel_id=1, source_target_pairs={{0,1},{1,0},{2,3},{3,2},{4,5},{5,4},{6,7},{7,6},{8,9},{9,8},{10,11... | collective-permute-start | bytes 1572872 | tf_op jit(solution)/shard_map/ppermute | solution.py:220
  129.3 2.2 %copy-start.8 = (bf16[2048,1024]{1,0:T(8,128)(2,1)S(1)}, bf16[2048,1024]{1,0:T(8,128)(2,1)}, u32[]{:S(2)}) copy-start(bf16[2048,1024]{1,0:T(8,128)(2,1)} %param.33) | copy-start | bytes 12582916
  129.5 2.0 %copy-start.12 = (f32[2048]{0:T(1024)S(1)}, f32[2048]{0:T(1024)}, u32[]{:S(2)}) copy-start(f32[2048]{0:T(1024)} %param.32) | copy-start | bytes 24580
  131.5 2.4 %copy-start.9 = (bf16[2048,1024]{1,0:T(8,128)(2,1)S(1)}, bf16[2048,1024]{1,0:T(8,128)(2,1)}, u32[]{:S(2)}) copy-start(bf16[2048,1024]{1,0:T(8,128)(2,1)} %param.34) | copy-start | bytes 12582916
  133.9 3.3 %copy-start.10 = (bf16[1024,2048]{1,0:T(8,128)(2,1)S(1)}, bf16[1024,2048]{1,0:T(8,128)(2,1)}, u32[]{:S(2)}) copy-start(bf16[1024,2048]{1,0:T(8,128)(2,1)} %param.35) | copy-start | bytes 12582916
  137.2 4.3 %copy-start.13 = (bf16[512,1024]{1,0:T(8,128)(2,1)}, bf16[512,1024]{1,0:T(8,128)(2,1)S(1)}, u32[]{:S(2)}) copy-start(bf16[512,1024]{1,0:T(8,128)(2,1)S(1)} %multiply_convert_fusion) | copy-start | bytes 3145732
  138.8 2.7 %collective-permute-start.5 = (bf16[2,512,512]{2,1,0:T(8,128)(2,1)S(1)}, bf16[2,512,512]{2,1,0:T(8,128)(2,1)S(1)}, u32[]{:S(2)}, u32[]{:S(2)}) collective-permute-start(bf16[2,512,512]{2,1,0:T(8,128)(2,1)S(1)} %pad_maximum_fusion.3), channel_id=1, source_target_pairs={{0,1},{1,0},{2,3},{3,2},{4,5},{5,4},{6,7},{7,6},{8,9},{9,8},{10,11... | collective-permute-start | bytes 3145736 | tf_op jit(solution)/shard_map/ppermute | solution.py:204
  141.5 1.5 copy-start.3
  143.1 19.3 %collective-permute-start.6 = (bf16[512,512]{1,0:T(8,128)(2,1)}, bf16[512,512]{1,0:T(8,128)(2,1)S(1)}, u32[]{:S(2)}, u32[]{:S(2)}) collective-permute-start(bf16[512,512]{1,0:T(8,128)(2,1)} %fusion.12), channel_id=1, source_target_pairs={{0,2},{1,3},{2,0},{3,1},{4,6},{5,7},{6,4},{7,5},{8,10},{9,11},{10,... | collective-permute-start | bytes 1572872 | tf_op jit(solution)/shard_map/ppermute | solution.py:206
  160.0 2.4 %copy-start.4 = (bf16[2,512,512]{2,1,0:T(8,128)(2,1)S(1)}, bf16[2,512,512]{2,1,0:T(8,128)(2,1)}, u32[]{:S(2)}) copy-start(bf16[2,512,512]{2,1,0:T(8,128)(2,1)} %copy-done.3) | copy-start | bytes 3145732
  164.6 29.6 %all-to-all-start.3 = ((bf16[8,127,512]{2,1,0:T(8,128)(2,1)}), bf16[8,127,512]{2,1,0:T(8,128)(2,1)S(1)}, u32[]{:S(2)}, u32[]{:S(2)}) async-start(bf16[8,127,512]{2,1,0:T(8,128)(2,1)} %broadcast_select_fusion), calls=%async_computation.3 | async-start | bytes 2097152 | tf_op jit(solution)/shard_map/all_to_all | solution.py:317

commit v13 on v12

--- a/solution.py
+++ b/solution.py
@@ -18,7 +18,7 @@
 
 
 SCALE = HEAD_DIM ** (-0.5)
-QBLK = 128
+QBLK = 512
 
 
 def span_kernel(kv_index, start_ref, q_ref, kp_ref, vp_ref, kf_ref, vf_ref, o_ref):

time: 198 us -> 190 us (0.960)
  Pallas kernels: 35.4 us -> 24.2 us
  waiting for transfers between devices: 57.4 us -> 62.9 us
  starting transfers between devices: 27.8 us -> 25.7 us
    pallas_call x2, Pallas kernels: 35.4 us -> 24.2 us  [span_attention(): pl.pallas_call(functools.partial(span_kernel, kv_index), out_shape=jax.Sh...]
    all_to_all x1, waiting for transfers between devices: 0.01 us -> 5.14 us  [shards(): lax.all_to_all(send_resid, 'req', split_axis=0, concat_axis=0, tiled=True)]
  transfers between devices with their start and end apart: 11 -> 11, of which waited for: 7 -> 8; matrix products, arithmetic and copies ran while one was open for 14% -> 14% of each run, Pallas kernels for 18% -> 13%
where the time goes in v13:
time: 190 us; the launch traced here: 189 us
  waiting for transfers between devices  62.9 us (33%)
  starting transfers between devices  25.7 us (14%)
  Pallas kernels  24.2 us (13%)
  other arithmetic  20.8 us (11%)
  local copies, waits for them, and re-layouts  20.2 us (11%)
  between operations  18.5 us (10%)
  matrix products  16.4 us (9%)
    all_to_all x1, waiting for transfers between devices, shards(): lax.all_to_all(picked, 'req', split_axis=0, concat_axis=0, tiled=True)  24.8 us
    pallas_call x2, Pallas kernels, span_attention(): pl.pallas_call(functools.partial(span_kernel, kv_index), out_shape=jax.Sh...  24.2 us
    ppermute x1, waiting for transfers between devices, grp_all_gather(): across = lax.ppermute(block, 'grp', far)  11.6 us
    all_to_all x2, starting transfers between devices, shards(): lax.all_to_all(part, 'req', split_axis=0, concat_axis=0, tiled=True)  10 us
    ppermute x1, waiting for transfers between devices, grp_reduce_scatter(): arrived = lax.ppermute(other.astype(jnp.bfloat16), 'grp', far)  8.6 us
    all_to_all x1, starting transfers between devices, shards(): lax.all_to_all(send_resid, 'req', split_axis=0, concat_axis=0, tiled=True)  7.25 us
    all_to_all x2, waiting for transfers between devices, shards(): lax.all_to_all(part, 'req', split_axis=0, concat_axis=0, tiled=True)  5.35 us
    dot_general x4, matrix products, finish(): jnp.dot(inner, grp_block(down_weight, index, width), preferred_element_ty...  5.32 us
  transfers between devices with their start and end apart: 11, of which 8 were waited for; matrix products, arithmetic and copies ran while one was open for 14% of the time, Pallas kernels for 13%

profile of v13, /device:TPU:0, one launch (start us, length us, event | category | flops | bytes accessed | tf_op | source)
XLA Modules:
  0.0 188.7 jit_solution(1665625582172194424)
XLA Ops:
  6.0 1.4 fusion.11
  7.4 7.3 %all-to-all-start = ((bf16[8,127,512]{2,1,0:T(8,128)(2,1)}), bf16[8,127,512]{2,1,0:T(8,128)(2,1)S(1)}, u32[]{:S(2)}, u32[]{:S(2)}) async-start(bf16[8,127,512]{2,1,0:T(8,128)(2,1)} %fusion.11), calls=%async_computation | async-start | bytes 2097152 | tf_op jit(solution)/shard_map/all_to_all | solution.py:284
  15.7 1.9 %fusion.89 = (f32[8,8]{1,0:T(8,128)S(1)}, f32[8,8,4096]{2,1,0:T(8,128)S(1)}) fusion(bf16[4608,128]{1,0:T(8,128)(2,1)} %kp_ref.3, bf16[8,8,64]{2,1,0:T(8,128)(2,1)S(1)} %get-tuple-element.25, bf16[8,8,64]{2,1,0:T(8,128)(2,1)S(1)} %get-tuple-element.24, pred[8,4096]{1,0:T(8,128)(4,1)S(1)} %fusion.60), kind=kOutput, calls=%fused_computation.192 | convolution fusion | flops 67928000 | bytes 2146560 | tf_op jit(solution)/shard_map/rhc,tc->rht/dot_general | solution.py:113
  20.4 12.1 %shard_map.154 = bf16[1024,256]{1,0:T(8,128)(2,1)} custom-call(s32[1]{0:T(128)S(6)} %copy.51.start_ref, bf16[1024,512]{1,0:T(8,128)(2,1)} %q_ref.2, bf16[4608,128]{1,0:T(8,128)(2,1)} %kp_ref.3, bf16[4608,128]{1,0:T(8,128)(2,1)} %vp_ref.3, bf16[1024,128]{1,0:T(8,128)(2,1)} %kf_ref.3, bf16[1024,128]{1,0:T(8,128)(2,1)} %vf_ref.3), custom_call_target="tpu_custom_call" | custom-call | flops 17179869184 | bytes 1835008 | tf_op jit(solution)/shard_map/pallas_call | solution.py:89
  35.3 5.1 %all-to-all-done = bf16[8,127,512]{2,1,0:T(8,128)(2,1)S(1)} async-done(((bf16[8,127,512]{2,1,0:T(8,128)(2,1)}), bf16[8,127,512]{2,1,0:T(8,128)(2,1)S(1)}, u32[]{:S(2)}, u32[]{:S(2)}) %all-to-all-start) | async-done | bytes 1040416 | tf_op jit(solution)/shard_map/all_to_all | solution.py:284
  40.4 4.3 %all-to-all-start.1 = ((bf16[8,127,256]{2,1,0:T(8,128)(2,1)}), bf16[8,127,256]{2,1,0:T(8,128)(2,1)}, u32[]{:S(2)}, u32[]{:S(2)}) async-start(bf16[8,127,256]{2,1,0:T(8,128)(2,1)} %fusion.36), calls=%async_computation.1 | async-start | bytes 1048576 | tf_op jit(solution)/shard_map/all_to_all | solution.py:291
  44.8 12.1 %shard_map.155 = bf16[1024,256]{1,0:T(8,128)(2,1)} custom-call(s32[1]{0:T(128)S(6)} %copy.51.start_ref, bf16[1024,512]{1,0:T(8,128)(2,1)} %q_ref.2, bf16[4608,128]{1,0:T(8,128)(2,1)} %kp_ref.3, bf16[4608,128]{1,0:T(8,128)(2,1)} %vp_ref.3, bf16[1024,128]{1,0:T(8,128)(2,1)} %kf_ref.3, bf16[1024,128]{1,0:T(8,128)(2,1)} %vf_ref.3), custom_call_target="tpu_custom_call" | custom-call | flops 17179869184 | bytes 1835008 | tf_op jit(solution)/shard_map/pallas_call | solution.py:89
  59.8 5.7 %all-to-all-start.2 = ((bf16[8,127,256]{2,1,0:T(8,128)(2,1)}), bf16[8,127,256]{2,1,0:T(8,128)(2,1)S(1)}, u32[]{:S(2)}, u32[]{:S(2)}) async-start(bf16[8,127,256]{2,1,0:T(8,128)(2,1)} %fusion.34), calls=%async_computation.2 | async-start | bytes 1048576 | tf_op jit(solution)/shard_map/all_to_all | solution.py:291
  65.5 4.4 %compare_select_fusion.2 = s32[512,1]{0,1:T(1,128)S(1)} fusion(s32[]{:T(128)} %bitcast.16, s32[]{:T(128)} %bitcast.17, s32[]{:T(128)} %bitcast.18, s32[]{:T(128)} %bitcast.19, s32[]{:T(128)} %bitcast.20, s32[]{:T(128)} %bitcast.22, s32[]{:T(128)} %bitcast.21, s32[512,1]{0,1:T(1,128)S(1)} %bitcast.143), kind=kLoop, calls=%fused_computation.141 | loop fusion | flops 7680 | bytes 4124 | tf_op jit(solution)/shard_map/gather | solution.py:299
  71.8 2.0 %gather_fusion.1 = bf16[512,256]{1,0:T(8,128)(2,1)S(1)} fusion(bf16[1016,256]{1,0:T(8,128)(2,1)S(1)} %reshape.401, s32[1024]{0:T(1024)S(1)} %pad_clamp_fusion), kind=kCustom, calls=%fused_computation.1 | custom fusion | bytes 526336 | tf_op jit(solution)/shard_map/gather | solution.py:302
  73.8 5.3 %all-to-all-done.2 = bf16[8,127,256]{2,1,0:T(8,128)(2,1)S(1)} async-done(((bf16[8,127,256]{2,1,0:T(8,128)(2,1)}), bf16[8,127,256]{2,1,0:T(8,128)(2,1)S(1)}, u32[]{:S(2)}, u32[]{:S(2)}) %all-to-all-start.2) | async-done | bytes 520224 | tf_op jit(solution)/shard_map/all_to_all | solution.py:291
  79.3 2.0 %gather_fusion.2 = bf16[512,256]{1,0:T(8,128)(2,1)S(1)} fusion(bf16[1016,256]{1,0:T(8,128)(2,1)S(1)} %reshape.402, s32[1024]{0:T(1024)S(1)} %pad_clamp_fusion), kind=kCustom, calls=%fused_computation.2 | custom fusion | bytes 526336 | tf_op jit(solution)/shard_map/gather | solution.py:302
  83.9 2.8 %collective-permute-done = bf16[2,512,512]{2,1,0:T(8,128)(2,1)} collective-permute-done((bf16[2,512,512]{2,1,0:T(8,128)(2,1)S(1)}, bf16[2,512,512]{2,1,0:T(8,128)(2,1)}, u32[]{:S(2)}, u32[]{:S(2)}) %collective-permute-start) | collective-permute-done | bytes 1048608 | tf_op jit(solution)/shard_map/ppermute | solution.py:185
  86.7 2.1 %fusion.16 = bf16[512,512]{1,0:T(8,128)(2,1)} fusion(bf16[2,512,512]{2,1,0:T(8,128)(2,1)} %collective-permute-done, bf16[512,2048]{1,0:T(8,128)(2,1)} %copy-done.2, s32[]{:T(128)S(6)} %select_n.208), kind=kLoop, calls=%fused_computation.45 | loop fusion | flops 1048576 | bytes 1572868 | tf_op jit(solution)/shard_map/convert_element_type | solution.py:190
  88.8 1.5 collective-permute-start.1
  90.3 1.5 reshape.400
  91.9 2.6 %gather_fusion = bf16[512,512]{1,0:T(8,128)(2,1)} fusion(bf16[1016,512]{1,0:T(8,128)(2,1)S(1)} %reshape.400, s32[1024]{0:T(1024)S(1)} %pad_clamp_fusion), kind=kCustom, calls=%fused_computation | custom fusion | bytes 1050624 | tf_op jit(solution)/shard_map/gather | solution.py:304
  94.5 8.6 %collective-permute-done.1 = bf16[512,512]{1,0:T(8,128)(2,1)} collective-permute-done((bf16[512,512]{1,0:T(8,128)(2,1)}, bf16[512,512]{1,0:T(8,128)(2,1)}, u32[]{:S(2)}, u32[]{:S(2)}) %collective-permute-start.1) | collective-permute-done | bytes 524320 | tf_op jit(solution)/shard_map/ppermute | solution.py:190
  103.1 1.8 fusion.19
  104.9 1.6 collective-permute-start.3
  106.5 11.6 %collective-permute-done.3 = bf16[512,512]{1,0:T(8,128)(2,1)S(1)} collective-permute-done((bf16[512,512]{1,0:T(8,128)(2,1)S(1)}, bf16[512,512]{1,0:T(8,128)(2,1)S(1)}, u32[]{:S(2)}, u32[]{:S(2)}) %collective-permute-start.3) | collective-permute-done | bytes 524320 | tf_op jit(solution)/shard_map/ppermute | solution.py:219
  118.1 2.0 %collective-permute-done.4 = bf16[512,512]{1,0:T(8,128)(2,1)} collective-permute-done((bf16[512,512]{1,0:T(8,128)(2,1)S(1)}, bf16[512,512]{1,0:T(8,128)(2,1)}, u32[]{:S(2)}, u32[]{:S(2)}) %collective-permute-start.4) | collective-permute-done | bytes 524320 | tf_op jit(solution)/shard_map/ppermute | solution.py:220
  120.1 1.5 pad_maximum_fusion
  122.3 1.5 copy-done.8
  123.8 2.4 %fusion.31 = f32[512,1024]{1,0:T(8,128)S(1)} fusion(bf16[2048,1024]{1,0:T(8,128)(2,1)S(1)} %copy-done.8, f32[2048]{0:T(1024)S(1)} %copy-done.12, f32[512]{0:T(512)S(1)} %add_rsqrt_fusion, bf16[512,512]{1,0:T(8,128)(2,1)S(1)} %get-tuple-element.19, bf16[512,512]{1,0:T(8,128)(2,1)S(1)} %get-tuple-element.20, bf16[512,512]{1,0:T(8,128)(2,1)S(1)} %get-tuple-element.21, ...), kind=kOutput, calls=%fused_computation.66 | convolution fusion | flops 2159017984 | bytes 8398848 | tf_op jit(solution)/shard_map/dot_general | solution.py:235
  126.2 3.3 %multiply_convert_fusion = bf16[512,1024]{1,0:T(8,128)(2,1)S(1)} fusion(f32[512,1024]{1,0:T(8,128)S(1)} %fusion.31, bf16[2048,1024]{1,0:T(8,128)(2,1)S(1)} %copy-done.9, f32[2048]{0:T(1024)S(1)} %copy-done.12, f32[512]{0:T(512)S(1)} %add_rsqrt_fusion, bf16[512,512]{1,0:T(8,128)(2,1)S(1)} %get-tuple-element.19, bf16[512,512]{1,0:T(8,128)(2,1)S(1)} %get-tuple-element.20, ...), kind=kOutput, calls=%fused_computation.17 | convolution fusion | flops 2162163712 | bytes 9447424 | tf_op jit(solution)/shard_map/dot_general | solution.py:236
  131.3 2.5 %collective-permute-done.5 = bf16[2,512,512]{2,1,0:T(8,128)(2,1)S(1)} collective-permute-done((bf16[2,512,512]{2,1,0:T(8,128)(2,1)S(1)}, bf16[2,512,512]{2,1,0:T(8,128)(2,1)S(1)}, u32[]{:S(2)}, u32[]{:S(2)}) %collective-permute-start.5) | collective-permute-done | bytes 1048608 | tf_op jit(solution)/shard_map/ppermute | solution.py:204
  133.8 1.5 fusion.12
  135.4 1.5 collective-permute-start.6
  152.3 2.3 %fusion.5 = f32[512,512]{1,0:T(8,128)S(1)} fusion(bf16[512,1024]{1,0:T(8,128)(2,1)} %copy-done.13, bf16[1024,2048]{1,0:T(8,128)(2,1)} %param.35, s32[]{:T(128)S(6)} %select_n.205), kind=kOutput, calls=%fused_computation.23 | convolution fusion | flops 537395200 | bytes 3145732 | tf_op jit(solution)/shard_map/dot_general | solution.py:239
  156.9 3.6 %all-to-all-start.3 = ((bf16[8,127,512]{2,1,0:T(8,128)(2,1)}), bf16[8,127,512]{2,1,0:T(8,128)(2,1)S(1)}, u32[]{:S(2)}, u32[]{:S(2)}) async-start(bf16[8,127,512]{2,1,0:T(8,128)(2,1)} %broadcast_select_fusion), calls=%async_computation.3 | async-start | bytes 2097152 | tf_op jit(solution)/shard_map/all_to_all | solution.py:317
  161.7 24.8 %all-to-all-done.3 = bf16[8,127,512]{2,1,0:T(8,128)(2,1)S(1)} async-done(((bf16[8,127,512]{2,1,0:T(8,128)(2,1)}), bf16[8,127,512]{2,1,0:T(8,128)(2,1)S(1)}, u32[]{:S(2)}, u32[]{:S(2)}) %all-to-all-start.3) | async-done | bytes 1040416 | tf_op jit(solution)/shard_map/all_to_all | solution.py:317
  (100 shorter events, 25.4 us)
Async XLA Ops:
  0.0 81.3 %copy-start = (bf16[512,2048]{1,0:T(8,128)(2,1)S(1)}, bf16[512,2048]{1,0:T(8,128)(2,1)}, u32[]{:S(2)}) copy-start(bf16[512,2048]{1,0:T(8,128)(2,1)} %param.31) | copy-start | bytes 6291460
  6.0 9.4 %slice-start = ((bf16[1024,512]{1,0:T(8,128)(2,1)}), bf16[8,512]{1,0:T(8,128)(2,1)S(1)}, s32[]{:S(2)}) async-start(bf16[1024,512]{1,0:T(8,128)(2,1)} %q_ref.2), calls=%async_computation.4 | async-start | bytes 16384 | tf_op jit(solution)/shard_map/slice | solution.py:107
  6.0 9.5 %copy-start.5 = (s32[8]{0:T(128)S(1)}, s32[8]{0:T(128)}, u32[]{:S(2)}) copy-start(s32[8]{0:T(128)} %param.26) | copy-start | bytes 100
  6.0 9.5 %copy-start.6 = (s32[8]{0:T(128)S(1)}, s32[8]{0:T(128)}, u32[]{:S(2)}) copy-start(s32[8]{0:T(128)} %param.27) | copy-start | bytes 100
  6.0 9.5 %copy-start.7 = (s32[8]{0:T(128)S(1)}, s32[8]{0:T(128)}, u32[]{:S(2)}) copy-start(s32[8]{0:T(128)} %param.28) | copy-start | bytes 100
  7.4 33.0 %all-to-all-start = ((bf16[8,127,512]{2,1,0:T(8,128)(2,1)}), bf16[8,127,512]{2,1,0:T(8,128)(2,1)S(1)}, u32[]{:S(2)}, u32[]{:S(2)}) async-start(bf16[8,127,512]{2,1,0:T(8,128)(2,1)} %fusion.11), calls=%async_computation | async-start | bytes 2097152 | tf_op jit(solution)/shard_map/all_to_all | solution.py:284
  15.4 3.5 %copy-start.11 = (bf16[4608,128]{1,0:T(8,128)(2,1)S(1)}, bf16[4608,128]{1,0:T(8,128)(2,1)}, u32[]{:S(2)}) copy-start(bf16[4608,128]{1,0:T(8,128)(2,1)} %vp_ref.3) | copy-start | bytes 3538948
  40.4 16.4 %copy-start.1 = (bf16[8,127,512]{2,1,0:T(8,128)(2,1)}, bf16[8,127,512]{2,1,0:T(8,128)(2,1)S(1)}, u32[]{:S(2)}) copy-start(bf16[8,127,512]{2,1,0:T(8,128)(2,1)S(1)} %all-to-all-done) | copy-start | bytes 3121156
  40.4 19.3 %all-to-all-start.1 = ((bf16[8,127,256]{2,1,0:T(8,128)(2,1)}), bf16[8,127,256]{2,1,0:T(8,128)(2,1)}, u32[]{:S(2)}, u32[]{:S(2)}) async-start(bf16[8,127,256]{2,1,0:T(8,128)(2,1)} %fusion.36), calls=%async_computation.1 | async-start | bytes 1048576 | tf_op jit(solution)/shard_map/all_to_all | solution.py:291
  59.8 19.4 %all-to-all-start.2 = ((bf16[8,127,256]{2,1,0:T(8,128)(2,1)}), bf16[8,127,256]{2,1,0:T(8,128)(2,1)S(1)}, u32[]{:S(2)}, u32[]{:S(2)}) async-start(bf16[8,127,256]{2,1,0:T(8,128)(2,1)} %fusion.34), calls=%async_computation.2 | async-start | bytes 1048576 | tf_op jit(solution)/shard_map/all_to_all | solution.py:291
  82.6 1.3 copy-start.2
  83.9 2.8 %collective-permute-start = (bf16[2,512,512]{2,1,0:T(8,128)(2,1)S(1)}, bf16[2,512,512]{2,1,0:T(8,128)(2,1)}, u32[]{:S(2)}, u32[]{:S(2)}) collective-permute-start(bf16[2,512,512]{2,1,0:T(8,128)(2,1)S(1)} %pad_maximum_fusion.2), channel_id=1, source_target_pairs={{0,1},{1,0},{2,3},{3,2},{4,5},{5,4},{6,7},{7,6},{8,9},{9,8},{10,11... | collective-permute-start | bytes 3145736 | tf_op jit(solution)/shard_map/ppermute | solution.py:185
  88.8 14.3 %collective-permute-start.1 = (bf16[512,512]{1,0:T(8,128)(2,1)}, bf16[512,512]{1,0:T(8,128)(2,1)}, u32[]{:S(2)}, u32[]{:S(2)}) collective-permute-start(bf16[512,512]{1,0:T(8,128)(2,1)} %fusion.16), channel_id=1, source_target_pairs={{0,2},{1,3},{2,0},{3,1},{4,6},{5,7},{6,4},{7,5},{8,10},{9,11},{10,... | collective-permute-start | bytes 1572872 | tf_op jit(solution)/shard_map/ppermute | solution.py:190
  104.9 13.2 %collective-permute-start.3 = (bf16[512,512]{1,0:T(8,128)(2,1)S(1)}, bf16[512,512]{1,0:T(8,128)(2,1)S(1)}, u32[]{:S(2)}, u32[]{:S(2)}) collective-permute-start(bf16[512,512]{1,0:T(8,128)(2,1)S(1)} %fusion.19), channel_id=1, source_target_pairs={{0,2},{1,3},{2,0},{3,1},{4,6},{5,7},{6,4},{7,5},{8,10},{9,11},{10,... | collective-permute-start | bytes 1572872 | tf_op jit(solution)/shard_map/ppermute | solution.py:219
  106.5 11.6 %collective-permute-start.2 = (bf16[512,512]{1,0:T(8,128)(2,1)S(1)}, bf16[512,512]{1,0:T(8,128)(2,1)}, u32[]{:S(2)}, u32[]{:S(2)}) collective-permute-start(bf16[512,512]{1,0:T(8,128)(2,1)S(1)} %fusion.19), channel_id=1, source_target_pairs={{0,1},{1,0},{2,3},{3,2},{4,5},{5,4},{6,7},{7,6},{8,9},{9,8},{10,11... | collective-permute-start | bytes 1572872 | tf_op jit(solution)/shard_map/ppermute | solution.py:218
  118.1 2.0 %collective-permute-start.4 = (bf16[512,512]{1,0:T(8,128)(2,1)S(1)}, bf16[512,512]{1,0:T(8,128)(2,1)}, u32[]{:S(2)}, u32[]{:S(2)}) collective-permute-start(bf16[512,512]{1,0:T(8,128)(2,1)S(1)} %collective-permute-done.3), channel_id=1, source_target_pairs={{0,1},{1,0},{2,3},{3,2},{4,5},{5,4},{6,7},{7,6},{8,9},{9,8},{10,11... | collective-permute-start | bytes 1572872 | tf_op jit(solution)/shard_map/ppermute | solution.py:220
  121.6 2.2 %copy-start.8 = (bf16[2048,1024]{1,0:T(8,128)(2,1)S(1)}, bf16[2048,1024]{1,0:T(8,128)(2,1)}, u32[]{:S(2)}) copy-start(bf16[2048,1024]{1,0:T(8,128)(2,1)} %param.33) | copy-start | bytes 12582916
  121.8 2.0 %copy-start.12 = (f32[2048]{0:T(1024)S(1)}, f32[2048]{0:T(1024)}, u32[]{:S(2)}) copy-start(f32[2048]{0:T(1024)} %param.32) | copy-start | bytes 24580
  123.8 2.4 %copy-start.9 = (bf16[2048,1024]{1,0:T(8,128)(2,1)S(1)}, bf16[2048,1024]{1,0:T(8,128)(2,1)}, u32[]{:S(2)}) copy-start(bf16[2048,1024]{1,0:T(8,128)(2,1)} %param.34) | copy-start | bytes 12582916
  126.2 3.3 %copy-start.10 = (bf16[1024,2048]{1,0:T(8,128)(2,1)S(1)}, bf16[1024,2048]{1,0:T(8,128)(2,1)}, u32[]{:S(2)}) copy-start(bf16[1024,2048]{1,0:T(8,128)(2,1)} %param.35) | copy-start | bytes 12582916
  129.5 4.3 %copy-start.13 = (bf16[512,1024]{1,0:T(8,128)(2,1)}, bf16[512,1024]{1,0:T(8,128)(2,1)S(1)}, u32[]{:S(2)}) copy-start(bf16[512,1024]{1,0:T(8,128)(2,1)S(1)} %multiply_convert_fusion) | copy-start | bytes 3145732
  131.1 2.7 %collective-permute-start.5 = (bf16[2,512,512]{2,1,0:T(8,128)(2,1)S(1)}, bf16[2,512,512]{2,1,0:T(8,128)(2,1)S(1)}, u32[]{:S(2)}, u32[]{:S(2)}) collective-permute-start(bf16[2,512,512]{2,1,0:T(8,128)(2,1)S(1)} %pad_maximum_fusion.3), channel_id=1, source_target_pairs={{0,1},{1,0},{2,3},{3,2},{4,5},{5,4},{6,7},{7,6},{8,9},{9,8},{10,11... | collective-permute-start | bytes 3145736 | tf_op jit(solution)/shard_map/ppermute | solution.py:204
  133.8 1.5 copy-start.3
  135.4 19.3 %collective-permute-start.6 = (bf16[512,512]{1,0:T(8,128)(2,1)}, bf16[512,512]{1,0:T(8,128)(2,1)S(1)}, u32[]{:S(2)}, u32[]{:S(2)}) collective-permute-start(bf16[512,512]{1,0:T(8,128)(2,1)} %fusion.12), channel_id=1, source_target_pairs={{0,2},{1,3},{2,0},{3,1},{4,6},{5,7},{6,4},{7,5},{8,10},{9,11},{10,... | collective-permute-start | bytes 1572872 | tf_op jit(solution)/shard_map/ppermute | solution.py:206
  152.3 2.4 %copy-start.4 = (bf16[2,512,512]{2,1,0:T(8,128)(2,1)S(1)}, bf16[2,512,512]{2,1,0:T(8,128)(2,1)}, u32[]{:S(2)}) copy-start(bf16[2,512,512]{2,1,0:T(8,128)(2,1)} %copy-done.3) | copy-start | bytes 3145732
  156.9 29.6 %all-to-all-start.3 = ((bf16[8,127,512]{2,1,0:T(8,128)(2,1)}), bf16[8,127,512]{2,1,0:T(8,128)(2,1)S(1)}, u32[]{:S(2)}, u32[]{:S(2)}) async-start(bf16[8,127,512]{2,1,0:T(8,128)(2,1)} %broadcast_select_fusion), calls=%async_computation.3 | async-start | bytes 2097152 | tf_op jit(solution)/shard_map/all_to_all | solution.py:317

commit v14 on v13

--- a/solution.py
+++ b/solution.py
@@ -266,7 +266,7 @@
     width = residual.shape[1]
     device = lax.axis_index("req")
     devices = lax.axis_size("req")
-    bucket = (total_rows - DEC + devices - 1) // devices
+    bucket = total_rows // devices
     spread = bucket * devices
     bal = total_rows // 2
     counts = DEC + span_rows

time: 190 us -> 192 us (1.011)
  local copies, waits for them, and re-layouts: 20.2 us -> 17.8 us
  waiting for transfers between devices: 62.9 us -> 65.2 us
    reshape x3 -> x0, local copies, waits for them, and re-layouts: 2.9 us -> none  [the longest x1 1.54 us: shards(): dense_resid = got_resid.reshape(spread, width)[flat_idx]]
    gather x2, local copies, waits for them, and re-layouts: 3.91 us -> 5.98 us  [shards(): got.reshape(spread, got.shape[2])[flat_idx]]
    reshape x6 -> x3, local copies, waits for them, and re-layouts: 3.96 us -> 3.82 us  [outbound(): grid = rows[:spread].reshape(bucket, devices, rows.shape[1])]
  transfers between devices with their start and end apart: 11 -> 11, of which waited for: 8 -> 8; matrix products, arithmetic and copies ran while one was open for 14% -> 13% of each run, Pallas kernels for 13% -> 13%
where the time goes in v14:
time: 192 us; the launch traced here: 191 us
  waiting for transfers between devices  65.2 us (34%)
  starting transfers between devices  25.7 us (13%)
  Pallas kernels  24.2 us (13%)
  other arithmetic  22.3 us (12%)
  between operations  18.5 us (10%)
  local copies, waits for them, and re-layouts  17.8 us (9%)
  matrix products  17.1 us (9%)
    all_to_all x1, waiting for transfers between devices, shards(): lax.all_to_all(picked, 'req', split_axis=0, concat_axis=0, tiled=True)  24.7 us
    pallas_call x2, Pallas kernels, span_attention(): pl.pallas_call(functools.partial(span_kernel, kv_index), out_shape=jax.Sh...  24.2 us
    ppermute x1, waiting for transfers between devices, grp_all_gather(): across = lax.ppermute(block, 'grp', far)  11.6 us
    ppermute x1, waiting for transfers between devices, grp_reduce_scatter(): arrived = lax.ppermute(other.astype(jnp.bfloat16), 'grp', far)  10.2 us
    all_to_all x2, starting transfers between devices, shards(): lax.all_to_all(part, 'req', split_axis=0, concat_axis=0, tiled=True)  10 us
    all_to_all x1, starting transfers between devices, shards(): lax.all_to_all(send_resid, 'req', split_axis=0, concat_axis=0, tiled=True)  7.25 us
    all_to_all x2, waiting for transfers between devices, shards(): lax.all_to_all(part, 'req', split_axis=0, concat_axis=0, tiled=True)  6 us
    gather x2, local copies, waits for them, and re-layouts, shards(): got.reshape(spread, got.shape[2])[flat_idx]  5.98 us
  transfers between devices with their start and end apart: 11, of which 8 were waited for; matrix products, arithmetic and copies ran while one was open for 13% of the time, Pallas kernels for 13%

profile of v14, /device:TPU:0, one launch (start us, length us, event | category | flops | bytes accessed | tf_op | source)
XLA Modules:
  0.0 190.8 jit_solution(6212143585445030261)
XLA Ops:
  4.4 1.5 copy.37
  7.3 7.3 %all-to-all-start = ((bf16[8,128,512]{2,1,0:T(8,128)(2,1)}), bf16[8,128,512]{2,1,0:T(8,128)(2,1)S(1)}, u32[]{:S(2)}, u32[]{:S(2)}) async-start(bf16[8,128,512]{2,1,0:T(8,128)(2,1)} %fusion.11), calls=%async_computation | async-start | bytes 2097152 | tf_op jit(solution)/shard_map/all_to_all | solution.py:284
  15.6 1.9 %fusion.89 = (f32[8,8]{1,0:T(8,128)S(1)}, f32[8,8,4096]{2,1,0:T(8,128)S(1)}) fusion(bf16[4608,128]{1,0:T(8,128)(2,1)} %kp_ref.3, bf16[8,8,64]{2,1,0:T(8,128)(2,1)S(1)} %get-tuple-element.25, bf16[8,8,64]{2,1,0:T(8,128)(2,1)S(1)} %get-tuple-element.24, pred[8,4096]{1,0:T(8,128)(4,1)S(1)} %fusion.60), kind=kOutput, calls=%fused_computation.188 | convolution fusion | flops 67928000 | bytes 2146560 | tf_op jit(solution)/shard_map/rhc,tc->rht/dot_general | solution.py:113
  20.3 12.1 %shard_map.154 = bf16[1024,256]{1,0:T(8,128)(2,1)} custom-call(s32[1]{0:T(128)S(6)} %copy.56.start_ref, bf16[1024,512]{1,0:T(8,128)(2,1)} %q_ref.2, bf16[4608,128]{1,0:T(8,128)(2,1)} %kp_ref.3, bf16[4608,128]{1,0:T(8,128)(2,1)} %vp_ref.3, bf16[1024,128]{1,0:T(8,128)(2,1)} %kf_ref.3, bf16[1024,128]{1,0:T(8,128)(2,1)} %vf_ref.3), custom_call_target="tpu_custom_call" | custom-call | flops 17179869184 | bytes 1835008 | tf_op jit(solution)/shard_map/pallas_call | solution.py:89
  35.2 5.2 %all-to-all-done = bf16[8,128,512]{2,1,0:T(8,128)(2,1)S(1)} async-done(((bf16[8,128,512]{2,1,0:T(8,128)(2,1)}), bf16[8,128,512]{2,1,0:T(8,128)(2,1)S(1)}, u32[]{:S(2)}, u32[]{:S(2)}) %all-to-all-start) | async-done | bytes 1048608 | tf_op jit(solution)/shard_map/all_to_all | solution.py:284
  40.4 4.3 %all-to-all-start.1 = ((bf16[8,128,256]{2,1,0:T(8,128)(2,1)}), bf16[8,128,256]{2,1,0:T(8,128)(2,1)}, u32[]{:S(2)}, u32[]{:S(2)}) async-start(bf16[8,128,256]{2,1,0:T(8,128)(2,1)} %fusion.36), calls=%async_computation.1 | async-start | bytes 1048576 | tf_op jit(solution)/shard_map/all_to_all | solution.py:291
  44.7 12.1 %shard_map.155 = bf16[1024,256]{1,0:T(8,128)(2,1)} custom-call(s32[1]{0:T(128)S(6)} %copy.56.start_ref, bf16[1024,512]{1,0:T(8,128)(2,1)} %q_ref.2, bf16[4608,128]{1,0:T(8,128)(2,1)} %kp_ref.3, bf16[4608,128]{1,0:T(8,128)(2,1)} %vp_ref.3, bf16[1024,128]{1,0:T(8,128)(2,1)} %kf_ref.3, bf16[1024,128]{1,0:T(8,128)(2,1)} %vf_ref.3), custom_call_target="tpu_custom_call" | custom-call | flops 17179869184 | bytes 1835008 | tf_op jit(solution)/shard_map/pallas_call | solution.py:89
  59.6 5.7 %all-to-all-start.2 = ((bf16[8,128,256]{2,1,0:T(8,128)(2,1)}), bf16[8,128,256]{2,1,0:T(8,128)(2,1)}, u32[]{:S(2)}, u32[]{:S(2)}) async-start(bf16[8,128,256]{2,1,0:T(8,128)(2,1)} %fusion.34), calls=%async_computation.2 | async-start | bytes 1048576 | tf_op jit(solution)/shard_map/all_to_all | solution.py:291
  65.4 4.4 %compare_select_fusion.2 = s32[512,1]{0,1:T(1,128)S(1)} fusion(s32[]{:T(128)} %bitcast.17, s32[]{:T(128)} %bitcast.18, s32[]{:T(128)} %bitcast.19, s32[]{:T(128)} %bitcast.20, s32[]{:T(128)} %bitcast.21, s32[]{:T(128)} %bitcast.23, s32[]{:T(128)} %bitcast.22, s32[512,1]{0,1:T(1,128)S(1)} %bitcast.145), kind=kLoop, calls=%fused_computation.137 | loop fusion | flops 7680 | bytes 4124 | tf_op jit(solution)/shard_map/gather | solution.py:299
  70.4 2.7 %gather_fusion.1 = bf16[512,256]{1,0:T(8,128)(2,1)S(1)} fusion(bf16[1024,256]{1,0:T(8,128)(2,1)} %bitcast.27, s32[1024]{0:T(1024)S(1)} %pad_clamp_fusion), kind=kCustom, calls=%fused_computation.1 | custom fusion | bytes 526336 | tf_op jit(solution)/shard_map/gather | solution.py:302
  73.1 6.0 %all-to-all-done.2 = bf16[8,128,256]{2,1,0:T(8,128)(2,1)} async-done(((bf16[8,128,256]{2,1,0:T(8,128)(2,1)}), bf16[8,128,256]{2,1,0:T(8,128)(2,1)}, u32[]{:S(2)}, u32[]{:S(2)}) %all-to-all-start.2) | async-done | bytes 524320 | tf_op jit(solution)/shard_map/all_to_all | solution.py:291
  79.1 3.3 %gather_fusion.2 = bf16[512,256]{1,0:T(8,128)(2,1)} fusion(bf16[1024,256]{1,0:T(8,128)(2,1)} %bitcast.28, s32[1024]{0:T(1024)S(1)} %pad_clamp_fusion), kind=kCustom, calls=%fused_computation.2 | custom fusion | bytes 526336 | tf_op jit(solution)/shard_map/gather | solution.py:302
  82.4 2.2 %convolution_convert_fusion = bf16[512,2048]{1,0:T(8,128)(2,1)S(1)} fusion(bf16[512,2048]{1,0:T(8,128)(2,1)S(1)} %copy-done, bf16[512,256]{1,0:T(8,128)(2,1)} %gather_fusion.2, bf16[512,256]{1,0:T(8,128)(2,1)S(1)} %gather_fusion.1), kind=kOutput, calls=%fused_computation.10 | convolution fusion | flops 1075838976 | bytes 4718592 | tf_op jit(solution)/shard_map/dot_general | solution.py:227
  86.3 3.0 %collective-permute-done = bf16[2,512,512]{2,1,0:T(8,128)(2,1)} collective-permute-done((bf16[2,512,512]{2,1,0:T(8,128)(2,1)}, bf16[2,512,512]{2,1,0:T(8,128)(2,1)}, u32[]{:S(2)}, u32[]{:S(2)}) %collective-permute-start) | collective-permute-done | bytes 1048608 | tf_op jit(solution)/shard_map/ppermute | solution.py:185
  89.3 2.1 %fusion.16 = bf16[512,512]{1,0:T(8,128)(2,1)} fusion(bf16[2,512,512]{2,1,0:T(8,128)(2,1)} %collective-permute-done, bf16[512,2048]{1,0:T(8,128)(2,1)} %copy-done.1, s32[]{:T(128)S(6)} %select_n.208), kind=kLoop, calls=%fused_computation.45 | loop fusion | flops 1048576 | bytes 1572868 | tf_op jit(solution)/shard_map/convert_element_type | solution.py:190
  91.4 1.5 collective-permute-start.1
  92.9 2.6 %gather_fusion = bf16[512,512]{1,0:T(8,128)(2,1)} fusion(bf16[1024,512]{1,0:T(8,128)(2,1)S(1)} %bitcast.137, s32[1024]{0:T(1024)S(1)} %pad_clamp_fusion), kind=kCustom, calls=%fused_computation | custom fusion | bytes 1050624 | tf_op jit(solution)/shard_map/gather | solution.py:304
  95.5 10.2 %collective-permute-done.1 = bf16[512,512]{1,0:T(8,128)(2,1)} collective-permute-done((bf16[512,512]{1,0:T(8,128)(2,1)}, bf16[512,512]{1,0:T(8,128)(2,1)}, u32[]{:S(2)}, u32[]{:S(2)}) %collective-permute-start.1) | collective-permute-done | bytes 524320 | tf_op jit(solution)/shard_map/ppermute | solution.py:190
  105.7 1.8 fusion.19
  107.5 1.6 collective-permute-start.3
  109.1 11.6 %collective-permute-done.3 = bf16[512,512]{1,0:T(8,128)(2,1)S(1)} collective-permute-done((bf16[512,512]{1,0:T(8,128)(2,1)S(1)}, bf16[512,512]{1,0:T(8,128)(2,1)S(1)}, u32[]{:S(2)}, u32[]{:S(2)}) %collective-permute-start.3) | collective-permute-done | bytes 524320 | tf_op jit(solution)/shard_map/ppermute | solution.py:219
  120.7 2.0 %collective-permute-done.4 = bf16[512,512]{1,0:T(8,128)(2,1)} collective-permute-done((bf16[512,512]{1,0:T(8,128)(2,1)S(1)}, bf16[512,512]{1,0:T(8,128)(2,1)}, u32[]{:S(2)}, u32[]{:S(2)}) %collective-permute-start.4) | collective-permute-done | bytes 524320 | tf_op jit(solution)/shard_map/ppermute | solution.py:220
  124.9 1.5 copy-done.7
  126.4 2.4 %fusion.31 = f32[512,1024]{1,0:T(8,128)S(1)} fusion(bf16[2048,1024]{1,0:T(8,128)(2,1)S(1)} %copy-done.7, f32[2048]{0:T(1024)S(1)} %copy-done.11, f32[512]{0:T(512)S(1)} %add_rsqrt_fusion, bf16[512,512]{1,0:T(8,128)(2,1)S(1)} %get-tuple-element.19, bf16[512,512]{1,0:T(8,128)(2,1)S(1)} %get-tuple-element.20, bf16[512,512]{1,0:T(8,128)(2,1)S(1)} %get-tuple-element.21, ...), kind=kOutput, calls=%fused_computation.64 | convolution fusion | flops 2159017984 | bytes 8398848 | tf_op jit(solution)/shard_map/dot_general | solution.py:235
  128.8 3.0 %multiply_convert_fusion = bf16[512,1024]{1,0:T(8,128)(2,1)S(1)} fusion(f32[512,1024]{1,0:T(8,128)S(1)} %fusion.31, bf16[2048,1024]{1,0:T(8,128)(2,1)S(1)} %copy-done.8, f32[2048]{0:T(1024)S(1)} %copy-done.11, f32[512]{0:T(512)S(1)} %add_rsqrt_fusion, bf16[512,512]{1,0:T(8,128)(2,1)S(1)} %get-tuple-element.19, bf16[512,512]{1,0:T(8,128)(2,1)S(1)} %get-tuple-element.20, ...), kind=kOutput, calls=%fused_computation.17 | convolution fusion | flops 2162163712 | bytes 9447424 | tf_op jit(solution)/shard_map/dot_general | solution.py:236
  133.6 2.5 %collective-permute-done.5 = bf16[2,512,512]{2,1,0:T(8,128)(2,1)S(1)} collective-permute-done((bf16[2,512,512]{2,1,0:T(8,128)(2,1)S(1)}, bf16[2,512,512]{2,1,0:T(8,128)(2,1)S(1)}, u32[]{:S(2)}, u32[]{:S(2)}) %collective-permute-start.5) | collective-permute-done | bytes 1048608 | tf_op jit(solution)/shard_map/ppermute | solution.py:204
  136.1 1.5 fusion.12
  137.7 1.5 collective-permute-start.6
  154.7 2.3 %fusion.5 = f32[512,512]{1,0:T(8,128)S(1)} fusion(bf16[512,1024]{1,0:T(8,128)(2,1)} %copy-done.12, bf16[1024,2048]{1,0:T(8,128)(2,1)} %param.35, s32[]{:T(128)S(6)} %select_n.205), kind=kOutput, calls=%fused_computation.23 | convolution fusion | flops 537395200 | bytes 3145732 | tf_op jit(solution)/shard_map/dot_general | solution.py:239
  159.3 3.6 %all-to-all-start.3 = ((bf16[8,128,512]{2,1,0:T(8,128)(2,1)}), bf16[8,128,512]{2,1,0:T(8,128)(2,1)S(1)}, u32[]{:S(2)}, u32[]{:S(2)}) async-start(bf16[8,128,512]{2,1,0:T(8,128)(2,1)} %broadcast_select_fusion), calls=%async_computation.3 | async-start | bytes 2097152 | tf_op jit(solution)/shard_map/all_to_all | solution.py:317
  164.2 24.7 %all-to-all-done.3 = bf16[8,128,512]{2,1,0:T(8,128)(2,1)S(1)} async-done(((bf16[8,128,512]{2,1,0:T(8,128)(2,1)}), bf16[8,128,512]{2,1,0:T(8,128)(2,1)S(1)}, u32[]{:S(2)}, u32[]{:S(2)}) %all-to-all-start.3) | async-done | bytes 1048608 | tf_op jit(solution)/shard_map/all_to_all | solution.py:317
  189.2 1.6 bitcast_select_fusion
  (91 shorter events, 22.5 us)
Async XLA Ops:
  0.0 82.4 %copy-start = (bf16[512,2048]{1,0:T(8,128)(2,1)S(1)}, bf16[512,2048]{1,0:T(8,128)(2,1)}, u32[]{:S(2)}) copy-start(bf16[512,2048]{1,0:T(8,128)(2,1)} %param.31) | copy-start | bytes 6291460
  5.9 9.3 %slice-start = ((bf16[1024,512]{1,0:T(8,128)(2,1)}), bf16[8,512]{1,0:T(8,128)(2,1)S(1)}, s32[]{:S(2)}) async-start(bf16[1024,512]{1,0:T(8,128)(2,1)} %q_ref.2), calls=%async_computation.4 | async-start | bytes 16384 | tf_op jit(solution)/shard_map/slice | solution.py:107
  5.9 9.5 %copy-start.4 = (s32[8]{0:T(128)S(1)}, s32[8]{0:T(128)}, u32[]{:S(2)}) copy-start(s32[8]{0:T(128)} %param.26) | copy-start | bytes 100
  6.0 9.5 %copy-start.5 = (s32[8]{0:T(128)S(1)}, s32[8]{0:T(128)}, u32[]{:S(2)}) copy-start(s32[8]{0:T(128)} %param.27) | copy-start | bytes 100
  6.0 9.5 %copy-start.6 = (s32[8]{0:T(128)S(1)}, s32[8]{0:T(128)}, u32[]{:S(2)}) copy-start(s32[8]{0:T(128)} %param.28) | copy-start | bytes 100
  7.3 33.0 %all-to-all-start = ((bf16[8,128,512]{2,1,0:T(8,128)(2,1)}), bf16[8,128,512]{2,1,0:T(8,128)(2,1)S(1)}, u32[]{:S(2)}, u32[]{:S(2)}) async-start(bf16[8,128,512]{2,1,0:T(8,128)(2,1)} %fusion.11), calls=%async_computation | async-start | bytes 2097152 | tf_op jit(solution)/shard_map/all_to_all | solution.py:284
  15.4 3.5 %copy-start.10 = (bf16[4608,128]{1,0:T(8,128)(2,1)S(1)}, bf16[4608,128]{1,0:T(8,128)(2,1)}, u32[]{:S(2)}) copy-start(bf16[4608,128]{1,0:T(8,128)(2,1)} %vp_ref.3) | copy-start | bytes 3538948
  40.4 19.3 %all-to-all-start.1 = ((bf16[8,128,256]{2,1,0:T(8,128)(2,1)}), bf16[8,128,256]{2,1,0:T(8,128)(2,1)}, u32[]{:S(2)}, u32[]{:S(2)}) async-start(bf16[8,128,256]{2,1,0:T(8,128)(2,1)} %fusion.36), calls=%async_computation.1 | async-start | bytes 1048576 | tf_op jit(solution)/shard_map/all_to_all | solution.py:291
  59.6 19.5 %all-to-all-start.2 = ((bf16[8,128,256]{2,1,0:T(8,128)(2,1)}), bf16[8,128,256]{2,1,0:T(8,128)(2,1)}, u32[]{:S(2)}, u32[]{:S(2)}) async-start(bf16[8,128,256]{2,1,0:T(8,128)(2,1)} %fusion.34), calls=%async_computation.2 | async-start | bytes 1048576 | tf_op jit(solution)/shard_map/all_to_all | solution.py:291
  84.6 1.7 copy-start.1
  86.3 3.0 %collective-permute-start = (bf16[2,512,512]{2,1,0:T(8,128)(2,1)}, bf16[2,512,512]{2,1,0:T(8,128)(2,1)}, u32[]{:S(2)}, u32[]{:S(2)}) collective-permute-start(bf16[2,512,512]{2,1,0:T(8,128)(2,1)} %pad_maximum_fusion.2), channel_id=1, source_target_pairs={{0,1},{1,0},{2,3},{3,2},{4,5},{5,4},{6,7},{7,6},{8,9},{9,8},{10,11... | collective-permute-start | bytes 3145736 | tf_op jit(solution)/shard_map/ppermute | solution.py:185
  91.4 14.3 %collective-permute-start.1 = (bf16[512,512]{1,0:T(8,128)(2,1)}, bf16[512,512]{1,0:T(8,128)(2,1)}, u32[]{:S(2)}, u32[]{:S(2)}) collective-permute-start(bf16[512,512]{1,0:T(8,128)(2,1)} %fusion.16), channel_id=1, source_target_pairs={{0,2},{1,3},{2,0},{3,1},{4,6},{5,7},{6,4},{7,5},{8,10},{9,11},{10,... | collective-permute-start | bytes 1572872 | tf_op jit(solution)/shard_map/ppermute | solution.py:190
  107.5 13.2 %collective-permute-start.3 = (bf16[512,512]{1,0:T(8,128)(2,1)S(1)}, bf16[512,512]{1,0:T(8,128)(2,1)S(1)}, u32[]{:S(2)}, u32[]{:S(2)}) collective-permute-start(bf16[512,512]{1,0:T(8,128)(2,1)S(1)} %fusion.19), channel_id=1, source_target_pairs={{0,2},{1,3},{2,0},{3,1},{4,6},{5,7},{6,4},{7,5},{8,10},{9,11},{10,... | collective-permute-start | bytes 1572872 | tf_op jit(solution)/shard_map/ppermute | solution.py:219
  109.1 11.6 %collective-permute-start.2 = (bf16[512,512]{1,0:T(8,128)(2,1)S(1)}, bf16[512,512]{1,0:T(8,128)(2,1)}, u32[]{:S(2)}, u32[]{:S(2)}) collective-permute-start(bf16[512,512]{1,0:T(8,128)(2,1)S(1)} %fusion.19), channel_id=1, source_target_pairs={{0,1},{1,0},{2,3},{3,2},{4,5},{5,4},{6,7},{7,6},{8,9},{9,8},{10,11... | collective-permute-start | bytes 1572872 | tf_op jit(solution)/shard_map/ppermute | solution.py:218
  120.7 2.0 %collective-permute-start.4 = (bf16[512,512]{1,0:T(8,128)(2,1)S(1)}, bf16[512,512]{1,0:T(8,128)(2,1)}, u32[]{:S(2)}, u32[]{:S(2)}) collective-permute-start(bf16[512,512]{1,0:T(8,128)(2,1)S(1)} %collective-permute-done.3), channel_id=1, source_target_pairs={{0,1},{1,0},{2,3},{3,2},{4,5},{5,4},{6,7},{7,6},{8,9},{9,8},{10,11... | collective-permute-start | bytes 1572872 | tf_op jit(solution)/shard_map/ppermute | solution.py:220
  124.2 2.2 %copy-start.7 = (bf16[2048,1024]{1,0:T(8,128)(2,1)S(1)}, bf16[2048,1024]{1,0:T(8,128)(2,1)}, u32[]{:S(2)}) copy-start(bf16[2048,1024]{1,0:T(8,128)(2,1)} %param.33) | copy-start | bytes 12582916
  124.4 2.0 %copy-start.11 = (f32[2048]{0:T(1024)S(1)}, f32[2048]{0:T(1024)}, u32[]{:S(2)}) copy-start(f32[2048]{0:T(1024)} %param.32) | copy-start | bytes 24580
  126.4 2.4 %copy-start.8 = (bf16[2048,1024]{1,0:T(8,128)(2,1)S(1)}, bf16[2048,1024]{1,0:T(8,128)(2,1)}, u32[]{:S(2)}) copy-start(bf16[2048,1024]{1,0:T(8,128)(2,1)} %param.34) | copy-start | bytes 12582916
  128.8 3.0 %copy-start.9 = (bf16[1024,2048]{1,0:T(8,128)(2,1)S(1)}, bf16[1024,2048]{1,0:T(8,128)(2,1)}, u32[]{:S(2)}) copy-start(bf16[1024,2048]{1,0:T(8,128)(2,1)} %param.35) | copy-start | bytes 12582916
  131.8 4.3 %copy-start.12 = (bf16[512,1024]{1,0:T(8,128)(2,1)}, bf16[512,1024]{1,0:T(8,128)(2,1)S(1)}, u32[]{:S(2)}) copy-start(bf16[512,1024]{1,0:T(8,128)(2,1)S(1)} %multiply_convert_fusion) | copy-start | bytes 3145732
  133.4 2.7 %collective-permute-start.5 = (bf16[2,512,512]{2,1,0:T(8,128)(2,1)S(1)}, bf16[2,512,512]{2,1,0:T(8,128)(2,1)S(1)}, u32[]{:S(2)}, u32[]{:S(2)}) collective-permute-start(bf16[2,512,512]{2,1,0:T(8,128)(2,1)S(1)} %pad_maximum_fusion.3), channel_id=1, source_target_pairs={{0,1},{1,0},{2,3},{3,2},{4,5},{5,4},{6,7},{7,6},{8,9},{9,8},{10,11... | collective-permute-start | bytes 3145736 | tf_op jit(solution)/shard_map/ppermute | solution.py:204
  136.1 1.5 copy-start.2
  137.7 19.4 %collective-permute-start.6 = (bf16[512,512]{1,0:T(8,128)(2,1)}, bf16[512,512]{1,0:T(8,128)(2,1)S(1)}, u32[]{:S(2)}, u32[]{:S(2)}) collective-permute-start(bf16[512,512]{1,0:T(8,128)(2,1)} %fusion.12), channel_id=1, source_target_pairs={{0,2},{1,3},{2,0},{3,1},{4,6},{5,7},{6,4},{7,5},{8,10},{9,11},{10,... | collective-permute-start | bytes 1572872 | tf_op jit(solution)/shard_map/ppermute | solution.py:206
  154.7 2.4 %copy-start.3 = (bf16[2,512,512]{2,1,0:T(8,128)(2,1)S(1)}, bf16[2,512,512]{2,1,0:T(8,128)(2,1)}, u32[]{:S(2)}) copy-start(bf16[2,512,512]{2,1,0:T(8,128)(2,1)} %copy-done.2) | copy-start | bytes 3145732
  159.3 29.6 %all-to-all-start.3 = ((bf16[8,128,512]{2,1,0:T(8,128)(2,1)}), bf16[8,128,512]{2,1,0:T(8,128)(2,1)S(1)}, u32[]{:S(2)}, u32[]{:S(2)}) async-start(bf16[8,128,512]{2,1,0:T(8,128)(2,1)} %broadcast_select_fusion), calls=%async_computation.3 | async-start | bytes 2097152 | tf_op jit(solution)/shard_map/all_to_all | solution.py:317

commit v15 on v13

--- a/solution.py
+++ b/solution.py
@@ -320,8 +320,7 @@
         restored = jnp.concatenate(
             [restored, jnp.zeros((total_rows - spread, width), restored.dtype)], axis=0
         )
-    is_live = jnp.arange(total_rows, dtype=jnp.int32) < own_count
-    return jnp.where(is_live[:, None], restored, jnp.zeros((), jnp.bfloat16))
+    return restored
 
 
 def solution(mesh):

time: 190 us -> 190 us (level)
  no operation moved by 1% of the time
where the time goes in v15:
time: 190 us; the launch traced here: 188 us
  waiting for transfers between devices  64 us (34%)
  starting transfers between devices  25.7 us (14%)
  Pallas kernels  24.2 us (13%)
  local copies, waits for them, and re-layouts  20.7 us (11%)
  other arithmetic  19 us (10%)
  between operations  18.5 us (10%)
  matrix products  16.4 us (9%)
    all_to_all x1, waiting for transfers between devices, shards(): lax.all_to_all(picked, 'req', split_axis=0, concat_axis=0, tiled=True)  25.9 us
    pallas_call x2, Pallas kernels, span_attention(): pl.pallas_call(functools.partial(span_kernel, kv_index), out_shape=jax.Sh...  24.2 us
    ppermute x1, waiting for transfers between devices, grp_all_gather(): across = lax.ppermute(block, 'grp', far)  11.6 us
    all_to_all x2, starting transfers between devices, shards(): lax.all_to_all(part, 'req', split_axis=0, concat_axis=0, tiled=True)  10 us
    ppermute x1, waiting for transfers between devices, grp_reduce_scatter(): arrived = lax.ppermute(other.astype(jnp.bfloat16), 'grp', far)  8.6 us
    all_to_all x1, starting transfers between devices, shards(): lax.all_to_all(send_resid, 'req', split_axis=0, concat_axis=0, tiled=True)  7.25 us
    all_to_all x2, waiting for transfers between devices, shards(): lax.all_to_all(part, 'req', split_axis=0, concat_axis=0, tiled=True)  5.36 us
    dot_general x4, matrix products, finish(): jnp.dot(inner, grp_block(down_weight, index, width), preferred_element_ty...  5.32 us
  transfers between devices with their start and end apart: 11, of which 8 were waited for; matrix products, arithmetic and copies ran while one was open for 14% of the time, Pallas kernels for 13%

profile of v15, /device:TPU:0, one launch (start us, length us, event | category | flops | bytes accessed | tf_op | source)
XLA Modules:
  0.0 188.5 jit_solution(13024616026305419144)
XLA Ops:
  6.0 1.4 fusion.11
  7.4 7.3 %all-to-all-start = ((bf16[8,127,512]{2,1,0:T(8,128)(2,1)}), bf16[8,127,512]{2,1,0:T(8,128)(2,1)S(1)}, u32[]{:S(2)}, u32[]{:S(2)}) async-start(bf16[8,127,512]{2,1,0:T(8,128)(2,1)} %fusion.11), calls=%async_computation | async-start | bytes 2097152 | tf_op jit(solution)/shard_map/all_to_all | solution.py:284
  16.7 1.8 fusion.89
  20.4 12.1 %shard_map.154 = bf16[1024,256]{1,0:T(8,128)(2,1)} custom-call(s32[1]{0:T(128)S(6)} %copy.51.start_ref, bf16[1024,512]{1,0:T(8,128)(2,1)} %q_ref.2, bf16[4608,128]{1,0:T(8,128)(2,1)} %kp_ref.3, bf16[4608,128]{1,0:T(8,128)(2,1)} %vp_ref.3, bf16[1024,128]{1,0:T(8,128)(2,1)} %kf_ref.3, bf16[1024,128]{1,0:T(8,128)(2,1)} %vf_ref.3), custom_call_target="tpu_custom_call" | custom-call | flops 17179869184 | bytes 1835008 | tf_op jit(solution)/shard_map/pallas_call | solution.py:89
  35.3 5.2 %all-to-all-done = bf16[8,127,512]{2,1,0:T(8,128)(2,1)S(1)} async-done(((bf16[8,127,512]{2,1,0:T(8,128)(2,1)}), bf16[8,127,512]{2,1,0:T(8,128)(2,1)S(1)}, u32[]{:S(2)}, u32[]{:S(2)}) %all-to-all-start) | async-done | bytes 1040416 | tf_op jit(solution)/shard_map/all_to_all | solution.py:284
  40.4 4.3 %all-to-all-start.1 = ((bf16[8,127,256]{2,1,0:T(8,128)(2,1)}), bf16[8,127,256]{2,1,0:T(8,128)(2,1)}, u32[]{:S(2)}, u32[]{:S(2)}) async-start(bf16[8,127,256]{2,1,0:T(8,128)(2,1)} %fusion.36), calls=%async_computation.1 | async-start | bytes 1048576 | tf_op jit(solution)/shard_map/all_to_all | solution.py:291
  44.8 12.1 %shard_map.155 = bf16[1024,256]{1,0:T(8,128)(2,1)} custom-call(s32[1]{0:T(128)S(6)} %copy.51.start_ref, bf16[1024,512]{1,0:T(8,128)(2,1)} %q_ref.2, bf16[4608,128]{1,0:T(8,128)(2,1)} %kp_ref.3, bf16[4608,128]{1,0:T(8,128)(2,1)} %vp_ref.3, bf16[1024,128]{1,0:T(8,128)(2,1)} %kf_ref.3, bf16[1024,128]{1,0:T(8,128)(2,1)} %vf_ref.3), custom_call_target="tpu_custom_call" | custom-call | flops 17179869184 | bytes 1835008 | tf_op jit(solution)/shard_map/pallas_call | solution.py:89
  59.8 5.7 %all-to-all-start.2 = ((bf16[8,127,256]{2,1,0:T(8,128)(2,1)}), bf16[8,127,256]{2,1,0:T(8,128)(2,1)S(1)}, u32[]{:S(2)}, u32[]{:S(2)}) async-start(bf16[8,127,256]{2,1,0:T(8,128)(2,1)} %fusion.34), calls=%async_computation.2 | async-start | bytes 1048576 | tf_op jit(solution)/shard_map/all_to_all | solution.py:291
  65.5 4.4 %compare_select_fusion.2 = s32[512,1]{0,1:T(1,128)S(1)} fusion(s32[]{:T(128)} %bitcast.15, s32[]{:T(128)} %bitcast.16, s32[]{:T(128)} %bitcast.17, s32[]{:T(128)} %bitcast.18, s32[]{:T(128)} %bitcast.19, s32[]{:T(128)} %bitcast.21, s32[]{:T(128)} %bitcast.20, s32[512,1]{0,1:T(1,128)S(1)} %bitcast.142), kind=kLoop, calls=%fused_computation.140 | loop fusion | flops 7680 | bytes 4124 | tf_op jit(solution)/shard_map/gather | solution.py:299
  71.8 2.0 %gather_fusion.1 = bf16[512,256]{1,0:T(8,128)(2,1)S(1)} fusion(bf16[1016,256]{1,0:T(8,128)(2,1)S(1)} %reshape.397, s32[1024]{0:T(1024)S(1)} %pad_clamp_fusion), kind=kCustom, calls=%fused_computation.1 | custom fusion | bytes 526336 | tf_op jit(solution)/shard_map/gather | solution.py:302
  73.8 5.4 %all-to-all-done.2 = bf16[8,127,256]{2,1,0:T(8,128)(2,1)S(1)} async-done(((bf16[8,127,256]{2,1,0:T(8,128)(2,1)}), bf16[8,127,256]{2,1,0:T(8,128)(2,1)S(1)}, u32[]{:S(2)}, u32[]{:S(2)}) %all-to-all-start.2) | async-done | bytes 520224 | tf_op jit(solution)/shard_map/all_to_all | solution.py:291
  79.3 2.0 %gather_fusion.2 = bf16[512,256]{1,0:T(8,128)(2,1)S(1)} fusion(bf16[1016,256]{1,0:T(8,128)(2,1)S(1)} %reshape.398, s32[1024]{0:T(1024)S(1)} %pad_clamp_fusion), kind=kCustom, calls=%fused_computation.2 | custom fusion | bytes 526336 | tf_op jit(solution)/shard_map/gather | solution.py:302
  83.9 2.8 %collective-permute-done = bf16[2,512,512]{2,1,0:T(8,128)(2,1)} collective-permute-done((bf16[2,512,512]{2,1,0:T(8,128)(2,1)S(1)}, bf16[2,512,512]{2,1,0:T(8,128)(2,1)}, u32[]{:S(2)}, u32[]{:S(2)}) %collective-permute-start) | collective-permute-done | bytes 1048608 | tf_op jit(solution)/shard_map/ppermute | solution.py:185
  86.7 2.1 %fusion.16 = bf16[512,512]{1,0:T(8,128)(2,1)} fusion(bf16[2,512,512]{2,1,0:T(8,128)(2,1)} %collective-permute-done, bf16[512,2048]{1,0:T(8,128)(2,1)} %copy-done.2, s32[]{:T(128)S(6)} %select_n.203), kind=kLoop, calls=%fused_computation.45 | loop fusion | flops 1048576 | bytes 1572868 | tf_op jit(solution)/shard_map/convert_element_type | solution.py:190
  88.8 1.5 collective-permute-start.1
  90.3 1.5 reshape.396
  91.9 2.6 %gather_fusion = bf16[512,512]{1,0:T(8,128)(2,1)} fusion(bf16[1016,512]{1,0:T(8,128)(2,1)S(1)} %reshape.396, s32[1024]{0:T(1024)S(1)} %pad_clamp_fusion), kind=kCustom, calls=%fused_computation | custom fusion | bytes 1050624 | tf_op jit(solution)/shard_map/gather | solution.py:304
  94.5 8.6 %collective-permute-done.1 = bf16[512,512]{1,0:T(8,128)(2,1)} collective-permute-done((bf16[512,512]{1,0:T(8,128)(2,1)}, bf16[512,512]{1,0:T(8,128)(2,1)}, u32[]{:S(2)}, u32[]{:S(2)}) %collective-permute-start.1) | collective-permute-done | bytes 524320 | tf_op jit(solution)/shard_map/ppermute | solution.py:190
  103.1 1.8 fusion.19
  104.9 1.6 collective-permute-start.3
  106.5 11.6 %collective-permute-done.3 = bf16[512,512]{1,0:T(8,128)(2,1)S(1)} collective-permute-done((bf16[512,512]{1,0:T(8,128)(2,1)S(1)}, bf16[512,512]{1,0:T(8,128)(2,1)S(1)}, u32[]{:S(2)}, u32[]{:S(2)}) %collective-permute-start.3) | collective-permute-done | bytes 524320 | tf_op jit(solution)/shard_map/ppermute | solution.py:219
  118.1 2.0 %collective-permute-done.4 = bf16[512,512]{1,0:T(8,128)(2,1)} collective-permute-done((bf16[512,512]{1,0:T(8,128)(2,1)S(1)}, bf16[512,512]{1,0:T(8,128)(2,1)}, u32[]{:S(2)}, u32[]{:S(2)}) %collective-permute-start.4) | collective-permute-done | bytes 524320 | tf_op jit(solution)/shard_map/ppermute | solution.py:220
  120.1 1.5 pad_maximum_fusion
  122.3 1.5 copy-done.8
  123.8 2.4 %fusion.31 = f32[512,1024]{1,0:T(8,128)S(1)} fusion(bf16[2048,1024]{1,0:T(8,128)(2,1)S(1)} %copy-done.8, f32[2048]{0:T(1024)S(1)} %copy-done.12, f32[512]{0:T(512)S(1)} %add_rsqrt_fusion, bf16[512,512]{1,0:T(8,128)(2,1)S(1)} %get-tuple-element.19, bf16[512,512]{1,0:T(8,128)(2,1)S(1)} %get-tuple-element.20, bf16[512,512]{1,0:T(8,128)(2,1)S(1)} %get-tuple-element.21, ...), kind=kOutput, calls=%fused_computation.65 | convolution fusion | flops 2159017984 | bytes 8398848 | tf_op jit(solution)/shard_map/dot_general | solution.py:235
  126.2 3.3 %multiply_convert_fusion = bf16[512,1024]{1,0:T(8,128)(2,1)S(1)} fusion(f32[512,1024]{1,0:T(8,128)S(1)} %fusion.31, bf16[2048,1024]{1,0:T(8,128)(2,1)S(1)} %copy-done.9, f32[2048]{0:T(1024)S(1)} %copy-done.12, f32[512]{0:T(512)S(1)} %add_rsqrt_fusion, bf16[512,512]{1,0:T(8,128)(2,1)S(1)} %get-tuple-element.19, bf16[512,512]{1,0:T(8,128)(2,1)S(1)} %get-tuple-element.20, ...), kind=kOutput, calls=%fused_computation.17 | convolution fusion | flops 2162163712 | bytes 9447424 | tf_op jit(solution)/shard_map/dot_general | solution.py:236
  131.3 2.5 %collective-permute-done.5 = bf16[2,512,512]{2,1,0:T(8,128)(2,1)S(1)} collective-permute-done((bf16[2,512,512]{2,1,0:T(8,128)(2,1)S(1)}, bf16[2,512,512]{2,1,0:T(8,128)(2,1)S(1)}, u32[]{:S(2)}, u32[]{:S(2)}) %collective-permute-start.5) | collective-permute-done | bytes 1048608 | tf_op jit(solution)/shard_map/ppermute | solution.py:204
  133.8 1.5 fusion.12
  135.4 1.5 collective-permute-start.6
  152.3 2.3 %fusion.5 = f32[512,512]{1,0:T(8,128)S(1)} fusion(bf16[512,1024]{1,0:T(8,128)(2,1)} %copy-done.13, bf16[1024,2048]{1,0:T(8,128)(2,1)} %param.35, s32[]{:T(128)S(6)} %select_n.200), kind=kOutput, calls=%fused_computation.23 | convolution fusion | flops 537395200 | bytes 3145732 | tf_op jit(solution)/shard_map/dot_general | solution.py:239
  156.9 3.6 %all-to-all-start.3 = ((bf16[8,127,512]{2,1,0:T(8,128)(2,1)}), bf16[8,127,512]{2,1,0:T(8,128)(2,1)S(1)}, u32[]{:S(2)}, u32[]{:S(2)}) async-start(bf16[8,127,512]{2,1,0:T(8,128)(2,1)} %broadcast_select_fusion), calls=%async_computation.3 | async-start | bytes 2097152 | tf_op jit(solution)/shard_map/all_to_all | solution.py:317
  160.6 25.9 %all-to-all-done.3 = bf16[8,127,512]{2,1,0:T(8,128)(2,1)S(1)} async-done(((bf16[8,127,512]{2,1,0:T(8,128)(2,1)}), bf16[8,127,512]{2,1,0:T(8,128)(2,1)S(1)}, u32[]{:S(2)}, u32[]{:S(2)}) %all-to-all-start.3) | async-done | bytes 1040416 | tf_op jit(solution)/shard_map/all_to_all | solution.py:317
  (98 shorter events, 24.2 us)
Async XLA Ops:
  0.0 81.3 %copy-start = (bf16[512,2048]{1,0:T(8,128)(2,1)S(1)}, bf16[512,2048]{1,0:T(8,128)(2,1)}, u32[]{:S(2)}) copy-start(bf16[512,2048]{1,0:T(8,128)(2,1)} %param.31) | copy-start | bytes 6291460
  6.0 9.4 %slice-start = ((bf16[1024,512]{1,0:T(8,128)(2,1)}), bf16[8,512]{1,0:T(8,128)(2,1)S(1)}, s32[]{:S(2)}) async-start(bf16[1024,512]{1,0:T(8,128)(2,1)} %q_ref.2), calls=%async_computation.4 | async-start | bytes 16384 | tf_op jit(solution)/shard_map/slice | solution.py:107
  6.0 10.6 %copy-start.5 = (s32[8]{0:T(128)S(1)}, s32[8]{0:T(128)}, u32[]{:S(2)}) copy-start(s32[8]{0:T(128)} %param.26) | copy-start | bytes 100
  6.0 10.6 %copy-start.6 = (s32[8]{0:T(128)S(1)}, s32[8]{0:T(128)}, u32[]{:S(2)}) copy-start(s32[8]{0:T(128)} %param.27) | copy-start | bytes 100
  6.0 10.6 %copy-start.7 = (s32[8]{0:T(128)S(1)}, s32[8]{0:T(128)}, u32[]{:S(2)}) copy-start(s32[8]{0:T(128)} %param.28) | copy-start | bytes 100
  7.4 33.0 %all-to-all-start = ((bf16[8,127,512]{2,1,0:T(8,128)(2,1)}), bf16[8,127,512]{2,1,0:T(8,128)(2,1)S(1)}, u32[]{:S(2)}, u32[]{:S(2)}) async-start(bf16[8,127,512]{2,1,0:T(8,128)(2,1)} %fusion.11), calls=%async_computation | async-start | bytes 2097152 | tf_op jit(solution)/shard_map/all_to_all | solution.py:284
  15.4 3.5 %copy-start.11 = (bf16[4608,128]{1,0:T(8,128)(2,1)S(1)}, bf16[4608,128]{1,0:T(8,128)(2,1)}, u32[]{:S(2)}) copy-start(bf16[4608,128]{1,0:T(8,128)(2,1)} %vp_ref.3) | copy-start | bytes 3538948
  40.4 16.4 %copy-start.1 = (bf16[8,127,512]{2,1,0:T(8,128)(2,1)}, bf16[8,127,512]{2,1,0:T(8,128)(2,1)S(1)}, u32[]{:S(2)}) copy-start(bf16[8,127,512]{2,1,0:T(8,128)(2,1)S(1)} %all-to-all-done) | copy-start | bytes 3121156
  40.4 19.3 %all-to-all-start.1 = ((bf16[8,127,256]{2,1,0:T(8,128)(2,1)}), bf16[8,127,256]{2,1,0:T(8,128)(2,1)}, u32[]{:S(2)}, u32[]{:S(2)}) async-start(bf16[8,127,256]{2,1,0:T(8,128)(2,1)} %fusion.36), calls=%async_computation.1 | async-start | bytes 1048576 | tf_op jit(solution)/shard_map/all_to_all | solution.py:291
  59.8 19.4 %all-to-all-start.2 = ((bf16[8,127,256]{2,1,0:T(8,128)(2,1)}), bf16[8,127,256]{2,1,0:T(8,128)(2,1)S(1)}, u32[]{:S(2)}, u32[]{:S(2)}) async-start(bf16[8,127,256]{2,1,0:T(8,128)(2,1)} %fusion.34), calls=%async_computation.2 | async-start | bytes 1048576 | tf_op jit(solution)/shard_map/all_to_all | solution.py:291
  82.6 1.3 copy-start.2
  83.9 2.8 %collective-permute-start = (bf16[2,512,512]{2,1,0:T(8,128)(2,1)S(1)}, bf16[2,512,512]{2,1,0:T(8,128)(2,1)}, u32[]{:S(2)}, u32[]{:S(2)}) collective-permute-start(bf16[2,512,512]{2,1,0:T(8,128)(2,1)S(1)} %pad_maximum_fusion.2), channel_id=1, source_target_pairs={{0,1},{1,0},{2,3},{3,2},{4,5},{5,4},{6,7},{7,6},{8,9},{9,8},{10,11... | collective-permute-start | bytes 3145736 | tf_op jit(solution)/shard_map/ppermute | solution.py:185
  88.8 14.3 %collective-permute-start.1 = (bf16[512,512]{1,0:T(8,128)(2,1)}, bf16[512,512]{1,0:T(8,128)(2,1)}, u32[]{:S(2)}, u32[]{:S(2)}) collective-permute-start(bf16[512,512]{1,0:T(8,128)(2,1)} %fusion.16), channel_id=1, source_target_pairs={{0,2},{1,3},{2,0},{3,1},{4,6},{5,7},{6,4},{7,5},{8,10},{9,11},{10,... | collective-permute-start | bytes 1572872 | tf_op jit(solution)/shard_map/ppermute | solution.py:190
  104.9 13.2 %collective-permute-start.3 = (bf16[512,512]{1,0:T(8,128)(2,1)S(1)}, bf16[512,512]{1,0:T(8,128)(2,1)S(1)}, u32[]{:S(2)}, u32[]{:S(2)}) collective-permute-start(bf16[512,512]{1,0:T(8,128)(2,1)S(1)} %fusion.19), channel_id=1, source_target_pairs={{0,2},{1,3},{2,0},{3,1},{4,6},{5,7},{6,4},{7,5},{8,10},{9,11},{10,... | collective-permute-start | bytes 1572872 | tf_op jit(solution)/shard_map/ppermute | solution.py:219
  106.5 11.6 %collective-permute-start.2 = (bf16[512,512]{1,0:T(8,128)(2,1)S(1)}, bf16[512,512]{1,0:T(8,128)(2,1)}, u32[]{:S(2)}, u32[]{:S(2)}) collective-permute-start(bf16[512,512]{1,0:T(8,128)(2,1)S(1)} %fusion.19), channel_id=1, source_target_pairs={{0,1},{1,0},{2,3},{3,2},{4,5},{5,4},{6,7},{7,6},{8,9},{9,8},{10,11... | collective-permute-start | bytes 1572872 | tf_op jit(solution)/shard_map/ppermute | solution.py:218
  118.1 2.0 %collective-permute-start.4 = (bf16[512,512]{1,0:T(8,128)(2,1)S(1)}, bf16[512,512]{1,0:T(8,128)(2,1)}, u32[]{:S(2)}, u32[]{:S(2)}) collective-permute-start(bf16[512,512]{1,0:T(8,128)(2,1)S(1)} %collective-permute-done.3), channel_id=1, source_target_pairs={{0,1},{1,0},{2,3},{3,2},{4,5},{5,4},{6,7},{7,6},{8,9},{9,8},{10,11... | collective-permute-start | bytes 1572872 | tf_op jit(solution)/shard_map/ppermute | solution.py:220
  121.6 2.2 %copy-start.8 = (bf16[2048,1024]{1,0:T(8,128)(2,1)S(1)}, bf16[2048,1024]{1,0:T(8,128)(2,1)}, u32[]{:S(2)}) copy-start(bf16[2048,1024]{1,0:T(8,128)(2,1)} %param.33) | copy-start | bytes 12582916
  121.8 2.0 %copy-start.12 = (f32[2048]{0:T(1024)S(1)}, f32[2048]{0:T(1024)}, u32[]{:S(2)}) copy-start(f32[2048]{0:T(1024)} %param.32) | copy-start | bytes 24580
  123.8 2.4 %copy-start.9 = (bf16[2048,1024]{1,0:T(8,128)(2,1)S(1)}, bf16[2048,1024]{1,0:T(8,128)(2,1)}, u32[]{:S(2)}) copy-start(bf16[2048,1024]{1,0:T(8,128)(2,1)} %param.34) | copy-start | bytes 12582916
  126.2 3.3 %copy-start.10 = (bf16[1024,2048]{1,0:T(8,128)(2,1)S(1)}, bf16[1024,2048]{1,0:T(8,128)(2,1)}, u32[]{:S(2)}) copy-start(bf16[1024,2048]{1,0:T(8,128)(2,1)} %param.35) | copy-start | bytes 12582916
  129.5 4.3 %copy-start.13 = (bf16[512,1024]{1,0:T(8,128)(2,1)}, bf16[512,1024]{1,0:T(8,128)(2,1)S(1)}, u32[]{:S(2)}) copy-start(bf16[512,1024]{1,0:T(8,128)(2,1)S(1)} %multiply_convert_fusion) | copy-start | bytes 3145732
  131.1 2.7 %collective-permute-start.5 = (bf16[2,512,512]{2,1,0:T(8,128)(2,1)S(1)}, bf16[2,512,512]{2,1,0:T(8,128)(2,1)S(1)}, u32[]{:S(2)}, u32[]{:S(2)}) collective-permute-start(bf16[2,512,512]{2,1,0:T(8,128)(2,1)S(1)} %pad_maximum_fusion.3), channel_id=1, source_target_pairs={{0,1},{1,0},{2,3},{3,2},{4,5},{5,4},{6,7},{7,6},{8,9},{9,8},{10,11... | collective-permute-start | bytes 3145736 | tf_op jit(solution)/shard_map/ppermute | solution.py:204
  133.8 1.5 copy-start.3
  135.4 19.3 %collective-permute-start.6 = (bf16[512,512]{1,0:T(8,128)(2,1)}, bf16[512,512]{1,0:T(8,128)(2,1)S(1)}, u32[]{:S(2)}, u32[]{:S(2)}) collective-permute-start(bf16[512,512]{1,0:T(8,128)(2,1)} %fusion.12), channel_id=1, source_target_pairs={{0,2},{1,3},{2,0},{3,1},{4,6},{5,7},{6,4},{7,5},{8,10},{9,11},{10,... | collective-permute-start | bytes 1572872 | tf_op jit(solution)/shard_map/ppermute | solution.py:206
  152.3 2.4 %copy-start.4 = (bf16[2,512,512]{2,1,0:T(8,128)(2,1)S(1)}, bf16[2,512,512]{2,1,0:T(8,128)(2,1)}, u32[]{:S(2)}) copy-start(bf16[2,512,512]{2,1,0:T(8,128)(2,1)} %copy-done.3) | copy-start | bytes 3145732
  156.9 29.6 %all-to-all-start.3 = ((bf16[8,127,512]{2,1,0:T(8,128)(2,1)}), bf16[8,127,512]{2,1,0:T(8,128)(2,1)S(1)}, u32[]{:S(2)}, u32[]{:S(2)}) async-start(bf16[8,127,512]{2,1,0:T(8,128)(2,1)} %broadcast_select_fusion), calls=%async_computation.3 | async-start | bytes 2097152 | tf_op jit(solution)/shard_map/all_to_all | solution.py:317

commit v16 on v15

--- a/solution.py
+++ b/solution.py
@@ -109,19 +109,20 @@
     lanes = [
         jnp.where((owner == j)[None, :, None], q, jnp.zeros((), q.dtype)) for j in range(kv)
     ]
-    q_ext = jnp.concatenate(lanes, axis=2)
+    q_ext = jnp.concatenate(lanes, axis=2) * jnp.asarray(SCALE, q.dtype)
     s_c = jnp.einsum("rhc,tc->rht", q_ext, pool_keys[:cached], preferred_element_type=jnp.float32)
     s_n = jnp.einsum("rhc,tc->rht", q_ext, new_keys[:DEC], preferred_element_type=jnp.float32)
-    s_c = jnp.where(decode_mask[:, None, :cached], s_c * SCALE, MASKED_SCORE)
-    s_n = jnp.where(decode_mask[:, None, cached:], s_n * SCALE, MASKED_SCORE)
+    s_c = jnp.where(decode_mask[:, None, :cached], s_c, MASKED_SCORE)
+    s_n = jnp.where(decode_mask[:, None, cached:], s_n, MASKED_SCORE)
     highest = jnp.maximum(
         jnp.max(s_c, axis=2, keepdims=True), jnp.max(s_n, axis=2, keepdims=True)
     )
     e_c = jnp.exp(s_c - highest)
     e_n = jnp.exp(s_n - highest)
     totals = jnp.sum(e_c, axis=2, keepdims=True) + jnp.sum(e_n, axis=2, keepdims=True)
-    p_c = (e_c / totals).astype(jnp.bfloat16)
-    p_n = (e_n / totals).astype(jnp.bfloat16)
+    inverse = 1.0 / totals
+    p_c = (e_c * inverse).astype(jnp.bfloat16)
+    p_n = (e_n * inverse).astype(jnp.bfloat16)
     full = jnp.einsum(
         "rht,tc->rhc", p_c, pool_values[:cached], preferred_element_type=jnp.float32
     ) + jnp.einsum("rht,tc->rhc", p_n, new_values[:DEC], preferred_element_type=jnp.float32)

time: 190 us -> 190 us (level)
  no operation moved by 1% of the time
where the time goes in v16:
time: 190 us; the launch traced here: 188 us
  waiting for transfers between devices  64 us (34%)
  starting transfers between devices  25.7 us (14%)
  Pallas kernels  24.2 us (13%)
  local copies, waits for them, and re-layouts  20.7 us (11%)
  other arithmetic  19 us (10%)
  between operations  18.5 us (10%)
  matrix products  16.4 us (9%)
    all_to_all x1, waiting for transfers between devices, shards(): lax.all_to_all(picked, 'req', split_axis=0, concat_axis=0, tiled=True)  25.9 us
    pallas_call x2, Pallas kernels, span_attention(): pl.pallas_call(functools.partial(span_kernel, kv_index), out_shape=jax.Sh...  24.2 us
    ppermute x1, waiting for transfers between devices, grp_all_gather(): across = lax.ppermute(block, 'grp', far)  11.6 us
    all_to_all x2, starting transfers between devices, shards(): lax.all_to_all(part, 'req', split_axis=0, concat_axis=0, tiled=True)  10 us
    ppermute x1, waiting for transfers between devices, grp_reduce_scatter(): arrived = lax.ppermute(other.astype(jnp.bfloat16), 'grp', far)  8.6 us
    all_to_all x1, starting transfers between devices, shards(): lax.all_to_all(send_resid, 'req', split_axis=0, concat_axis=0, tiled=True)  7.25 us
    all_to_all x2, waiting for transfers between devices, shards(): lax.all_to_all(part, 'req', split_axis=0, concat_axis=0, tiled=True)  5.36 us
    dot_general x4, matrix products, finish(): jnp.dot(inner, grp_block(down_weight, index, width), preferred_element_ty...  5.32 us
  transfers between devices with their start and end apart: 11, of which 8 were waited for; matrix products, arithmetic and copies ran while one was open for 14% of the time, Pallas kernels for 13%

profile of v16, /device:TPU:0, one launch (start us, length us, event | category | flops | bytes accessed | tf_op | source)
XLA Modules:
  0.0 188.5 jit_solution(8990912747176584553)
XLA Ops:
  6.0 1.4 fusion.9
  7.4 7.3 %all-to-all-start = ((bf16[8,127,512]{2,1,0:T(8,128)(2,1)}), bf16[8,127,512]{2,1,0:T(8,128)(2,1)S(1)}, u32[]{:S(2)}, u32[]{:S(2)}) async-start(bf16[8,127,512]{2,1,0:T(8,128)(2,1)} %fusion.9), calls=%async_computation | async-start | bytes 2097152 | tf_op jit(solution)/shard_map/all_to_all | solution.py:285
  16.7 1.8 fusion.89
  20.4 12.1 %shard_map.154 = bf16[1024,256]{1,0:T(8,128)(2,1)} custom-call(s32[1]{0:T(128)S(6)} %copy.51.start_ref, bf16[1024,512]{1,0:T(8,128)(2,1)} %q_ref.2, bf16[4608,128]{1,0:T(8,128)(2,1)} %kp_ref.3, bf16[4608,128]{1,0:T(8,128)(2,1)} %vp_ref.3, bf16[1024,128]{1,0:T(8,128)(2,1)} %kf_ref.3, bf16[1024,128]{1,0:T(8,128)(2,1)} %vf_ref.3), custom_call_target="tpu_custom_call" | custom-call | flops 17179869184 | bytes 1835008 | tf_op jit(solution)/shard_map/pallas_call | solution.py:89
  35.3 5.2 %all-to-all-done = bf16[8,127,512]{2,1,0:T(8,128)(2,1)S(1)} async-done(((bf16[8,127,512]{2,1,0:T(8,128)(2,1)}), bf16[8,127,512]{2,1,0:T(8,128)(2,1)S(1)}, u32[]{:S(2)}, u32[]{:S(2)}) %all-to-all-start) | async-done | bytes 1040416 | tf_op jit(solution)/shard_map/all_to_all | solution.py:285
  40.4 4.3 %all-to-all-start.1 = ((bf16[8,127,256]{2,1,0:T(8,128)(2,1)}), bf16[8,127,256]{2,1,0:T(8,128)(2,1)}, u32[]{:S(2)}, u32[]{:S(2)}) async-start(bf16[8,127,256]{2,1,0:T(8,128)(2,1)} %fusion.34), calls=%async_computation.1 | async-start | bytes 1048576 | tf_op jit(solution)/shard_map/all_to_all | solution.py:292
  44.8 12.1 %shard_map.155 = bf16[1024,256]{1,0:T(8,128)(2,1)} custom-call(s32[1]{0:T(128)S(6)} %copy.51.start_ref, bf16[1024,512]{1,0:T(8,128)(2,1)} %q_ref.2, bf16[4608,128]{1,0:T(8,128)(2,1)} %kp_ref.3, bf16[4608,128]{1,0:T(8,128)(2,1)} %vp_ref.3, bf16[1024,128]{1,0:T(8,128)(2,1)} %kf_ref.3, bf16[1024,128]{1,0:T(8,128)(2,1)} %vf_ref.3), custom_call_target="tpu_custom_call" | custom-call | flops 17179869184 | bytes 1835008 | tf_op jit(solution)/shard_map/pallas_call | solution.py:89
  59.8 5.7 %all-to-all-start.2 = ((bf16[8,127,256]{2,1,0:T(8,128)(2,1)}), bf16[8,127,256]{2,1,0:T(8,128)(2,1)S(1)}, u32[]{:S(2)}, u32[]{:S(2)}) async-start(bf16[8,127,256]{2,1,0:T(8,128)(2,1)} %fusion.32), calls=%async_computation.2 | async-start | bytes 1048576 | tf_op jit(solution)/shard_map/all_to_all | solution.py:292
  65.5 4.4 %compare_select_fusion.2 = s32[512,1]{0,1:T(1,128)S(1)} fusion(s32[]{:T(128)} %bitcast.15, s32[]{:T(128)} %bitcast.16, s32[]{:T(128)} %bitcast.17, s32[]{:T(128)} %bitcast.18, s32[]{:T(128)} %bitcast.19, s32[]{:T(128)} %bitcast.21, s32[]{:T(128)} %bitcast.20, s32[512,1]{0,1:T(1,128)S(1)} %bitcast.142), kind=kLoop, calls=%fused_computation.138 | loop fusion | flops 7680 | bytes 4124 | tf_op jit(solution)/shard_map/gather | solution.py:300
  71.8 2.0 %gather_fusion.1 = bf16[512,256]{1,0:T(8,128)(2,1)S(1)} fusion(bf16[1016,256]{1,0:T(8,128)(2,1)S(1)} %reshape.399, s32[1024]{0:T(1024)S(1)} %pad_clamp_fusion), kind=kCustom, calls=%fused_computation.1 | custom fusion | bytes 526336 | tf_op jit(solution)/shard_map/gather | solution.py:303
  73.8 5.4 %all-to-all-done.2 = bf16[8,127,256]{2,1,0:T(8,128)(2,1)S(1)} async-done(((bf16[8,127,256]{2,1,0:T(8,128)(2,1)}), bf16[8,127,256]{2,1,0:T(8,128)(2,1)S(1)}, u32[]{:S(2)}, u32[]{:S(2)}) %all-to-all-start.2) | async-done | bytes 520224 | tf_op jit(solution)/shard_map/all_to_all | solution.py:292
  79.3 2.0 %gather_fusion.2 = bf16[512,256]{1,0:T(8,128)(2,1)S(1)} fusion(bf16[1016,256]{1,0:T(8,128)(2,1)S(1)} %reshape.400, s32[1024]{0:T(1024)S(1)} %pad_clamp_fusion), kind=kCustom, calls=%fused_computation.2 | custom fusion | bytes 526336 | tf_op jit(solution)/shard_map/gather | solution.py:303
  83.9 2.8 %collective-permute-done = bf16[2,512,512]{2,1,0:T(8,128)(2,1)} collective-permute-done((bf16[2,512,512]{2,1,0:T(8,128)(2,1)S(1)}, bf16[2,512,512]{2,1,0:T(8,128)(2,1)}, u32[]{:S(2)}, u32[]{:S(2)}) %collective-permute-start) | collective-permute-done | bytes 1048608 | tf_op jit(solution)/shard_map/ppermute | solution.py:186
  86.7 2.1 %fusion.14 = bf16[512,512]{1,0:T(8,128)(2,1)} fusion(bf16[2,512,512]{2,1,0:T(8,128)(2,1)} %collective-permute-done, bf16[512,2048]{1,0:T(8,128)(2,1)} %copy-done.2, s32[]{:T(128)S(6)} %select_n.203), kind=kLoop, calls=%fused_computation.43 | loop fusion | flops 1048576 | bytes 1572868 | tf_op jit(solution)/shard_map/convert_element_type | solution.py:191
  88.8 1.5 collective-permute-start.1
  90.3 1.5 reshape.398
  91.9 2.6 %gather_fusion = bf16[512,512]{1,0:T(8,128)(2,1)} fusion(bf16[1016,512]{1,0:T(8,128)(2,1)S(1)} %reshape.398, s32[1024]{0:T(1024)S(1)} %pad_clamp_fusion), kind=kCustom, calls=%fused_computation | custom fusion | bytes 1050624 | tf_op jit(solution)/shard_map/gather | solution.py:305
  94.5 8.6 %collective-permute-done.1 = bf16[512,512]{1,0:T(8,128)(2,1)} collective-permute-done((bf16[512,512]{1,0:T(8,128)(2,1)}, bf16[512,512]{1,0:T(8,128)(2,1)}, u32[]{:S(2)}, u32[]{:S(2)}) %collective-permute-start.1) | collective-permute-done | bytes 524320 | tf_op jit(solution)/shard_map/ppermute | solution.py:191
  103.1 1.8 fusion.17
  104.9 1.6 collective-permute-start.3
  106.5 11.6 %collective-permute-done.3 = bf16[512,512]{1,0:T(8,128)(2,1)S(1)} collective-permute-done((bf16[512,512]{1,0:T(8,128)(2,1)S(1)}, bf16[512,512]{1,0:T(8,128)(2,1)S(1)}, u32[]{:S(2)}, u32[]{:S(2)}) %collective-permute-start.3) | collective-permute-done | bytes 524320 | tf_op jit(solution)/shard_map/ppermute | solution.py:220
  118.1 2.0 %collective-permute-done.4 = bf16[512,512]{1,0:T(8,128)(2,1)} collective-permute-done((bf16[512,512]{1,0:T(8,128)(2,1)S(1)}, bf16[512,512]{1,0:T(8,128)(2,1)}, u32[]{:S(2)}, u32[]{:S(2)}) %collective-permute-start.4) | collective-permute-done | bytes 524320 | tf_op jit(solution)/shard_map/ppermute | solution.py:221
  120.1 1.5 pad_maximum_fusion
  122.3 1.5 copy-done.9
  123.8 2.4 %fusion.29 = f32[512,1024]{1,0:T(8,128)S(1)} fusion(bf16[2048,1024]{1,0:T(8,128)(2,1)S(1)} %copy-done.9, f32[2048]{0:T(1024)S(1)} %copy-done.12, f32[512]{0:T(512)S(1)} %add_rsqrt_fusion, bf16[512,512]{1,0:T(8,128)(2,1)S(1)} %get-tuple-element.19, bf16[512,512]{1,0:T(8,128)(2,1)S(1)} %get-tuple-element.20, bf16[512,512]{1,0:T(8,128)(2,1)S(1)} %get-tuple-element.21, ...), kind=kOutput, calls=%fused_computation.63 | convolution fusion | flops 2159017984 | bytes 8398848 | tf_op jit(solution)/shard_map/dot_general | solution.py:236
  126.2 3.3 %multiply_convert_fusion = bf16[512,1024]{1,0:T(8,128)(2,1)S(1)} fusion(f32[512,1024]{1,0:T(8,128)S(1)} %fusion.29, bf16[2048,1024]{1,0:T(8,128)(2,1)S(1)} %copy-done.10, f32[2048]{0:T(1024)S(1)} %copy-done.12, f32[512]{0:T(512)S(1)} %add_rsqrt_fusion, bf16[512,512]{1,0:T(8,128)(2,1)S(1)} %get-tuple-element.19, bf16[512,512]{1,0:T(8,128)(2,1)S(1)} %get-tuple-element.20, ...), kind=kOutput, calls=%fused_computation.16 | convolution fusion | flops 2162163712 | bytes 9447424 | tf_op jit(solution)/shard_map/dot_general | solution.py:237
  131.3 2.5 %collective-permute-done.5 = bf16[2,512,512]{2,1,0:T(8,128)(2,1)S(1)} collective-permute-done((bf16[2,512,512]{2,1,0:T(8,128)(2,1)S(1)}, bf16[2,512,512]{2,1,0:T(8,128)(2,1)S(1)}, u32[]{:S(2)}, u32[]{:S(2)}) %collective-permute-start.5) | collective-permute-done | bytes 1048608 | tf_op jit(solution)/shard_map/ppermute | solution.py:205
  133.8 1.5 fusion.10
  135.4 1.5 collective-permute-start.6
  152.3 2.3 %fusion.4 = f32[512,512]{1,0:T(8,128)S(1)} fusion(bf16[512,1024]{1,0:T(8,128)(2,1)} %copy-done.13, bf16[1024,2048]{1,0:T(8,128)(2,1)} %param.35, s32[]{:T(128)S(6)} %select_n.200), kind=kOutput, calls=%fused_computation.22 | convolution fusion | flops 537395200 | bytes 3145732 | tf_op jit(solution)/shard_map/dot_general | solution.py:240
  156.9 3.6 %all-to-all-start.3 = ((bf16[8,127,512]{2,1,0:T(8,128)(2,1)}), bf16[8,127,512]{2,1,0:T(8,128)(2,1)S(1)}, u32[]{:S(2)}, u32[]{:S(2)}) async-start(bf16[8,127,512]{2,1,0:T(8,128)(2,1)} %broadcast_select_fusion), calls=%async_computation.3 | async-start | bytes 2097152 | tf_op jit(solution)/shard_map/all_to_all | solution.py:318
  160.6 25.9 %all-to-all-done.3 = bf16[8,127,512]{2,1,0:T(8,128)(2,1)S(1)} async-done(((bf16[8,127,512]{2,1,0:T(8,128)(2,1)}), bf16[8,127,512]{2,1,0:T(8,128)(2,1)S(1)}, u32[]{:S(2)}, u32[]{:S(2)}) %all-to-all-start.3) | async-done | bytes 1040416 | tf_op jit(solution)/shard_map/all_to_all | solution.py:318
  (98 shorter events, 24.2 us)
Async XLA Ops:
  0.0 81.3 %copy-start = (bf16[512,2048]{1,0:T(8,128)(2,1)S(1)}, bf16[512,2048]{1,0:T(8,128)(2,1)}, u32[]{:S(2)}) copy-start(bf16[512,2048]{1,0:T(8,128)(2,1)} %param.31) | copy-start | bytes 6291460
  6.0 9.4 %slice-start = ((bf16[1024,512]{1,0:T(8,128)(2,1)}), bf16[8,512]{1,0:T(8,128)(2,1)S(1)}, s32[]{:S(2)}) async-start(bf16[1024,512]{1,0:T(8,128)(2,1)} %q_ref.2), calls=%async_computation.4 | async-start | bytes 16384 | tf_op jit(solution)/shard_map/slice | solution.py:107
  6.0 10.6 %copy-start.6 = (s32[8]{0:T(128)S(1)}, s32[8]{0:T(128)}, u32[]{:S(2)}) copy-start(s32[8]{0:T(128)} %param.26) | copy-start | bytes 100
  6.0 10.6 %copy-start.7 = (s32[8]{0:T(128)S(1)}, s32[8]{0:T(128)}, u32[]{:S(2)}) copy-start(s32[8]{0:T(128)} %param.27) | copy-start | bytes 100
  6.0 10.6 %copy-start.8 = (s32[8]{0:T(128)S(1)}, s32[8]{0:T(128)}, u32[]{:S(2)}) copy-start(s32[8]{0:T(128)} %param.28) | copy-start | bytes 100
  7.4 33.0 %all-to-all-start = ((bf16[8,127,512]{2,1,0:T(8,128)(2,1)}), bf16[8,127,512]{2,1,0:T(8,128)(2,1)S(1)}, u32[]{:S(2)}, u32[]{:S(2)}) async-start(bf16[8,127,512]{2,1,0:T(8,128)(2,1)} %fusion.9), calls=%async_computation | async-start | bytes 2097152 | tf_op jit(solution)/shard_map/all_to_all | solution.py:285
  15.4 3.5 %copy-start.3 = (bf16[4608,128]{1,0:T(8,128)(2,1)S(1)}, bf16[4608,128]{1,0:T(8,128)(2,1)}, u32[]{:S(2)}) copy-start(bf16[4608,128]{1,0:T(8,128)(2,1)} %vp_ref.3) | copy-start | bytes 3538948
  40.4 16.4 %copy-start.1 = (bf16[8,127,512]{2,1,0:T(8,128)(2,1)}, bf16[8,127,512]{2,1,0:T(8,128)(2,1)S(1)}, u32[]{:S(2)}) copy-start(bf16[8,127,512]{2,1,0:T(8,128)(2,1)S(1)} %all-to-all-done) | copy-start | bytes 3121156
  40.4 19.3 %all-to-all-start.1 = ((bf16[8,127,256]{2,1,0:T(8,128)(2,1)}), bf16[8,127,256]{2,1,0:T(8,128)(2,1)}, u32[]{:S(2)}, u32[]{:S(2)}) async-start(bf16[8,127,256]{2,1,0:T(8,128)(2,1)} %fusion.34), calls=%async_computation.1 | async-start | bytes 1048576 | tf_op jit(solution)/shard_map/all_to_all | solution.py:292
  59.8 19.4 %all-to-all-start.2 = ((bf16[8,127,256]{2,1,0:T(8,128)(2,1)}), bf16[8,127,256]{2,1,0:T(8,128)(2,1)S(1)}, u32[]{:S(2)}, u32[]{:S(2)}) async-start(bf16[8,127,256]{2,1,0:T(8,128)(2,1)} %fusion.32), calls=%async_computation.2 | async-start | bytes 1048576 | tf_op jit(solution)/shard_map/all_to_all | solution.py:292
  82.6 1.3 copy-start.2
  83.9 2.8 %collective-permute-start = (bf16[2,512,512]{2,1,0:T(8,128)(2,1)S(1)}, bf16[2,512,512]{2,1,0:T(8,128)(2,1)}, u32[]{:S(2)}, u32[]{:S(2)}) collective-permute-start(bf16[2,512,512]{2,1,0:T(8,128)(2,1)S(1)} %pad_maximum_fusion.2), channel_id=1, source_target_pairs={{0,1},{1,0},{2,3},{3,2},{4,5},{5,4},{6,7},{7,6},{8,9},{9,8},{10,11... | collective-permute-start | bytes 3145736 | tf_op jit(solution)/shard_map/ppermute | solution.py:186
  88.8 14.3 %collective-permute-start.1 = (bf16[512,512]{1,0:T(8,128)(2,1)}, bf16[512,512]{1,0:T(8,128)(2,1)}, u32[]{:S(2)}, u32[]{:S(2)}) collective-permute-start(bf16[512,512]{1,0:T(8,128)(2,1)} %fusion.14), channel_id=1, source_target_pairs={{0,2},{1,3},{2,0},{3,1},{4,6},{5,7},{6,4},{7,5},{8,10},{9,11},{10,... | collective-permute-start | bytes 1572872 | tf_op jit(solution)/shard_map/ppermute | solution.py:191
  104.9 13.2 %collective-permute-start.3 = (bf16[512,512]{1,0:T(8,128)(2,1)S(1)}, bf16[512,512]{1,0:T(8,128)(2,1)S(1)}, u32[]{:S(2)}, u32[]{:S(2)}) collective-permute-start(bf16[512,512]{1,0:T(8,128)(2,1)S(1)} %fusion.17), channel_id=1, source_target_pairs={{0,2},{1,3},{2,0},{3,1},{4,6},{5,7},{6,4},{7,5},{8,10},{9,11},{10,... | collective-permute-start | bytes 1572872 | tf_op jit(solution)/shard_map/ppermute | solution.py:220
  106.5 11.6 %collective-permute-start.2 = (bf16[512,512]{1,0:T(8,128)(2,1)S(1)}, bf16[512,512]{1,0:T(8,128)(2,1)}, u32[]{:S(2)}, u32[]{:S(2)}) collective-permute-start(bf16[512,512]{1,0:T(8,128)(2,1)S(1)} %fusion.17), channel_id=1, source_target_pairs={{0,1},{1,0},{2,3},{3,2},{4,5},{5,4},{6,7},{7,6},{8,9},{9,8},{10,11... | collective-permute-start | bytes 1572872 | tf_op jit(solution)/shard_map/ppermute | solution.py:219
  118.1 2.0 %collective-permute-start.4 = (bf16[512,512]{1,0:T(8,128)(2,1)S(1)}, bf16[512,512]{1,0:T(8,128)(2,1)}, u32[]{:S(2)}, u32[]{:S(2)}) collective-permute-start(bf16[512,512]{1,0:T(8,128)(2,1)S(1)} %collective-permute-done.3), channel_id=1, source_target_pairs={{0,1},{1,0},{2,3},{3,2},{4,5},{5,4},{6,7},{7,6},{8,9},{9,8},{10,11... | collective-permute-start | bytes 1572872 | tf_op jit(solution)/shard_map/ppermute | solution.py:221
  121.6 2.2 %copy-start.9 = (bf16[2048,1024]{1,0:T(8,128)(2,1)S(1)}, bf16[2048,1024]{1,0:T(8,128)(2,1)}, u32[]{:S(2)}) copy-start(bf16[2048,1024]{1,0:T(8,128)(2,1)} %param.33) | copy-start | bytes 12582916
  121.8 2.0 %copy-start.12 = (f32[2048]{0:T(1024)S(1)}, f32[2048]{0:T(1024)}, u32[]{:S(2)}) copy-start(f32[2048]{0:T(1024)} %param.32) | copy-start | bytes 24580
  123.8 2.4 %copy-start.10 = (bf16[2048,1024]{1,0:T(8,128)(2,1)S(1)}, bf16[2048,1024]{1,0:T(8,128)(2,1)}, u32[]{:S(2)}) copy-start(bf16[2048,1024]{1,0:T(8,128)(2,1)} %param.34) | copy-start | bytes 12582916
  126.2 3.3 %copy-start.11 = (bf16[1024,2048]{1,0:T(8,128)(2,1)S(1)}, bf16[1024,2048]{1,0:T(8,128)(2,1)}, u32[]{:S(2)}) copy-start(bf16[1024,2048]{1,0:T(8,128)(2,1)} %param.35) | copy-start | bytes 12582916
  129.5 4.3 %copy-start.13 = (bf16[512,1024]{1,0:T(8,128)(2,1)}, bf16[512,1024]{1,0:T(8,128)(2,1)S(1)}, u32[]{:S(2)}) copy-start(bf16[512,1024]{1,0:T(8,128)(2,1)S(1)} %multiply_convert_fusion) | copy-start | bytes 3145732
  131.1 2.7 %collective-permute-start.5 = (bf16[2,512,512]{2,1,0:T(8,128)(2,1)S(1)}, bf16[2,512,512]{2,1,0:T(8,128)(2,1)S(1)}, u32[]{:S(2)}, u32[]{:S(2)}) collective-permute-start(bf16[2,512,512]{2,1,0:T(8,128)(2,1)S(1)} %pad_maximum_fusion.3), channel_id=1, source_target_pairs={{0,1},{1,0},{2,3},{3,2},{4,5},{5,4},{6,7},{7,6},{8,9},{9,8},{10,11... | collective-permute-start | bytes 3145736 | tf_op jit(solution)/shard_map/ppermute | solution.py:205
  133.8 1.5 copy-start.4
  135.4 19.3 %collective-permute-start.6 = (bf16[512,512]{1,0:T(8,128)(2,1)}, bf16[512,512]{1,0:T(8,128)(2,1)S(1)}, u32[]{:S(2)}, u32[]{:S(2)}) collective-permute-start(bf16[512,512]{1,0:T(8,128)(2,1)} %fusion.10), channel_id=1, source_target_pairs={{0,2},{1,3},{2,0},{3,1},{4,6},{5,7},{6,4},{7,5},{8,10},{9,11},{10,... | collective-permute-start | bytes 1572872 | tf_op jit(solution)/shard_map/ppermute | solution.py:207
  152.3 2.4 %copy-start.5 = (bf16[2,512,512]{2,1,0:T(8,128)(2,1)S(1)}, bf16[2,512,512]{2,1,0:T(8,128)(2,1)}, u32[]{:S(2)}) copy-start(bf16[2,512,512]{2,1,0:T(8,128)(2,1)} %copy-done.4) | copy-start | bytes 3145732
  156.9 29.6 %all-to-all-start.3 = ((bf16[8,127,512]{2,1,0:T(8,128)(2,1)}), bf16[8,127,512]{2,1,0:T(8,128)(2,1)S(1)}, u32[]{:S(2)}, u32[]{:S(2)}) async-start(bf16[8,127,512]{2,1,0:T(8,128)(2,1)} %broadcast_select_fusion), calls=%async_computation.3 | async-start | bytes 2097152 | tf_op jit(solution)/shard_map/all_to_all | solution.py:318
